TPU v7x, 32 devices: a whole 2x2x4 slice. The times are simulated.
32 devices in a mesh: ctx: 8 (over z, y), ch: 4 (over x, core).
Axes of the slice: x: 2, y: 2, z: 4, core: 2. Of those that a mesh axis runs over, the one named last changes fastest.
Arguments:
- projected: bfloat16 [3, 8192, 4096], P(None, 'ctx', 'ch'), may hold values from -6 to 6
- tap_weights: bfloat16 [3, 3, 4096], P(None, None, 'ch'), may hold values from -3.59375 to 3.59375
- pole_rates: float32 [16, 4096], P(None, 'ch'), may hold values from 1.2207031e-05 to 0.0625
- residues: float32 [16, 4096], P(None, 'ch'), may hold values from -1.4143862 to 1.4143862
- long_bias: float32 [4096], P('ch'), may hold values from -4 to 4
- out_weight: bfloat16 [4096, 4096], P(None, 'ch'), may hold values from -0.09375 to 0.09375
Outputs:
- mixed_out: bfloat16 [8192, 4096], P('ctx', 'ch')
All inputs are finite; a program needn't handle non-finite values.
Results may differ from a plain program's by a relative error of at most 0.012.
Values may be sent and summed in bfloat16 or wider, within the bound.
No kernel may reach another device: no remote copies, remote signals or barrier semaphores. Data moves between devices by JAX's collectives and lax.ppermute only.
A program may use at most 256 MiB of HBM per device.

v0:
```python
import jax
import jax.numpy as jnp
from jax import lax
from jax.sharding import PartitionSpec as P

BLOCK = 64


def shifted(value, axis, steps):
    count = lax.axis_size(axis)
    initial, last = (max(0, -steps), min(count, count - steps))
    return lax.ppermute(value, axis, [(source, source + steps) for source in range(initial, last)])


def make_tables(pole_rates, residues, block_size):
    lag_steps = jnp.arange(block_size, dtype=jnp.float32)
    powers = jnp.exp(-pole_rates[None, :, :] * lag_steps[:, None, None])
    kernel = jnp.sum(powers * residues[None, :, :], axis=1)
    offsets = (
        jnp.arange(block_size, dtype=jnp.int32)[:, None]
        - jnp.arange(block_size, dtype=jnp.int32)[None, :]
    )
    toeplitz = jnp.where(
        (offsets >= 0)[:, :, None], kernel[jnp.maximum(offsets, 0)], jnp.float32(0.0)
    )
    end_weights = powers[::-1]
    read_weights = powers * jnp.exp(-pole_rates)[None, :, :] * residues[None, :, :]
    block_decay = jnp.exp(-pole_rates * block_size)
    return (toeplitz, end_weights, read_weights, block_decay)


def combine(earlier, latter):
    return (earlier[0] * latter[0], latter[0] * earlier[1] + latter[1])


def channel_conv(rows_last, pole_rates, residues):
    highest = lax.Precision.HIGHEST
    channel_count = rows_last.shape[0]
    length = rows_last.shape[1]
    block_count = length // BLOCK
    pole_count = pole_rates.shape[0]
    toeplitz, end_weights, read_weights, block_decay = make_tables(pole_rates, residues, BLOCK)
    toeplitz_c = jnp.transpose(toeplitz, (2, 0, 1))
    blocks = rows_last.astype(jnp.float32).reshape(channel_count, block_count, BLOCK)
    inner_part = jnp.einsum("cij,cnj->cni", toeplitz_c, blocks, precision=highest)
    closing = jnp.einsum("jpc,cnj->ncp", end_weights, blocks, precision=highest)
    closing = closing.reshape(block_count, channel_count * pole_count)
    decay_row = jnp.transpose(block_decay).reshape(1, channel_count * pole_count)
    decays = jnp.broadcast_to(decay_row, closing.shape)
    _, states = lax.associative_scan(combine, (decays, closing), axis=0)
    before_state = jnp.concatenate([jnp.zeros_like(states[:1]), states[:-1]], 0)
    before_state = before_state.reshape(block_count, channel_count, pole_count)
    carried = jnp.einsum("ipc,ncp->cni", read_weights, before_state, precision=highest)
    return (inner_part + carried).reshape(channel_count, length)


def shards(projected, tap_weights, pole_rates, residues, long_bias, out_weight):
    row_count = projected.shape[1]
    rim_rows = tap_weights.shape[0] - 1
    prior_rows = shifted(projected[:, row_count - rim_rows :], "ctx", 1)
    extended = jnp.concatenate([prior_rows, projected], 1)
    featured = jnp.zeros(projected.shape, jnp.float32)
    for tap_index in range(rim_rows + 1):
        lead_row = rim_rows - tap_index
        featured = featured + tap_weights[tap_index].astype(jnp.float32)[:, None, :] * extended[
            :, lead_row : lead_row + row_count
        ].astype(jnp.float32)
    mixed_input = (featured[1] * featured[2]).astype(jnp.bfloat16)
    channel_major = jnp.transpose(mixed_input)
    spread = lax.all_to_all(channel_major, "ctx", split_axis=0, concat_axis=1, tiled=True)
    share_width = spread.shape[0]
    first_channel = lax.axis_index("ctx") * share_width
    rates_here = lax.dynamic_slice_in_dim(pole_rates, first_channel, share_width, 1)
    residues_here = lax.dynamic_slice_in_dim(residues, first_channel, share_width, 1)
    long_part = channel_conv(spread, rates_here, residues_here).astype(jnp.bfloat16)
    returned = lax.all_to_all(long_part, "ctx", split_axis=1, concat_axis=0, tiled=True)
    long_mix = jnp.transpose(returned)
    gated_mix = featured[0] * (
        long_mix.astype(jnp.float32) + long_bias[None, :] * mixed_input.astype(jnp.float32)
    )
    gated_mix = gated_mix.astype(jnp.bfloat16)
    mixed_out = jnp.dot(
        lax.all_gather(gated_mix, "ch", axis=1, tiled=True),
        out_weight,
        preferred_element_type=jnp.float32,
    )
    return mixed_out.astype(jnp.bfloat16)


def solution(mesh):
    in_specs = (
        P(None, "ctx", "ch"),
        P(None, None, "ch"),
        P(None, "ch"),
        P(None, "ch"),
        P("ch"),
        P(None, "ch"),
    )
    out_specs = P("ctx", "ch")
    return jax.shard_map(shards, mesh=mesh, in_specs=in_specs, out_specs=out_specs, check_vma=False)
```

profile of v0, /device:TPU:1, one launch (start us, length us, event | category | flops | bytes accessed | tf_op | source)
XLA Modules:
  0.0 405.0 jit_solution(4329657434524788336)
XLA Ops:
  7.4 4.0 collective-permute-start
  12.1 8.7 %copy.43 = bf16[3,1024,1024]{1,2,0:T(8,128)(2,1)} copy(bf16[3,1024,1024]{2,1,0:T(8,128)(2,1)} %param.6) | data formatting | bytes 12582912 | tf_op args[0]
  21.2 15.7 %multiply_add_fusion = f32[3,1024,1024]{1,2,0:T(8,128)S(1)} fusion(bf16[3,1024,1024]{1,2,0:T(8,128)(2,1)} %copy.43, bf16[3,2,1024]{1,2,0:T(8,128)(2,1)S(1)} %copy.44, f32[3,1024]{1,0:T(4,128)S(1)} %get-tuple-element.12, f32[3,1024]{1,0:T(4,128)S(1)} %get-tuple-element.13, f32[3,1024]{1,0:T(4,128)S(1)} %get-tuple-element.11), kind=kLoop, calls=%fused_computation.1 | loop fusion | flops 44040192 | bytes 18923520 | tf_op jit(solution)/shard_map/add | solution.py:65
  36.9 4.5 %copy-done = f32[3,1024,1024]{1,2,0:T(8,128)} copy-done((f32[3,1024,1024]{1,2,0:T(8,128)}, f32[3,1024,1024]{1,2,0:T(8,128)S(1)}, u32[]{:S(2)}) %copy-start) | copy-done | bytes 12582936
  43.4 4.6 %all-to-all-start = ((bf16[8,128,1024]{2,1,0:T(8,128)(2,1)}), bf16[8,128,1024]{2,1,0:T(8,128)(2,1)}, u32[]{:S(2)}, u32[]{:S(2)}) async-start(bf16[8,128,1024]{2,1,0:T(8,128)(2,1)} %bitcast.6), calls=%async_computation | async-start | bytes 4194304 | tf_op jit(solution)/shard_map/all_to_all | solution.py:70
  52.3 10.8 %gather_fusion = f32[4096,128]{1,0:T(8,128)S(1)} fusion(f32[64,128]{1,0:T(8,128)S(1)} %copy.49, s32[4096]{0:T(1024)S(1)} %broadcast_clamp_fusion), kind=kCustom, calls=%fused_computation | custom fusion | bytes 4210688 | tf_op jit(solution)/shard_map/gather | solution.py:24
  63.1 4.6 %copy.50 = f32[64,64,128]{1,0,2:T(8,128)} copy(f32[64,64,128]{2,1,0:T(8,128)S(1)} %bitcast.56) | data formatting | bytes 4194304 | tf_op jit(solution)/shard_map/gather | solution.py:24
  69.6 25.6 %all-to-all-done = bf16[8,128,1024]{2,1,0:T(8,128)(2,1)} async-done(((bf16[8,128,1024]{2,1,0:T(8,128)(2,1)}), bf16[8,128,1024]{2,1,0:T(8,128)(2,1)}, u32[]{:S(2)}, u32[]{:S(2)}) %all-to-all-start) | async-done | bytes 2097184 | tf_op jit(solution)/shard_map/all_to_all | solution.py:70
  95.2 3.9 copy.46
  99.1 3.8 copy.51
  103.0 3.0 fusion.25
  105.9 20.3 %slice.187 = f32[64,2048]{0,1:T(8,128)} slice(f32[128,2048]{0,1:T(8,128)S(1)} %bitcast.52), slice={[0:127:2], [0:2048:1]} | slice | bytes 1048576 | tf_op jit(solution)/shard_map/slice | solution.py:50
  126.2 21.9 %slice.188 = f32[64,2048]{0,1:T(8,128)} slice(f32[128,2048]{0,1:T(8,128)S(1)} %bitcast.53), slice={[1:128:2], [0:2048:1]} | slice | bytes 1048576 | tf_op jit(solution)/shard_map/slice | solution.py:50
  148.1 2.4 copy.62
  150.5 2.4 copy.63
  152.8 2.1 multiply_add_fusion.1
  182.4 21.6 %slice.226 = f32[63,2048]{0,1:T(8,128)} slice(f32[128,2048]{0,1:T(8,128)S(1)} %bitcast.54), slice={[2:128:2], [0:2048:1]} | slice | bytes 1032192 | tf_op jit(solution)/shard_map/slice | solution.py:50
  218.8 2.7 pad.55
  223.5 4.6 %pad.116 = f32[128,2048]{1,0:T(8,128)} pad(f32[64,2048]{1,0:T(8,128)} %add.128, f32[]{:T(128)} %constant.5.clone.1), padding=1_0_1x0_0_0 | pad | bytes 1572868
  228.1 2.4 copy.64
  230.5 2.2 fusion.11
  235.1 2.1 pad.76
  237.2 2.3 slice_add_fusion.2
  241.5 4.2 %fusion.4 = f32[128,128,64]{1,2,0:T(8,128)S(1)} fusion(bf16[128,128,64]{1,2,0:T(8,128)(2,1)S(1)} %copy.51, f32[64,64,128]{1,0,2:T(8,128)} %copy.50, pred[64,64]{1,0:T(8,128)(4,1)S(1)} %copy-done.8), kind=kOutput, calls=%fused_computation.12 | convolution fusion | flops 805830656 | bytes 8392704 | tf_op jit(solution)/shard_map/cij,cnj->cni/dot_general | solution.py:45
  245.7 7.8 %add_convert_fusion = bf16[128,128,64]{1,2,0:T(8,128)(2,1)S(1)} fusion(f32[128,128,64]{1,2,0:T(8,128)S(1)} %fusion.4, f32[128,128,16]{0,2,1:T(8,128)S(1)} %bitcast.59, f32[16,128]{0,1:T(8,128)S(1)} %copy-done.6, f32[16,128]{0,1:T(8,128)S(1)} %copy-done.5, f32[16,128]{0,1:T(8,128)S(1)} %copy-done.3), kind=kOutput, calls=%fused_computation.15 | convolution fusion | flops 203816960 | bytes 7364608 | tf_op jit(solution)/shard_map/ipc,ncp->cni/dot_general | solution.py:53
  253.5 3.3 copy.60
  256.8 52.2 %all_to_all.26 = bf16[128,8,1024]{0,2,1:T(8,128)(2,1)S(1)} all-to-all(bf16[128,8,1024]{0,2,1:T(8,128)(2,1)} %bitcast.58), channel_id=1, replica_groups=mesh['ctx'=8,'ch'=4] {'ctx'}, dimensions={1} | all-to-all | bytes 4194304 | tf_op jit(solution)/shard_map/all_to_all | solution.py:76
  309.0 2.2 convert_bitcast_fusion
  311.2 5.4 %copy.61 = f32[8,128,1024]{2,1,0:T(8,128)} copy(f32[8,128,1024]{1,2,0:T(8,128)} %convert_bitcast_fusion) | data formatting | bytes 8388608 | tf_op jit(solution)/shard_map/convert_element_type | solution.py:79
  316.6 7.7 %fusion.3 = bf16[1024,1024]{0,1:T(8,128)(2,1)} fusion(f32[3,1024,1024]{1,2,0:T(8,128)} %copy-done, f32[8,128,1024]{2,1,0:T(8,128)} %copy.61, f32[1024]{0:T(1024)S(1)} %copy-done.9), kind=kLoop, calls=%fused_computation.10 | loop fusion | flops 7340032 | bytes 18878464 | tf_op jit(solution)/shard_map/convert_element_type | solution.py:81
  324.3 59.2 %all-gather.2.cloned.1.call-done = bf16[1024,4096]{0,1:T(8,128)(2,1)} async-done(((bf16[1024,1024]{0,1:T(8,128)(2,1)}), bf16[1024,4096]{0,1:T(8,128)(2,1)}) %all-gather.2.cloned.1.call-update) | async-done | bytes 8388624 | tf_op jit(solution)/shard_map/all_gather | solution.py:83
  383.5 14.7 %convolution_convert_fusion = bf16[1024,1024]{1,0:T(8,128)(2,1)} fusion(bf16[1024,4096]{0,1:T(8,128)(2,1)} %all-gather.2.cloned.1.call-done, bf16[4096,1024]{1,0:T(8,128)(2,1)} %param.11), kind=kOutput, calls=%fused_computation.19 | convolution fusion | flops 8590983168 | bytes 18874368 | tf_op jit(solution)/shard_map/dot_general | solution.py:82
  (99 shorter events, 58.7 us)
Async XLA Ops:
  7.4 13.4 %collective-permute-start = (bf16[3,2,1024]{2,1,0:T(2,128)(2,1)S(1)}, bf16[3,2,1024]{2,1,0:T(2,128)(2,1)S(1)}, u32[]{:S(2)}, u32[]{:S(2)}) collective-permute-start(bf16[3,2,1024]{2,1,0:T(2,128)(2,1)S(1)} %slice.176), channel_id=1, source_target_pairs={{0,4},{4,8},{8,12},{12,16},{16,20},{20,24},{24,28},{1,5},{5,9},{9,... | collective-permute-start | bytes 36872 | tf_op jit(solution)/shard_map/ppermute | solution.py:12
  36.9 4.5 %copy-start = (f32[3,1024,1024]{1,2,0:T(8,128)}, f32[3,1024,1024]{1,2,0:T(8,128)S(1)}, u32[]{:S(2)}) copy-start(f32[3,1024,1024]{1,2,0:T(8,128)S(1)} %multiply_add_fusion) | copy-start | bytes 37748740
  43.4 51.8 %all-to-all-start = ((bf16[8,128,1024]{2,1,0:T(8,128)(2,1)}), bf16[8,128,1024]{2,1,0:T(8,128)(2,1)}, u32[]{:S(2)}, u32[]{:S(2)}) async-start(bf16[8,128,1024]{2,1,0:T(8,128)(2,1)} %bitcast.6), calls=%async_computation | async-start | bytes 4194304 | tf_op jit(solution)/shard_map/all_to_all | solution.py:70
  48.0 335.4 %all-gather.2.cloned.1.call-start = ((), (), s32[]{:S(2)}) async-start(), calls=%async_computation.2 | async-start | bytes 10485760 | tf_op jit(solution)/shard_map/all_gather | solution.py:83
  48.9 3.4 copy-start.2
  49.0 3.3 copy-start.4
  69.6 88.7 %copy-start.7 = (f32[2048]{0:T(1024)}, f32[2048]{0:T(1024)S(1)}, u32[]{:S(2)}) copy-start(f32[2048]{0:T(1024)S(1)} %get-tuple-element.17) | copy-start | bytes 24580
  179.3 37.7 %slice-start = ((f32[64,2048]{1,0:T(8,128)}), f32[1,2048]{1,0:T(1,128)S(1)}, s32[]{:S(2)}) async-start(f32[64,2048]{1,0:T(8,128)} %multiply_add_fusion.1), calls=%async_computation.3 | async-start | bytes 16384 | tf_op jit(solution)/shard_map/slice | solution.py:50
  208.8 0.7 copy-start.1
  235.1 6.3 %copy-start.8 = (pred[64,64]{1,0:T(8,128)(4,1)S(1)}, pred[64,64]{1,0:T(8,128)(4,1)}, u32[]{:S(2)}) copy-start(pred[64,64]{1,0:T(8,128)(4,1)} %subtract_compare_fusion) | copy-start | bytes 12292
  241.4 4.2 %copy-start.3 = (f32[16,128]{0,1:T(8,128)S(1)}, f32[16,128]{0,1:T(8,128)}, u32[]{:S(2)}) copy-start(f32[16,128]{0,1:T(8,128)} %copy-done.2) | copy-start | bytes 24580
  241.4 4.2 %copy-start.5 = (f32[16,128]{0,1:T(8,128)S(1)}, f32[16,128]{0,1:T(8,128)}, u32[]{:S(2)}) copy-start(f32[16,128]{0,1:T(8,128)} %copy-done.4) | copy-start | bytes 24580
  241.5 4.2 %copy-start.6 = (f32[16,128]{0,1:T(8,128)S(1)}, f32[16,128]{0,1:T(8,128)}, u32[]{:S(2)}) copy-start(f32[16,128]{0,1:T(8,128)} %copy.59) | copy-start | bytes 24580
  311.2 5.4 %copy-start.9 = (f32[1024]{0:T(1024)S(1)}, f32[1024]{0:T(1024)}, u32[]{:S(2)}) copy-start(f32[1024]{0:T(1024)} %param.10) | copy-start | bytes 12292
Sparse Core Ops, SparseCore 0:
  324.4 59.0 all-gather.1
where the time goes:
time: 408 us; the launch traced here: 405 us
  local copies, waits for them, and re-layouts  157 us (38%)
  waiting for transfers between devices  84.8 us (21%)
  other arithmetic  59.2 us (15%)
  blocking collectives  52.2 us (13%)
  matrix products  29.6 us (7%)
  between operations  13.7 us (3%)
  starting transfers between devices  8.61 us (2%)
    slice x24, local copies, waits for them, and re-layouts, channel_conv(): _, states = lax.associative_scan(combine, (decays, closing), axis=0)  83.2 us
    all_gather x1, waiting for transfers between devices, shards(): lax.all_gather(gated_mix, 'ch', axis=1, tiled=True)  59.2 us
    all_to_all x1, blocking collectives, shards(): lax.all_to_all(long_part, 'ctx', split_axis=1, concat_axis=0, tiled=True)  52.2 us
    unnamed x26, local copies, waits for them, and re-layouts  27.2 us
    all_to_all x1, waiting for transfers between devices, shards(): lax.all_to_all(channel_major, 'ctx', split_axis=0, concat_axis=1, tiled=T...  25.6 us
    add x1, other arithmetic, shards(): featured + tap_weights[tap_index].astype(jnp.float32)[:, None, :] * exten...  15.7 us
    gather x2, local copies, waits for them, and re-layouts, make_tables(): kernel[jnp.maximum(offsets, 0)]  15.3 us
    dot_general x1, matrix products, shards(): jnp.dot(lax.all_gather(gated_mix, 'ch', axis=1, tiled=True), out_weight,...  14.7 us
  transfers between devices with their start and end apart: 3, of which 2 were waited for; matrix products, arithmetic and copies ran while one was open for 8% of the time, Pallas kernels for 0%

commit v1 on v0

v1 whole, which is shorter than its diff:
```python
import jax
import jax.numpy as jnp
from jax import lax
from jax.experimental import pallas as pl
from jax.experimental.pallas import tpu as pltpu
from jax.sharding import PartitionSpec as P

LANES = 128
ROWS_PER_STEP = 128


def shifted(value, axis, steps):
    count = lax.axis_size(axis)
    initial, last = (max(0, -steps), min(count, count - steps))
    return lax.ppermute(value, axis, [(source, source + steps) for source in range(initial, last)])


def recurrence_kernel(x_ref, decay_ref, residue_ref, start_ref, y_ref, end_ref, state_ref):
    pole_count = decay_ref.shape[0]
    step_count = x_ref.shape[0]

    @pl.when(pl.program_id(0) == 0)
    def _():
        state_ref[...] = start_ref[...]

    def body(t, states):
        x = x_ref[t]
        updated = []
        total = None
        for p in range(pole_count):
            h = decay_ref[p] * states[p] + x
            updated.append(h)
            term = residue_ref[p] * h
            total = term if total is None else total + term
        y_ref[t] = total
        return tuple(updated)

    states = tuple(state_ref[p] for p in range(pole_count))
    states = lax.fori_loop(0, step_count, body, states, unroll=4)
    for p in range(pole_count):
        state_ref[p] = states[p]
    end_ref[...] = state_ref[...]


def end_state_kernel(x_ref, decay_ref, end_ref, state_ref):
    pole_count = decay_ref.shape[0]
    step_count = x_ref.shape[0]

    @pl.when(pl.program_id(0) == 0)
    def _():
        state_ref[...] = jnp.zeros(state_ref.shape, state_ref.dtype)

    def body(t, states):
        x = x_ref[t]
        return tuple(decay_ref[p] * states[p] + x for p in range(pole_count))

    states = tuple(state_ref[p] for p in range(pole_count))
    states = lax.fori_loop(0, step_count, body, states, unroll=4)
    for p in range(pole_count):
        state_ref[p] = states[p]
    end_ref[...] = state_ref[...]


def run_recurrence(x3, decay3, residue3, start3):
    length, rows, lanes = x3.shape
    pole_count = decay3.shape[0]
    chunk = min(ROWS_PER_STEP, length)
    row_spec = pl.BlockSpec((chunk, rows, lanes), lambda i: (i, 0, 0))
    pole_spec = pl.BlockSpec((pole_count, rows, lanes), lambda i: (0, 0, 0))
    return pl.pallas_call(
        recurrence_kernel,
        grid=(length // chunk,),
        in_specs=[row_spec, pole_spec, pole_spec, pole_spec],
        out_specs=[row_spec, pole_spec],
        out_shape=[
            jax.ShapeDtypeStruct(x3.shape, jnp.float32),
            jax.ShapeDtypeStruct(decay3.shape, jnp.float32),
        ],
        scratch_shapes=[pltpu.VMEM(decay3.shape, jnp.float32)],
    )(x3, decay3, residue3, start3)


def run_end_state(x3, decay3):
    length, rows, lanes = x3.shape
    pole_count = decay3.shape[0]
    chunk = min(ROWS_PER_STEP, length)
    row_spec = pl.BlockSpec((chunk, rows, lanes), lambda i: (i, 0, 0))
    pole_spec = pl.BlockSpec((pole_count, rows, lanes), lambda i: (0, 0, 0))
    return pl.pallas_call(
        end_state_kernel,
        grid=(length // chunk,),
        in_specs=[row_spec, pole_spec],
        out_specs=pole_spec,
        out_shape=jax.ShapeDtypeStruct(decay3.shape, jnp.float32),
        scratch_shapes=[pltpu.VMEM(decay3.shape, jnp.float32)],
    )(x3, decay3)


def shards(projected, tap_weights, pole_rates, residues, long_bias, out_weight):
    row_count = projected.shape[1]
    width = projected.shape[2]
    rows = width // LANES
    pole_count = pole_rates.shape[0]
    rim_rows = tap_weights.shape[0] - 1
    prior_rows = shifted(projected[:, row_count - rim_rows :], "ctx", 1)
    extended = jnp.concatenate([prior_rows, projected], 1)
    featured = jnp.zeros(projected.shape, jnp.float32)
    for tap_index in range(rim_rows + 1):
        lead_row = rim_rows - tap_index
        featured = featured + tap_weights[tap_index].astype(jnp.float32)[:, None, :] * extended[
            :, lead_row : lead_row + row_count
        ].astype(jnp.float32)
    mixed_input = (featured[1] * featured[2]).astype(jnp.bfloat16)
    x3 = mixed_input.astype(jnp.float32).reshape(row_count, rows, LANES)

    decay = jnp.exp(-pole_rates)
    decay3 = decay.reshape(pole_count, rows, LANES)
    residue3 = residues.reshape(pole_count, rows, LANES)
    local_end = run_end_state(x3, decay3).reshape(pole_count, width)

    ends = lax.all_gather(local_end, "ctx", axis=0, tiled=False)
    ctx_count = ends.shape[0]
    here = lax.axis_index("ctx")
    earlier = jnp.arange(ctx_count, dtype=jnp.int32)
    gaps = (here - 1 - earlier).astype(jnp.float32)
    weights = jnp.where(
        (earlier < here)[:, None, None],
        jnp.exp(-pole_rates[None] * (jnp.float32(row_count) * jnp.maximum(gaps, 0.0))[:, None, None]),
        jnp.float32(0.0),
    )
    start = jnp.sum(weights * ends, axis=0)

    long_part, _ = run_recurrence(x3, decay3, residue3, start.reshape(pole_count, rows, LANES))
    long_mix = long_part.reshape(row_count, width).astype(jnp.bfloat16)
    gated_mix = featured[0] * (
        long_mix.astype(jnp.float32) + long_bias[None, :] * mixed_input.astype(jnp.float32)
    )
    gated_mix = gated_mix.astype(jnp.bfloat16)
    mixed_out = jnp.dot(
        lax.all_gather(gated_mix, "ch", axis=1, tiled=True),
        out_weight,
        preferred_element_type=jnp.float32,
    )
    return mixed_out.astype(jnp.bfloat16)


def solution(mesh):
    in_specs = (
        P(None, "ctx", "ch"),
        P(None, None, "ch"),
        P(None, "ch"),
        P(None, "ch"),
        P("ch"),
        P(None, "ch"),
    )
    out_specs = P("ctx", "ch")
    return jax.shard_map(shards, mesh=mesh, in_specs=in_specs, out_specs=out_specs, check_vma=False)
```

time: 408 us -> 177 us (0.43)
  local copies, waits for them, and re-layouts: 157 us -> 10.9 us
  other arithmetic: 59.2 us -> 22 us
  blocking collectives: 52.2 us -> 25.6 us
  Pallas kernels: 0 us -> 21.2 us
  waiting for transfers between devices: 84.8 us -> 64.5 us
  matrix products: 29.6 us -> 14.6 us
  starting transfers between devices: 8.61 us -> 3.98 us
    slice x25 -> x0, local copies, waits for them, and re-layouts: 85.3 us -> none  [the longest x24 83.2 us: channel_conv(): _, states = lax.associative_scan(combine, (decays, closing), axis=0)]
    all_to_all x1 -> x0, blocking collectives: 52.2 us -> none  [shards(): lax.all_to_all(long_part, 'ctx', split_axis=1, concat_axis=0, tiled=True)]
    all_to_all x1 -> x0, waiting for transfers between devices: 25.6 us -> none  [shards(): lax.all_to_all(channel_major, 'ctx', split_axis=0, concat_axis=1, tiled=T...]
    all_gather x0 -> x1, blocking collectives: none -> 25.6 us  [shards(): ends = lax.all_gather(local_end, 'ctx', axis=0, tiled=False)]
    add x19 -> x0, other arithmetic: 21.9 us -> none  [the longest x12 14.5 us: combine(): return (earlier[0] * latter[0], latter[0] * earlier[1] + latter[1])]
    pallas_call x0 -> x2, Pallas kernels: none -> 21.2 us  [the longest x1 12.9 us: run_recurrence(): pl.pallas_call(recurrence_kernel, grid=(length // chunk,), in_specs=[row_...]
    unnamed x26 -> x8, local copies, waits for them, and re-layouts: 27.2 us -> 9.27 us
    gather x2 -> x0, local copies, waits for them, and re-layouts: 15.3 us -> none  [make_tables(): kernel[jnp.maximum(offsets, 0)]]
  transfers between devices with their start and end apart: 3 -> 2, of which waited for: 2 -> 1; matrix products, arithmetic and copies ran while one was open for 8% -> 2% of each run, Pallas kernels for 0% -> 0%
where the time goes in v1:
time: 177 us; the launch traced here: 176 us
  waiting for transfers between devices  64.5 us (36%)
  blocking collectives  25.6 us (14%)
  other arithmetic  22 us (12%)
  Pallas kernels  21.2 us (12%)
  matrix products  14.6 us (8%)
  between operations  13.5 us (8%)
  local copies, waits for them, and re-layouts  10.9 us (6%)
  starting transfers between devices  3.98 us (2%)
    all_gather x1, waiting for transfers between devices, shards(): lax.all_gather(gated_mix, 'ch', axis=1, tiled=True)  64.5 us
    all_gather x1, blocking collectives, shards(): ends = lax.all_gather(local_end, 'ctx', axis=0, tiled=False)  25.6 us
    dot_general x1, matrix products, shards(): jnp.dot(lax.all_gather(gated_mix, 'ch', axis=1, tiled=True), out_weight,...  14.6 us
    pallas_call x1, Pallas kernels, run_recurrence(): pl.pallas_call(recurrence_kernel, grid=(length // chunk,), in_specs=[row_...  12.9 us
    add x1, other arithmetic, shards(): featured + tap_weights[tap_index].astype(jnp.float32)[:, None, :] * exten...  11 us
    unnamed x8, local copies, waits for them, and re-layouts  9.27 us
    pallas_call x1, Pallas kernels, run_end_state(): pl.pallas_call(end_state_kernel, grid=(length // chunk,), in_specs=[row_s...  8.29 us
    convert_element_type x1, other arithmetic, shards(): gated_mix = gated_mix.astype(jnp.bfloat16)  5.29 us
  transfers between devices with their start and end apart: 2, of which 1 were waited for; matrix products, arithmetic and copies ran while one was open for 2% of the time, Pallas kernels for 0%

profile of v1, /device:TPU:1, one launch (start us, length us, event | category | flops | bytes accessed | tf_op | source)
XLA Modules:
  0.0 176.2 jit_solution(15361097766570048029)
XLA Ops:
  6.5 0.0 all-gather.2.cloned.1.call-start
  6.5 0.8 slice.29
  7.4 4.0 %collective-permute-start = (bf16[3,2,1024]{2,1,0:T(2,128)(2,1)S(1)}, bf16[3,2,1024]{2,1,0:T(2,128)(2,1)S(1)}, u32[]{:S(2)}, u32[]{:S(2)}) collective-permute-start(bf16[3,2,1024]{2,1,0:T(2,128)(2,1)S(1)} %slice.29), channel_id=1, source_target_pairs={{0,4},{4,8},{8,12},{12,16},{16,20},{20,24},{24,28},{1,5},{5,9},{9,... | collective-permute-start | bytes 36872 | tf_op jit(solution)/shard_map/ppermute | solution.py:15
  11.4 0.7 bitcast_convert_fusion.2
  12.1 0.9 fusion.7
  13.0 1.5 copy.9
  14.4 0.6 copy.8
  15.1 0.0 collective-permute-done
  15.1 11.0 %multiply_add_fusion = f32[3,1024,1024]{2,1,0:T(8,128)S(1)} fusion(bf16[3,1024,1024]{2,1,0:T(8,128)(2,1)} %param.6, bf16[3,2,1024]{2,1,0:T(2,128)(2,1)S(1)} %collective-permute-done, f32[3,1024]{1,0:T(4,128)S(1)} %get-tuple-element.12, f32[3,1024]{1,0:T(4,128)S(1)} %get-tuple-element.13, f32[3,1024]{1,0:T(4,128)S(1)} %get-tuple-element.11), kind=kLoop, calls=%fused_computation | loop fusion | flops 44040192 | bytes 18923520 | tf_op jit(solution)/shard_map/add | solution.py:110
  26.1 0.0 copy-start
  26.1 1.5 convert_bitcast_fusion.1
  27.5 3.6 %copy-done = f32[3,1024,1024]{2,1,0:T(8,128)} copy-done((f32[3,1024,1024]{2,1,0:T(8,128)}, f32[3,1024,1024]{2,1,0:T(8,128)S(1)}, u32[]{:S(2)}) %copy-start) | copy-done | bytes 12582936
  31.1 2.9 %copy.7 = f32[128,8,8,128]{3,2,1,0:T(8,128)} copy(f32[128,8,8,128]{3,1,2,0:T(8,128)S(1)} %get-tuple-element.7) | data formatting | bytes 8388608
  34.1 8.3 %shard_map.64 = f32[16,8,128]{2,1,0:T(8,128)} custom-call(f32[1024,8,128]{2,1,0:T(8,128)} %bitcast.39, f32[16,8,128]{2,1,0:T(8,128)} %bitcast.42), custom_call_target="tpu_custom_call" | custom-call | tf_op jit(solution)/shard_map/pallas_call | solution.py:89
  42.3 0.9 all_gather_reshape.3
  43.2 25.6 %all_gather.6 = f32[8,16,1024]{2,1,0:T(8,128)S(1)} all-gather(f32[1,16,1024]{2,1,0:T(8,128)S(1)} %all_gather_reshape.3), channel_id=1, replica_groups=mesh['ctx'=8,'ch'=4] {'ctx'}, dimensions={0}, use_global_device_ids=true | all-gather | bytes 589824 | tf_op jit(solution)/shard_map/all_gather | solution.py:121
  68.8 0.2 multiply_reduce_fusion
  69.0 0.6 copy.10
  69.6 0.0 copy-start.1
  69.6 12.9 %shard_map.65 = (f32[1024,8,128]{2,1,0:T(8,128)}, f32[16,8,128]{2,1,0:T(8,128)}) custom-call(f32[1024,8,128]{2,1,0:T(8,128)} %bitcast.40, f32[16,8,128]{2,1,0:T(8,128)} %bitcast.43, f32[16,8,128]{2,1,0:T(8,128)} %bitcast.44, f32[16,8,128]{2,1,0:T(8,128)} %bitcast.45), custom_call_target="tpu_custom_call" | custom-call | tf_op jit(solution)/shard_map/pallas_call | solution.py:70
  82.5 2.5 %convert_convert_fusion = f32[1024,8,128]{2,1,0:T(8,128)S(1)} fusion(f32[1024,8,128]{2,1,0:T(8,128)} %get-tuple-element.6), kind=kLoop, calls=%fused_computation.14 | loop fusion | flops 2097152 | bytes 8388608 | tf_op jit(solution)/shard_map/convert_element_type | solution.py:136
  85.0 0.0 copy-done.1
  85.0 5.3 %fusion.4 = bf16[1024,1024]{1,0:T(8,128)(2,1)} fusion(bf16[1,1024,1024]{2,1,0:T(8,128)(2,1)S(1)} %get-tuple-element.8, f32[128,8,8,128]{3,2,1,0:T(8,128)S(1)} %bitcast.41, f32[3,1024,1024]{2,1,0:T(8,128)} %copy-done, f32[1024]{0:T(1024)S(1)} %copy-done.1), kind=kLoop, calls=%fused_computation.10 | loop fusion | flops 5242880 | bytes 12587008 | tf_op jit(solution)/shard_map/convert_element_type | solution.py:138
  90.3 0.0 all-gather.2.cloned.1.call-update
  90.3 64.5 %all-gather.2.cloned.1.call-done = bf16[1024,4096]{1,0:T(8,128)(2,1)} async-done(((bf16[1024,1024]{1,0:T(8,128)(2,1)}), bf16[1024,4096]{1,0:T(8,128)(2,1)}) %all-gather.2.cloned.1.call-update) | async-done | bytes 8388624 | tf_op jit(solution)/shard_map/all_gather | solution.py:140
  154.8 14.6 %convolution_convert_fusion = bf16[1024,1024]{1,0:T(8,128)(2,1)} fusion(bf16[1024,4096]{1,0:T(8,128)(2,1)} %all-gather.2.cloned.1.call-done, bf16[4096,1024]{1,0:T(8,128)(2,1)} %param.11), kind=kOutput, calls=%fused_computation.15 | convolution fusion | flops 8590983168 | bytes 18874368 | tf_op jit(solution)/shard_map/dot_general | solution.py:139
  (2 shorter events, 0.0 us)
Async XLA Ops:
  6.5 148.2 %all-gather.2.cloned.1.call-start = ((), (), s32[]{:S(2)}) async-start(), calls=%async_computation | async-start | bytes 10485760 | tf_op jit(solution)/shard_map/all_gather | solution.py:140
  7.4 7.7 %collective-permute-start = (bf16[3,2,1024]{2,1,0:T(2,128)(2,1)S(1)}, bf16[3,2,1024]{2,1,0:T(2,128)(2,1)S(1)}, u32[]{:S(2)}, u32[]{:S(2)}) collective-permute-start(bf16[3,2,1024]{2,1,0:T(2,128)(2,1)S(1)} %slice.29), channel_id=1, source_target_pairs={{0,4},{4,8},{8,12},{12,16},{16,20},{20,24},{24,28},{1,5},{5,9},{9,... | collective-permute-start | bytes 36872 | tf_op jit(solution)/shard_map/ppermute | solution.py:15
  26.1 5.1 %copy-start = (f32[3,1024,1024]{2,1,0:T(8,128)}, f32[3,1024,1024]{2,1,0:T(8,128)S(1)}, u32[]{:S(2)}) copy-start(f32[3,1024,1024]{2,1,0:T(8,128)S(1)} %multiply_add_fusion) | copy-start | bytes 37748740
  69.6 15.3 %copy-start.1 = (f32[1024]{0:T(1024)S(1)}, f32[1024]{0:T(1024)}, u32[]{:S(2)}) copy-start(f32[1024]{0:T(1024)} %param.10) | copy-start | bytes 12292
Sparse Core Ops, SparseCore 0:
  90.4 64.3 all-gather.1

commit v2 on v1

--- a/solution.py
+++ b/solution.py
@@ -7,6 +7,7 @@
 
 LANES = 128
 ROWS_PER_STEP = 128
+CHUNKS = 4
 
 
 def shifted(value, axis, steps):
@@ -96,6 +97,32 @@
     )(x3, decay3)
 
 
+def incoming_state(local_end, pole_rates, row_count):
+    ctx_count = lax.axis_size("ctx")
+    here = lax.axis_index("ctx")
+    later = jnp.arange(ctx_count, dtype=jnp.int32)
+    gaps = (later - 1 - here).astype(jnp.float32)
+    weights = jnp.where(
+        (later > here)[:, None, None],
+        jnp.exp(-pole_rates[None] * (jnp.float32(row_count) * jnp.maximum(gaps, 0.0))[:, None, None]),
+        jnp.float32(0.0),
+    )
+    shares = weights * local_end[None]
+    return lax.psum_scatter(shares, "ctx", scatter_dimension=0, tiled=True)[0]
+
+
+def featurize(extended, tap_weights, stream, first, count):
+    taps = tap_weights.shape[0]
+    total = None
+    for tap_index in range(taps):
+        lead_row = taps - 1 - tap_index
+        term = tap_weights[tap_index, stream].astype(jnp.float32)[None, :] * extended[
+            stream, first + lead_row : first + lead_row + count
+        ].astype(jnp.float32)
+        total = term if total is None else total + term
+    return total
+
+
 def shards(projected, tap_weights, pole_rates, residues, long_bias, out_weight):
     row_count = projected.shape[1]
     width = projected.shape[2]
@@ -104,44 +131,36 @@
     rim_rows = tap_weights.shape[0] - 1
     prior_rows = shifted(projected[:, row_count - rim_rows :], "ctx", 1)
     extended = jnp.concatenate([prior_rows, projected], 1)
-    featured = jnp.zeros(projected.shape, jnp.float32)
-    for tap_index in range(rim_rows + 1):
-        lead_row = rim_rows - tap_index
-        featured = featured + tap_weights[tap_index].astype(jnp.float32)[:, None, :] * extended[
-            :, lead_row : lead_row + row_count
-        ].astype(jnp.float32)
-    mixed_input = (featured[1] * featured[2]).astype(jnp.bfloat16)
+    mixed_input = (
+        featurize(extended, tap_weights, 1, 0, row_count) * featurize(extended, tap_weights, 2, 0, row_count)
+    ).astype(jnp.bfloat16)
     x3 = mixed_input.astype(jnp.float32).reshape(row_count, rows, LANES)
 
     decay = jnp.exp(-pole_rates)
     decay3 = decay.reshape(pole_count, rows, LANES)
     residue3 = residues.reshape(pole_count, rows, LANES)
     local_end = run_end_state(x3, decay3).reshape(pole_count, width)
+    state = incoming_state(local_end, pole_rates, row_count).reshape(pole_count, rows, LANES)
 
-    ends = lax.all_gather(local_end, "ctx", axis=0, tiled=False)
-    ctx_count = ends.shape[0]
-    here = lax.axis_index("ctx")
-    earlier = jnp.arange(ctx_count, dtype=jnp.int32)
-    gaps = (here - 1 - earlier).astype(jnp.float32)
-    weights = jnp.where(
-        (earlier < here)[:, None, None],
-        jnp.exp(-pole_rates[None] * (jnp.float32(row_count) * jnp.maximum(gaps, 0.0))[:, None, None]),
-        jnp.float32(0.0),
-    )
-    start = jnp.sum(weights * ends, axis=0)
-
-    long_part, _ = run_recurrence(x3, decay3, residue3, start.reshape(pole_count, rows, LANES))
-    long_mix = long_part.reshape(row_count, width).astype(jnp.bfloat16)
-    gated_mix = featured[0] * (
-        long_mix.astype(jnp.float32) + long_bias[None, :] * mixed_input.astype(jnp.float32)
-    )
-    gated_mix = gated_mix.astype(jnp.bfloat16)
-    mixed_out = jnp.dot(
-        lax.all_gather(gated_mix, "ch", axis=1, tiled=True),
-        out_weight,
-        preferred_element_type=jnp.float32,
-    )
-    return mixed_out.astype(jnp.bfloat16)
+    chunk_count = CHUNKS if row_count % (CHUNKS * 8) == 0 else 1
+    chunk = row_count // chunk_count
+    outputs = []
+    for index in range(chunk_count):
+        first = index * chunk
+        long_part, state = run_recurrence(x3[first : first + chunk], decay3, residue3, state)
+        long_mix = long_part.reshape(chunk, width).astype(jnp.bfloat16)
+        inputs_here = mixed_input[first : first + chunk].astype(jnp.float32)
+        gated_mix = featurize(extended, tap_weights, 0, first, chunk) * (
+            long_mix.astype(jnp.float32) + long_bias[None, :] * inputs_here
+        )
+        gated_mix = gated_mix.astype(jnp.bfloat16)
+        mixed_out = jnp.dot(
+            lax.all_gather(gated_mix, "ch", axis=1, tiled=True),
+            out_weight,
+            preferred_element_type=jnp.float32,
+        )
+        outputs.append(mixed_out.astype(jnp.bfloat16))
+    return jnp.concatenate(outputs, 0)
 
 
 def solution(mesh):

time: 177 us -> 253 us (1.43)
  waiting for transfers between devices: 64.5 us -> 114 us
  blocking collectives: 25.6 us -> 0 us
  other arithmetic: 22 us -> 40.3 us
  local copies, waits for them, and re-layouts: 10.9 us -> 28.1 us
  matrix products: 14.6 us -> 25.4 us
  Pallas kernels: 21.2 us -> 26.7 us
    reduce_scatter x0 -> x1, waiting for transfers between devices: none -> 49.7 us  [incoming_state(): return lax.psum_scatter(shares, 'ctx', scatter_dimension=0, tiled=True)[0]]
    all_gather x1 -> x0, blocking collectives: 25.6 us -> none  [shards(): ends = lax.all_gather(local_end, 'ctx', axis=0, tiled=False)]
    unnamed x8 -> x25, local copies, waits for them, and re-layouts: 9.27 us -> 27.3 us
    convert_element_type x2 -> x7, other arithmetic: 3.2 us -> 17.6 us  [the longest x2 11.4 us: shards(): x3 = mixed_input.astype(jnp.float32).reshape(row_count, rows, LANES)]
    add x1 -> x0, other arithmetic: 11 us -> none  [shards(): featured + tap_weights[tap_index].astype(jnp.float32)[:, None, :] * exten...]
    dot_general x1 -> x4, matrix products: 14.6 us -> 25.4 us  [shards(): jnp.dot(lax.all_gather(gated_mix, 'ch', axis=1, tiled=True), out_weight,...]
    unnamed x1, other arithmetic: 1.46 us -> 10.5 us
    pallas_call x1 -> x4, Pallas kernels: 12.9 us -> 18.4 us  [run_recurrence(): pl.pallas_call(recurrence_kernel, grid=(length // chunk,), in_specs=[row_...]
  transfers between devices with their start and end apart: 2 -> 6, of which waited for: 1 -> 5; matrix products, arithmetic and copies ran while one was open for 2% -> 17% of each run, Pallas kernels for 0% -> 2%
where the time goes in v2:
time: 253 us; the launch traced here: 252 us
  waiting for transfers between devices  114 us (45%)
  other arithmetic  40.3 us (16%)
  local copies, waits for them, and re-layouts  28.1 us (11%)
  Pallas kernels  26.7 us (11%)
  matrix products  25.4 us (10%)
  between operations  13.3 us (5%)
  starting transfers between devices  4.54 us (2%)
    all_gather x4, waiting for transfers between devices, shards(): lax.all_gather(gated_mix, 'ch', axis=1, tiled=True)  63.2 us
    reduce_scatter x1, waiting for transfers between devices, incoming_state(): return lax.psum_scatter(shares, 'ctx', scatter_dimension=0, tiled=True)[0]  49.7 us
    unnamed x25, local copies, waits for them, and re-layouts  27.3 us
    dot_general x4, matrix products, shards(): jnp.dot(lax.all_gather(gated_mix, 'ch', axis=1, tiled=True), out_weight,...  25.4 us
    pallas_call x4, Pallas kernels, run_recurrence(): pl.pallas_call(recurrence_kernel, grid=(length // chunk,), in_specs=[row_...  18.4 us
    convert_element_type x2, other arithmetic, shards(): x3 = mixed_input.astype(jnp.float32).reshape(row_count, rows, LANES)  11.4 us
    unnamed x1, other arithmetic  10.5 us
    convert_element_type x2, other arithmetic, shards(): gated_mix = gated_mix.astype(jnp.bfloat16)  8.92 us
  transfers between devices with their start and end apart: 6, of which 5 were waited for; matrix products, arithmetic and copies ran while one was open for 17% of the time, Pallas kernels for 2%

profile of v2, /device:TPU:1, one launch (start us, length us, event | category | flops | bytes accessed | tf_op | source)
XLA Modules:
  0.0 252.2 jit_solution(6011697755849818732)
XLA Ops:
  7.4 4.0 %collective-permute-start = (bf16[3,2,1024]{2,1,0:T(2,128)(2,1)S(1)}, bf16[3,2,1024]{2,1,0:T(2,128)(2,1)S(1)}, u32[]{:S(2)}, u32[]{:S(2)}) collective-permute-start(bf16[3,2,1024]{2,1,0:T(2,128)(2,1)S(1)} %slice.132), channel_id=1, source_target_pairs={{0,4},{4,8},{8,12},{12,16},{16,20},{20,24},{24,28},{1,5},{5,9},{9,... | collective-permute-start | bytes 36872 | tf_op jit(solution)/shard_map/ppermute | solution.py:16
  13.8 1.5 copy.9
  15.2 10.5 %convert_bitcast_fusion = (f32[128,8,8,128]{3,1,2,0:T(8,128)S(1)}, bf16[1,1024,1024]{2,1,0:T(8,128)(2,1)}, f32[128,8,8,128]{3,1,2,0:T(8,128)}, f32[128,8,8,128]{...) fusion(bf16[3,1024,1024]{2,1,0:T(8,128)(2,1)} %param.6, ...), kind=kLoop, calls=%fused_computation.3 | loop fusion | flops 19922944 | bytes 37761024
  25.7 3.4 %copy.10 = f32[128,8,8,128]{3,2,1,0:T(8,128)S(1)} copy(f32[128,8,8,128]{3,1,2,0:T(8,128)} %get-tuple-element.30) | data formatting | bytes 8388608
  31.3 3.0 %copy.12 = f32[128,8,8,128]{3,2,1,0:T(8,128)} copy(f32[128,8,8,128]{3,1,2,0:T(8,128)S(1)} %copy-done) | data formatting | bytes 8388608
  34.3 3.0 %copy.13 = f32[128,8,8,128]{3,2,1,0:T(8,128)} copy(f32[128,8,8,128]{3,1,2,0:T(8,128)S(1)} %get-tuple-element.31) | data formatting | bytes 8388608
  38.4 3.2 %copy.15 = f32[128,8,8,128]{3,2,1,0:T(8,128)} copy(f32[128,8,8,128]{3,1,2,0:T(8,128)S(1)} %get-tuple-element.19) | data formatting | bytes 8388608
  41.5 1.8 copy-done.3
  43.3 4.6 %fusion.18.x_ref = f32[1024,8,128]{2,1,0:T(8,128)} fusion(f32[128,8,8,128]{3,2,1,0:T(8,128)} %copy.15, f32[128,8,8,128]{3,2,1,0:T(8,128)S(1)} %copy.14, f32[128,8,8,128]{3,2,1,0:T(8,128)S(1)} %copy-done.3, f32[128,8,8,128]{3,2,1,0:T(8,128)S(1)} %copy-done.1, f32[128,8,8,128]{3,2,1,0:T(8,128)S(1)} %copy.11, f32[128,8,8,128]{3,2,1,0:T(8,128)S(1)} %copy.10, ...), kind=kLoop, calls=%fused_computation.42 | loop fusion | flops 13631488 | bytes 29384704 | tf_op jit(solution)/shard_map/convert_element_type | solution.py:137
  47.9 8.3 %shard_map.64 = f32[16,8,128]{2,1,0:T(8,128)} custom-call(f32[1024,8,128]{2,1,0:T(8,128)} %fusion.18.x_ref, f32[16,8,128]{2,1,0:T(8,128)} %bitcast.239), custom_call_target="tpu_custom_call" | custom-call | tf_op jit(solution)/shard_map/pallas_call | solution.py:90
  58.3 6.8 %fusion.38 = (f32[1024,1024]{1,0:T(8,128)S(1)}, bf16[1024,1024]{1,0:T(8,128)(2,1)S(1)}) fusion(bf16[1,1024,1024]{2,1,0:T(8,128)(2,1)} %get-tuple-element.20, f32[1024]{0:T(1024)S(1)} %bitcast.268, f32[1024]{0:T(1024)S(1)} %bitcast.270, bf16[3,1024,1024]{2,1,0:T(8,128)(2,1)} %param.6, f32[1024]{0:T(1024)S(1)} %bitcast.260, f32[1024]{0:T(1024)S(1)} %bitcast.262, ...), kind=kLoop, calls=%fused_computation.108 | loop fusion | flops 29360128 | bytes 18911232 | tf_op jit(solution)/shard_map/convert_element_type | solution.py:137
  69.2 49.7 %reduce-scatter.2.cloned.1.call-done = f32[1,16,1024]{2,1,0:T(8,128)} async-done(((f32[8,16,1024]{2,1,0:T(8,128)}), f32[1,16,1024]{2,1,0:T(8,128)}) %reduce-scatter.2.cloned.1.call-update) | async-done | bytes 65552 | tf_op jit(solution)/shard_map/reduce_scatter | solution.py:111
  118.9 1.5 copy.17
  120.3 4.6 %shard_map.65 = (f32[256,8,128]{2,1,0:T(8,128)}, f32[16,8,128]{2,1,0:T(8,128)}) custom-call(f32[256,8,128]{2,1,0:T(8,128)} %bitcast.237, f32[16,8,128]{2,1,0:T(8,128)} %bitcast.240, f32[16,8,128]{2,1,0:T(8,128)} %bitcast.244, f32[16,8,128]{2,1,0:T(8,128)} %bitcast.250), custom_call_target="tpu_custom_call" | custom-call | tf_op jit(solution)/shard_map/pallas_call | solution.py:71
  124.9 4.6 %shard_map.66 = (f32[256,8,128]{2,1,0:T(8,128)}, f32[16,8,128]{2,1,0:T(8,128)}) custom-call(f32[256,8,128]{2,1,0:T(8,128)} %bitcast.236, f32[16,8,128]{2,1,0:T(8,128)} %bitcast.241, f32[16,8,128]{2,1,0:T(8,128)} %bitcast.245, f32[16,8,128]{2,1,0:T(8,128)} %get-tuple-element.13.start_ref), custom_call_target="tpu_custom_call" | custom-call | tf_op jit(solution)/shard_map/pallas_call | solution.py:71
  129.6 4.6 %shard_map.67 = (f32[256,8,128]{2,1,0:T(8,128)}, f32[16,8,128]{2,1,0:T(8,128)}) custom-call(f32[256,8,128]{2,1,0:T(8,128)} %bitcast.235, f32[16,8,128]{2,1,0:T(8,128)} %bitcast.242, f32[16,8,128]{2,1,0:T(8,128)} %bitcast.246, f32[16,8,128]{2,1,0:T(8,128)} %get-tuple-element.15.start_ref), custom_call_target="tpu_custom_call" | custom-call | tf_op jit(solution)/shard_map/pallas_call | solution.py:71
  134.2 1.3 convert_convert_fusion.1
  135.5 1.3 convert_convert_fusion.3
  136.8 4.5 %fusion.29 = (bf16[256,1024]{1,0:T(8,128)(2,1)}, bf16[256,1024]{1,0:T(8,128)(2,1)}) fusion(f32[32,8,8,128]{3,2,1,0:T(8,128)S(1)} %bitcast.234, bf16[1024,1024]{1,0:T(8,128)(2,1)S(1)} %get-tuple-element.22, bf16[3,1024,1024]{2,1,0:T(8,128)(2,1)} %param.6, bf16[3,2,1024]{2,1,0:T(2,128)(2,1)S(1)} %collective-permute-done, f32[1024]{0:T(1024)S(1)} %copy-done.4, ...), kind=kLoop, calls=%fused_computation.63 | loop fusion | flops 8912896 | bytes 12611584 | tf_op jit(solution)/shard_map/convert_element_type | solution.py:156
  143.2 4.6 %shard_map.68 = (f32[256,8,128]{2,1,0:T(8,128)}, f32[16,8,128]{2,1,0:T(8,128)}) custom-call(f32[256,8,128]{2,1,0:T(8,128)} %bitcast.238, f32[16,8,128]{2,1,0:T(8,128)} %bitcast.243, f32[16,8,128]{2,1,0:T(8,128)} %bitcast.247, f32[16,8,128]{2,1,0:T(8,128)} %get-tuple-element.17.start_ref), custom_call_target="tpu_custom_call" | custom-call | tf_op jit(solution)/shard_map/pallas_call | solution.py:71
  147.9 1.4 convert_convert_fusion
  149.2 1.4 convert_convert_fusion.2
  150.6 4.4 %fusion.27 = (bf16[256,1024]{1,0:T(8,128)(2,1)}, bf16[256,1024]{1,0:T(8,128)(2,1)}) fusion(f32[32,8,8,128]{3,2,1,0:T(8,128)S(1)} %bitcast.233, bf16[1024,1024]{1,0:T(8,128)(2,1)S(1)} %get-tuple-element.22, bf16[3,1024,1024]{2,1,0:T(8,128)(2,1)} %param.6, f32[1024]{0:T(1024)S(1)} %copy-done.4, f32[1024]{0:T(1024)S(1)} %bitcast.256, f32[1024]{0:T(1024)S(1)} %bitcast.258, ...), kind=kLoop, calls=%fused_computation.60 | loop fusion | flops 6815744 | bytes 7356416 | tf_op jit(solution)/shard_map/convert_element_type | solution.py:156
  155.6 9.7 %all-gather.9.cloned.1.call-done = bf16[256,4096]{1,0:T(8,128)(2,1)} async-done(((bf16[256,1024]{1,0:T(8,128)(2,1)}), bf16[256,4096]{1,0:T(8,128)(2,1)}) %all-gather.9.cloned.1.call-update) | async-done | bytes 2097168 | tf_op jit(solution)/shard_map/all_gather | solution.py:158
  165.3 6.3 %convolution_convert_fusion.1 = bf16[256,1024]{1,0:T(8,128)(2,1)S(1)} fusion(bf16[256,4096]{1,0:T(8,128)(2,1)} %all-gather.9.cloned.1.call-done, bf16[4096,1024]{1,0:T(8,128)(2,1)} %param.11), kind=kOutput, calls=%fused_computation.49 | convolution fusion | flops 2147745792 | bytes 11010048 | tf_op jit(solution)/shard_map/dot_general | solution.py:157
  171.7 17.9 %all-gather.5.cloned.1.call-done = bf16[256,4096]{1,0:T(8,128)(2,1)} async-done(((bf16[256,1024]{1,0:T(8,128)(2,1)}), bf16[256,4096]{1,0:T(8,128)(2,1)}) %all-gather.5.cloned.1.call-update) | async-done | bytes 2097168 | tf_op jit(solution)/shard_map/all_gather | solution.py:158
  189.6 6.3 %convolution_convert_fusion.3 = bf16[256,1024]{1,0:T(8,128)(2,1)S(1)} fusion(bf16[256,4096]{1,0:T(8,128)(2,1)} %all-gather.5.cloned.1.call-done, bf16[4096,1024]{1,0:T(8,128)(2,1)} %param.11), kind=kOutput, calls=%fused_computation.51 | convolution fusion | flops 2147745792 | bytes 11010048 | tf_op jit(solution)/shard_map/dot_general | solution.py:157
  195.9 17.8 %all-gather.11.cloned.1.call-done = bf16[256,4096]{1,0:T(8,128)(2,1)} async-done(((bf16[256,1024]{1,0:T(8,128)(2,1)}), bf16[256,4096]{1,0:T(8,128)(2,1)}) %all-gather.11.cloned.1.call-update) | async-done | bytes 2097168 | tf_op jit(solution)/shard_map/all_gather | solution.py:158
  213.7 6.3 %convolution_convert_fusion = bf16[256,1024]{1,0:T(8,128)(2,1)S(1)} fusion(bf16[256,4096]{1,0:T(8,128)(2,1)} %all-gather.11.cloned.1.call-done, bf16[4096,1024]{1,0:T(8,128)(2,1)} %param.11), kind=kOutput, calls=%fused_computation.48 | convolution fusion | flops 2147745792 | bytes 11010048 | tf_op jit(solution)/shard_map/dot_general | solution.py:157
  220.1 17.8 %all-gather.7.cloned.1.call-done = bf16[256,4096]{1,0:T(8,128)(2,1)} async-done(((bf16[256,1024]{1,0:T(8,128)(2,1)}), bf16[256,4096]{1,0:T(8,128)(2,1)}) %all-gather.7.cloned.1.call-update) | async-done | bytes 2097168 | tf_op jit(solution)/shard_map/all_gather | solution.py:158
  237.8 6.3 %convolution_convert_fusion.2 = bf16[256,1024]{1,0:T(8,128)(2,1)S(1)} fusion(bf16[256,4096]{1,0:T(8,128)(2,1)} %all-gather.7.cloned.1.call-done, bf16[4096,1024]{1,0:T(8,128)(2,1)} %param.11), kind=kOutput, calls=%fused_computation.50 | convolution fusion | flops 2147745792 | bytes 11010048 | tf_op jit(solution)/shard_map/dot_general | solution.py:157
  244.2 1.5 pad_maximum_fusion.1
  (35 shorter events, 15.1 us)
Async XLA Ops:
  6.5 112.3 %reduce-scatter.2.cloned.1.call-start = ((), (), s32[]{:S(2)}) async-start(), calls=%async_computation.1 | async-start | bytes 589824 | tf_op jit(solution)/shard_map/reduce_scatter | solution.py:111
  7.4 7.9 %collective-permute-start = (bf16[3,2,1024]{2,1,0:T(2,128)(2,1)S(1)}, bf16[3,2,1024]{2,1,0:T(2,128)(2,1)S(1)}, u32[]{:S(2)}, u32[]{:S(2)}) collective-permute-start(bf16[3,2,1024]{2,1,0:T(2,128)(2,1)S(1)} %slice.132), channel_id=1, source_target_pairs={{0,4},{4,8},{8,12},{12,16},{16,20},{20,24},{24,28},{1,5},{5,9},{9,... | collective-permute-start | bytes 36872 | tf_op jit(solution)/shard_map/ppermute | solution.py:16
  25.7 3.4 %copy-start.2 = (f32[128,8,8,128]{3,1,2,0:T(8,128)S(1)}, f32[128,8,8,128]{3,1,2,0:T(8,128)}, u32[]{:S(2)}) copy-start(f32[128,8,8,128]{3,1,2,0:T(8,128)} %get-tuple-element.27) | copy-start | bytes 12582916
  29.1 2.2 copy-start
  38.4 3.2 %copy-start.1 = (f32[128,8,8,128]{3,2,1,0:T(8,128)S(1)}, f32[128,8,8,128]{3,2,1,0:T(8,128)}, u32[]{:S(2)}) copy-start(f32[128,8,8,128]{3,2,1,0:T(8,128)} %copy.12) | copy-start | bytes 12582916
  38.4 5.0 %copy-start.3 = (f32[128,8,8,128]{3,2,1,0:T(8,128)S(1)}, f32[128,8,8,128]{3,2,1,0:T(8,128)}, u32[]{:S(2)}) copy-start(f32[128,8,8,128]{3,2,1,0:T(8,128)} %copy.13) | copy-start | bytes 12582916
  58.1 107.2 %all-gather.9.cloned.1.call-start = ((), (), s32[]{:S(2)}) async-start(), calls=%async_computation.4 | async-start | bytes 2621440 | tf_op jit(solution)/shard_map/all_gather | solution.py:158
  69.2 67.5 %copy-start.4 = (f32[1024]{0:T(1024)S(1)}, f32[1024]{0:T(1024)}, u32[]{:S(2)}) copy-start(f32[1024]{0:T(1024)} %param.10) | copy-start | bytes 12292
  141.3 48.3 %all-gather.5.cloned.1.call-start = ((), (), s32[]{:S(2)}) async-start(), calls=%async_computation.2 | async-start | bytes 2621440 | tf_op jit(solution)/shard_map/all_gather | solution.py:158
  142.0 71.7 %all-gather.11.cloned.1.call-start = ((), (), s32[]{:S(2)}) async-start(), calls=%async_computation.5 | async-start | bytes 2621440 | tf_op jit(solution)/shard_map/all_gather | solution.py:158
  155.0 82.8 %all-gather.7.cloned.1.call-start = ((), (), s32[]{:S(2)}) async-start(), calls=%async_computation.3 | async-start | bytes 2621440 | tf_op jit(solution)/shard_map/all_gather | solution.py:158
Sparse Core Ops, SparseCore 0:
  58.2 60.6 reduce-scatter.1
  141.4 23.8 all-gather.8
  167.0 22.5 all-gather.4
  191.1 22.5 all-gather.10
  215.2 22.5 all-gather.6

commit v3 on v1

--- a/solution.py
+++ b/solution.py
@@ -96,6 +96,45 @@
     )(x3, decay3)
 
 
+def incoming_state(local_end, pole_rates, row_count):
+    ctx_count = lax.axis_size("ctx")
+    total = jnp.zeros_like(local_end)
+    for distance in range(1, ctx_count):
+        received = shifted(local_end, "ctx", distance)
+        total = total + jnp.exp(-pole_rates * jnp.float32(row_count * (distance - 1))) * received
+    return total
+
+
+def featurize(extended, tap_weights, stream, count):
+    taps = tap_weights.shape[0]
+    total = None
+    for tap_index in range(taps):
+        lead_row = taps - 1 - tap_index
+        term = tap_weights[tap_index, stream].astype(jnp.float32)[None, :] * extended[
+            stream, lead_row : lead_row + count
+        ].astype(jnp.float32)
+        total = term if total is None else total + term
+    return total
+
+
+def project(gated_mix, out_weight):
+    ch_count = lax.axis_size("ch")
+    width = gated_mix.shape[1]
+    if ch_count != 4:
+        gathered = lax.all_gather(gated_mix, "ch", axis=1, tiled=True)
+        return jnp.dot(gathered, out_weight, preferred_element_type=jnp.float32)
+    here = lax.axis_index("ch")
+    far = lax.ppermute(gated_mix, "ch", [(i, i ^ 2) for i in range(ch_count)])
+    near = lax.ppermute(gated_mix, "ch", [(i, i ^ 1) for i in range(ch_count)])
+    near_far = lax.ppermute(far, "ch", [(i, i ^ 1) for i in range(ch_count)])
+    total = None
+    for piece, owner in ((gated_mix, here), (near, here ^ 1), (far, here ^ 2), (near_far, here ^ 3)):
+        rows = lax.dynamic_slice_in_dim(out_weight, owner * width, width, 0)
+        part = jnp.dot(piece, rows, preferred_element_type=jnp.float32)
+        total = part if total is None else total + part
+    return total
+
+
 def shards(projected, tap_weights, pole_rates, residues, long_bias, out_weight):
     row_count = projected.shape[1]
     width = projected.shape[2]
@@ -104,44 +143,24 @@
     rim_rows = tap_weights.shape[0] - 1
     prior_rows = shifted(projected[:, row_count - rim_rows :], "ctx", 1)
     extended = jnp.concatenate([prior_rows, projected], 1)
-    featured = jnp.zeros(projected.shape, jnp.float32)
-    for tap_index in range(rim_rows + 1):
-        lead_row = rim_rows - tap_index
-        featured = featured + tap_weights[tap_index].astype(jnp.float32)[:, None, :] * extended[
-            :, lead_row : lead_row + row_count
-        ].astype(jnp.float32)
-    mixed_input = (featured[1] * featured[2]).astype(jnp.bfloat16)
+    mixed_input = (
+        featurize(extended, tap_weights, 1, row_count) * featurize(extended, tap_weights, 2, row_count)
+    ).astype(jnp.bfloat16)
     x3 = mixed_input.astype(jnp.float32).reshape(row_count, rows, LANES)
 
     decay = jnp.exp(-pole_rates)
     decay3 = decay.reshape(pole_count, rows, LANES)
     residue3 = residues.reshape(pole_count, rows, LANES)
     local_end = run_end_state(x3, decay3).reshape(pole_count, width)
-
-    ends = lax.all_gather(local_end, "ctx", axis=0, tiled=False)
-    ctx_count = ends.shape[0]
-    here = lax.axis_index("ctx")
-    earlier = jnp.arange(ctx_count, dtype=jnp.int32)
-    gaps = (here - 1 - earlier).astype(jnp.float32)
-    weights = jnp.where(
-        (earlier < here)[:, None, None],
-        jnp.exp(-pole_rates[None] * (jnp.float32(row_count) * jnp.maximum(gaps, 0.0))[:, None, None]),
-        jnp.float32(0.0),
-    )
-    start = jnp.sum(weights * ends, axis=0)
+    start = incoming_state(local_end, pole_rates, row_count)
 
     long_part, _ = run_recurrence(x3, decay3, residue3, start.reshape(pole_count, rows, LANES))
     long_mix = long_part.reshape(row_count, width).astype(jnp.bfloat16)
-    gated_mix = featured[0] * (
+    gated_mix = featurize(extended, tap_weights, 0, row_count) * (
         long_mix.astype(jnp.float32) + long_bias[None, :] * mixed_input.astype(jnp.float32)
     )
     gated_mix = gated_mix.astype(jnp.bfloat16)
-    mixed_out = jnp.dot(
-        lax.all_gather(gated_mix, "ch", axis=1, tiled=True),
-        out_weight,
-        preferred_element_type=jnp.float32,
-    )
-    return mixed_out.astype(jnp.bfloat16)
+    return project(gated_mix, out_weight).astype(jnp.bfloat16)
 
 
 def solution(mesh):

time: 177 us -> 159 us (0.90)
  blocking collectives: 25.6 us -> 0 us
  starting transfers between devices: 3.98 us -> 26.9 us
  waiting for transfers between devices: 64.5 us -> 42.4 us
  between operations: 13.5 us -> 0.25 us
  local copies, waits for them, and re-layouts: 10.9 us -> 22.6 us
  other arithmetic: 22 us -> 26.4 us
  matrix products: 14.6 us -> 18.1 us
    all_gather x1 -> x0, waiting for transfers between devices: 64.5 us -> none  [shards(): lax.all_gather(gated_mix, 'ch', axis=1, tiled=True)]
    ppermute x0 -> x3, waiting for transfers between devices: none -> 41.2 us  [the longest x1 41.2 us: project(): far = lax.ppermute(gated_mix, 'ch', [(i, i ^ 2) for i in range(ch_count)])]
    all_gather x1 -> x0, blocking collectives: 25.6 us -> none  [shards(): ends = lax.all_gather(local_end, 'ctx', axis=0, tiled=False)]
    ppermute x1 -> x8, starting transfers between devices: 3.97 us -> 19.8 us  [shifted(): lax.ppermute(value, axis, [(source, source + steps) for source in range(i...]
    unnamed x8 -> x34, local copies, waits for them, and re-layouts: 9.27 us -> 21.8 us
    add x1 -> x0, other arithmetic: 11 us -> none  [shards(): featured + tap_weights[tap_index].astype(jnp.float32)[:, None, :] * exten...]
    unnamed x1 -> x5, other arithmetic: 1.46 us -> 11.6 us
    ppermute x0 -> x3, starting transfers between devices: none -> 7.03 us  [the longest x1 3.23 us: project(): near_far = lax.ppermute(far, 'ch', [(i, i ^ 1) for i in range(ch_count)])]
  transfers between devices with their start and end apart: 2 -> 11, of which waited for: 1 -> 2; matrix products, arithmetic and copies ran while one was open for 2% -> 10% of each run, Pallas kernels for 0% -> 0%
where the time goes in v3:
time: 159 us; the launch traced here: 158 us
  waiting for transfers between devices  42.4 us (27%)
  starting transfers between devices  26.9 us (17%)
  other arithmetic  26.4 us (17%)
  local copies, waits for them, and re-layouts  22.6 us (14%)
  Pallas kernels  21.4 us (13%)
  matrix products  18.1 us (11%)
    ppermute x1, waiting for transfers between devices, project(): far = lax.ppermute(gated_mix, 'ch', [(i, i ^ 2) for i in range(ch_count)])  41.2 us
    unnamed x34, local copies, waits for them, and re-layouts  21.8 us
    ppermute x8, starting transfers between devices, shifted(): lax.ppermute(value, axis, [(source, source + steps) for source in range(i...  19.8 us
    dot_general x4, matrix products, project(): part = jnp.dot(piece, rows, preferred_element_type=jnp.float32)  18.1 us
    pallas_call x1, Pallas kernels, run_recurrence(): pl.pallas_call(recurrence_kernel, grid=(length // chunk,), in_specs=[row_...  13.1 us
    unnamed x5, other arithmetic  11.6 us
    pallas_call x1, Pallas kernels, run_end_state(): pl.pallas_call(end_state_kernel, grid=(length // chunk,), in_specs=[row_s...  8.32 us
    convert_element_type x1, other arithmetic, shards(): gated_mix = gated_mix.astype(jnp.bfloat16)  6.35 us
  transfers between devices with their start and end apart: 11, of which 2 were waited for; matrix products, arithmetic and copies ran while one was open for 10% of the time, Pallas kernels for 0%

profile of v3, /device:TPU:1, one launch (start us, length us, event | category | flops | bytes accessed | tf_op | source)
XLA Modules:
  0.0 158.1 jit_solution(2773883540312426716)
XLA Ops:
  0.8 4.0 %collective-permute-start = (bf16[3,2,1024]{2,1,0:T(2,128)(2,1)S(1)}, bf16[3,2,1024]{2,1,0:T(2,128)(2,1)S(1)}, u32[]{:S(2)}, u32[]{:S(2)}) collective-permute-start(bf16[3,2,1024]{2,1,0:T(2,128)(2,1)S(1)} %slice.60), channel_id=1, source_target_pairs={{0,4},{4,8},{8,12},{12,16},{16,20},{20,24},{24,28},{1,5},{5,9},{9,... | collective-permute-start | bytes 36872 | tf_op jit(solution)/shard_map/ppermute | solution.py:15
  5.7 0.9 slice_convert_fusion.8
  7.2 10.7 %convert_bitcast_fusion.9 = (f32[128,8,8,128]{3,1,2,0:T(8,128)S(1)}, f32[128,8,8,128]{3,1,2,0:T(8,128)S(1)}, f32[128,8,8,128]{3,1,2,0:T(8,128)}, bf16[1,1024,102...) fusion(bf16[3,1024,1024]{2,1,0:T(8,128)(2,1)} %param.6, ...), kind=kLoop, calls=%fused_computation.14 | loop fusion | flops 19922944 | bytes 37761024
  17.9 3.4 %copy.10 = f32[128,8,8,128]{3,2,1,0:T(8,128)S(1)} copy(f32[128,8,8,128]{3,1,2,0:T(8,128)} %get-tuple-element.15) | data formatting | bytes 8388608
  21.3 1.0 copy.11
  22.3 1.2 copy-done
  23.5 3.0 %copy.12 = f32[128,8,8,128]{3,2,1,0:T(8,128)} copy(f32[128,8,8,128]{3,1,2,0:T(8,128)S(1)} %copy-done) | data formatting | bytes 8388608
  26.5 3.0 %copy.7 = f32[128,8,8,128]{3,2,1,0:T(8,128)} copy(f32[128,8,8,128]{3,1,2,0:T(8,128)S(1)} %get-tuple-element.14) | data formatting | bytes 8388608
  29.4 1.0 copy.8
  30.5 3.2 %copy.9 = f32[128,8,8,128]{3,2,1,0:T(8,128)} copy(f32[128,8,8,128]{3,1,2,0:T(8,128)S(1)} %get-tuple-element.10) | data formatting | bytes 8388608
  33.7 1.8 %copy-done.3 = f32[128,8,8,128]{3,2,1,0:T(8,128)S(1)} copy-done((f32[128,8,8,128]{3,2,1,0:T(8,128)S(1)}, f32[128,8,8,128]{3,2,1,0:T(8,128)}, u32[]{:S(2)}) %copy-start.3) | copy-done | bytes 4194328
  35.4 4.9 %fusion.29.x_ref = f32[1024,8,128]{2,1,0:T(8,128)} fusion(f32[128,8,8,128]{3,2,1,0:T(8,128)S(1)} %copy-done.1, f32[128,8,8,128]{3,2,1,0:T(8,128)S(1)} %copy.11, f32[128,8,8,128]{3,2,1,0:T(8,128)S(1)} %copy.10, f32[128,8,8,128]{3,2,1,0:T(8,128)} %copy.9, f32[128,8,8,128]{3,2,1,0:T(8,128)S(1)} %copy.8, f32[128,8,8,128]{3,2,1,0:T(8,128)S(1)} %copy-done.3, ...), kind=kLoop, calls=%fused_computation.62 | loop fusion | flops 13631488 | bytes 29384704 | tf_op jit(solution)/shard_map/convert_element_type | solution.py:149
  40.4 8.3 %shard_map.64 = f32[16,8,128]{2,1,0:T(8,128)} custom-call(f32[1024,8,128]{2,1,0:T(8,128)} %fusion.29.x_ref, f32[16,8,128]{2,1,0:T(8,128)} %bitcast.176), custom_call_target="tpu_custom_call" | custom-call | tf_op jit(solution)/shard_map/pallas_call | solution.py:89
  49.5 3.2 %collective-permute-start.1 = (f32[16,1024]{1,0:T(8,128)S(1)}, f32[16,1024]{1,0:T(8,128)S(1)}, u32[]{:S(2)}, u32[]{:S(2)}) collective-permute-start(f32[16,1024]{1,0:T(8,128)S(1)} %bitcast.182), channel_id=1, source_target_pairs={{0,4},{4,8},{8,12},{12,16},{16,20},{20,24},{24,28},{1,5},{5,9},{9,... | collective-permute-start | bytes 196616 | tf_op jit(solution)/shard_map/ppermute | solution.py:15
  52.7 3.2 %collective-permute-start.2 = (f32[16,1024]{1,0:T(8,128)S(1)}, f32[16,1024]{1,0:T(8,128)S(1)}, u32[]{:S(2)}, u32[]{:S(2)}) collective-permute-start(f32[16,1024]{1,0:T(8,128)S(1)} %bitcast.183), channel_id=1, source_target_pairs={{0,8},{4,12},{8,16},{12,20},{16,24},{20,28},{1,9},{5,13},{9,17},{1... | collective-permute-start | bytes 196616 | tf_op jit(solution)/shard_map/ppermute | solution.py:15
  55.9 4.2 %collective-permute-start.3 = (f32[16,1024]{1,0:T(8,128)S(1)}, f32[16,1024]{1,0:T(8,128)S(1)}, u32[]{:S(2)}, u32[]{:S(2)}) collective-permute-start(f32[16,1024]{1,0:T(8,128)S(1)} %bitcast.184), channel_id=1, source_target_pairs={{0,12},{4,16},{8,20},{12,24},{16,28},{1,13},{5,17},{9,21},{13,25},... | collective-permute-start | bytes 196616 | tf_op jit(solution)/shard_map/ppermute | solution.py:15
  60.1 1.3 collective-permute-start.4
  61.4 1.3 collective-permute-start.5
  62.7 1.3 collective-permute-start.6
  64.0 1.5 collective-permute-start.7
  66.2 1.2 collective-permute-done.7
  68.1 13.1 %shard_map.65 = (f32[1024,8,128]{2,1,0:T(8,128)}, f32[16,8,128]{2,1,0:T(8,128)}) custom-call(f32[1024,8,128]{2,1,0:T(8,128)} %fusion.29.x_ref, f32[16,8,128]{2,1,0:T(8,128)} %bitcast.177, f32[16,8,128]{2,1,0:T(8,128)} %bitcast.178, f32[16,8,128]{2,1,0:T(8,128)} %bitcast.179), custom_call_target="tpu_custom_call" | custom-call | tf_op jit(solution)/shard_map/pallas_call | solution.py:70
  81.2 2.6 %convert_convert_fusion = f32[1024,8,128]{2,1,0:T(8,128)S(1)} fusion(f32[1024,8,128]{2,1,0:T(8,128)} %get-tuple-element.6), kind=kLoop, calls=%fused_computation.72 | loop fusion | flops 2097152 | bytes 8388608 | tf_op jit(solution)/shard_map/convert_element_type | solution.py:160
  85.3 6.4 %fusion.13 = bf16[1024,1024]{1,0:T(8,128)(2,1)} fusion(f32[128,8,8,128]{3,2,1,0:T(8,128)S(1)} %bitcast.175, bf16[3,1024,1024]{2,1,0:T(8,128)(2,1)S(1)} %bitcast.174, bf16[1,1024,1024]{2,1,0:T(8,128)(2,1)S(1)} %copy-done.4, bf16[3,2,1024]{2,1,0:T(2,128)(2,1)S(1)} %collective-permute-done, f32[1024]{0:T(1024)S(1)} %bitcast.198, f32[1024]{0:T(1024)S(1)} %bitcast.200, ...), kind=kLoop, calls=%fused_computation.31 | loop fusion | flops 50331648 | bytes 21024768 | tf_op jit(solution)/shard_map/convert_element_type | solution.py:162
  91.7 1.2 collective-permute-start.9
  92.9 2.6 %collective-permute-start.8 = (bf16[1024,1024]{1,0:T(8,128)(2,1)}, bf16[1024,1024]{1,0:T(8,128)(2,1)}, u32[]{:S(2)}, u32[]{:S(2)}) collective-permute-start(bf16[1024,1024]{1,0:T(8,128)(2,1)} %fusion.13), channel_id=1, source_target_pairs={{0,1},{1,0},{2,3},{3,2},{4,5},{5,4},{6,7},{7,6},{8,9},{9,8},{10,11... | collective-permute-start | bytes 6291464 | tf_op jit(solution)/shard_map/ppermute | solution.py:128
  95.5 41.2 %collective-permute-done.9 = bf16[1024,1024]{1,0:T(8,128)(2,1)S(1)} collective-permute-done((bf16[1024,1024]{1,0:T(8,128)(2,1)}, bf16[1024,1024]{1,0:T(8,128)(2,1)S(1)}, u32[]{:S(2)}, u32[]{:S(2)}) %collective-permute-start.9) | collective-permute-done | bytes 2097184 | tf_op jit(solution)/shard_map/ppermute | solution.py:127
  136.7 3.2 %collective-permute-start.10 = (bf16[1024,1024]{1,0:T(8,128)(2,1)S(1)}, bf16[1024,1024]{1,0:T(8,128)(2,1)}, u32[]{:S(2)}, u32[]{:S(2)}) collective-permute-start(bf16[1024,1024]{1,0:T(8,128)(2,1)S(1)} %collective-permute-done.9), channel_id=1, source_target_pairs={{0,1},{1,0},{2,3},{3,2},{4,5},{5,4},{6,7},{7,6},{8,9},{9,8},{10,11... | collective-permute-start | bytes 6291464 | tf_op jit(solution)/shard_map/ppermute | solution.py:129
  139.9 4.7 %fusion.36 = f32[1024,1024]{1,0:T(8,128)S(1)} fusion(bf16[1024,1024]{1,0:T(8,128)(2,1)} %fusion.13, bf16[4096,1024]{1,0:T(8,128)(2,1)} %param.11, s32[]{:T(128)S(6)} %select_n.12), kind=kOutput, calls=%fused_computation.70 | convolution fusion | flops 2147483648 | bytes 8388612 | tf_op jit(solution)/shard_map/dot_general | solution.py:133
  144.6 4.1 %fusion.32 = f32[1024,1024]{1,0:T(8,128)S(1)} fusion(bf16[1024,1024]{1,0:T(8,128)(2,1)S(1)} %collective-permute-done.9, bf16[4096,1024]{1,0:T(8,128)(2,1)} %param.11, s32[]{:T(128)S(6)} %select_n.14), kind=kOutput, calls=%fused_computation.66 | convolution fusion | flops 2147483648 | bytes 8388612 | tf_op jit(solution)/shard_map/dot_general | solution.py:133
  148.7 3.9 %fusion.34 = f32[1024,1024]{1,0:T(8,128)S(1)} fusion(bf16[1024,1024]{1,0:T(8,128)(2,1)} %collective-permute-done.8, bf16[4096,1024]{1,0:T(8,128)(2,1)S(1)} %bitcast.205, s32[]{:T(128)S(6)} %select_n.13), kind=kOutput, calls=%fused_computation.68 | convolution fusion | flops 2147483648 | bytes 8388612 | tf_op jit(solution)/shard_map/dot_general | solution.py:133
  152.7 5.4 %add_convert_fusion = bf16[1024,1024]{1,0:T(8,128)(2,1)} fusion(f32[1024,1024]{1,0:T(8,128)S(1)} %fusion.32, f32[1024,1024]{1,0:T(8,128)S(1)} %fusion.36, f32[1024,1024]{1,0:T(8,128)S(1)} %fusion.34, bf16[1024,1024]{1,0:T(8,128)(2,1)} %collective-permute-done.10, bf16[4096,1024]{1,0:T(8,128)(2,1)S(1)} %bitcast.205, s32[]{:T(128)S(6)} %select_n.15), kind=kOutput, calls=%fused_computation.49 | convolution fusion | flops 2151677952 | bytes 18874372 | tf_op jit(solution)/shard_map/dot_general | solution.py:133
  (40 shorter events, 6.1 us)
Async XLA Ops:
  0.8 6.4 %collective-permute-start = (bf16[3,2,1024]{2,1,0:T(2,128)(2,1)S(1)}, bf16[3,2,1024]{2,1,0:T(2,128)(2,1)S(1)}, u32[]{:S(2)}, u32[]{:S(2)}) collective-permute-start(bf16[3,2,1024]{2,1,0:T(2,128)(2,1)S(1)} %slice.60), channel_id=1, source_target_pairs={{0,4},{4,8},{8,12},{12,16},{16,20},{20,24},{24,28},{1,5},{5,9},{9,... | collective-permute-start | bytes 36872 | tf_op jit(solution)/shard_map/ppermute | solution.py:15
  17.9 3.4 %copy-start.2 = (f32[128,8,8,128]{3,1,2,0:T(8,128)S(1)}, f32[128,8,8,128]{3,1,2,0:T(8,128)}, u32[]{:S(2)}) copy-start(f32[128,8,8,128]{3,1,2,0:T(8,128)} %get-tuple-element.13) | copy-start | bytes 12582916
  21.3 2.2 %copy-start = (f32[128,8,8,128]{3,1,2,0:T(8,128)S(1)}, f32[128,8,8,128]{3,1,2,0:T(8,128)}, u32[]{:S(2)}) copy-start(f32[128,8,8,128]{3,1,2,0:T(8,128)} %get-tuple-element.11) | copy-start | bytes 12582916
  30.5 3.2 %copy-start.1 = (f32[128,8,8,128]{3,2,1,0:T(8,128)S(1)}, f32[128,8,8,128]{3,2,1,0:T(8,128)}, u32[]{:S(2)}) copy-start(f32[128,8,8,128]{3,2,1,0:T(8,128)} %copy.12) | copy-start | bytes 12582916
  30.5 5.0 %copy-start.3 = (f32[128,8,8,128]{3,2,1,0:T(8,128)S(1)}, f32[128,8,8,128]{3,2,1,0:T(8,128)}, u32[]{:S(2)}) copy-start(f32[128,8,8,128]{3,2,1,0:T(8,128)} %copy.7) | copy-start | bytes 12582916
  40.4 25.1 %copy-start.6 = (f32[16,1024]{1,0:T(8,128)S(1)}, f32[16,1024]{1,0:T(8,128)}, u32[]{:S(2)}) copy-start(f32[16,1024]{1,0:T(8,128)} %param.9) | copy-start | bytes 196612
  40.4 27.0 %copy-start.5 = (f32[16,1024]{1,0:T(8,128)S(1)}, f32[16,1024]{1,0:T(8,128)}, u32[]{:S(2)}) copy-start(f32[16,1024]{1,0:T(8,128)} %param.8) | copy-start | bytes 196612
  49.5 13.1 %collective-permute-start.1 = (f32[16,1024]{1,0:T(8,128)S(1)}, f32[16,1024]{1,0:T(8,128)S(1)}, u32[]{:S(2)}, u32[]{:S(2)}) collective-permute-start(f32[16,1024]{1,0:T(8,128)S(1)} %bitcast.182), channel_id=1, source_target_pairs={{0,4},{4,8},{8,12},{12,16},{16,20},{20,24},{24,28},{1,5},{5,9},{9,... | collective-permute-start | bytes 196616 | tf_op jit(solution)/shard_map/ppermute | solution.py:15
  52.7 11.3 %collective-permute-start.2 = (f32[16,1024]{1,0:T(8,128)S(1)}, f32[16,1024]{1,0:T(8,128)S(1)}, u32[]{:S(2)}, u32[]{:S(2)}) collective-permute-start(f32[16,1024]{1,0:T(8,128)S(1)} %bitcast.183), channel_id=1, source_target_pairs={{0,8},{4,12},{8,16},{12,20},{16,24},{20,28},{1,9},{5,13},{9,17},{1... | collective-permute-start | bytes 196616 | tf_op jit(solution)/shard_map/ppermute | solution.py:15
  55.9 10.2 %collective-permute-start.3 = (f32[16,1024]{1,0:T(8,128)S(1)}, f32[16,1024]{1,0:T(8,128)S(1)}, u32[]{:S(2)}, u32[]{:S(2)}) collective-permute-start(f32[16,1024]{1,0:T(8,128)S(1)} %bitcast.184), channel_id=1, source_target_pairs={{0,12},{4,16},{8,20},{12,24},{16,28},{1,13},{5,17},{9,21},{13,25},... | collective-permute-start | bytes 196616 | tf_op jit(solution)/shard_map/ppermute | solution.py:15
  60.1 6.1 %collective-permute-start.4 = (f32[16,1024]{1,0:T(8,128)S(1)}, f32[16,1024]{1,0:T(8,128)S(1)}, u32[]{:S(2)}, u32[]{:S(2)}) collective-permute-start(f32[16,1024]{1,0:T(8,128)S(1)} %bitcast.185), channel_id=1, source_target_pairs={{0,16},{4,20},{8,24},{12,28},{1,17},{5,21},{9,25},{13,29},{2,18},{... | collective-permute-start | bytes 196616 | tf_op jit(solution)/shard_map/ppermute | solution.py:15
  61.4 4.8 %collective-permute-start.5 = (f32[16,1024]{1,0:T(8,128)S(1)}, f32[16,1024]{1,0:T(8,128)S(1)}, u32[]{:S(2)}, u32[]{:S(2)}) collective-permute-start(f32[16,1024]{1,0:T(8,128)S(1)} %bitcast.186), channel_id=1, source_target_pairs={{0,20},{4,24},{8,28},{1,21},{5,25},{9,29},{2,22},{6,26},{10,30},{3... | collective-permute-start | bytes 196616 | tf_op jit(solution)/shard_map/ppermute | solution.py:15
  62.7 3.5 %collective-permute-start.6 = (f32[16,1024]{1,0:T(8,128)S(1)}, f32[16,1024]{1,0:T(8,128)S(1)}, u32[]{:S(2)}, u32[]{:S(2)}) collective-permute-start(f32[16,1024]{1,0:T(8,128)S(1)} %bitcast.187), channel_id=1, source_target_pairs={{0,24},{4,28},{1,25},{5,29},{2,26},{6,30},{3,27},{7,31}} | collective-permute-start | bytes 196616 | tf_op jit(solution)/shard_map/ppermute | solution.py:15
  64.0 3.3 %collective-permute-start.7 = (f32[16,1024]{1,0:T(8,128)S(1)}, f32[16,1024]{1,0:T(8,128)S(1)}, u32[]{:S(2)}, u32[]{:S(2)}) collective-permute-start(f32[16,1024]{1,0:T(8,128)S(1)} %bitcast.188), channel_id=1, source_target_pairs={{0,28},{1,29},{2,30},{3,31}} | collective-permute-start | bytes 196616 | tf_op jit(solution)/shard_map/ppermute | solution.py:15
  68.1 15.7 %slice-start = ((s8[6291456]{0:T(1024)(128)(4,1)}), s8[2097152]{0:T(1024)(128)(4,1)S(1)}, s32[]{:S(2)}) async-start(s8[6291456]{0:T(1024)(128)(4,1)} %bitcast.173), calls=%async_computation | async-start | bytes 4194304
  81.2 3.5 %slice-start.1 = ((s8[6291456]{0:T(1024)(128)(4,1)}), s8[4194304]{0:T(1024)(128)(4,1)S(1)}, s32[]{:S(2)}) async-start(s8[6291456]{0:T(1024)(128)(4,1)} %bitcast.173), calls=%async_computation.1 | async-start | bytes 8388608
  81.2 4.1 %copy-start.4 = (bf16[1,1024,1024]{2,1,0:T(8,128)(2,1)S(1)}, bf16[1,1024,1024]{2,1,0:T(8,128)(2,1)}, u32[]{:S(2)}) copy-start(bf16[1,1024,1024]{2,1,0:T(8,128)(2,1)} %get-tuple-element.12) | copy-start | bytes 6291460
  81.2 4.1 %copy-start.7 = (f32[1024]{0:T(1024)S(1)}, f32[1024]{0:T(1024)}, u32[]{:S(2)}) copy-start(f32[1024]{0:T(1024)} %param.10) | copy-start | bytes 12292
  91.7 45.0 %collective-permute-start.9 = (bf16[1024,1024]{1,0:T(8,128)(2,1)}, bf16[1024,1024]{1,0:T(8,128)(2,1)S(1)}, u32[]{:S(2)}, u32[]{:S(2)}) collective-permute-start(bf16[1024,1024]{1,0:T(8,128)(2,1)} %fusion.13), channel_id=1, source_target_pairs={{0,2},{1,3},{2,0},{3,1},{4,6},{5,7},{6,4},{7,5},{8,10},{9,11},{10,... | collective-permute-start | bytes 6291464 | tf_op jit(solution)/shard_map/ppermute | solution.py:127
  92.9 55.8 %collective-permute-start.8 = (bf16[1024,1024]{1,0:T(8,128)(2,1)}, bf16[1024,1024]{1,0:T(8,128)(2,1)}, u32[]{:S(2)}, u32[]{:S(2)}) collective-permute-start(bf16[1024,1024]{1,0:T(8,128)(2,1)} %fusion.13), channel_id=1, source_target_pairs={{0,1},{1,0},{2,3},{3,2},{4,5},{5,4},{6,7},{7,6},{8,9},{9,8},{10,11... | collective-permute-start | bytes 6291464 | tf_op jit(solution)/shard_map/ppermute | solution.py:128
  136.7 16.0 %collective-permute-start.10 = (bf16[1024,1024]{1,0:T(8,128)(2,1)S(1)}, bf16[1024,1024]{1,0:T(8,128)(2,1)}, u32[]{:S(2)}, u32[]{:S(2)}) collective-permute-start(bf16[1024,1024]{1,0:T(8,128)(2,1)S(1)} %collective-permute-done.9), channel_id=1, source_target_pairs={{0,1},{1,0},{2,3},{3,2},{4,5},{5,4},{6,7},{7,6},{8,9},{9,8},{10,11... | collective-permute-start | bytes 6291464 | tf_op jit(solution)/shard_map/ppermute | solution.py:129
  139.9 8.8 %slice-start.2 = ((s8[8388608]{0:T(1024)(128)(4,1)}), s8[4194304]{0:T(1024)(128)(4,1)S(1)}, s32[]{:S(2)}) async-start(s8[8388608]{0:T(1024)(128)(4,1)} %bitcast.204), calls=%async_computation.2 | async-start | bytes 8388608
  144.6 4.1 %slice-start.3 = ((s8[8388608]{0:T(1024)(128)(4,1)}), s8[4194304]{0:T(1024)(128)(4,1)S(1)}, s32[]{:S(2)}) async-start(s8[8388608]{0:T(1024)(128)(4,1)} %bitcast.204), calls=%async_computation.3 | async-start | bytes 8388608

commit v4 on v3

v4 whole, which is shorter than its diff:
```python
import jax
import jax.numpy as jnp
from jax import lax
from jax.experimental import pallas as pl
from jax.experimental.pallas import tpu as pltpu
from jax.sharding import PartitionSpec as P

LANES = 128
SEGMENTS = 8


def shifted(value, axis, steps):
    count = lax.axis_size(axis)
    initial, last = (max(0, -steps), min(count, count - steps))
    return lax.ppermute(value, axis, [(source, source + steps) for source in range(initial, last)])


def segment_pass(x_ref, decay_ref, residue_ref, start_ref, y_ref, end_ref):
    pole_count = decay_ref.shape[0]
    segments = SEGMENTS
    span = x_ref.shape[0] // segments
    lanes = x_ref.shape[1]
    decays = [jnp.broadcast_to(decay_ref[p : p + 1, :], (segments, lanes)) for p in range(pole_count)]
    if residue_ref is not None:
        residues = [jnp.broadcast_to(residue_ref[p : p + 1, :], (segments, lanes)) for p in range(pole_count)]
    if start_ref is None:
        states = tuple(jnp.zeros((segments, lanes), jnp.float32) for _ in range(pole_count))
    else:
        states = tuple(start_ref[p] for p in range(pole_count))

    def body(t, states):
        x = x_ref[pl.ds(t, segments, stride=span), :]
        updated = []
        total = None
        for p in range(pole_count):
            h = decays[p] * states[p] + x
            updated.append(h)
            if y_ref is not None:
                term = residues[p] * h
                total = term if total is None else total + term
        if y_ref is not None:
            y_ref[pl.ds(t, segments, stride=span), :] = total
        return tuple(updated)

    states = lax.fori_loop(0, span, body, states, unroll=4)
    if end_ref is not None:
        for p in range(pole_count):
            end_ref[p] = states[p]


def end_state_kernel(x_ref, decay_ref, end_ref):
    segment_pass(x_ref, decay_ref, None, None, None, end_ref)


def recurrence_kernel(x_ref, decay_ref, residue_ref, start_ref, y_ref):
    segment_pass(x_ref, decay_ref, residue_ref, start_ref, y_ref, None)


def run_end_state(x, decay):
    length, width = x.shape
    pole_count = decay.shape[0]
    return pl.pallas_call(
        end_state_kernel,
        grid=(width // LANES,),
        in_specs=[
            pl.BlockSpec((length, LANES), lambda g: (0, g)),
            pl.BlockSpec((pole_count, LANES), lambda g: (0, g)),
        ],
        out_specs=pl.BlockSpec((pole_count, SEGMENTS, LANES), lambda g: (0, 0, g)),
        out_shape=jax.ShapeDtypeStruct((pole_count, SEGMENTS, width), jnp.float32),
    )(x, decay)


def run_recurrence(x, decay, residue, start):
    length, width = x.shape
    pole_count = decay.shape[0]
    pole_spec = pl.BlockSpec((pole_count, LANES), lambda g: (0, g))
    return pl.pallas_call(
        recurrence_kernel,
        grid=(width // LANES,),
        in_specs=[
            pl.BlockSpec((length, LANES), lambda g: (0, g)),
            pole_spec,
            pole_spec,
            pl.BlockSpec((pole_count, SEGMENTS, LANES), lambda g: (0, 0, g)),
        ],
        out_specs=pl.BlockSpec((length, LANES), lambda g: (0, g)),
        out_shape=jax.ShapeDtypeStruct(x.shape, jnp.float32),
    )(x, decay, residue, start)


def segment_starts(ends, incoming, pole_rates, span):
    segments = ends.shape[1]
    index = jnp.arange(segments, dtype=jnp.int32)
    gaps = (index[:, None] - 1 - index[None, :]).astype(jnp.float32)
    weights = jnp.where(
        (index[None, :] < index[:, None])[:, :, None, None],
        jnp.exp(-pole_rates[None, None] * (jnp.float32(span) * jnp.maximum(gaps, 0.0))[:, :, None, None]),
        jnp.float32(0.0),
    )
    carried = jnp.einsum("abpc,pbc->pac", weights, ends, precision=lax.Precision.HIGHEST)
    lead = jnp.exp(-pole_rates[:, None, :] * (jnp.float32(span) * index.astype(jnp.float32))[None, :, None])
    return carried + lead * incoming[:, None, :]


def device_end(ends, pole_rates, span):
    segments = ends.shape[1]
    index = jnp.arange(segments, dtype=jnp.float32)
    weights = jnp.exp(-pole_rates[:, None, :] * (jnp.float32(span) * (segments - 1 - index))[None, :, None])
    return jnp.sum(weights * ends, axis=1)


def incoming_state(local_end, pole_rates, row_count):
    ctx_count = lax.axis_size("ctx")
    total = jnp.zeros_like(local_end)
    for distance in range(1, ctx_count):
        received = shifted(local_end, "ctx", distance)
        total = total + jnp.exp(-pole_rates * jnp.float32(row_count * (distance - 1))) * received
    return total


def featurize(extended, tap_weights, stream, count):
    taps = tap_weights.shape[0]
    total = None
    for tap_index in range(taps):
        lead_row = taps - 1 - tap_index
        term = tap_weights[tap_index, stream].astype(jnp.float32)[None, :] * extended[
            stream, lead_row : lead_row + count
        ].astype(jnp.float32)
        total = term if total is None else total + term
    return total


def project(gated_mix, out_weight):
    ch_count = lax.axis_size("ch")
    width = gated_mix.shape[1]
    if ch_count != 4:
        gathered = lax.all_gather(gated_mix, "ch", axis=1, tiled=True)
        return jnp.dot(gathered, out_weight, preferred_element_type=jnp.float32)
    here = lax.axis_index("ch")
    far = lax.ppermute(gated_mix, "ch", [(i, i ^ 2) for i in range(ch_count)])
    near = lax.ppermute(gated_mix, "ch", [(i, i ^ 1) for i in range(ch_count)])
    near_far = lax.ppermute(far, "ch", [(i, i ^ 1) for i in range(ch_count)])
    total = None
    for piece, owner in ((gated_mix, here), (near, here ^ 1), (far, here ^ 2), (near_far, here ^ 3)):
        rows = lax.dynamic_slice_in_dim(out_weight, owner * width, width, 0)
        part = jnp.dot(piece, rows, preferred_element_type=jnp.float32)
        total = part if total is None else total + part
    return total


def shards(projected, tap_weights, pole_rates, residues, long_bias, out_weight):
    row_count = projected.shape[1]
    width = projected.shape[2]
    rows = width // LANES
    pole_count = pole_rates.shape[0]
    rim_rows = tap_weights.shape[0] - 1
    prior_rows = shifted(projected[:, row_count - rim_rows :], "ctx", 1)
    extended = jnp.concatenate([prior_rows, projected], 1)
    mixed_input = (
        featurize(extended, tap_weights, 1, row_count) * featurize(extended, tap_weights, 2, row_count)
    ).astype(jnp.bfloat16)
    x = mixed_input.astype(jnp.float32)
    span = row_count // SEGMENTS

    decay = jnp.exp(-pole_rates)
    ends = run_end_state(x, decay)
    start = incoming_state(device_end(ends, pole_rates, span), pole_rates, row_count)
    long_part = run_recurrence(x, decay, residues, segment_starts(ends, start, pole_rates, span))
    long_mix = long_part.astype(jnp.bfloat16)
    gated_mix = featurize(extended, tap_weights, 0, row_count) * (
        long_mix.astype(jnp.float32) + long_bias[None, :] * mixed_input.astype(jnp.float32)
    )
    gated_mix = gated_mix.astype(jnp.bfloat16)
    return project(gated_mix, out_weight).astype(jnp.bfloat16)


def solution(mesh):
    in_specs = (
        P(None, "ctx", "ch"),
        P(None, None, "ch"),
        P(None, "ch"),
        P(None, "ch"),
        P("ch"),
        P(None, "ch"),
    )
    out_specs = P("ctx", "ch")
    return jax.shard_map(shards, mesh=mesh, in_specs=in_specs, out_specs=out_specs, check_vma=False)
```

time: 159 us -> 137 us (0.86)
  local copies, waits for them, and re-layouts: 22.6 us -> 2.17 us
  other arithmetic: 26.4 us -> 21.4 us
  Pallas kernels: 21.4 us -> 26 us
  waiting for transfers between devices: 42.4 us -> 39.6 us
    unnamed x34 -> x5, local copies, waits for them, and re-layouts: 21.8 us -> 1.36 us
    unnamed x5 -> x1, other arithmetic: 11.6 us -> 1.23 us
    pallas_call x2, Pallas kernels: 21.4 us -> 26 us  [the longest x1 16.5 us: run_recurrence(): pl.pallas_call(recurrence_kernel, grid=(width // LANES,), in_specs=[pl.Bl...]
    ppermute x1, waiting for transfers between devices: 41.2 us -> 39.6 us  [project(): far = lax.ppermute(gated_mix, 'ch', [(i, i ^ 2) for i in range(ch_count)])]
    convert_element_type x2 -> x1, other arithmetic: 7.53 us -> 8.71 us  [shards(): x = mixed_input.astype(jnp.float32)]
  transfers between devices with their start and end apart: 11 -> 11, of which waited for: 2 -> 1; matrix products, arithmetic and copies ran while one was open for 10% -> 13% of each run, Pallas kernels for 0% -> 0%
where the time goes in v4:
time: 137 us; the launch traced here: 136 us
  waiting for transfers between devices  39.6 us (29%)
  starting transfers between devices  27.9 us (20%)
  Pallas kernels  26 us (19%)
  other arithmetic  21.4 us (16%)
  matrix products  19 us (14%)
  local copies, waits for them, and re-layouts  2.17 us (2%)
    ppermute x1, waiting for transfers between devices, project(): far = lax.ppermute(gated_mix, 'ch', [(i, i ^ 2) for i in range(ch_count)])  39.6 us
    ppermute x8, starting transfers between devices, shifted(): lax.ppermute(value, axis, [(source, source + steps) for source in range(i...  19.3 us
    dot_general x4, matrix products, project(): part = jnp.dot(piece, rows, preferred_element_type=jnp.float32)  19 us
    pallas_call x1, Pallas kernels, run_recurrence(): pl.pallas_call(recurrence_kernel, grid=(width // LANES,), in_specs=[pl.Bl...  16.5 us
    pallas_call x1, Pallas kernels, run_end_state(): pl.pallas_call(end_state_kernel, grid=(width // LANES,), in_specs=[pl.Blo...  9.47 us
    convert_element_type x1, other arithmetic, shards(): x = mixed_input.astype(jnp.float32)  8.71 us
    convert_element_type x1, other arithmetic, shards(): gated_mix = gated_mix.astype(jnp.bfloat16)  6.43 us
    ppermute x1, starting transfers between devices, project(): near_far = lax.ppermute(far, 'ch', [(i, i ^ 1) for i in range(ch_count)])  3.99 us
  transfers between devices with their start and end apart: 11, of which 1 were waited for; matrix products, arithmetic and copies ran while one was open for 13% of the time, Pallas kernels for 0%

profile of v4, /device:TPU:1, one launch (start us, length us, event | category | flops | bytes accessed | tf_op | source)
XLA Modules:
  0.0 136.3 jit_solution(3089015867767592303)
XLA Ops:
  0.0 0.8 slice.60
  0.8 4.0 %collective-permute-start = (bf16[3,2,1024]{2,1,0:T(2,128)(2,1)S(1)}, bf16[3,2,1024]{2,1,0:T(2,128)(2,1)S(1)}, u32[]{:S(2)}, u32[]{:S(2)}) collective-permute-start(bf16[3,2,1024]{2,1,0:T(2,128)(2,1)S(1)} %slice.60), channel_id=1, source_target_pairs={{0,4},{4,8},{8,12},{12,16},{16,20},{20,24},{24,28},{1,5},{5,9},{9,... | collective-permute-start | bytes 36872 | tf_op jit(solution)/shard_map/ppermute | solution.py:15
  4.8 0.1 maximum_multiply_fusion
  4.9 0.9 slice_convert_fusion.8
  5.8 1.5 %fusion.36 = (f32[16,1024]{1,0:T(8,128)S(1)}, f32[16,1024]{1,0:T(8,128)}) fusion(f32[16,1024]{1,0:T(8,128)} %param.8), kind=kLoop, calls=%fused_computation.74 | loop fusion | flops 16384 | bytes 196608 | tf_op jit(solution)/shard_map/neg | solution.py:166
  7.3 0.0 collective-permute-done
  7.3 8.7 %fusion.29.x_ref = f32[1024,1024]{1,0:T(8,128)} fusion(bf16[3,1024,1024]{2,1,0:T(8,128)(2,1)} %param.6, bf16[3,2,1024]{2,1,0:T(2,128)(2,1)S(1)} %collective-permute-done, f32[1024]{0:T(1024)S(1)} %bitcast.77, f32[1024]{0:T(1024)S(1)} %bitcast.78, f32[1024]{0:T(1024)S(1)} %bitcast.73, f32[1024]{0:T(1024)S(1)} %bitcast.74, f32[1024]{0:T(1024)S(1)} %bitcast.75, ...), kind=kLoop, calls=%fused_computation.51 | loop fusion | flops 36700160 | bytes 14716928 | tf_op jit(solution)/shard_map/convert_element_type | solution.py:163
  16.0 9.5 %shard_map.64 = f32[16,8,1024]{2,1,0:T(8,128)} custom-call(f32[1024,1024]{1,0:T(8,128)} %fusion.29.x_ref, f32[16,1024]{1,0:T(8,128)} %get-tuple-element.6.decay_ref), custom_call_target="tpu_custom_call" | custom-call | tf_op jit(solution)/shard_map/pallas_call | solution.py:62
  25.4 1.3 multiply_reduce_fusion.1
  26.8 5.0 %collective-permute-start.7 = (f32[16,1024]{1,0:T(8,128)S(1)}, f32[16,1024]{1,0:T(8,128)S(1)}, u32[]{:S(2)}, u32[]{:S(2)}) collective-permute-start(f32[16,1024]{1,0:T(8,128)S(1)} %multiply_reduce_fusion.1), channel_id=1, source_target_pairs={{0,28},{1,29},{2,30},{3,31}} | collective-permute-start | bytes 196616 | tf_op jit(solution)/shard_map/ppermute | solution.py:15
  31.8 1.3 collective-permute-start.6
  33.1 1.3 collective-permute-start.5
  34.4 1.3 collective-permute-start.4
  35.7 2.2 %collective-permute-start.3 = (f32[16,1024]{1,0:T(8,128)S(1)}, f32[16,1024]{1,0:T(8,128)S(1)}, u32[]{:S(2)}, u32[]{:S(2)}) collective-permute-start(f32[16,1024]{1,0:T(8,128)S(1)} %multiply_reduce_fusion.1), channel_id=1, source_target_pairs={{0,12},{4,16},{8,20},{12,24},{16,28},{1,13},{5,17},{9,21},{13,25},... | collective-permute-start | bytes 196616 | tf_op jit(solution)/shard_map/ppermute | solution.py:15
  37.9 1.4 copy.15
  39.3 1.3 collective-permute-start.2
  40.6 0.0 collective-permute-done.6
  40.6 3.0 %collective-permute-start.1 = (f32[16,1024]{1,0:T(8,128)S(1)}, f32[16,1024]{1,0:T(8,128)S(1)}, u32[]{:S(2)}, u32[]{:S(2)}) collective-permute-start(f32[16,1024]{1,0:T(8,128)S(1)} %multiply_reduce_fusion.1), channel_id=1, source_target_pairs={{0,4},{4,8},{8,12},{12,16},{16,20},{20,24},{24,28},{1,5},{5,9},{9,... | collective-permute-start | bytes 196616 | tf_op jit(solution)/shard_map/ppermute | solution.py:15
  43.6 1.2 multiply_reduce_fusion
  44.8 0.0 collective-permute-done.5
  44.9 0.1 multiply_add_fusion
  45.0 1.2 bitcast_add_fusion.start_ref
  46.1 16.5 %shard_map.65 = f32[1024,1024]{1,0:T(8,128)} custom-call(f32[1024,1024]{1,0:T(8,128)} %fusion.29.x_ref, f32[16,1024]{1,0:T(8,128)} %get-tuple-element.6.decay_ref, f32[16,1024]{1,0:T(8,128)} %residue_ref.1, f32[16,8,1024]{2,1,0:T(8,128)} %bitcast_add_fusion.start_ref), custom_call_target="tpu_custom_call" | custom-call | tf_op jit(solution)/shard_map/pallas_call | solution.py:78
  62.7 6.4 %fusion.8 = bf16[1024,1024]{1,0:T(8,128)(2,1)S(1)} fusion(f32[1024,1024]{1,0:T(8,128)} %fusion.29.x_ref, bf16[3,1024,1024]{2,1,0:T(8,128)(2,1)} %param.6, bf16[3,2,1024]{2,1,0:T(2,128)(2,1)S(1)} %collective-permute-done, f32[1024]{0:T(1024)S(1)} %copy-done.1, f32[1024,1024]{1,0:T(8,128)} %shard_map.65, f32[1024]{0:T(1024)S(1)} %bitcast.71, ...), kind=kLoop, calls=%fused_computation.20 | loop fusion | flops 23068672 | bytes 18903040 | tf_op jit(solution)/shard_map/convert_element_type | solution.py:174
  69.1 1.3 collective-permute-start.9
  70.4 3.4 %collective-permute-start.8 = (bf16[1024,1024]{1,0:T(8,128)(2,1)S(1)}, bf16[1024,1024]{1,0:T(8,128)(2,1)}, u32[]{:S(2)}, u32[]{:S(2)}) collective-permute-start(bf16[1024,1024]{1,0:T(8,128)(2,1)S(1)} %fusion.8), channel_id=1, source_target_pairs={{0,1},{1,0},{2,3},{3,2},{4,5},{5,4},{6,7},{7,6},{8,9},{9,8},{10,11... | collective-permute-start | bytes 6291464 | tf_op jit(solution)/shard_map/ppermute | solution.py:142
  73.7 39.6 %collective-permute-done.9 = bf16[1024,1024]{1,0:T(8,128)(2,1)} collective-permute-done((bf16[1024,1024]{1,0:T(8,128)(2,1)S(1)}, bf16[1024,1024]{1,0:T(8,128)(2,1)}, u32[]{:S(2)}, u32[]{:S(2)}) %collective-permute-start.9) | collective-permute-done | bytes 2097184 | tf_op jit(solution)/shard_map/ppermute | solution.py:141
  113.3 4.0 %collective-permute-start.10 = (bf16[1024,1024]{1,0:T(8,128)(2,1)}, bf16[1024,1024]{1,0:T(8,128)(2,1)}, u32[]{:S(2)}, u32[]{:S(2)}) collective-permute-start(bf16[1024,1024]{1,0:T(8,128)(2,1)} %collective-permute-done.9), channel_id=1, source_target_pairs={{0,1},{1,0},{2,3},{3,2},{4,5},{5,4},{6,7},{7,6},{8,9},{9,8},{10,11... | collective-permute-start | bytes 6291464 | tf_op jit(solution)/shard_map/ppermute | solution.py:143
  117.3 3.9 %fusion.27 = f32[1024,1024]{1,0:T(8,128)S(1)} fusion(bf16[1024,1024]{1,0:T(8,128)(2,1)S(1)} %fusion.8, bf16[4096,1024]{1,0:T(8,128)(2,1)} %param.11, s32[]{:T(128)S(6)} %select_n.17), kind=kOutput, calls=%fused_computation.49 | convolution fusion | flops 2147483648 | bytes 8388612 | tf_op jit(solution)/shard_map/dot_general | solution.py:147
  121.3 4.6 %fusion.23 = f32[1024,1024]{1,0:T(8,128)S(1)} fusion(bf16[1024,1024]{1,0:T(8,128)(2,1)} %collective-permute-done.9, bf16[4096,1024]{1,0:T(8,128)(2,1)} %param.11, s32[]{:T(128)S(6)} %select_n.19), kind=kOutput, calls=%fused_computation.45 | convolution fusion | flops 2147483648 | bytes 8388612 | tf_op jit(solution)/shard_map/dot_general | solution.py:147
  125.8 4.6 %fusion.25 = f32[1024,1024]{1,0:T(8,128)S(1)} fusion(bf16[1024,1024]{1,0:T(8,128)(2,1)} %collective-permute-done.8, bf16[4096,1024]{1,0:T(8,128)(2,1)} %param.11, s32[]{:T(128)S(6)} %select_n.18), kind=kOutput, calls=%fused_computation.47 | convolution fusion | flops 2147483648 | bytes 8388612 | tf_op jit(solution)/shard_map/dot_general | solution.py:147
  130.4 5.9 %add_convert_fusion = bf16[1024,1024]{1,0:T(8,128)(2,1)} fusion(f32[1024,1024]{1,0:T(8,128)S(1)} %fusion.23, f32[1024,1024]{1,0:T(8,128)S(1)} %fusion.27, f32[1024,1024]{1,0:T(8,128)S(1)} %fusion.25, bf16[1024,1024]{1,0:T(8,128)(2,1)} %collective-permute-done.10, bf16[4096,1024]{1,0:T(8,128)(2,1)} %param.11, s32[]{:T(128)S(6)} %select_n.20), kind=kOutput, calls=%fused_computation.25 | convolution fusion | flops 2151677952 | bytes 18874372 | tf_op jit(solution)/shard_map/dot_general | solution.py:147
  (15 shorter events, 0.0 us)
Async XLA Ops:
  0.8 6.5 %collective-permute-start = (bf16[3,2,1024]{2,1,0:T(2,128)(2,1)S(1)}, bf16[3,2,1024]{2,1,0:T(2,128)(2,1)S(1)}, u32[]{:S(2)}, u32[]{:S(2)}) collective-permute-start(bf16[3,2,1024]{2,1,0:T(2,128)(2,1)S(1)} %slice.60), channel_id=1, source_target_pairs={{0,4},{4,8},{8,12},{12,16},{16,20},{20,24},{24,28},{1,5},{5,9},{9,... | collective-permute-start | bytes 36872 | tf_op jit(solution)/shard_map/ppermute | solution.py:15
  16.0 28.9 %copy-start = (f32[16,1024]{1,0:T(8,128)S(1)}, f32[16,1024]{1,0:T(8,128)}, u32[]{:S(2)}) copy-start(f32[16,1024]{1,0:T(8,128)} %param.8) | copy-start | bytes 196612
  26.8 12.5 %collective-permute-start.7 = (f32[16,1024]{1,0:T(8,128)S(1)}, f32[16,1024]{1,0:T(8,128)S(1)}, u32[]{:S(2)}, u32[]{:S(2)}) collective-permute-start(f32[16,1024]{1,0:T(8,128)S(1)} %multiply_reduce_fusion.1), channel_id=1, source_target_pairs={{0,28},{1,29},{2,30},{3,31}} | collective-permute-start | bytes 196616 | tf_op jit(solution)/shard_map/ppermute | solution.py:15
  31.8 8.8 %collective-permute-start.6 = (f32[16,1024]{1,0:T(8,128)S(1)}, f32[16,1024]{1,0:T(8,128)S(1)}, u32[]{:S(2)}, u32[]{:S(2)}) collective-permute-start(f32[16,1024]{1,0:T(8,128)S(1)} %multiply_reduce_fusion.1), channel_id=1, source_target_pairs={{0,24},{4,28},{1,25},{5,29},{2,26},{6,30},{3,27},{7,31}} | collective-permute-start | bytes 196616 | tf_op jit(solution)/shard_map/ppermute | solution.py:15
  33.1 11.7 %collective-permute-start.5 = (f32[16,1024]{1,0:T(8,128)S(1)}, f32[16,1024]{1,0:T(8,128)S(1)}, u32[]{:S(2)}, u32[]{:S(2)}) collective-permute-start(f32[16,1024]{1,0:T(8,128)S(1)} %multiply_reduce_fusion.1), channel_id=1, source_target_pairs={{0,20},{4,24},{8,28},{1,21},{5,25},{9,29},{2,22},{6,26},{10,30},{3... | collective-permute-start | bytes 196616 | tf_op jit(solution)/shard_map/ppermute | solution.py:15
  34.4 10.4 %collective-permute-start.4 = (f32[16,1024]{1,0:T(8,128)S(1)}, f32[16,1024]{1,0:T(8,128)S(1)}, u32[]{:S(2)}, u32[]{:S(2)}) collective-permute-start(f32[16,1024]{1,0:T(8,128)S(1)} %multiply_reduce_fusion.1), channel_id=1, source_target_pairs={{0,16},{4,20},{8,24},{12,28},{1,17},{5,21},{9,25},{13,29},{2,18},{... | collective-permute-start | bytes 196616 | tf_op jit(solution)/shard_map/ppermute | solution.py:15
  35.7 9.1 %collective-permute-start.3 = (f32[16,1024]{1,0:T(8,128)S(1)}, f32[16,1024]{1,0:T(8,128)S(1)}, u32[]{:S(2)}, u32[]{:S(2)}) collective-permute-start(f32[16,1024]{1,0:T(8,128)S(1)} %multiply_reduce_fusion.1), channel_id=1, source_target_pairs={{0,12},{4,16},{8,20},{12,24},{16,28},{1,13},{5,17},{9,21},{13,25},... | collective-permute-start | bytes 196616 | tf_op jit(solution)/shard_map/ppermute | solution.py:15
  39.3 5.6 %collective-permute-start.2 = (f32[16,1024]{1,0:T(8,128)S(1)}, f32[16,1024]{1,0:T(8,128)S(1)}, u32[]{:S(2)}, u32[]{:S(2)}) collective-permute-start(f32[16,1024]{1,0:T(8,128)S(1)} %multiply_reduce_fusion.1), channel_id=1, source_target_pairs={{0,8},{4,12},{8,16},{12,20},{16,24},{20,28},{1,9},{5,13},{9,17},{1... | collective-permute-start | bytes 196616 | tf_op jit(solution)/shard_map/ppermute | solution.py:15
  40.6 4.3 %collective-permute-start.1 = (f32[16,1024]{1,0:T(8,128)S(1)}, f32[16,1024]{1,0:T(8,128)S(1)}, u32[]{:S(2)}, u32[]{:S(2)}) collective-permute-start(f32[16,1024]{1,0:T(8,128)S(1)} %multiply_reduce_fusion.1), channel_id=1, source_target_pairs={{0,4},{4,8},{8,12},{12,16},{16,20},{20,24},{24,28},{1,5},{5,9},{9,... | collective-permute-start | bytes 196616 | tf_op jit(solution)/shard_map/ppermute | solution.py:15
  46.1 16.5 %copy-start.1 = (f32[1024]{0:T(1024)S(1)}, f32[1024]{0:T(1024)}, u32[]{:S(2)}) copy-start(f32[1024]{0:T(1024)} %param.10) | copy-start | bytes 12292
  69.1 44.2 %collective-permute-start.9 = (bf16[1024,1024]{1,0:T(8,128)(2,1)S(1)}, bf16[1024,1024]{1,0:T(8,128)(2,1)}, u32[]{:S(2)}, u32[]{:S(2)}) collective-permute-start(bf16[1024,1024]{1,0:T(8,128)(2,1)S(1)} %fusion.8), channel_id=1, source_target_pairs={{0,2},{1,3},{2,0},{3,1},{4,6},{5,7},{6,4},{7,5},{8,10},{9,11},{10,... | collective-permute-start | bytes 6291464 | tf_op jit(solution)/shard_map/ppermute | solution.py:141
  70.4 55.4 %collective-permute-start.8 = (bf16[1024,1024]{1,0:T(8,128)(2,1)S(1)}, bf16[1024,1024]{1,0:T(8,128)(2,1)}, u32[]{:S(2)}, u32[]{:S(2)}) collective-permute-start(bf16[1024,1024]{1,0:T(8,128)(2,1)S(1)} %fusion.8), channel_id=1, source_target_pairs={{0,1},{1,0},{2,3},{3,2},{4,5},{5,4},{6,7},{7,6},{8,9},{9,8},{10,11... | collective-permute-start | bytes 6291464 | tf_op jit(solution)/shard_map/ppermute | solution.py:142
  113.3 17.1 %collective-permute-start.10 = (bf16[1024,1024]{1,0:T(8,128)(2,1)}, bf16[1024,1024]{1,0:T(8,128)(2,1)}, u32[]{:S(2)}, u32[]{:S(2)}) collective-permute-start(bf16[1024,1024]{1,0:T(8,128)(2,1)} %collective-permute-done.9), channel_id=1, source_target_pairs={{0,1},{1,0},{2,3},{3,2},{4,5},{5,4},{6,7},{7,6},{8,9},{9,8},{10,11... | collective-permute-start | bytes 6291464 | tf_op jit(solution)/shard_map/ppermute | solution.py:143

commit v5 on v4

--- a/solution.py
+++ b/solution.py
@@ -138,15 +138,18 @@
         gathered = lax.all_gather(gated_mix, "ch", axis=1, tiled=True)
         return jnp.dot(gathered, out_weight, preferred_element_type=jnp.float32)
     here = lax.axis_index("ch")
+
+    def part(piece, owner):
+        rows = lax.dynamic_slice_in_dim(out_weight, owner * width, width, 0)
+        return jnp.dot(piece, rows, preferred_element_type=jnp.float32)
+
     far = lax.ppermute(gated_mix, "ch", [(i, i ^ 2) for i in range(ch_count)])
     near = lax.ppermute(gated_mix, "ch", [(i, i ^ 1) for i in range(ch_count)])
+    total = part(gated_mix, here) + part(near, here ^ 1)
+    far, total = lax.optimization_barrier((far, total))
     near_far = lax.ppermute(far, "ch", [(i, i ^ 1) for i in range(ch_count)])
-    total = None
-    for piece, owner in ((gated_mix, here), (near, here ^ 1), (far, here ^ 2), (near_far, here ^ 3)):
-        rows = lax.dynamic_slice_in_dim(out_weight, owner * width, width, 0)
-        part = jnp.dot(piece, rows, preferred_element_type=jnp.float32)
-        total = part if total is None else total + part
-    return total
+    total = total + part(far, here ^ 2)
+    return total + part(near_far, here ^ 3)
 
 
 def shards(projected, tap_weights, pole_rates, residues, long_bias, out_weight):

time: 137 us -> 131 us (0.956)
  waiting for transfers between devices: 39.6 us -> 35.6 us
  starting transfers between devices: 27.9 us -> 24.5 us
  matrix products: 19 us -> 20.5 us
    ppermute x1, waiting for transfers between devices: 39.6 us -> 32.9 us  [project(): far = lax.ppermute(gated_mix, 'ch', [(i, i ^ 2) for i in range(ch_count)])]
    ppermute x1, starting transfers between devices: 3.99 us -> 0.85 us  [project(): near_far = lax.ppermute(far, 'ch', [(i, i ^ 1) for i in range(ch_count)])]
    ppermute x1, waiting for transfers between devices: 0.01 us -> 2.69 us  [project(): near = lax.ppermute(gated_mix, 'ch', [(i, i ^ 1) for i in range(ch_count)])]
    dot_general x4, matrix products: 19 us -> 20.5 us  [part(): return jnp.dot(piece, rows, preferred_element_type=jnp.float32)]
  transfers between devices with their start and end apart: 11 -> 11, of which waited for: 1 -> 2; matrix products, arithmetic and copies ran while one was open for 13% -> 15% of each run, Pallas kernels for 0% -> 0%
where the time goes in v5:
time: 131 us; the launch traced here: 130 us
  waiting for transfers between devices  35.6 us (27%)
  Pallas kernels  26 us (20%)
  starting transfers between devices  24.5 us (19%)
  other arithmetic  21.4 us (16%)
  matrix products  20.5 us (16%)
  local copies, waits for them, and re-layouts  2.18 us (2%)
    ppermute x1, waiting for transfers between devices, project(): far = lax.ppermute(gated_mix, 'ch', [(i, i ^ 2) for i in range(ch_count)])  32.9 us
    dot_general x4, matrix products, part(): return jnp.dot(piece, rows, preferred_element_type=jnp.float32)  20.5 us
    ppermute x8, starting transfers between devices, shifted(): lax.ppermute(value, axis, [(source, source + steps) for source in range(i...  19.3 us
    pallas_call x1, Pallas kernels, run_recurrence(): pl.pallas_call(recurrence_kernel, grid=(width // LANES,), in_specs=[pl.Bl...  16.5 us
    pallas_call x1, Pallas kernels, run_end_state(): pl.pallas_call(end_state_kernel, grid=(width // LANES,), in_specs=[pl.Blo...  9.47 us
    convert_element_type x1, other arithmetic, shards(): x = mixed_input.astype(jnp.float32)  8.69 us
    convert_element_type x1, other arithmetic, shards(): gated_mix = gated_mix.astype(jnp.bfloat16)  6.43 us
    ppermute x1, starting transfers between devices, project(): near = lax.ppermute(gated_mix, 'ch', [(i, i ^ 1) for i in range(ch_count)])  3.14 us
  transfers between devices with their start and end apart: 11, of which 2 were waited for; matrix products, arithmetic and copies ran while one was open for 15% of the time, Pallas kernels for 0%

profile of v5, /device:TPU:1, one launch (start us, length us, event | category | flops | bytes accessed | tf_op | source)
XLA Modules:
  0.0 130.4 jit_solution(11894111247149908706)
XLA Ops:
  0.0 0.8 slice.60
  0.8 4.0 %collective-permute-start = (bf16[3,2,1024]{2,1,0:T(2,128)(2,1)S(1)}, bf16[3,2,1024]{2,1,0:T(2,128)(2,1)S(1)}, u32[]{:S(2)}, u32[]{:S(2)}) collective-permute-start(bf16[3,2,1024]{2,1,0:T(2,128)(2,1)S(1)} %slice.60), channel_id=1, source_target_pairs={{0,4},{4,8},{8,12},{12,16},{16,20},{20,24},{24,28},{1,5},{5,9},{9,... | collective-permute-start | bytes 36872 | tf_op jit(solution)/shard_map/ppermute | solution.py:15
  4.8 0.1 maximum_multiply_fusion
  4.9 0.9 slice_convert_fusion.8
  5.8 1.5 %fusion.39 = (f32[16,1024]{1,0:T(8,128)S(1)}, f32[16,1024]{1,0:T(8,128)}) fusion(f32[16,1024]{1,0:T(8,128)} %param.8), kind=kLoop, calls=%fused_computation.75 | loop fusion | flops 16384 | bytes 196608 | tf_op jit(solution)/shard_map/neg | solution.py:169
  7.3 0.0 collective-permute-done
  7.3 8.7 %fusion.29.x_ref = f32[1024,1024]{1,0:T(8,128)} fusion(bf16[3,1024,1024]{2,1,0:T(8,128)(2,1)} %param.6, bf16[3,2,1024]{2,1,0:T(2,128)(2,1)S(1)} %collective-permute-done, f32[1024]{0:T(1024)S(1)} %bitcast.77, f32[1024]{0:T(1024)S(1)} %bitcast.78, f32[1024]{0:T(1024)S(1)} %bitcast.73, f32[1024]{0:T(1024)S(1)} %bitcast.74, f32[1024]{0:T(1024)S(1)} %bitcast.75, ...), kind=kLoop, calls=%fused_computation.51 | loop fusion | flops 36700160 | bytes 14716928 | tf_op jit(solution)/shard_map/convert_element_type | solution.py:166
  16.0 9.5 %shard_map.64 = f32[16,8,1024]{2,1,0:T(8,128)} custom-call(f32[1024,1024]{1,0:T(8,128)} %fusion.29.x_ref, f32[16,1024]{1,0:T(8,128)} %get-tuple-element.10.decay_ref), custom_call_target="tpu_custom_call" | custom-call | tf_op jit(solution)/shard_map/pallas_call | solution.py:62
  25.4 1.3 %multiply_reduce_fusion.1 = f32[16,1024]{1,0:T(8,128)S(1)} fusion(f32[16,8,1024]{2,1,0:T(8,128)} %shard_map.64, f32[8]{0:T(128)S(1)} %subtract_multiply_fusion, f32[16,1024]{1,0:T(8,128)S(1)} %get-tuple-element.9), kind=kLoop, calls=%fused_computation.54 | loop fusion | flops 376832 | bytes 655392 | tf_op jit(solution)/shard_map/reduce_sum | solution.py:110
  26.8 5.0 %collective-permute-start.7 = (f32[16,1024]{1,0:T(8,128)S(1)}, f32[16,1024]{1,0:T(8,128)S(1)}, u32[]{:S(2)}, u32[]{:S(2)}) collective-permute-start(f32[16,1024]{1,0:T(8,128)S(1)} %multiply_reduce_fusion.1), channel_id=1, source_target_pairs={{0,28},{1,29},{2,30},{3,31}} | collective-permute-start | bytes 196616 | tf_op jit(solution)/shard_map/ppermute | solution.py:15
  31.8 1.3 collective-permute-start.6
  33.1 1.3 collective-permute-start.5
  34.4 1.3 collective-permute-start.4
  35.7 2.2 %collective-permute-start.3 = (f32[16,1024]{1,0:T(8,128)S(1)}, f32[16,1024]{1,0:T(8,128)S(1)}, u32[]{:S(2)}, u32[]{:S(2)}) collective-permute-start(f32[16,1024]{1,0:T(8,128)S(1)} %multiply_reduce_fusion.1), channel_id=1, source_target_pairs={{0,12},{4,16},{8,20},{12,24},{16,28},{1,13},{5,17},{9,21},{13,25},... | collective-permute-start | bytes 196616 | tf_op jit(solution)/shard_map/ppermute | solution.py:15
  37.9 1.4 %copy.15 = f32[16,1024,8]{1,0,2:T(8,128)S(1)} copy(f32[16,1024,8]{1,2,0:T(8,128)} %bitcast.69) | data formatting | bytes 1048576
  39.2 0.0 collective-permute-done.7
  39.2 1.3 collective-permute-start.2
  40.6 3.0 %collective-permute-start.1 = (f32[16,1024]{1,0:T(8,128)S(1)}, f32[16,1024]{1,0:T(8,128)S(1)}, u32[]{:S(2)}, u32[]{:S(2)}) collective-permute-start(f32[16,1024]{1,0:T(8,128)S(1)} %multiply_reduce_fusion.1), channel_id=1, source_target_pairs={{0,4},{4,8},{8,12},{12,16},{16,20},{20,24},{24,28},{1,5},{5,9},{9,... | collective-permute-start | bytes 196616 | tf_op jit(solution)/shard_map/ppermute | solution.py:15
  43.6 1.2 multiply_reduce_fusion
  44.9 0.1 multiply_add_fusion
  45.0 1.2 bitcast_add_fusion.start_ref
  46.1 16.5 %shard_map.65 = f32[1024,1024]{1,0:T(8,128)} custom-call(f32[1024,1024]{1,0:T(8,128)} %fusion.29.x_ref, f32[16,1024]{1,0:T(8,128)} %get-tuple-element.10.decay_ref, f32[16,1024]{1,0:T(8,128)} %residue_ref.1, f32[16,8,1024]{2,1,0:T(8,128)} %bitcast_add_fusion.start_ref), custom_call_target="tpu_custom_call" | custom-call | tf_op jit(solution)/shard_map/pallas_call | solution.py:78
  62.6 6.4 %fusion.8 = bf16[1024,1024]{1,0:T(8,128)(2,1)S(1)} fusion(f32[1024,1024]{1,0:T(8,128)} %fusion.29.x_ref, bf16[3,1024,1024]{2,1,0:T(8,128)(2,1)} %param.6, bf16[3,2,1024]{2,1,0:T(2,128)(2,1)S(1)} %collective-permute-done, f32[1024]{0:T(1024)S(1)} %copy-done.1, f32[1024,1024]{1,0:T(8,128)} %shard_map.65, f32[1024]{0:T(1024)S(1)} %bitcast.71, ...), kind=kLoop, calls=%fused_computation.20 | loop fusion | flops 23068672 | bytes 18903040 | tf_op jit(solution)/shard_map/convert_element_type | solution.py:177
  69.1 3.1 %collective-permute-start.9 = (bf16[1024,1024]{1,0:T(8,128)(2,1)S(1)}, bf16[1024,1024]{1,0:T(8,128)(2,1)}, u32[]{:S(2)}, u32[]{:S(2)}) collective-permute-start(bf16[1024,1024]{1,0:T(8,128)(2,1)S(1)} %fusion.8), channel_id=1, source_target_pairs={{0,1},{1,0},{2,3},{3,2},{4,5},{5,4},{6,7},{7,6},{8,9},{9,8},{10,11... | collective-permute-start | bytes 6291464 | tf_op jit(solution)/shard_map/ppermute | solution.py:147
  72.2 1.2 collective-permute-start.8
  73.4 2.7 %collective-permute-done.9 = bf16[1024,1024]{1,0:T(8,128)(2,1)} collective-permute-done((bf16[1024,1024]{1,0:T(8,128)(2,1)S(1)}, bf16[1024,1024]{1,0:T(8,128)(2,1)}, u32[]{:S(2)}, u32[]{:S(2)}) %collective-permute-start.9) | collective-permute-done | bytes 2097184 | tf_op jit(solution)/shard_map/ppermute | solution.py:147
  76.1 4.5 %fusion.25 = f32[1024,1024]{1,0:T(8,128)S(1)} fusion(bf16[1024,1024]{1,0:T(8,128)(2,1)} %collective-permute-done.9, bf16[4096,1024]{1,0:T(8,128)(2,1)} %param.11, s32[]{:T(128)S(6)} %select_n.18), kind=kOutput, calls=%fused_computation.47 | convolution fusion | flops 2147483648 | bytes 8388612 | tf_op jit(solution)/shard_map/dot_general | solution.py:144
  80.7 5.9 %fusion.30 = f32[1024,1024]{1,0:T(8,128)} fusion(f32[1024,1024]{1,0:T(8,128)S(1)} %fusion.25, bf16[1024,1024]{1,0:T(8,128)(2,1)S(1)} %fusion.8, bf16[4096,1024]{1,0:T(8,128)(2,1)} %param.11, s32[]{:T(128)S(6)} %select_n.17), kind=kOutput, calls=%fused_computation.52 | convolution fusion | flops 2148532224 | bytes 12582916 | tf_op jit(solution)/shard_map/dot_general | solution.py:144
  86.6 32.9 %collective-permute-done.8 = bf16[1024,1024]{1,0:T(8,128)(2,1)} collective-permute-done((bf16[1024,1024]{1,0:T(8,128)(2,1)S(1)}, bf16[1024,1024]{1,0:T(8,128)(2,1)}, u32[]{:S(2)}, u32[]{:S(2)}) %collective-permute-start.8) | collective-permute-done | bytes 2097184 | tf_op jit(solution)/shard_map/ppermute | solution.py:146
  119.5 0.8 collective-permute-start.10
  120.4 4.7 %fusion.23 = f32[1024,1024]{1,0:T(8,128)S(1)} fusion(bf16[1024,1024]{1,0:T(8,128)(2,1)} %collective-permute-done.8, bf16[4096,1024]{1,0:T(8,128)(2,1)} %param.11, s32[]{:T(128)S(6)} %select_n.19), kind=kOutput, calls=%fused_computation.45 | convolution fusion | flops 2147483648 | bytes 8388612 | tf_op jit(solution)/shard_map/dot_general | solution.py:144
  125.1 5.3 %add_convert_fusion = bf16[1024,1024]{1,0:T(8,128)(2,1)} fusion(f32[1024,1024]{1,0:T(8,128)S(1)} %copy-done.2, f32[1024,1024]{1,0:T(8,128)S(1)} %fusion.23, bf16[1024,1024]{1,0:T(8,128)(2,1)S(1)} %collective-permute-done.10, bf16[4096,1024]{1,0:T(8,128)(2,1)} %param.11, s32[]{:T(128)S(6)} %select_n.20), kind=kOutput, calls=%fused_computation.25 | convolution fusion | flops 2150629376 | bytes 14680068 | tf_op jit(solution)/shard_map/dot_general | solution.py:144
  (17 shorter events, 0.1 us)
Async XLA Ops:
  0.8 6.5 %collective-permute-start = (bf16[3,2,1024]{2,1,0:T(2,128)(2,1)S(1)}, bf16[3,2,1024]{2,1,0:T(2,128)(2,1)S(1)}, u32[]{:S(2)}, u32[]{:S(2)}) collective-permute-start(bf16[3,2,1024]{2,1,0:T(2,128)(2,1)S(1)} %slice.60), channel_id=1, source_target_pairs={{0,4},{4,8},{8,12},{12,16},{16,20},{20,24},{24,28},{1,5},{5,9},{9,... | collective-permute-start | bytes 36872 | tf_op jit(solution)/shard_map/ppermute | solution.py:15
  16.0 28.9 %copy-start = (f32[16,1024]{1,0:T(8,128)S(1)}, f32[16,1024]{1,0:T(8,128)}, u32[]{:S(2)}) copy-start(f32[16,1024]{1,0:T(8,128)} %param.8) | copy-start | bytes 196612
  26.8 12.5 %collective-permute-start.7 = (f32[16,1024]{1,0:T(8,128)S(1)}, f32[16,1024]{1,0:T(8,128)S(1)}, u32[]{:S(2)}, u32[]{:S(2)}) collective-permute-start(f32[16,1024]{1,0:T(8,128)S(1)} %multiply_reduce_fusion.1), channel_id=1, source_target_pairs={{0,28},{1,29},{2,30},{3,31}} | collective-permute-start | bytes 196616 | tf_op jit(solution)/shard_map/ppermute | solution.py:15
  31.8 8.8 %collective-permute-start.6 = (f32[16,1024]{1,0:T(8,128)S(1)}, f32[16,1024]{1,0:T(8,128)S(1)}, u32[]{:S(2)}, u32[]{:S(2)}) collective-permute-start(f32[16,1024]{1,0:T(8,128)S(1)} %multiply_reduce_fusion.1), channel_id=1, source_target_pairs={{0,24},{4,28},{1,25},{5,29},{2,26},{6,30},{3,27},{7,31}} | collective-permute-start | bytes 196616 | tf_op jit(solution)/shard_map/ppermute | solution.py:15
  33.1 11.7 %collective-permute-start.5 = (f32[16,1024]{1,0:T(8,128)S(1)}, f32[16,1024]{1,0:T(8,128)S(1)}, u32[]{:S(2)}, u32[]{:S(2)}) collective-permute-start(f32[16,1024]{1,0:T(8,128)S(1)} %multiply_reduce_fusion.1), channel_id=1, source_target_pairs={{0,20},{4,24},{8,28},{1,21},{5,25},{9,29},{2,22},{6,26},{10,30},{3... | collective-permute-start | bytes 196616 | tf_op jit(solution)/shard_map/ppermute | solution.py:15
  34.4 10.4 %collective-permute-start.4 = (f32[16,1024]{1,0:T(8,128)S(1)}, f32[16,1024]{1,0:T(8,128)S(1)}, u32[]{:S(2)}, u32[]{:S(2)}) collective-permute-start(f32[16,1024]{1,0:T(8,128)S(1)} %multiply_reduce_fusion.1), channel_id=1, source_target_pairs={{0,16},{4,20},{8,24},{12,28},{1,17},{5,21},{9,25},{13,29},{2,18},{... | collective-permute-start | bytes 196616 | tf_op jit(solution)/shard_map/ppermute | solution.py:15
  35.7 9.1 %collective-permute-start.3 = (f32[16,1024]{1,0:T(8,128)S(1)}, f32[16,1024]{1,0:T(8,128)S(1)}, u32[]{:S(2)}, u32[]{:S(2)}) collective-permute-start(f32[16,1024]{1,0:T(8,128)S(1)} %multiply_reduce_fusion.1), channel_id=1, source_target_pairs={{0,12},{4,16},{8,20},{12,24},{16,28},{1,13},{5,17},{9,21},{13,25},... | collective-permute-start | bytes 196616 | tf_op jit(solution)/shard_map/ppermute | solution.py:15
  39.2 5.6 %collective-permute-start.2 = (f32[16,1024]{1,0:T(8,128)S(1)}, f32[16,1024]{1,0:T(8,128)S(1)}, u32[]{:S(2)}, u32[]{:S(2)}) collective-permute-start(f32[16,1024]{1,0:T(8,128)S(1)} %multiply_reduce_fusion.1), channel_id=1, source_target_pairs={{0,8},{4,12},{8,16},{12,20},{16,24},{20,28},{1,9},{5,13},{9,17},{1... | collective-permute-start | bytes 196616 | tf_op jit(solution)/shard_map/ppermute | solution.py:15
  40.6 4.3 %collective-permute-start.1 = (f32[16,1024]{1,0:T(8,128)S(1)}, f32[16,1024]{1,0:T(8,128)S(1)}, u32[]{:S(2)}, u32[]{:S(2)}) collective-permute-start(f32[16,1024]{1,0:T(8,128)S(1)} %multiply_reduce_fusion.1), channel_id=1, source_target_pairs={{0,4},{4,8},{8,12},{12,16},{16,20},{20,24},{24,28},{1,5},{5,9},{9,... | collective-permute-start | bytes 196616 | tf_op jit(solution)/shard_map/ppermute | solution.py:15
  46.1 16.5 %copy-start.1 = (f32[1024]{0:T(1024)S(1)}, f32[1024]{0:T(1024)}, u32[]{:S(2)}) copy-start(f32[1024]{0:T(1024)} %param.10) | copy-start | bytes 12292
  69.1 7.1 %collective-permute-start.9 = (bf16[1024,1024]{1,0:T(8,128)(2,1)S(1)}, bf16[1024,1024]{1,0:T(8,128)(2,1)}, u32[]{:S(2)}, u32[]{:S(2)}) collective-permute-start(bf16[1024,1024]{1,0:T(8,128)(2,1)S(1)} %fusion.8), channel_id=1, source_target_pairs={{0,1},{1,0},{2,3},{3,2},{4,5},{5,4},{6,7},{7,6},{8,9},{9,8},{10,11... | collective-permute-start | bytes 6291464 | tf_op jit(solution)/shard_map/ppermute | solution.py:147
  72.2 47.3 %collective-permute-start.8 = (bf16[1024,1024]{1,0:T(8,128)(2,1)S(1)}, bf16[1024,1024]{1,0:T(8,128)(2,1)}, u32[]{:S(2)}, u32[]{:S(2)}) collective-permute-start(bf16[1024,1024]{1,0:T(8,128)(2,1)S(1)} %fusion.8), channel_id=1, source_target_pairs={{0,2},{1,3},{2,0},{3,1},{4,6},{5,7},{6,4},{7,5},{8,10},{9,11},{10,... | collective-permute-start | bytes 6291464 | tf_op jit(solution)/shard_map/ppermute | solution.py:146
  119.5 5.6 %collective-permute-start.10 = (bf16[1024,1024]{1,0:T(8,128)(2,1)}, bf16[1024,1024]{1,0:T(8,128)(2,1)S(1)}, u32[]{:S(2)}, u32[]{:S(2)}) collective-permute-start(bf16[1024,1024]{1,0:T(8,128)(2,1)} %collective-permute-done.8), channel_id=1, source_target_pairs={{0,1},{1,0},{2,3},{3,2},{4,5},{5,4},{6,7},{7,6},{8,9},{9,8},{10,11... | collective-permute-start | bytes 6291464 | tf_op jit(solution)/shard_map/ppermute | solution.py:150
  120.4 4.7 %copy-start.2 = (f32[1024,1024]{1,0:T(8,128)S(1)}, f32[1024,1024]{1,0:T(8,128)}, u32[]{:S(2)}) copy-start(f32[1024,1024]{1,0:T(8,128)} %fusion.30) | copy-start | bytes 12582916

commit v6 on v4

--- a/solution.py
+++ b/solution.py
@@ -7,6 +7,8 @@
 
 LANES = 128
 SEGMENTS = 8
+CHANNEL_PIECES = 4
+LAG = 2
 
 
 def shifted(value, axis, steps):
@@ -68,6 +70,9 @@
         ],
         out_specs=pl.BlockSpec((pole_count, SEGMENTS, LANES), lambda g: (0, 0, g)),
         out_shape=jax.ShapeDtypeStruct((pole_count, SEGMENTS, width), jnp.float32),
+        cost_estimate=pl.CostEstimate(
+            flops=2 * pole_count * length * width, transcendentals=0, bytes_accessed=4 * length * width
+        ),
     )(x, decay)
 
 
@@ -86,6 +91,9 @@
         ],
         out_specs=pl.BlockSpec((length, LANES), lambda g: (0, g)),
         out_shape=jax.ShapeDtypeStruct(x.shape, jnp.float32),
+        cost_estimate=pl.CostEstimate(
+            flops=4 * pole_count * length * width, transcendentals=0, bytes_accessed=8 * length * width
+        ),
     )(x, decay, residue, start)
 
 
@@ -131,29 +139,18 @@
     return total
 
 
-def project(gated_mix, out_weight):
-    ch_count = lax.axis_size("ch")
-    width = gated_mix.shape[1]
-    if ch_count != 4:
-        gathered = lax.all_gather(gated_mix, "ch", axis=1, tiled=True)
-        return jnp.dot(gathered, out_weight, preferred_element_type=jnp.float32)
-    here = lax.axis_index("ch")
-    far = lax.ppermute(gated_mix, "ch", [(i, i ^ 2) for i in range(ch_count)])
-    near = lax.ppermute(gated_mix, "ch", [(i, i ^ 1) for i in range(ch_count)])
-    near_far = lax.ppermute(far, "ch", [(i, i ^ 1) for i in range(ch_count)])
-    total = None
-    for piece, owner in ((gated_mix, here), (near, here ^ 1), (far, here ^ 2), (near_far, here ^ 3)):
-        rows = lax.dynamic_slice_in_dim(out_weight, owner * width, width, 0)
-        part = jnp.dot(piece, rows, preferred_element_type=jnp.float32)
-        total = part if total is None else total + part
-    return total
+def project_whole(gated_mix, out_weight):
+    gathered = lax.all_gather(gated_mix, "ch", axis=1, tiled=True)
+    return jnp.dot(gathered, out_weight, preferred_element_type=jnp.float32)
+
+
+def weight_rows(out_weight, owners, width):
+    return jnp.concatenate([lax.dynamic_slice_in_dim(out_weight, owner * width, width, 0) for owner in owners], 0)
 
 
 def shards(projected, tap_weights, pole_rates, residues, long_bias, out_weight):
     row_count = projected.shape[1]
     width = projected.shape[2]
-    rows = width // LANES
-    pole_count = pole_rates.shape[0]
     rim_rows = tap_weights.shape[0] - 1
     prior_rows = shifted(projected[:, row_count - rim_rows :], "ctx", 1)
     extended = jnp.concatenate([prior_rows, projected], 1)
@@ -166,13 +163,44 @@
     decay = jnp.exp(-pole_rates)
     ends = run_end_state(x, decay)
     start = incoming_state(device_end(ends, pole_rates, span), pole_rates, row_count)
-    long_part = run_recurrence(x, decay, residues, segment_starts(ends, start, pole_rates, span))
-    long_mix = long_part.astype(jnp.bfloat16)
-    gated_mix = featurize(extended, tap_weights, 0, row_count) * (
-        long_mix.astype(jnp.float32) + long_bias[None, :] * mixed_input.astype(jnp.float32)
-    )
-    gated_mix = gated_mix.astype(jnp.bfloat16)
-    return project(gated_mix, out_weight).astype(jnp.bfloat16)
+    starts = segment_starts(ends, start, pole_rates, span)
+    stream0 = featurize(extended, tap_weights, 0, row_count)
+
+    ch_count = lax.axis_size("ch")
+    pieces = CHANNEL_PIECES if (ch_count == 4 and width % (CHANNEL_PIECES * LANES) == 0) else 1
+    piece = width // pieces
+    here = lax.axis_index("ch")
+    other_core = [(i, i ^ 1) for i in range(ch_count)]
+    other_chip = [(i, i ^ 2) for i in range(ch_count)]
+    gated = []
+    far = []
+    for index in range(pieces):
+        cols = slice(index * piece, (index + 1) * piece)
+        x_here = x[:, cols]
+        if index >= LAG and pieces > 1:
+            x_here, far[index - LAG] = lax.optimization_barrier((x_here, far[index - LAG]))
+        long_part = run_recurrence(x_here, decay[:, cols], residues[:, cols], starts[:, :, cols])
+        long_mix = long_part.astype(jnp.bfloat16)
+        gated_mix = stream0[:, cols] * (
+            long_mix.astype(jnp.float32) + long_bias[None, cols] * mixed_input[:, cols].astype(jnp.float32)
+        )
+        gated_mix = gated_mix.astype(jnp.bfloat16)
+        gated.append(gated_mix)
+        if ch_count == 4:
+            far.append(lax.ppermute(gated_mix, "ch", other_chip))
+    if ch_count != 4:
+        return project_whole(jnp.concatenate(gated, 1), out_weight).astype(jnp.bfloat16)
+
+    own = jnp.concatenate(gated, 1)
+    near = lax.ppermute(own, "ch", other_core)
+    local_rows = weight_rows(out_weight, (here, here ^ 1), width)
+    remote_rows = weight_rows(out_weight, (here ^ 2, here ^ 3), width)
+    total = jnp.dot(jnp.concatenate([own, near], 1), local_rows, preferred_element_type=jnp.float32)
+    far, total = lax.optimization_barrier((far, total))
+    far = jnp.concatenate(far, 1)
+    near_far = lax.ppermute(far, "ch", other_core)
+    total = total + jnp.dot(jnp.concatenate([far, near_far], 1), remote_rows, preferred_element_type=jnp.float32)
+    return total.astype(jnp.bfloat16)
 
 
 def solution(mesh):

time: 137 us -> 152 us (1.11)
  other arithmetic: 21.4 us -> 35.8 us
  local copies, waits for them, and re-layouts: 2.17 us -> 15 us
  matrix products: 19 us -> 10.8 us
  waiting for transfers between devices: 39.6 us -> 32.1 us
  Pallas kernels: 26 us -> 31.5 us
  starting transfers between devices: 27.9 us -> 25.5 us
    unnamed x1 -> x5, other arithmetic: 1.23 us -> 12 us
    dot_general x4 -> x2, matrix products: 19 us -> 10.8 us  [the longest x1 6.34 us: shards(): jnp.dot(jnp.concatenate([own, near], 1), local_rows, preferred_element_ty...]
    ppermute x3 -> x6, waiting for transfers between devices: 39.6 us -> 32.1 us  [the longest x4 28.6 us: shards(): far.append(lax.ppermute(gated_mix, 'ch', other_chip))]
    convert_element_type x1, other arithmetic: 8.71 us -> 14.9 us  [shards(): x = mixed_input.astype(jnp.float32)]
    slice x0 -> x5, local copies, waits for them, and re-layouts: none -> 5.81 us  [the longest x1 2.13 us: shards(): x_here = x[:, cols]]
    pallas_call x1 -> x4, Pallas kernels: 16.5 us -> 22 us  [run_recurrence(): pl.pallas_call(recurrence_kernel, grid=(width // LANES,), in_specs=[pl.Bl...]
    dynamic_slice x0 -> x1, local copies, waits for them, and re-layouts: none -> 4.64 us  [weight_rows(): lax.dynamic_slice_in_dim(out_weight, owner * width, width, 0)]
    convert_element_type x1, other arithmetic: 6.43 us -> 2.01 us  [shards(): return total.astype(jnp.bfloat16)]
  transfers between devices with their start and end apart: 11 -> 14, of which waited for: 1 -> 5; matrix products, arithmetic and copies ran while one was open for 13% -> 15% of each run, Pallas kernels for 0% -> 4%
where the time goes in v6:
time: 152 us; the launch traced here: 151 us
  other arithmetic  35.8 us (24%)
  waiting for transfers between devices  32.1 us (21%)
  Pallas kernels  31.5 us (21%)
  starting transfers between devices  25.5 us (17%)
  local copies, waits for them, and re-layouts  15 us (10%)
  matrix products  10.8 us (7%)
    ppermute x4, waiting for transfers between devices, shards(): far.append(lax.ppermute(gated_mix, 'ch', other_chip))  28.6 us
    pallas_call x4, Pallas kernels, run_recurrence(): pl.pallas_call(recurrence_kernel, grid=(width // LANES,), in_specs=[pl.Bl...  22 us
    ppermute x8, starting transfers between devices, shifted(): lax.ppermute(value, axis, [(source, source + steps) for source in range(i...  19.2 us
    convert_element_type x1, other arithmetic, shards(): x = mixed_input.astype(jnp.float32)  14.9 us
    unnamed x5, other arithmetic  12 us
    pallas_call x1, Pallas kernels, run_end_state(): pl.pallas_call(end_state_kernel, grid=(width // LANES,), in_specs=[pl.Blo...  9.45 us
    dot_general x1, matrix products, shards(): jnp.dot(jnp.concatenate([own, near], 1), local_rows, preferred_element_ty...  6.34 us
    dynamic_slice x1, local copies, waits for them, and re-layouts, weight_rows(): lax.dynamic_slice_in_dim(out_weight, owner * width, width, 0)  4.64 us
  transfers between devices with their start and end apart: 14, of which 5 were waited for; matrix products, arithmetic and copies ran while one was open for 15% of the time, Pallas kernels for 4%

profile of v6, /device:TPU:1, one launch (start us, length us, event | category | flops | bytes accessed | tf_op | source)
XLA Modules:
  0.0 151.1 jit_solution(4346294151553409894)
XLA Ops:
  0.8 4.0 %collective-permute-start = (bf16[3,2,1024]{2,1,0:T(2,128)(2,1)S(1)}, bf16[3,2,1024]{2,1,0:T(2,128)(2,1)S(1)}, u32[]{:S(2)}, u32[]{:S(2)}) collective-permute-start(bf16[3,2,1024]{2,1,0:T(2,128)(2,1)S(1)} %slice.144), channel_id=1, source_target_pairs={{0,4},{4,8},{8,12},{12,16},{16,20},{20,24},{24,28},{1,5},{5,9},{9,... | collective-permute-start | bytes 36872 | tf_op jit(solution)/shard_map/ppermute | solution.py:17
  8.1 1.4 fusion.41
  9.6 14.9 %fusion.37 = (f32[1024,1024]{1,0:T(8,128)}, bf16[1024,1024]{1,0:T(8,128)(2,1)S(1)}, f32[1024,1024]{1,0:T(8,128)}) fusion(f32[1024]{0:T(1024)S(1)} %bitcast.63, f32[1024]{0:T(1024)S(1)} %bitcast.64, bf16[3,1024,1024]{2,1,0:T(8,128)(2,1)} %param.6, f32[1024]{0:T(1024)S(1)} %bitcast.65, f32[1024]{0:T(1024)S(1)} %bitcast.66, ...), kind=kLoop, calls=%fused_computation.93 | loop fusion | flops 53477376 | bytes 23117824 | tf_op jit(solution)/shard_map/convert_element_type | solution.py:160
  24.4 9.4 %shard_map.64 = f32[16,8,1024]{2,1,0:T(8,128)} custom-call(f32[1024,1024]{1,0:T(8,128)} %get-tuple-element.31.x_ref, f32[16,1024]{1,0:T(8,128)} %copy-done.5), custom_call_target="tpu_custom_call" | custom-call | flops 33554432 | bytes 4194304 | tf_op jit(solution)/shard_map/pallas_call | solution.py:64
  33.9 1.3 multiply_reduce_fusion.1
  35.2 4.3 %collective-permute-start.7 = (f32[16,1024]{1,0:T(8,128)S(1)}, f32[16,1024]{1,0:T(8,128)S(1)}, u32[]{:S(2)}, u32[]{:S(2)}) collective-permute-start(f32[16,1024]{1,0:T(8,128)S(1)} %multiply_reduce_fusion.1), channel_id=1, source_target_pairs={{0,28},{1,29},{2,30},{3,31}} | collective-permute-start | bytes 196616 | tf_op jit(solution)/shard_map/ppermute | solution.py:17
  39.5 1.6 %collective-permute-start.6 = (f32[16,1024]{1,0:T(8,128)S(1)}, f32[16,1024]{1,0:T(8,128)S(1)}, u32[]{:S(2)}, u32[]{:S(2)}) collective-permute-start(f32[16,1024]{1,0:T(8,128)S(1)} %multiply_reduce_fusion.1), channel_id=1, source_target_pairs={{0,24},{4,28},{1,25},{5,29},{2,26},{6,30},{3,27},{7,31}} | collective-permute-start | bytes 196616 | tf_op jit(solution)/shard_map/ppermute | solution.py:17
  41.1 1.3 collective-permute-start.5
  43.7 1.9 %collective-permute-start.3 = (f32[16,1024]{1,0:T(8,128)S(1)}, f32[16,1024]{1,0:T(8,128)S(1)}, u32[]{:S(2)}, u32[]{:S(2)}) collective-permute-start(f32[16,1024]{1,0:T(8,128)S(1)} %multiply_reduce_fusion.1), channel_id=1, source_target_pairs={{0,12},{4,16},{8,20},{12,24},{16,28},{1,13},{5,17},{9,21},{13,25},... | collective-permute-start | bytes 196616 | tf_op jit(solution)/shard_map/ppermute | solution.py:17
  45.7 2.1 %fusion.39 = (f32[1024,256]{1,0:T(8,128)}, f32[1024,256]{1,0:T(8,128)}, f32[1024,256]{1,0:T(8,128)}, f32[1024,256]{1,0:T(8,128)}) fusion(bf16[1024,1024]{1,0:T(8,128)(2,1)S(1)} %get-tuple-element.32), kind=kLoop, calls=%fused_computation.94 | loop fusion | bytes 8388608 | tf_op jit(solution)/shard_map/slice | solution.py:179
  48.1 1.6 %collective-permute-start.2 = (f32[16,1024]{1,0:T(8,128)S(1)}, f32[16,1024]{1,0:T(8,128)S(1)}, u32[]{:S(2)}, u32[]{:S(2)}) collective-permute-start(f32[16,1024]{1,0:T(8,128)S(1)} %multiply_reduce_fusion.1), channel_id=1, source_target_pairs={{0,8},{4,12},{8,16},{12,20},{16,24},{20,28},{1,9},{5,13},{9,17},{1... | collective-permute-start | bytes 196616 | tf_op jit(solution)/shard_map/ppermute | solution.py:17
  49.7 3.3 %collective-permute-start.1 = (f32[16,1024]{1,0:T(8,128)S(1)}, f32[16,1024]{1,0:T(8,128)S(1)}, u32[]{:S(2)}, u32[]{:S(2)}) collective-permute-start(f32[16,1024]{1,0:T(8,128)S(1)} %multiply_reduce_fusion.1), channel_id=1, source_target_pairs={{0,4},{4,8},{8,12},{12,16},{16,20},{20,24},{24,28},{1,5},{5,9},{9,... | collective-permute-start | bytes 196616 | tf_op jit(solution)/shard_map/ppermute | solution.py:17
  55.5 5.5 %shard_map.65 = f32[1024,256]{1,0:T(8,128)} custom-call(f32[1024,256]{1,0:T(8,128)} %get-tuple-element.40.x_ref, f32[16,256]{1,0:T(8,128)} %get-tuple-element.53.decay_ref, f32[16,256]{1,0:T(8,128)} %get-tuple-element.48.residue_ref, f32[16,8,256]{2,1,0:T(8,128)} %get-tuple-element.45.start_ref), custom_call_target="tpu_custom_call" | custom-call | flops 16777216 | bytes 2097152 | tf_op jit(solution)/shard_map/pallas_call | solution.py:83
  61.1 2.8 %constant_dynamic-update-slice_fusion.4 = (bf16[1024,2048]{1,0:T(8,128)(2,1)}, bf16[1024,256]{1,0:T(8,128)(2,1)}) fusion(bf16[1024,1024]{1,0:T(8,128)(2,1)S(1)} %get-tuple-element.32, f32[256]{0:T(256)S(1)} %get-tuple-element.67, f32[1024,256]{1,0:T(8,128)} %shard_map.65, f32[1024,1024]{1,0:T(8,128)} %get-tuple-element.37), kind=kLoop, calls=%fused_computation.66 | loop fusion | flops 1835007 | bytes 3671040
  65.1 5.5 %shard_map.66 = f32[1024,256]{1,0:T(8,128)} custom-call(f32[1024,256]{1,0:T(8,128)} %get-tuple-element.38.x_ref, f32[16,256]{1,0:T(8,128)} %get-tuple-element.52.decay_ref, f32[16,256]{1,0:T(8,128)} %get-tuple-element.47.residue_ref, f32[16,8,256]{2,1,0:T(8,128)} %get-tuple-element.44.start_ref), custom_call_target="tpu_custom_call" | custom-call | flops 16777216 | bytes 2097152 | tf_op jit(solution)/shard_map/pallas_call | solution.py:83
  70.6 2.6 %constant_dynamic-update-slice_fusion.3 = (bf16[1024,2048]{1,0:T(8,128)(2,1)}, bf16[1024,256]{1,0:T(8,128)(2,1)S(1)}) fusion(bf16[1024,2048]{1,0:T(8,128)(2,1)} %get-tuple-element.29, bf16[1024,1024]{1,0:T(8,128)(2,1)S(1)} %get-tuple-element.32, f32[256]{0:T(256)S(1)} %get-tuple-element.66, f32[1024,256]{1,0:T(8,128)} %shard_map.66, ...), kind=kLoop, calls=%fused_computation.65 | loop fusion | flops 1835008 | bytes 3671040
  73.5 1.8 %collective-permute-done.8 = bf16[1024,256]{1,0:T(8,128)(2,1)S(1)} collective-permute-done((bf16[1024,256]{1,0:T(8,128)(2,1)}, bf16[1024,256]{1,0:T(8,128)(2,1)S(1)}, u32[]{:S(2)}, u32[]{:S(2)}) %collective-permute-start.8) | collective-permute-done | bytes 524320 | tf_op jit(solution)/shard_map/ppermute | solution.py:190
  75.3 11.9 %collective-permute-done.9 = bf16[1024,256]{1,0:T(8,128)(2,1)S(1)} collective-permute-done((bf16[1024,256]{1,0:T(8,128)(2,1)S(1)}, bf16[1024,256]{1,0:T(8,128)(2,1)S(1)}, u32[]{:S(2)}, u32[]{:S(2)}) %collective-permute-start.9) | collective-permute-done | bytes 524320 | tf_op jit(solution)/shard_map/ppermute | solution.py:190
  87.2 5.5 %shard_map.67 = f32[1024,256]{1,0:T(8,128)} custom-call(f32[1024,256]{1,0:T(8,128)} %get-tuple-element.16.x_ref, f32[16,256]{1,0:T(8,128)} %get-tuple-element.51.decay_ref, f32[16,256]{1,0:T(8,128)} %get-tuple-element.49.residue_ref, f32[16,8,256]{2,1,0:T(8,128)} %get-tuple-element.43.start_ref), custom_call_target="tpu_custom_call" | custom-call | flops 16777216 | bytes 2097152 | tf_op jit(solution)/shard_map/pallas_call | solution.py:83
  92.7 2.8 %constant_dynamic-update-slice_fusion.2 = (bf16[1024,2048]{1,0:T(8,128)(2,1)}, bf16[1024,256]{1,0:T(8,128)(2,1)}) fusion(bf16[1024,2048]{1,0:T(8,128)(2,1)} %get-tuple-element.27, bf16[1024,1024]{1,0:T(8,128)(2,1)S(1)} %get-tuple-element.32, f32[256]{0:T(256)S(1)} %get-tuple-element.68, f32[1024,256]{1,0:T(8,128)} %shard_map.67, ...), kind=kLoop, calls=%fused_computation.64 | loop fusion | flops 1835008 | bytes 3671040
  95.5 5.5 %shard_map.68 = f32[1024,256]{1,0:T(8,128)} custom-call(f32[1024,256]{1,0:T(8,128)} %get-tuple-element.17.x_ref, f32[16,256]{1,0:T(8,128)} %get-tuple-element.50.decay_ref, f32[16,256]{1,0:T(8,128)} %get-tuple-element.46.residue_ref, f32[16,8,256]{2,1,0:T(8,128)} %get-tuple-element.42.start_ref), custom_call_target="tpu_custom_call" | custom-call | flops 16777216 | bytes 2097152 | tf_op jit(solution)/shard_map/pallas_call | solution.py:83
  101.0 2.6 %constant_dynamic-update-slice_fusion.1 = (bf16[1024,2048]{1,0:T(8,128)(2,1)}, bf16[1024,256]{1,0:T(8,128)(2,1)S(1)}) fusion(bf16[1024,2048]{1,0:T(8,128)(2,1)} %get-tuple-element.25, bf16[1024,1024]{1,0:T(8,128)(2,1)S(1)} %get-tuple-element.32, f32[256]{0:T(256)S(1)} %get-tuple-element.65, f32[1024,256]{1,0:T(8,128)} %shard_map.68, ...), kind=kLoop, calls=%fused_computation.63 | loop fusion | flops 1835008 | bytes 3671040
  104.5 3.0 %pad_maximum_fusion.1 = bf16[1024,1024]{1,0:T(8,128)(2,1)} fusion(bf16[1024,256]{1,0:T(8,128)(2,1)S(1)} %get-tuple-element.24, bf16[1024,256]{1,0:T(8,128)(2,1)} %get-tuple-element.26, bf16[1024,256]{1,0:T(8,128)(2,1)} %copy-done.4, bf16[1024,256]{1,0:T(8,128)(2,1)} %get-tuple-element.30), kind=kLoop, calls=%fused_computation.49 | loop fusion | flops 8388608 | bytes 4194304 | tf_op jit(solution)/shard_map/concatenate | solution.py:194
  107.5 2.5 %collective-permute-start.12 = (bf16[1024,1024]{1,0:T(8,128)(2,1)}, bf16[1024,1024]{1,0:T(8,128)(2,1)S(1)}, u32[]{:S(2)}, u32[]{:S(2)}) collective-permute-start(bf16[1024,1024]{1,0:T(8,128)(2,1)} %pad_maximum_fusion.1), channel_id=1, source_target_pairs={{0,1},{1,0},{2,3},{3,2},{4,5},{5,4},{6,7},{7,6},{8,9},{9,8},{10,11... | collective-permute-start | bytes 6291464 | tf_op jit(solution)/shard_map/ppermute | solution.py:195
  109.9 4.6 %constant_dynamic-slice_fusion.1 = (bf16[1024,1024]{1,0:T(8,128)(2,1)S(1)}, bf16[1024,1024]{1,0:T(8,128)(2,1)S(1)}, bf16[1024,1024]{1,0:T(8,128)(2,1)S(1)}, bf16[1024,1024]{1,0:T(8,128)(2,1)S(1)}) fusion(bf16[4096,1024]{1,0:T(8,128)(2,1)} %param.11, s32[]{:T(128)S(6)} %select_n.19, s32[]{:T(128)S(6)} %select_n.18, s32[]{:T(128)S(6)} %select_n.17, ...), kind=kLoop, calls=%fused_computation.84 | loop fusion | bytes 16777232 | tf_op jit(solution)/shard_map/dynamic_slice | solution.py:148
  116.3 1.9 %copy-done.8 = bf16[1024,2048]{1,0:T(8,128)(2,1)} copy-done((bf16[1024,2048]{1,0:T(8,128)(2,1)}, bf16[1024,2048]{1,0:T(8,128)(2,1)S(1)}, u32[]{:S(2)}) %copy-start.8) | copy-done | bytes 4194328
  118.3 6.3 %fusion = f32[1024,1024]{1,0:T(8,128)S(1)} fusion(bf16[1024,2048]{1,0:T(8,128)(2,1)} %copy-done.8, bf16[1024,1024]{1,0:T(8,128)(2,1)S(1)} %get-tuple-element.34, bf16[1024,1024]{1,0:T(8,128)(2,1)S(1)} %get-tuple-element.35), kind=kOutput, calls=%fused_computation.5 | convolution fusion | flops 4303355904 | bytes 12582912 | tf_op jit(solution)/shard_map/dot_general | solution.py:198
  124.6 3.6 %collective-permute-done.10 = bf16[1024,256]{1,0:T(8,128)(2,1)S(1)} collective-permute-done((bf16[1024,256]{1,0:T(8,128)(2,1)S(1)}, bf16[1024,256]{1,0:T(8,128)(2,1)S(1)}, u32[]{:S(2)}, u32[]{:S(2)}) %collective-permute-start.10) | collective-permute-done | bytes 524320 | tf_op jit(solution)/shard_map/ppermute | solution.py:190
  128.2 11.2 %collective-permute-done.11 = bf16[1024,256]{1,0:T(8,128)(2,1)S(1)} collective-permute-done((bf16[1024,256]{1,0:T(8,128)(2,1)S(1)}, bf16[1024,256]{1,0:T(8,128)(2,1)S(1)}, u32[]{:S(2)}, u32[]{:S(2)}) %collective-permute-start.11) | collective-permute-done | bytes 524320 | tf_op jit(solution)/shard_map/ppermute | solution.py:190
  140.9 3.5 %collective-permute-done.13 = bf16[1024,1024]{1,0:T(8,128)(2,1)S(1)} collective-permute-done((bf16[1024,1024]{1,0:T(8,128)(2,1)S(1)}, bf16[1024,1024]{1,0:T(8,128)(2,1)S(1)}, u32[]{:S(2)}, u32[]{:S(2)}) %collective-permute-start.13) | collective-permute-done | bytes 2097184 | tf_op jit(solution)/shard_map/ppermute | solution.py:201
  144.5 4.5 %fusion.4 = f32[1024,1024]{1,0:T(8,128)S(1)} fusion(bf16[1024,2048]{1,0:T(8,128)(2,1)S(1)} %constant_dynamic-update-slice_fusion.5, bf16[1024,1024]{1,0:T(8,128)(2,1)S(1)} %get-tuple-element.36, bf16[1024,1024]{1,0:T(8,128)(2,1)S(1)} %get-tuple-element.33), kind=kOutput, calls=%fused_computation.9 | convolution fusion | flops 4303355904 | bytes 12582912 | tf_op jit(solution)/shard_map/dot_general | solution.py:202
  149.0 2.0 %add_convert_fusion = bf16[1024,1024]{1,0:T(8,128)(2,1)} fusion(f32[1024,1024]{1,0:T(8,128)S(1)} %fusion, f32[1024,1024]{1,0:T(8,128)S(1)} %fusion.4), kind=kLoop, calls=%fused_computation.31 | loop fusion | flops 2097152 | bytes 10485760 | tf_op jit(solution)/shard_map/convert_element_type | solution.py:203
  (54 shorter events, 13.9 us)
Async XLA Ops:
  0.8 8.7 %collective-permute-start = (bf16[3,2,1024]{2,1,0:T(2,128)(2,1)S(1)}, bf16[3,2,1024]{2,1,0:T(2,128)(2,1)S(1)}, u32[]{:S(2)}, u32[]{:S(2)}) collective-permute-start(bf16[3,2,1024]{2,1,0:T(2,128)(2,1)S(1)} %slice.144), channel_id=1, source_target_pairs={{0,4},{4,8},{8,12},{12,16},{16,20},{20,24},{24,28},{1,5},{5,9},{9,... | collective-permute-start | bytes 36872 | tf_op jit(solution)/shard_map/ppermute | solution.py:17
  7.4 17.0 %copy-start.5 = (f32[16,1024]{1,0:T(8,128)}, f32[16,1024]{1,0:T(8,128)S(1)}, u32[]{:S(2)}) copy-start(f32[16,1024]{1,0:T(8,128)S(1)} %get-tuple-element.55.decay_ref) | copy-start | bytes 196612
  35.2 12.9 %collective-permute-start.7 = (f32[16,1024]{1,0:T(8,128)S(1)}, f32[16,1024]{1,0:T(8,128)S(1)}, u32[]{:S(2)}, u32[]{:S(2)}) collective-permute-start(f32[16,1024]{1,0:T(8,128)S(1)} %multiply_reduce_fusion.1), channel_id=1, source_target_pairs={{0,28},{1,29},{2,30},{3,31}} | collective-permute-start | bytes 196616 | tf_op jit(solution)/shard_map/ppermute | solution.py:17
  39.5 10.1 %collective-permute-start.6 = (f32[16,1024]{1,0:T(8,128)S(1)}, f32[16,1024]{1,0:T(8,128)S(1)}, u32[]{:S(2)}, u32[]{:S(2)}) collective-permute-start(f32[16,1024]{1,0:T(8,128)S(1)} %multiply_reduce_fusion.1), channel_id=1, source_target_pairs={{0,24},{4,28},{1,25},{5,29},{2,26},{6,30},{3,27},{7,31}} | collective-permute-start | bytes 196616 | tf_op jit(solution)/shard_map/ppermute | solution.py:17
  41.1 13.1 %collective-permute-start.5 = (f32[16,1024]{1,0:T(8,128)S(1)}, f32[16,1024]{1,0:T(8,128)S(1)}, u32[]{:S(2)}, u32[]{:S(2)}) collective-permute-start(f32[16,1024]{1,0:T(8,128)S(1)} %multiply_reduce_fusion.1), channel_id=1, source_target_pairs={{0,20},{4,24},{8,28},{1,21},{5,25},{9,29},{2,22},{6,26},{10,30},{3... | collective-permute-start | bytes 196616 | tf_op jit(solution)/shard_map/ppermute | solution.py:17
  42.4 11.8 %collective-permute-start.4 = (f32[16,1024]{1,0:T(8,128)S(1)}, f32[16,1024]{1,0:T(8,128)S(1)}, u32[]{:S(2)}, u32[]{:S(2)}) collective-permute-start(f32[16,1024]{1,0:T(8,128)S(1)} %multiply_reduce_fusion.1), channel_id=1, source_target_pairs={{0,16},{4,20},{8,24},{12,28},{1,17},{5,21},{9,25},{13,29},{2,18},{... | collective-permute-start | bytes 196616 | tf_op jit(solution)/shard_map/ppermute | solution.py:17
  43.7 10.5 %collective-permute-start.3 = (f32[16,1024]{1,0:T(8,128)S(1)}, f32[16,1024]{1,0:T(8,128)S(1)}, u32[]{:S(2)}, u32[]{:S(2)}) collective-permute-start(f32[16,1024]{1,0:T(8,128)S(1)} %multiply_reduce_fusion.1), channel_id=1, source_target_pairs={{0,12},{4,16},{8,20},{12,24},{16,28},{1,13},{5,17},{9,21},{13,25},... | collective-permute-start | bytes 196616 | tf_op jit(solution)/shard_map/ppermute | solution.py:17
  45.6 2.2 %copy-start = (f32[16,8,1024]{2,1,0:T(8,128)S(1)}, f32[16,8,1024]{2,1,0:T(8,128)}, u32[]{:S(2)}) copy-start(f32[16,8,1024]{2,1,0:T(8,128)} %shard_map.64) | copy-start | bytes 1572868
  45.6 8.6 %copy-start.6 = (f32[16,1024]{1,0:T(8,128)S(1)}, f32[16,1024]{1,0:T(8,128)}, u32[]{:S(2)}) copy-start(f32[16,1024]{1,0:T(8,128)} %param.8) | copy-start | bytes 196612
  48.1 6.1 %collective-permute-start.2 = (f32[16,1024]{1,0:T(8,128)S(1)}, f32[16,1024]{1,0:T(8,128)S(1)}, u32[]{:S(2)}, u32[]{:S(2)}) collective-permute-start(f32[16,1024]{1,0:T(8,128)S(1)} %multiply_reduce_fusion.1), channel_id=1, source_target_pairs={{0,8},{4,12},{8,16},{12,20},{16,24},{20,28},{1,9},{5,13},{9,17},{1... | collective-permute-start | bytes 196616 | tf_op jit(solution)/shard_map/ppermute | solution.py:17
  49.7 4.5 %collective-permute-start.1 = (f32[16,1024]{1,0:T(8,128)S(1)}, f32[16,1024]{1,0:T(8,128)S(1)}, u32[]{:S(2)}, u32[]{:S(2)}) collective-permute-start(f32[16,1024]{1,0:T(8,128)S(1)} %multiply_reduce_fusion.1), channel_id=1, source_target_pairs={{0,4},{4,8},{8,12},{12,16},{16,20},{20,24},{24,28},{1,5},{5,9},{9,... | collective-permute-start | bytes 196616 | tf_op jit(solution)/shard_map/ppermute | solution.py:17
  63.9 11.4 %collective-permute-start.8 = (bf16[1024,256]{1,0:T(8,128)(2,1)}, bf16[1024,256]{1,0:T(8,128)(2,1)S(1)}, u32[]{:S(2)}, u32[]{:S(2)}) collective-permute-start(bf16[1024,256]{1,0:T(8,128)(2,1)} %get-tuple-element.30), channel_id=1, source_target_pairs={{0,2},{1,3},{2,0},{3,1},{4,6},{5,7},{6,4},{7,5},{8,10},{9,11},{10,... | collective-permute-start | bytes 1572872 | tf_op jit(solution)/shard_map/ppermute | solution.py:190
  73.2 14.0 %copy-start.4 = (bf16[1024,256]{1,0:T(8,128)(2,1)}, bf16[1024,256]{1,0:T(8,128)(2,1)S(1)}, u32[]{:S(2)}) copy-start(bf16[1024,256]{1,0:T(8,128)(2,1)S(1)} %get-tuple-element.28) | copy-start | bytes 1572868
  73.2 14.0 %collective-permute-start.9 = (bf16[1024,256]{1,0:T(8,128)(2,1)S(1)}, bf16[1024,256]{1,0:T(8,128)(2,1)S(1)}, u32[]{:S(2)}, u32[]{:S(2)}) collective-permute-start(bf16[1024,256]{1,0:T(8,128)(2,1)S(1)} %get-tuple-element.28), channel_id=1, source_target_pairs={{0,2},{1,3},{2,0},{3,1},{4,6},{5,7},{6,4},{7,5},{8,10},{9,11},{10,... | collective-permute-start | bytes 1572872 | tf_op jit(solution)/shard_map/ppermute | solution.py:190
  103.6 0.9 copy-start.2
  107.5 8.7 %collective-permute-start.12 = (bf16[1024,1024]{1,0:T(8,128)(2,1)}, bf16[1024,1024]{1,0:T(8,128)(2,1)S(1)}, u32[]{:S(2)}, u32[]{:S(2)}) collective-permute-start(bf16[1024,1024]{1,0:T(8,128)(2,1)} %pad_maximum_fusion.1), channel_id=1, source_target_pairs={{0,1},{1,0},{2,3},{3,2},{4,5},{5,4},{6,7},{7,6},{8,9},{9,8},{10,11... | collective-permute-start | bytes 6291464 | tf_op jit(solution)/shard_map/ppermute | solution.py:195
  109.9 4.7 %copy-start.1 = (bf16[1024,256]{1,0:T(8,128)(2,1)S(1)}, bf16[1024,256]{1,0:T(8,128)(2,1)}, u32[]{:S(2)}) copy-start(bf16[1024,256]{1,0:T(8,128)(2,1)} %get-tuple-element.26) | copy-start | bytes 1572868
  109.9 5.9 %copy-start.3 = (bf16[1024,256]{1,0:T(8,128)(2,1)S(1)}, bf16[1024,256]{1,0:T(8,128)(2,1)}, u32[]{:S(2)}) copy-start(bf16[1024,256]{1,0:T(8,128)(2,1)} %copy-done.2) | copy-start | bytes 1572868
  109.9 6.2 %copy-start.7 = (bf16[1024,2048]{1,0:T(8,128)(2,1)S(1)}, bf16[1024,2048]{1,0:T(8,128)(2,1)}, u32[]{:S(2)}) copy-start(bf16[1024,2048]{1,0:T(8,128)(2,1)} %get-tuple-element.23) | copy-start | bytes 12582916
  114.6 13.6 %collective-permute-start.10 = (bf16[1024,256]{1,0:T(8,128)(2,1)S(1)}, bf16[1024,256]{1,0:T(8,128)(2,1)S(1)}, u32[]{:S(2)}, u32[]{:S(2)}) collective-permute-start(bf16[1024,256]{1,0:T(8,128)(2,1)S(1)} %copy-done.1), channel_id=1, source_target_pairs={{0,2},{1,3},{2,0},{3,1},{4,6},{5,7},{6,4},{7,5},{8,10},{9,11},{10,... | collective-permute-start | bytes 1572872 | tf_op jit(solution)/shard_map/ppermute | solution.py:190
  115.9 23.6 %collective-permute-start.11 = (bf16[1024,256]{1,0:T(8,128)(2,1)S(1)}, bf16[1024,256]{1,0:T(8,128)(2,1)S(1)}, u32[]{:S(2)}, u32[]{:S(2)}) collective-permute-start(bf16[1024,256]{1,0:T(8,128)(2,1)S(1)} %copy-done.3), channel_id=1, source_target_pairs={{0,2},{1,3},{2,0},{3,1},{4,6},{5,7},{6,4},{7,5},{8,10},{9,11},{10,... | collective-permute-start | bytes 1572872 | tf_op jit(solution)/shard_map/ppermute | solution.py:190
  116.3 2.0 %copy-start.8 = (bf16[1024,2048]{1,0:T(8,128)(2,1)}, bf16[1024,2048]{1,0:T(8,128)(2,1)S(1)}, u32[]{:S(2)}) copy-start(bf16[1024,2048]{1,0:T(8,128)(2,1)S(1)} %constant_dynamic-update-slice_fusion) | copy-start | bytes 12582916
  139.7 4.7 %collective-permute-start.13 = (bf16[1024,1024]{1,0:T(8,128)(2,1)S(1)}, bf16[1024,1024]{1,0:T(8,128)(2,1)S(1)}, u32[]{:S(2)}, u32[]{:S(2)}) collective-permute-start(bf16[1024,1024]{1,0:T(8,128)(2,1)S(1)} %pad_maximum_fusion.2), channel_id=1, source_target_pairs={{0,1},{1,0},{2,3},{3,2},{4,5},{5,4},{6,7},{7,6},{8,9},{9,8},{10,11... | collective-permute-start | bytes 6291464 | tf_op jit(solution)/shard_map/ppermute | solution.py:201

commit v7 on v5

--- a/solution.py
+++ b/solution.py
@@ -112,11 +112,17 @@
 
 def incoming_state(local_end, pole_rates, row_count):
     ctx_count = lax.axis_size("ctx")
-    total = jnp.zeros_like(local_end)
-    for distance in range(1, ctx_count):
-        received = shifted(local_end, "ctx", distance)
-        total = total + jnp.exp(-pole_rates * jnp.float32(row_count * (distance - 1))) * received
-    return total
+    width = local_end.shape[1]
+    ends = lax.all_gather(local_end, "ctx", axis=1, tiled=True).reshape(local_end.shape[0], ctx_count, width)
+    here = lax.axis_index("ctx")
+    earlier = jnp.arange(ctx_count, dtype=jnp.int32)
+    gaps = (here - 1 - earlier).astype(jnp.float32)
+    weights = jnp.where(
+        (earlier < here)[None, :, None],
+        jnp.exp(-pole_rates[:, None, :] * (jnp.float32(row_count) * jnp.maximum(gaps, 0.0))[None, :, None]),
+        jnp.float32(0.0),
+    )
+    return jnp.sum(weights * ends, axis=1)
 
 
 def featurize(extended, tap_weights, stream, count):

time: 131 us -> 146 us (1.11)
  blocking collectives: 0 us -> 26.1 us
  starting transfers between devices: 24.5 us -> 13.4 us
    all_gather x0 -> x1, blocking collectives: none -> 26.1 us  [incoming_state(): lax.all_gather(local_end, 'ctx', axis=1, tiled=True)]
    ppermute x8 -> x1, starting transfers between devices: 19.3 us -> 3.97 us  [shifted(): lax.ppermute(value, axis, [(source, source + steps) for source in range(i...]
    ppermute x1, starting transfers between devices: 3.14 us -> 7.34 us  [project(): near = lax.ppermute(gated_mix, 'ch', [(i, i ^ 1) for i in range(ch_count)])]
  transfers between devices with their start and end apart: 11 -> 4, of which waited for: 2 -> 2; matrix products, arithmetic and copies ran while one was open for 15% -> 12% of each run, Pallas kernels for 0% -> 0%
where the time goes in v7:
time: 146 us
  waiting for transfers between devices  35.6 us (24%)
  blocking collectives  26.1 us (18%)
  Pallas kernels  26 us (18%)
  other arithmetic  21.5 us (15%)
  matrix products  20.5 us (14%)
  starting transfers between devices  13.4 us (9%)
  local copies, waits for them, and re-layouts  2.48 us (2%)
    ppermute x1, waiting for transfers between devices, project(): far = lax.ppermute(gated_mix, 'ch', [(i, i ^ 2) for i in range(ch_count)])  32.9 us
    all_gather x1, blocking collectives, incoming_state(): lax.all_gather(local_end, 'ctx', axis=1, tiled=True)  26.1 us
    dot_general x4, matrix products, part(): return jnp.dot(piece, rows, preferred_element_type=jnp.float32)  20.5 us
    pallas_call x1, Pallas kernels, run_recurrence(): pl.pallas_call(recurrence_kernel, grid=(width // LANES,), in_specs=[pl.Bl...  16.6 us
    pallas_call x1, Pallas kernels, run_end_state(): pl.pallas_call(end_state_kernel, grid=(width // LANES,), in_specs=[pl.Blo...  9.44 us
    convert_element_type x1, other arithmetic, shards(): x = mixed_input.astype(jnp.float32)  8.71 us
    ppermute x1, starting transfers between devices, project(): near = lax.ppermute(gated_mix, 'ch', [(i, i ^ 1) for i in range(ch_count)])  7.34 us
    convert_element_type x1, other arithmetic, shards(): gated_mix = gated_mix.astype(jnp.bfloat16)  6.36 us
  transfers between devices with their start and end apart: 4, of which 2 were waited for; matrix products, arithmetic and copies ran while one was open for 12% of the time, Pallas kernels for 0%

profile of v7, /device:TPU:1, one launch (start us, length us, event | category | flops | bytes accessed | tf_op | source)
XLA Modules:
  0.0 145.7 jit_solution(5180373537129315592)
XLA Ops:
  0.0 0.8 slice.60
  0.8 4.0 %collective-permute-start = (bf16[3,2,1024]{2,1,0:T(2,128)(2,1)S(1)}, bf16[3,2,1024]{2,1,0:T(2,128)(2,1)S(1)}, u32[]{:S(2)}, u32[]{:S(2)}) collective-permute-start(bf16[3,2,1024]{2,1,0:T(2,128)(2,1)S(1)} %slice.60), channel_id=1, source_target_pairs={{0,4},{4,8},{8,12},{12,16},{16,20},{20,24},{24,28},{1,5},{5,9},{9,... | collective-permute-start | bytes 36872 | tf_op jit(solution)/shard_map/ppermute | solution.py:15
  4.9 0.1 maximum_multiply_fusion
  4.9 0.9 slice_convert_fusion.8
  5.8 1.5 %fusion.42 = (f32[16,1024]{1,0:T(8,128)S(1)}, f32[16,1024]{1,0:T(8,128)}) fusion(f32[16,1024]{1,0:T(8,128)} %param.8), kind=kLoop, calls=%fused_computation.79 | loop fusion | flops 16384 | bytes 196608 | tf_op jit(solution)/shard_map/neg | solution.py:175
  7.3 0.0 collective-permute-done
  7.3 8.7 %fusion.30.x_ref = f32[1024,1024]{1,0:T(8,128)} fusion(bf16[3,1024,1024]{2,1,0:T(8,128)(2,1)} %param.6, bf16[3,2,1024]{2,1,0:T(2,128)(2,1)S(1)} %collective-permute-done, f32[1024]{0:T(1024)S(1)} %bitcast.82, f32[1024]{0:T(1024)S(1)} %bitcast.83, f32[1024]{0:T(1024)S(1)} %bitcast.78, f32[1024]{0:T(1024)S(1)} %bitcast.79, f32[1024]{0:T(1024)S(1)} %bitcast.80, ...), kind=kLoop, calls=%fused_computation.52 | loop fusion | flops 36700160 | bytes 14716928 | tf_op jit(solution)/shard_map/convert_element_type | solution.py:172
  16.0 9.4 %shard_map.64 = f32[16,8,1024]{2,1,0:T(8,128)} custom-call(f32[1024,1024]{1,0:T(8,128)} %fusion.30.x_ref, f32[16,1024]{1,0:T(8,128)} %get-tuple-element.10.decay_ref), custom_call_target="tpu_custom_call" | custom-call | tf_op jit(solution)/shard_map/pallas_call | solution.py:62
  25.5 1.3 multiply_reduce_fusion.1
  26.8 26.1 %all_gather.3 = f32[16,8192]{1,0:T(8,128)S(1)} all-gather(f32[16,1024]{1,0:T(8,128)S(1)} %multiply_reduce_fusion.1), channel_id=1, replica_groups=mesh['ctx'=8,'ch'=4] {'ctx'}, dimensions={1}, use_global_device_ids=true | all-gather | bytes 589824 | tf_op jit(solution)/shard_map/all_gather | solution.py:116
  52.9 0.3 copy.17
  53.3 1.4 copy.15
  54.6 0.2 bitcast_multiply_fusion
  54.8 1.2 multiply_reduce_fusion
  56.0 1.2 fusion.37.start_ref
  57.2 0.0 copy-start
  57.2 16.6 %shard_map.65 = f32[1024,1024]{1,0:T(8,128)} custom-call(f32[1024,1024]{1,0:T(8,128)} %fusion.30.x_ref, f32[16,1024]{1,0:T(8,128)} %get-tuple-element.10.decay_ref, f32[16,1024]{1,0:T(8,128)} %residue_ref.1, f32[16,8,1024]{2,1,0:T(8,128)} %fusion.37.start_ref), custom_call_target="tpu_custom_call" | custom-call | tf_op jit(solution)/shard_map/pallas_call | solution.py:78
  73.8 0.0 copy-done
  73.8 6.4 %fusion.9 = bf16[1024,1024]{1,0:T(8,128)(2,1)S(1)} fusion(f32[1024,1024]{1,0:T(8,128)} %fusion.30.x_ref, bf16[3,1024,1024]{2,1,0:T(8,128)(2,1)} %param.6, bf16[3,2,1024]{2,1,0:T(2,128)(2,1)S(1)} %collective-permute-done, f32[1024]{0:T(1024)S(1)} %copy-done, f32[1024,1024]{1,0:T(8,128)} %shard_map.65, f32[1024]{0:T(1024)S(1)} %bitcast.76, ...), kind=kLoop, calls=%fused_computation.21 | loop fusion | flops 23068672 | bytes 18903040 | tf_op jit(solution)/shard_map/convert_element_type | solution.py:183
  80.1 7.3 %collective-permute-start.2 = (bf16[1024,1024]{1,0:T(8,128)(2,1)S(1)}, bf16[1024,1024]{1,0:T(8,128)(2,1)}, u32[]{:S(2)}, u32[]{:S(2)}) collective-permute-start(bf16[1024,1024]{1,0:T(8,128)(2,1)S(1)} %fusion.9), channel_id=1, source_target_pairs={{0,1},{1,0},{2,3},{3,2},{4,5},{5,4},{6,7},{7,6},{8,9},{9,8},{10,11... | collective-permute-start | bytes 6291464 | tf_op jit(solution)/shard_map/ppermute | solution.py:153
  87.5 1.2 collective-permute-start.1
  88.7 2.7 %collective-permute-done.2 = bf16[1024,1024]{1,0:T(8,128)(2,1)} collective-permute-done((bf16[1024,1024]{1,0:T(8,128)(2,1)S(1)}, bf16[1024,1024]{1,0:T(8,128)(2,1)}, u32[]{:S(2)}, u32[]{:S(2)}) %collective-permute-start.2) | collective-permute-done | bytes 2097184 | tf_op jit(solution)/shard_map/ppermute | solution.py:153
  91.4 4.5 %fusion.26 = f32[1024,1024]{1,0:T(8,128)S(1)} fusion(bf16[1024,1024]{1,0:T(8,128)(2,1)} %collective-permute-done.2, bf16[4096,1024]{1,0:T(8,128)(2,1)} %param.11, s32[]{:T(128)S(6)} %select_n.23), kind=kOutput, calls=%fused_computation.48 | convolution fusion | flops 2147483648 | bytes 8388612 | tf_op jit(solution)/shard_map/dot_general | solution.py:150
  96.0 5.9 %fusion.31 = f32[1024,1024]{1,0:T(8,128)} fusion(f32[1024,1024]{1,0:T(8,128)S(1)} %fusion.26, bf16[1024,1024]{1,0:T(8,128)(2,1)S(1)} %fusion.9, bf16[4096,1024]{1,0:T(8,128)(2,1)} %param.11, s32[]{:T(128)S(6)} %select_n.22), kind=kOutput, calls=%fused_computation.53 | convolution fusion | flops 2148532224 | bytes 12582916 | tf_op jit(solution)/shard_map/dot_general | solution.py:150
  101.9 32.9 %collective-permute-done.1 = bf16[1024,1024]{1,0:T(8,128)(2,1)} collective-permute-done((bf16[1024,1024]{1,0:T(8,128)(2,1)S(1)}, bf16[1024,1024]{1,0:T(8,128)(2,1)}, u32[]{:S(2)}, u32[]{:S(2)}) %collective-permute-start.1) | collective-permute-done | bytes 2097184 | tf_op jit(solution)/shard_map/ppermute | solution.py:152
  134.8 0.8 collective-permute-start.3
  135.6 0.0 copy-start.1
  135.6 4.7 %fusion.24 = f32[1024,1024]{1,0:T(8,128)S(1)} fusion(bf16[1024,1024]{1,0:T(8,128)(2,1)} %collective-permute-done.1, bf16[4096,1024]{1,0:T(8,128)(2,1)} %param.11, s32[]{:T(128)S(6)} %select_n.24), kind=kOutput, calls=%fused_computation.46 | convolution fusion | flops 2147483648 | bytes 8388612 | tf_op jit(solution)/shard_map/dot_general | solution.py:150
  140.3 0.0 collective-permute-done.3
  140.4 0.0 copy-done.1
  140.4 5.3 %add_convert_fusion = bf16[1024,1024]{1,0:T(8,128)(2,1)} fusion(f32[1024,1024]{1,0:T(8,128)S(1)} %copy-done.1, f32[1024,1024]{1,0:T(8,128)S(1)} %fusion.24, bf16[1024,1024]{1,0:T(8,128)(2,1)S(1)} %collective-permute-done.3, bf16[4096,1024]{1,0:T(8,128)(2,1)} %param.11, s32[]{:T(128)S(6)} %select_n.25), kind=kOutput, calls=%fused_computation.26 | convolution fusion | flops 2150629376 | bytes 14680068 | tf_op jit(solution)/shard_map/dot_general | solution.py:150
  (6 shorter events, 0.0 us)
Async XLA Ops:
  0.8 6.5 %collective-permute-start = (bf16[3,2,1024]{2,1,0:T(2,128)(2,1)S(1)}, bf16[3,2,1024]{2,1,0:T(2,128)(2,1)S(1)}, u32[]{:S(2)}, u32[]{:S(2)}) collective-permute-start(bf16[3,2,1024]{2,1,0:T(2,128)(2,1)S(1)} %slice.60), channel_id=1, source_target_pairs={{0,4},{4,8},{8,12},{12,16},{16,20},{20,24},{24,28},{1,5},{5,9},{9,... | collective-permute-start | bytes 36872 | tf_op jit(solution)/shard_map/ppermute | solution.py:15
  57.2 16.6 %copy-start = (f32[1024]{0:T(1024)S(1)}, f32[1024]{0:T(1024)}, u32[]{:S(2)}) copy-start(f32[1024]{0:T(1024)} %param.10) | copy-start | bytes 12292
  80.1 11.3 %collective-permute-start.2 = (bf16[1024,1024]{1,0:T(8,128)(2,1)S(1)}, bf16[1024,1024]{1,0:T(8,128)(2,1)}, u32[]{:S(2)}, u32[]{:S(2)}) collective-permute-start(bf16[1024,1024]{1,0:T(8,128)(2,1)S(1)} %fusion.9), channel_id=1, source_target_pairs={{0,1},{1,0},{2,3},{3,2},{4,5},{5,4},{6,7},{7,6},{8,9},{9,8},{10,11... | collective-permute-start | bytes 6291464 | tf_op jit(solution)/shard_map/ppermute | solution.py:153
  87.5 47.3 %collective-permute-start.1 = (bf16[1024,1024]{1,0:T(8,128)(2,1)S(1)}, bf16[1024,1024]{1,0:T(8,128)(2,1)}, u32[]{:S(2)}, u32[]{:S(2)}) collective-permute-start(bf16[1024,1024]{1,0:T(8,128)(2,1)S(1)} %fusion.9), channel_id=1, source_target_pairs={{0,2},{1,3},{2,0},{3,1},{4,6},{5,7},{6,4},{7,5},{8,10},{9,11},{10,... | collective-permute-start | bytes 6291464 | tf_op jit(solution)/shard_map/ppermute | solution.py:152
  134.8 5.6 %collective-permute-start.3 = (bf16[1024,1024]{1,0:T(8,128)(2,1)}, bf16[1024,1024]{1,0:T(8,128)(2,1)S(1)}, u32[]{:S(2)}, u32[]{:S(2)}) collective-permute-start(bf16[1024,1024]{1,0:T(8,128)(2,1)} %collective-permute-done.1), channel_id=1, source_target_pairs={{0,1},{1,0},{2,3},{3,2},{4,5},{5,4},{6,7},{7,6},{8,9},{9,8},{10,11... | collective-permute-start | bytes 6291464 | tf_op jit(solution)/shard_map/ppermute | solution.py:156
  135.6 4.7 %copy-start.1 = (f32[1024,1024]{1,0:T(8,128)S(1)}, f32[1024,1024]{1,0:T(8,128)}, u32[]{:S(2)}) copy-start(f32[1024,1024]{1,0:T(8,128)} %fusion.31) | copy-start | bytes 12582916

commit v8 on v5

--- a/solution.py
+++ b/solution.py
@@ -169,13 +169,55 @@
     decay = jnp.exp(-pole_rates)
     ends = run_end_state(x, decay)
     start = incoming_state(device_end(ends, pole_rates, span), pole_rates, row_count)
-    long_part = run_recurrence(x, decay, residues, segment_starts(ends, start, pole_rates, span))
-    long_mix = long_part.astype(jnp.bfloat16)
-    gated_mix = featurize(extended, tap_weights, 0, row_count) * (
-        long_mix.astype(jnp.float32) + long_bias[None, :] * mixed_input.astype(jnp.float32)
-    )
-    gated_mix = gated_mix.astype(jnp.bfloat16)
-    return project(gated_mix, out_weight).astype(jnp.bfloat16)
+    starts = segment_starts(ends, start, pole_rates, span)
+    stream0 = featurize(extended, tap_weights, 0, row_count)
+    ch_count = lax.axis_size("ch")
+    pieces = 2 if (ch_count == 4 and width % (2 * LANES) == 0) else 1
+    piece = width // pieces
+    gated = []
+    x_next = x[:, :piece]
+    for index in range(pieces):
+        cols = slice(index * piece, (index + 1) * piece)
+        long_part = run_recurrence(x_next, decay[:, cols], residues[:, cols], starts[:, :, cols])
+        long_mix = long_part.astype(jnp.bfloat16)
+        gated_mix = stream0[:, cols] * (
+            long_mix.astype(jnp.float32) + long_bias[None, cols] * mixed_input[:, cols].astype(jnp.float32)
+        )
+        gated_mix = gated_mix.astype(jnp.bfloat16)
+        if index + 1 < pieces:
+            x_next, gated_mix = lax.optimization_barrier((x[:, cols.stop : cols.stop + piece], gated_mix))
+        gated.append(gated_mix)
+    if pieces == 1:
+        return project(gated[0], out_weight).astype(jnp.bfloat16)
+    return project_pieces(gated, out_weight).astype(jnp.bfloat16)
+
+
+def project_pieces(gated, out_weight):
+    ch_count = lax.axis_size("ch")
+    piece = gated[0].shape[1]
+    width = piece * len(gated)
+    here = lax.axis_index("ch")
+    other_core = [(i, i ^ 1) for i in range(ch_count)]
+    other_chip = [(i, i ^ 2) for i in range(ch_count)]
+
+    def part(value, owner, index):
+        rows = lax.dynamic_slice_in_dim(out_weight, owner * width + index * piece, value.shape[1], 0)
+        return jnp.dot(value, rows, preferred_element_type=jnp.float32)
+
+    far = [lax.ppermute(g, "ch", other_chip) for g in gated]
+    own = jnp.concatenate(gated, 1)
+    own, far[0] = lax.optimization_barrier((own, far[0]))
+    near = lax.ppermute(own, "ch", other_core)
+    near_far = [lax.ppermute(far[0], "ch", other_core)]
+    total = part(own, here, 0) + part(far[0], here ^ 2, 0)
+    total = total + part(near, here ^ 1, 0)
+    for index in range(1, len(far)):
+        far[index], total = lax.optimization_barrier((far[index], total))
+        near_far.append(lax.ppermute(far[index], "ch", other_core))
+        total = total + part(far[index], here ^ 2, index)
+    for index in range(len(far)):
+        total = total + part(near_far[index], here ^ 3, index)
+    return total
 
 
 def solution(mesh):

time: 131 us -> 133 us (1.015)
  waiting for transfers between devices: 35.6 us -> 18.5 us
  other arithmetic: 21.4 us -> 28.7 us
  local copies, waits for them, and re-layouts: 2.18 us -> 7.32 us
  matrix products: 20.5 us -> 22.9 us
  Pallas kernels: 26 us -> 27.9 us
  starting transfers between devices: 24.5 us -> 26.1 us
    ppermute x3 -> x5, waiting for transfers between devices: 35.6 us -> 18.4 us  [the longest x2 18.4 us: project_pieces(): far = [lax.ppermute(g, 'ch', other_chip) for g in gated]]
    convert_element_type x1, other arithmetic: 8.69 us -> 14.9 us  [shards(): x = mixed_input.astype(jnp.float32)]
    slice x0 -> x5, local copies, waits for them, and re-layouts: none -> 5.15 us  [the longest x1 1.51 us: shards(): x_next = x[:, :piece]]
    dot_general x4 -> x6, matrix products: 20.5 us -> 22.9 us  [part(): return jnp.dot(value, rows, preferred_element_type=jnp.float32)]
    pallas_call x1 -> x2, Pallas kernels: 16.5 us -> 18.5 us  [run_recurrence(): pl.pallas_call(recurrence_kernel, grid=(width // LANES,), in_specs=[pl.Bl...]
    concatenate x0 -> x1, other arithmetic: none -> 1.53 us  [project_pieces(): own = jnp.concatenate(gated, 1)]
    convert_element_type x1 -> x2, other arithmetic: 6.43 us -> 7.46 us  [shards(): gated_mix = gated_mix.astype(jnp.bfloat16)]
    ppermute x3 -> x5, starting transfers between devices: 5.21 us -> 6.21 us  [the longest x1 2.72 us: project_pieces(): near = lax.ppermute(own, 'ch', other_core)]
  transfers between devices with their start and end apart: 11 -> 13, of which waited for: 2 -> 2; matrix products, arithmetic and copies ran while one was open for 15% -> 24% of each run, Pallas kernels for 0% -> 7%
where the time goes in v8:
time: 133 us; the launch traced here: 132 us
  other arithmetic  28.7 us (22%)
  Pallas kernels  27.9 us (21%)
  starting transfers between devices  26.1 us (20%)
  matrix products  22.9 us (17%)
  waiting for transfers between devices  18.5 us (14%)
  local copies, waits for them, and re-layouts  7.32 us (6%)
    dot_general x6, matrix products, part(): return jnp.dot(value, rows, preferred_element_type=jnp.float32)  22.9 us
    ppermute x8, starting transfers between devices, shifted(): lax.ppermute(value, axis, [(source, source + steps) for source in range(i...  19.8 us
    pallas_call x2, Pallas kernels, run_recurrence(): pl.pallas_call(recurrence_kernel, grid=(width // LANES,), in_specs=[pl.Bl...  18.5 us
    ppermute x2, waiting for transfers between devices, project_pieces(): far = [lax.ppermute(g, 'ch', other_chip) for g in gated]  18.4 us
    convert_element_type x1, other arithmetic, shards(): x = mixed_input.astype(jnp.float32)  14.9 us
    pallas_call x1, Pallas kernels, run_end_state(): pl.pallas_call(end_state_kernel, grid=(width // LANES,), in_specs=[pl.Blo...  9.44 us
    convert_element_type x2, other arithmetic, shards(): gated_mix = gated_mix.astype(jnp.bfloat16)  7.46 us
    ppermute x1, starting transfers between devices, project_pieces(): near = lax.ppermute(own, 'ch', other_core)  2.72 us
  transfers between devices with their start and end apart: 13, of which 2 were waited for; matrix products, arithmetic and copies ran while one was open for 24% of the time, Pallas kernels for 7%

profile of v8, /device:TPU:1, one launch (start us, length us, event | category | flops | bytes accessed | tf_op | source)
XLA Modules:
  0.0 131.7 jit_solution(11836505303630469761)
XLA Ops:
  0.8 4.0 %collective-permute-start = (bf16[3,2,1024]{2,1,0:T(2,128)(2,1)S(1)}, bf16[3,2,1024]{2,1,0:T(2,128)(2,1)S(1)}, u32[]{:S(2)}, u32[]{:S(2)}) collective-permute-start(bf16[3,2,1024]{2,1,0:T(2,128)(2,1)S(1)} %slice.102), channel_id=1, source_target_pairs={{0,4},{4,8},{8,12},{12,16},{16,20},{20,24},{24,28},{1,5},{5,9},{9,... | collective-permute-start | bytes 36872 | tf_op jit(solution)/shard_map/ppermute | solution.py:15
  4.8 0.9 slice_convert_fusion.5
  7.3 1.4 %fusion.46 = (f32[16,512]{1,0:T(8,128)}, f32[16,512]{1,0:T(8,128)}) fusion(f32[16,1024]{1,0:T(8,128)} %param.9), kind=kLoop, calls=%fused_computation.85 | loop fusion | bytes 131072 | tf_op jit(solution)/shard_map/slice | solution.py:181
  9.5 14.9 %fusion.43 = (f32[1024,1024]{1,0:T(8,128)}, bf16[1024,1024]{1,0:T(8,128)(2,1)S(1)}, f32[1024,1024]{1,0:T(8,128)}) fusion(bf16[3,1024,1024]{2,1,0:T(8,128)(2,1)} %param.6, bf16[3,2,1024]{2,1,0:T(2,128)(2,1)S(1)} %collective-permute-done, f32[1024]{0:T(1024)S(1)} %bitcast.73, f32[1024]{0:T(1024)S(1)} %bitcast.74, f32[1024]{0:T(1024)S(1)} %bitcast.67, ...), kind=kLoop, calls=%fused_computation.83 | loop fusion | flops 53477376 | bytes 23117824 | tf_op jit(solution)/shard_map/convert_element_type | solution.py:166
  24.3 9.4 %shard_map.64 = f32[16,8,1024]{2,1,0:T(8,128)} custom-call(f32[1024,1024]{1,0:T(8,128)} %get-tuple-element.17.x_ref, f32[16,1024]{1,0:T(8,128)} %copy-done.1), custom_call_target="tpu_custom_call" | custom-call | tf_op jit(solution)/shard_map/pallas_call | solution.py:62
  33.8 1.3 %multiply_reduce_fusion.1 = f32[16,1024]{1,0:T(8,128)S(1)} fusion(f32[16,8,1024]{2,1,0:T(8,128)} %shard_map.64, f32[8]{0:T(128)S(1)} %subtract_multiply_fusion, f32[16,1024]{1,0:T(8,128)S(1)} %get-tuple-element.28), kind=kLoop, calls=%fused_computation.60 | loop fusion | flops 376832 | bytes 655392 | tf_op jit(solution)/shard_map/reduce_sum | solution.py:110
  35.1 3.2 %collective-permute-start.1 = (f32[16,1024]{1,0:T(8,128)S(1)}, f32[16,1024]{1,0:T(8,128)S(1)}, u32[]{:S(2)}, u32[]{:S(2)}) collective-permute-start(f32[16,1024]{1,0:T(8,128)S(1)} %multiply_reduce_fusion.1), channel_id=1, source_target_pairs={{0,4},{4,8},{8,12},{12,16},{16,20},{20,24},{24,28},{1,5},{5,9},{9,... | collective-permute-start | bytes 196616 | tf_op jit(solution)/shard_map/ppermute | solution.py:15
  38.3 3.2 %collective-permute-start.2 = (f32[16,1024]{1,0:T(8,128)S(1)}, f32[16,1024]{1,0:T(8,128)S(1)}, u32[]{:S(2)}, u32[]{:S(2)}) collective-permute-start(f32[16,1024]{1,0:T(8,128)S(1)} %multiply_reduce_fusion.1), channel_id=1, source_target_pairs={{0,8},{4,12},{8,16},{12,20},{16,24},{20,28},{1,9},{5,13},{9,17},{1... | collective-permute-start | bytes 196616 | tf_op jit(solution)/shard_map/ppermute | solution.py:15
  41.5 4.2 %collective-permute-start.3 = (f32[16,1024]{1,0:T(8,128)S(1)}, f32[16,1024]{1,0:T(8,128)S(1)}, u32[]{:S(2)}, u32[]{:S(2)}) collective-permute-start(f32[16,1024]{1,0:T(8,128)S(1)} %multiply_reduce_fusion.1), channel_id=1, source_target_pairs={{0,12},{4,16},{8,20},{12,24},{16,28},{1,13},{5,17},{9,21},{13,25},... | collective-permute-start | bytes 196616 | tf_op jit(solution)/shard_map/ppermute | solution.py:15
  45.7 1.3 collective-permute-start.4
  47.0 1.3 collective-permute-start.5
  48.3 1.4 %copy.15 = f32[16,1024,8]{1,0,2:T(8,128)S(1)} copy(f32[16,1024,8]{1,2,0:T(8,128)} %bitcast.65) | data formatting | bytes 1048576
  49.6 1.3 collective-permute-start.6
  51.0 1.5 %collective-permute-start.7 = (f32[16,1024]{1,0:T(8,128)S(1)}, f32[16,1024]{1,0:T(8,128)S(1)}, u32[]{:S(2)}, u32[]{:S(2)}) collective-permute-start(f32[16,1024]{1,0:T(8,128)S(1)} %multiply_reduce_fusion.1), channel_id=1, source_target_pairs={{0,28},{1,29},{2,30},{3,31}} | collective-permute-start | bytes 196616 | tf_op jit(solution)/shard_map/ppermute | solution.py:15
  52.4 1.2 multiply_reduce_fusion
  53.7 1.5 %slice.145.x_ref = f32[1024,512]{1,0:T(8,128)} slice(bf16[1024,1024]{1,0:T(8,128)(2,1)S(1)} %get-tuple-element.18), slice={[0:1024], [0:512]} | slice | bytes 4194304 | tf_op jit(solution)/shard_map/slice | solution.py:178
  56.5 9.2 %shard_map.65 = f32[1024,512]{1,0:T(8,128)} custom-call(f32[1024,512]{1,0:T(8,128)} %slice.145.x_ref, f32[16,512]{1,0:T(8,128)} %get-tuple-element.27.decay_ref, f32[16,512]{1,0:T(8,128)} %get-tuple-element.25.residue_ref, f32[16,8,512]{2,1,0:T(8,128)} %get-tuple-element.23.start_ref), custom_call_target="tpu_custom_call" | custom-call | tf_op jit(solution)/shard_map/pallas_call | solution.py:78
  65.8 4.6 %fusion.18 = (bf16[1024,512]{1,0:T(8,128)(2,1)}, f32[1024,512]{1,0:T(8,128)}) fusion(f32[1024,1024]{1,0:T(8,128)} %get-tuple-element.19, bf16[1024,1024]{1,0:T(8,128)(2,1)S(1)} %get-tuple-element.18, f32[512]{0:T(512)S(1)} %get-tuple-element.39, f32[1024,512]{1,0:T(8,128)} %shard_map.65), kind=kLoop, calls=%fused_computation.41 | loop fusion | flops 3670016 | bytes 10487808 | tf_op jit(solution)/shard_map/convert_element_type | solution.py:186
  70.4 1.2 collective-permute-start.9
  71.6 9.2 %shard_map.66 = f32[1024,512]{1,0:T(8,128)} custom-call(f32[1024,512]{1,0:T(8,128)} %get-tuple-element.11.x_ref, f32[16,512]{1,0:T(8,128)} %get-tuple-element.26.decay_ref, f32[16,512]{1,0:T(8,128)} %get-tuple-element.24.residue_ref, f32[16,8,512]{2,1,0:T(8,128)} %get-tuple-element.22.start_ref), custom_call_target="tpu_custom_call" | custom-call | tf_op jit(solution)/shard_map/pallas_call | solution.py:78
  80.9 2.8 %fusion.20 = bf16[1024,512]{1,0:T(8,128)(2,1)S(1)} fusion(f32[1024,1024]{1,0:T(8,128)} %get-tuple-element.19, bf16[1024,1024]{1,0:T(8,128)(2,1)S(1)} %get-tuple-element.18, f32[512]{0:T(512)S(1)} %get-tuple-element.40, f32[1024,512]{1,0:T(8,128)} %shard_map.66), kind=kLoop, calls=%fused_computation.45 | loop fusion | flops 3670016 | bytes 6293504 | tf_op jit(solution)/shard_map/convert_element_type | solution.py:186
  83.7 1.5 %pad_maximum_fusion.1 = bf16[1024,1024]{1,0:T(8,128)(2,1)S(1)} fusion(bf16[1024,512]{1,0:T(8,128)(2,1)S(1)} %fusion.20, bf16[1024,512]{1,0:T(8,128)(2,1)} %get-tuple-element.12), kind=kLoop, calls=%fused_computation.46 | loop fusion | flops 4194304 | bytes 4194304 | tf_op jit(solution)/shard_map/concatenate | solution.py:208
  85.3 8.3 %collective-permute-done.9 = bf16[1024,512]{1,0:T(8,128)(2,1)} collective-permute-done((bf16[1024,512]{1,0:T(8,128)(2,1)}, bf16[1024,512]{1,0:T(8,128)(2,1)}, u32[]{:S(2)}, u32[]{:S(2)}) %collective-permute-start.9) | collective-permute-done | bytes 1048608 | tf_op jit(solution)/shard_map/ppermute | solution.py:207
  93.6 2.7 %collective-permute-start.10 = (bf16[1024,1024]{1,0:T(8,128)(2,1)S(1)}, bf16[1024,1024]{1,0:T(8,128)(2,1)}, u32[]{:S(2)}, u32[]{:S(2)}) collective-permute-start(bf16[1024,1024]{1,0:T(8,128)(2,1)S(1)} %pad_maximum_fusion.1), channel_id=1, source_target_pairs={{0,1},{1,0},{2,3},{3,2},{4,5},{5,4},{6,7},{7,6},{8,9},{9,8},{10,11... | collective-permute-start | bytes 6291464 | tf_op jit(solution)/shard_map/ppermute | solution.py:210
  96.3 1.2 collective-permute-start.8
  97.8 3.9 %fusion.23 = f32[1024,1024]{1,0:T(8,128)S(1)} fusion(bf16[1024,1024]{1,0:T(8,128)(2,1)S(1)} %pad_maximum_fusion.1, bf16[4096,1024]{1,0:T(8,128)(2,1)} %param.11, s32[]{:T(128)S(6)} %select_n.23), kind=kOutput, calls=%fused_computation.49 | convolution fusion | flops 2147483648 | bytes 8388612 | tf_op jit(solution)/shard_map/dot_general | solution.py:205
  101.7 2.8 %fusion.35 = f32[1024,1024]{1,0:T(8,128)S(1)} fusion(bf16[1024,512]{1,0:T(8,128)(2,1)} %collective-permute-done.9, bf16[4096,1024]{1,0:T(8,128)(2,1)} %param.11, s32[]{:T(128)S(6)} %select_n.24), kind=kOutput, calls=%fused_computation.57 | convolution fusion | flops 1073741824 | bytes 6291460 | tf_op jit(solution)/shard_map/dot_general | solution.py:205
  104.5 6.6 %add_add_fusion = f32[1024,1024]{1,0:T(8,128)} fusion(f32[1024,1024]{1,0:T(8,128)S(1)} %fusion.23, f32[1024,1024]{1,0:T(8,128)S(1)} %fusion.35, bf16[1024,1024]{1,0:T(8,128)(2,1)} %collective-permute-done.10, bf16[4096,1024]{1,0:T(8,128)(2,1)} %param.11, s32[]{:T(128)S(6)} %select_n.25), kind=kOutput, calls=%fused_computation.24 | convolution fusion | flops 2149580800 | bytes 16777220 | tf_op jit(solution)/shard_map/dot_general | solution.py:205
  111.1 10.1 %collective-permute-done.8 = bf16[1024,512]{1,0:T(8,128)(2,1)} collective-permute-done((bf16[1024,512]{1,0:T(8,128)(2,1)S(1)}, bf16[1024,512]{1,0:T(8,128)(2,1)}, u32[]{:S(2)}, u32[]{:S(2)}) %collective-permute-start.8) | collective-permute-done | bytes 1048608 | tf_op jit(solution)/shard_map/ppermute | solution.py:207
  122.0 2.8 %fusion.31 = f32[1024,1024]{1,0:T(8,128)S(1)} fusion(bf16[1024,512]{1,0:T(8,128)(2,1)} %collective-permute-done.11, bf16[4096,1024]{1,0:T(8,128)(2,1)} %param.11, s32[]{:T(128)S(6)} %select_n.27), kind=kOutput, calls=%fused_computation.53 | convolution fusion | flops 1073741824 | bytes 6291460 | tf_op jit(solution)/shard_map/dot_general | solution.py:205
  124.8 2.9 %fusion.33 = f32[1024,1024]{1,0:T(8,128)S(1)} fusion(bf16[1024,512]{1,0:T(8,128)(2,1)} %collective-permute-done.8, bf16[4096,1024]{1,0:T(8,128)(2,1)} %param.11, s32[]{:T(128)S(6)} %select_n.26), kind=kOutput, calls=%fused_computation.55 | convolution fusion | flops 1073741824 | bytes 6291460 | tf_op jit(solution)/shard_map/dot_general | solution.py:205
  127.8 3.9 %add_convert_fusion = bf16[1024,1024]{1,0:T(8,128)(2,1)} fusion(f32[1024,1024]{1,0:T(8,128)S(1)} %fusion.31, f32[1024,1024]{1,0:T(8,128)S(1)} %copy-done, f32[1024,1024]{1,0:T(8,128)S(1)} %fusion.33, bf16[1024,512]{1,0:T(8,128)(2,1)S(1)} %collective-permute-done.12, bf16[4096,1024]{1,0:T(8,128)(2,1)} %param.11, s32[]{:T(128)S(6)} %select_n.28), kind=kOutput, calls=%fused_computation.23 | convolution fusion | flops 1077936128 | bytes 16777220 | tf_op jit(solution)/shard_map/dot_general | solution.py:205
  (31 shorter events, 5.6 us)
Async XLA Ops:
  0.8 8.6 %collective-permute-start = (bf16[3,2,1024]{2,1,0:T(2,128)(2,1)S(1)}, bf16[3,2,1024]{2,1,0:T(2,128)(2,1)S(1)}, u32[]{:S(2)}, u32[]{:S(2)}) collective-permute-start(bf16[3,2,1024]{2,1,0:T(2,128)(2,1)S(1)} %slice.102), channel_id=1, source_target_pairs={{0,4},{4,8},{8,12},{12,16},{16,20},{20,24},{24,28},{1,5},{5,9},{9,... | collective-permute-start | bytes 36872 | tf_op jit(solution)/shard_map/ppermute | solution.py:15
  6.6 17.8 %copy-start.1 = (f32[16,1024]{1,0:T(8,128)}, f32[16,1024]{1,0:T(8,128)S(1)}, u32[]{:S(2)}) copy-start(f32[16,1024]{1,0:T(8,128)S(1)} %get-tuple-element.29.decay_ref) | copy-start | bytes 196612
  33.8 21.4 %copy-start.2 = (f32[16,1024]{1,0:T(8,128)S(1)}, f32[16,1024]{1,0:T(8,128)}, u32[]{:S(2)}) copy-start(f32[16,1024]{1,0:T(8,128)} %param.8) | copy-start | bytes 196612
  35.1 14.5 %collective-permute-start.1 = (f32[16,1024]{1,0:T(8,128)S(1)}, f32[16,1024]{1,0:T(8,128)S(1)}, u32[]{:S(2)}, u32[]{:S(2)}) collective-permute-start(f32[16,1024]{1,0:T(8,128)S(1)} %multiply_reduce_fusion.1), channel_id=1, source_target_pairs={{0,4},{4,8},{8,12},{12,16},{16,20},{20,24},{24,28},{1,5},{5,9},{9,... | collective-permute-start | bytes 196616 | tf_op jit(solution)/shard_map/ppermute | solution.py:15
  38.3 12.7 %collective-permute-start.2 = (f32[16,1024]{1,0:T(8,128)S(1)}, f32[16,1024]{1,0:T(8,128)S(1)}, u32[]{:S(2)}, u32[]{:S(2)}) collective-permute-start(f32[16,1024]{1,0:T(8,128)S(1)} %multiply_reduce_fusion.1), channel_id=1, source_target_pairs={{0,8},{4,12},{8,16},{12,20},{16,24},{20,28},{1,9},{5,13},{9,17},{1... | collective-permute-start | bytes 196616 | tf_op jit(solution)/shard_map/ppermute | solution.py:15
  41.5 13.7 %collective-permute-start.3 = (f32[16,1024]{1,0:T(8,128)S(1)}, f32[16,1024]{1,0:T(8,128)S(1)}, u32[]{:S(2)}, u32[]{:S(2)}) collective-permute-start(f32[16,1024]{1,0:T(8,128)S(1)} %multiply_reduce_fusion.1), channel_id=1, source_target_pairs={{0,12},{4,16},{8,20},{12,24},{16,28},{1,13},{5,17},{9,21},{13,25},... | collective-permute-start | bytes 196616 | tf_op jit(solution)/shard_map/ppermute | solution.py:15
  45.7 9.5 %collective-permute-start.4 = (f32[16,1024]{1,0:T(8,128)S(1)}, f32[16,1024]{1,0:T(8,128)S(1)}, u32[]{:S(2)}, u32[]{:S(2)}) collective-permute-start(f32[16,1024]{1,0:T(8,128)S(1)} %multiply_reduce_fusion.1), channel_id=1, source_target_pairs={{0,16},{4,20},{8,24},{12,28},{1,17},{5,21},{9,25},{13,29},{2,18},{... | collective-permute-start | bytes 196616 | tf_op jit(solution)/shard_map/ppermute | solution.py:15
  47.0 8.2 %collective-permute-start.5 = (f32[16,1024]{1,0:T(8,128)S(1)}, f32[16,1024]{1,0:T(8,128)S(1)}, u32[]{:S(2)}, u32[]{:S(2)}) collective-permute-start(f32[16,1024]{1,0:T(8,128)S(1)} %multiply_reduce_fusion.1), channel_id=1, source_target_pairs={{0,20},{4,24},{8,28},{1,21},{5,25},{9,29},{2,22},{6,26},{10,30},{3... | collective-permute-start | bytes 196616 | tf_op jit(solution)/shard_map/ppermute | solution.py:15
  49.6 5.5 %collective-permute-start.6 = (f32[16,1024]{1,0:T(8,128)S(1)}, f32[16,1024]{1,0:T(8,128)S(1)}, u32[]{:S(2)}, u32[]{:S(2)}) collective-permute-start(f32[16,1024]{1,0:T(8,128)S(1)} %multiply_reduce_fusion.1), channel_id=1, source_target_pairs={{0,24},{4,28},{1,25},{5,29},{2,26},{6,30},{3,27},{7,31}} | collective-permute-start | bytes 196616 | tf_op jit(solution)/shard_map/ppermute | solution.py:15
  51.0 4.2 %collective-permute-start.7 = (f32[16,1024]{1,0:T(8,128)S(1)}, f32[16,1024]{1,0:T(8,128)S(1)}, u32[]{:S(2)}, u32[]{:S(2)}) collective-permute-start(f32[16,1024]{1,0:T(8,128)S(1)} %multiply_reduce_fusion.1), channel_id=1, source_target_pairs={{0,28},{1,29},{2,30},{3,31}} | collective-permute-start | bytes 196616 | tf_op jit(solution)/shard_map/ppermute | solution.py:15
  70.4 23.2 %collective-permute-start.9 = (bf16[1024,512]{1,0:T(8,128)(2,1)}, bf16[1024,512]{1,0:T(8,128)(2,1)}, u32[]{:S(2)}, u32[]{:S(2)}) collective-permute-start(bf16[1024,512]{1,0:T(8,128)(2,1)} %get-tuple-element.12), channel_id=1, source_target_pairs={{0,2},{1,3},{2,0},{3,1},{4,6},{5,7},{6,4},{7,5},{8,10},{9,11},{10,... | collective-permute-start | bytes 3145736 | tf_op jit(solution)/shard_map/ppermute | solution.py:207
  93.6 10.9 %collective-permute-start.10 = (bf16[1024,1024]{1,0:T(8,128)(2,1)S(1)}, bf16[1024,1024]{1,0:T(8,128)(2,1)}, u32[]{:S(2)}, u32[]{:S(2)}) collective-permute-start(bf16[1024,1024]{1,0:T(8,128)(2,1)S(1)} %pad_maximum_fusion.1), channel_id=1, source_target_pairs={{0,1},{1,0},{2,3},{3,2},{4,5},{5,4},{6,7},{7,6},{8,9},{9,8},{10,11... | collective-permute-start | bytes 6291464 | tf_op jit(solution)/shard_map/ppermute | solution.py:210
  96.3 24.9 %collective-permute-start.8 = (bf16[1024,512]{1,0:T(8,128)(2,1)S(1)}, bf16[1024,512]{1,0:T(8,128)(2,1)}, u32[]{:S(2)}, u32[]{:S(2)}) collective-permute-start(bf16[1024,512]{1,0:T(8,128)(2,1)S(1)} %fusion.20), channel_id=1, source_target_pairs={{0,2},{1,3},{2,0},{3,1},{4,6},{5,7},{6,4},{7,5},{8,10},{9,11},{10,... | collective-permute-start | bytes 3145736 | tf_op jit(solution)/shard_map/ppermute | solution.py:207
  97.5 24.5 %collective-permute-start.11 = (bf16[1024,512]{1,0:T(8,128)(2,1)}, bf16[1024,512]{1,0:T(8,128)(2,1)}, u32[]{:S(2)}, u32[]{:S(2)}) collective-permute-start(bf16[1024,512]{1,0:T(8,128)(2,1)} %collective-permute-done.9), channel_id=1, source_target_pairs={{0,1},{1,0},{2,3},{3,2},{4,5},{5,4},{6,7},{7,6},{8,9},{9,8},{10,11... | collective-permute-start | bytes 3145736 | tf_op jit(solution)/shard_map/ppermute | solution.py:211
  121.2 6.5 %collective-permute-start.12 = (bf16[1024,512]{1,0:T(8,128)(2,1)}, bf16[1024,512]{1,0:T(8,128)(2,1)S(1)}, u32[]{:S(2)}, u32[]{:S(2)}) collective-permute-start(bf16[1024,512]{1,0:T(8,128)(2,1)} %collective-permute-done.8), channel_id=1, source_target_pairs={{0,1},{1,0},{2,3},{3,2},{4,5},{5,4},{6,7},{7,6},{8,9},{9,8},{10,11... | collective-permute-start | bytes 3145736 | tf_op jit(solution)/shard_map/ppermute | solution.py:216
  124.8 3.0 %copy-start = (f32[1024,1024]{1,0:T(8,128)S(1)}, f32[1024,1024]{1,0:T(8,128)}, u32[]{:S(2)}) copy-start(f32[1024,1024]{1,0:T(8,128)} %add_add_fusion) | copy-start | bytes 12582916

commit v9 on v8

--- a/solution.py
+++ b/solution.py
@@ -71,21 +71,21 @@
     )(x, decay)
 
 
-def run_recurrence(x, decay, residue, start):
-    length, width = x.shape
+def run_recurrence(x, decay, residue, start, first_group, group_count):
+    length = x.shape[0]
     pole_count = decay.shape[0]
-    pole_spec = pl.BlockSpec((pole_count, LANES), lambda g: (0, g))
+    pole_spec = pl.BlockSpec((pole_count, LANES), lambda g: (0, g + first_group))
     return pl.pallas_call(
         recurrence_kernel,
-        grid=(width // LANES,),
+        grid=(group_count,),
         in_specs=[
-            pl.BlockSpec((length, LANES), lambda g: (0, g)),
+            pl.BlockSpec((length, LANES), lambda g: (0, g + first_group)),
             pole_spec,
             pole_spec,
-            pl.BlockSpec((pole_count, SEGMENTS, LANES), lambda g: (0, 0, g)),
+            pl.BlockSpec((pole_count, SEGMENTS, LANES), lambda g: (0, 0, g + first_group)),
         ],
         out_specs=pl.BlockSpec((length, LANES), lambda g: (0, g)),
-        out_shape=jax.ShapeDtypeStruct(x.shape, jnp.float32),
+        out_shape=jax.ShapeDtypeStruct((length, group_count * LANES), jnp.float32),
     )(x, decay, residue, start)
 
 
@@ -170,22 +170,22 @@
     ends = run_end_state(x, decay)
     start = incoming_state(device_end(ends, pole_rates, span), pole_rates, row_count)
     starts = segment_starts(ends, start, pole_rates, span)
-    stream0 = featurize(extended, tap_weights, 0, row_count)
     ch_count = lax.axis_size("ch")
     pieces = 2 if (ch_count == 4 and width % (2 * LANES) == 0) else 1
     piece = width // pieces
     gated = []
-    x_next = x[:, :piece]
+    x_next = x
     for index in range(pieces):
         cols = slice(index * piece, (index + 1) * piece)
-        long_part = run_recurrence(x_next, decay[:, cols], residues[:, cols], starts[:, :, cols])
+        long_part = run_recurrence(x_next, decay, residues, starts, index * piece // LANES, piece // LANES)
         long_mix = long_part.astype(jnp.bfloat16)
-        gated_mix = stream0[:, cols] * (
+        stream0 = featurize(extended[:, :, cols], tap_weights[:, :, cols], 0, row_count)
+        gated_mix = stream0 * (
             long_mix.astype(jnp.float32) + long_bias[None, cols] * mixed_input[:, cols].astype(jnp.float32)
         )
         gated_mix = gated_mix.astype(jnp.bfloat16)
         if index + 1 < pieces:
-            x_next, gated_mix = lax.optimization_barrier((x[:, cols.stop : cols.stop + piece], gated_mix))
+            x_next, gated_mix = lax.optimization_barrier((x, gated_mix))
         gated.append(gated_mix)
     if pieces == 1:
         return project(gated[0], out_weight).astype(jnp.bfloat16)

time: 133 us -> 124 us (0.932)
  local copies, waits for them, and re-layouts: 7.32 us -> 2.94 us
  other arithmetic: 28.7 us -> 25.8 us
    convert_element_type x1, other arithmetic: 14.9 us -> 8.73 us  [shards(): x = mixed_input.astype(jnp.float32)]
    slice x4 -> x0, local copies, waits for them, and re-layouts: 4.38 us -> none  [the longest x1 1.51 us: shards(): x_next = x[:, :piece]]
  transfers between devices with their start and end apart: 13 -> 13, of which waited for: 2 -> 2; matrix products, arithmetic and copies ran while one was open for 24% -> 25% of each run, Pallas kernels for 7% -> 7%
where the time goes in v9:
time: 124 us; the launch traced here: 123 us
  Pallas kernels  27.8 us (22%)
  starting transfers between devices  26.5 us (21%)
  other arithmetic  25.8 us (21%)
  matrix products  22.9 us (18%)
  waiting for transfers between devices  17.2 us (14%)
  local copies, waits for them, and re-layouts  2.94 us (2%)
    dot_general x6, matrix products, part(): return jnp.dot(value, rows, preferred_element_type=jnp.float32)  22.9 us
    ppermute x8, starting transfers between devices, shifted(): lax.ppermute(value, axis, [(source, source + steps) for source in range(i...  19.8 us
    pallas_call x2, Pallas kernels, run_recurrence(): pl.pallas_call(recurrence_kernel, grid=(group_count,), in_specs=[pl.Block...  18.3 us
    ppermute x2, waiting for transfers between devices, project_pieces(): far = [lax.ppermute(g, 'ch', other_chip) for g in gated]  17.2 us
    pallas_call x1, Pallas kernels, run_end_state(): pl.pallas_call(end_state_kernel, grid=(width // LANES,), in_specs=[pl.Blo...  9.47 us
    convert_element_type x1, other arithmetic, shards(): x = mixed_input.astype(jnp.float32)  8.73 us
    convert_element_type x2, other arithmetic, shards(): gated_mix = gated_mix.astype(jnp.bfloat16)  8.5 us
    ppermute x1, starting transfers between devices, project_pieces(): near = lax.ppermute(own, 'ch', other_core)  3.13 us
  transfers between devices with their start and end apart: 13, of which 2 were waited for; matrix products, arithmetic and copies ran while one was open for 25% of the time, Pallas kernels for 7%

profile of v9, /device:TPU:1, one launch (start us, length us, event | category | flops | bytes accessed | tf_op | source)
XLA Modules:
  0.0 123.3 jit_solution(15196586295922256318)
XLA Ops:
  0.0 0.8 slice.108
  0.8 4.0 %collective-permute-start = (bf16[3,2,1024]{2,1,0:T(2,128)(2,1)S(1)}, bf16[3,2,1024]{2,1,0:T(2,128)(2,1)S(1)}, u32[]{:S(2)}, u32[]{:S(2)}) collective-permute-start(bf16[3,2,1024]{2,1,0:T(2,128)(2,1)S(1)} %slice.108), channel_id=1, source_target_pairs={{0,4},{4,8},{8,12},{12,16},{16,20},{20,24},{24,28},{1,5},{5,9},{9,... | collective-permute-start | bytes 36872 | tf_op jit(solution)/shard_map/ppermute | solution.py:15
  6.4 1.5 %fusion.53 = (f32[16,1024]{1,0:T(8,128)S(1)}, f32[16,1024]{1,0:T(8,128)}) fusion(f32[16,1024]{1,0:T(8,128)} %param.8), kind=kLoop, calls=%fused_computation.98 | loop fusion | flops 16384 | bytes 196608 | tf_op jit(solution)/shard_map/neg | solution.py:169
  8.8 8.7 %fusion.51 = (f32[1024,1024]{1,0:T(8,128)}, bf16[1024,1024]{1,0:T(8,128)(2,1)S(1)}) fusion(f32[1024]{0:T(1024)S(1)} %bitcast.83, f32[1024]{0:T(1024)S(1)} %bitcast.84, bf16[3,1024,1024]{2,1,0:T(8,128)(2,1)} %param.6, f32[1024]{0:T(1024)S(1)} %bitcast.85, f32[1024]{0:T(1024)S(1)} %bitcast.86, bf16[3,2,1024]{2,1,0:T(2,128)(2,1)S(1)} %collective-permute-done, ...), kind=kLoop, calls=%fused_computation.97 | loop fusion | flops 36700160 | bytes 16814080 | tf_op jit(solution)/shard_map/convert_element_type | solution.py:166
  17.5 9.5 %shard_map.64 = f32[16,8,1024]{2,1,0:T(8,128)} custom-call(f32[1024,1024]{1,0:T(8,128)} %get-tuple-element.11.x_ref, f32[16,1024]{1,0:T(8,128)} %get-tuple-element.20.decay_ref), custom_call_target="tpu_custom_call" | custom-call | tf_op jit(solution)/shard_map/pallas_call | solution.py:62
  27.0 1.3 %multiply_reduce_fusion.1 = f32[16,1024]{1,0:T(8,128)S(1)} fusion(f32[16,8,1024]{2,1,0:T(8,128)} %shard_map.64, f32[8]{0:T(128)S(1)} %subtract_multiply_fusion, f32[16,1024]{1,0:T(8,128)S(1)} %get-tuple-element.19), kind=kLoop, calls=%fused_computation.71 | loop fusion | flops 376832 | bytes 655392 | tf_op jit(solution)/shard_map/reduce_sum | solution.py:110
  28.3 3.2 %collective-permute-start.1 = (f32[16,1024]{1,0:T(8,128)S(1)}, f32[16,1024]{1,0:T(8,128)S(1)}, u32[]{:S(2)}, u32[]{:S(2)}) collective-permute-start(f32[16,1024]{1,0:T(8,128)S(1)} %multiply_reduce_fusion.1), channel_id=1, source_target_pairs={{0,4},{4,8},{8,12},{12,16},{16,20},{20,24},{24,28},{1,5},{5,9},{9,... | collective-permute-start | bytes 196616 | tf_op jit(solution)/shard_map/ppermute | solution.py:15
  31.4 3.2 %collective-permute-start.2 = (f32[16,1024]{1,0:T(8,128)S(1)}, f32[16,1024]{1,0:T(8,128)S(1)}, u32[]{:S(2)}, u32[]{:S(2)}) collective-permute-start(f32[16,1024]{1,0:T(8,128)S(1)} %multiply_reduce_fusion.1), channel_id=1, source_target_pairs={{0,8},{4,12},{8,16},{12,20},{16,24},{20,28},{1,9},{5,13},{9,17},{1... | collective-permute-start | bytes 196616 | tf_op jit(solution)/shard_map/ppermute | solution.py:15
  34.7 4.2 %collective-permute-start.3 = (f32[16,1024]{1,0:T(8,128)S(1)}, f32[16,1024]{1,0:T(8,128)S(1)}, u32[]{:S(2)}, u32[]{:S(2)}) collective-permute-start(f32[16,1024]{1,0:T(8,128)S(1)} %multiply_reduce_fusion.1), channel_id=1, source_target_pairs={{0,12},{4,16},{8,20},{12,24},{16,28},{1,13},{5,17},{9,21},{13,25},... | collective-permute-start | bytes 196616 | tf_op jit(solution)/shard_map/ppermute | solution.py:15
  38.8 1.3 %collective-permute-start.4 = (f32[16,1024]{1,0:T(8,128)S(1)}, f32[16,1024]{1,0:T(8,128)S(1)}, u32[]{:S(2)}, u32[]{:S(2)}) collective-permute-start(f32[16,1024]{1,0:T(8,128)S(1)} %multiply_reduce_fusion.1), channel_id=1, source_target_pairs={{0,16},{4,20},{8,24},{12,28},{1,17},{5,21},{9,25},{13,29},{2,18},{... | collective-permute-start | bytes 196616 | tf_op jit(solution)/shard_map/ppermute | solution.py:15
  40.1 1.3 %collective-permute-start.5 = (f32[16,1024]{1,0:T(8,128)S(1)}, f32[16,1024]{1,0:T(8,128)S(1)}, u32[]{:S(2)}, u32[]{:S(2)}) collective-permute-start(f32[16,1024]{1,0:T(8,128)S(1)} %multiply_reduce_fusion.1), channel_id=1, source_target_pairs={{0,20},{4,24},{8,28},{1,21},{5,25},{9,29},{2,22},{6,26},{10,30},{3... | collective-permute-start | bytes 196616 | tf_op jit(solution)/shard_map/ppermute | solution.py:15
  41.4 1.4 %copy.15 = f32[16,1024,8]{1,0,2:T(8,128)S(1)} copy(f32[16,1024,8]{1,2,0:T(8,128)} %bitcast.81) | data formatting | bytes 1048576
  42.8 1.3 %collective-permute-start.6 = (f32[16,1024]{1,0:T(8,128)S(1)}, f32[16,1024]{1,0:T(8,128)S(1)}, u32[]{:S(2)}, u32[]{:S(2)}) collective-permute-start(f32[16,1024]{1,0:T(8,128)S(1)} %multiply_reduce_fusion.1), channel_id=1, source_target_pairs={{0,24},{4,28},{1,25},{5,29},{2,26},{6,30},{3,27},{7,31}} | collective-permute-start | bytes 196616 | tf_op jit(solution)/shard_map/ppermute | solution.py:15
  44.1 1.5 %collective-permute-start.7 = (f32[16,1024]{1,0:T(8,128)S(1)}, f32[16,1024]{1,0:T(8,128)S(1)}, u32[]{:S(2)}, u32[]{:S(2)}) collective-permute-start(f32[16,1024]{1,0:T(8,128)S(1)} %multiply_reduce_fusion.1), channel_id=1, source_target_pairs={{0,28},{1,29},{2,30},{3,31}} | collective-permute-start | bytes 196616 | tf_op jit(solution)/shard_map/ppermute | solution.py:15
  45.6 1.2 multiply_reduce_fusion
  47.0 1.2 bitcast_add_fusion.start_ref
  48.2 9.2 %shard_map.65 = f32[1024,512]{1,0:T(8,128)} custom-call(f32[1024,1024]{1,0:T(8,128)} %get-tuple-element.11.x_ref, f32[16,1024]{1,0:T(8,128)} %get-tuple-element.20.decay_ref, f32[16,1024]{1,0:T(8,128)} %residue_ref.3, f32[16,8,1024]{2,1,0:T(8,128)} %bitcast_add_fusion.start_ref), custom_call_target="tpu_custom_call" | custom-call | tf_op jit(solution)/shard_map/pallas_call | solution.py:78
  57.4 4.7 %fusion.16 = bf16[1024,512]{1,0:T(8,128)(2,1)} fusion(bf16[3,1024,1024]{2,1,0:T(8,128)(2,1)} %param.6, bf16[3,2,1024]{2,1,0:T(2,128)(2,1)S(1)} %collective-permute-done, bf16[1024,1024]{1,0:T(8,128)(2,1)S(1)} %get-tuple-element.18, f32[512]{0:T(512)S(1)} %get-tuple-element.33, f32[1024,512]{1,0:T(8,128)} %shard_map.65, f32[512]{0:T(512)S(1)} %bitcast.92, ...), kind=kLoop, calls=%fused_computation.39 | loop fusion | flops 12058624 | bytes 11554816 | tf_op jit(solution)/shard_map/convert_element_type | solution.py:186
  62.1 1.2 collective-permute-start.9
  63.3 9.2 %shard_map.66 = f32[1024,512]{1,0:T(8,128)} custom-call(f32[1024,1024]{1,0:T(8,128)} %get-tuple-element.11.x_ref, f32[16,1024]{1,0:T(8,128)} %get-tuple-element.20.decay_ref, f32[16,1024]{1,0:T(8,128)} %residue_ref.3, f32[16,8,1024]{2,1,0:T(8,128)} %bitcast_add_fusion.start_ref), custom_call_target="tpu_custom_call" | custom-call | tf_op jit(solution)/shard_map/pallas_call | solution.py:78
  72.5 3.8 %fusion.20 = bf16[1024,512]{1,0:T(8,128)(2,1)S(1)} fusion(bf16[3,1024,1024]{2,1,0:T(8,128)(2,1)} %param.6, bf16[3,2,1024]{2,1,0:T(2,128)(2,1)S(1)} %collective-permute-done, bf16[1024,1024]{1,0:T(8,128)(2,1)S(1)} %get-tuple-element.18, f32[512]{0:T(512)S(1)} %get-tuple-element.34, f32[1024,512]{1,0:T(8,128)} %shard_map.66, f32[512]{0:T(512)S(1)} %bitcast.89, ...), kind=kLoop, calls=%fused_computation.46 | loop fusion | flops 12058624 | bytes 11554816 | tf_op jit(solution)/shard_map/convert_element_type | solution.py:186
  76.2 1.5 %pad_maximum_fusion = bf16[1024,1024]{1,0:T(8,128)(2,1)S(1)} fusion(bf16[1024,512]{1,0:T(8,128)(2,1)S(1)} %fusion.20, bf16[1024,512]{1,0:T(8,128)(2,1)} %fusion.16), kind=kLoop, calls=%fused_computation.35 | loop fusion | flops 4194304 | bytes 4194304 | tf_op jit(solution)/shard_map/concatenate | solution.py:208
  77.8 7.1 %collective-permute-done.9 = bf16[1024,512]{1,0:T(8,128)(2,1)} collective-permute-done((bf16[1024,512]{1,0:T(8,128)(2,1)}, bf16[1024,512]{1,0:T(8,128)(2,1)}, u32[]{:S(2)}, u32[]{:S(2)}) %collective-permute-start.9) | collective-permute-done | bytes 1048608 | tf_op jit(solution)/shard_map/ppermute | solution.py:207
  84.9 3.1 %collective-permute-start.10 = (bf16[1024,1024]{1,0:T(8,128)(2,1)S(1)}, bf16[1024,1024]{1,0:T(8,128)(2,1)}, u32[]{:S(2)}, u32[]{:S(2)}) collective-permute-start(bf16[1024,1024]{1,0:T(8,128)(2,1)S(1)} %pad_maximum_fusion), channel_id=1, source_target_pairs={{0,1},{1,0},{2,3},{3,2},{4,5},{5,4},{6,7},{7,6},{8,9},{9,8},{10,11... | collective-permute-start | bytes 6291464 | tf_op jit(solution)/shard_map/ppermute | solution.py:210
  88.0 1.2 collective-permute-start.8
  89.5 3.9 %fusion.24 = f32[1024,1024]{1,0:T(8,128)S(1)} fusion(bf16[1024,1024]{1,0:T(8,128)(2,1)S(1)} %pad_maximum_fusion, bf16[4096,1024]{1,0:T(8,128)(2,1)} %param.11, s32[]{:T(128)S(6)} %select_n.23), kind=kOutput, calls=%fused_computation.52 | convolution fusion | flops 2147483648 | bytes 8388612 | tf_op jit(solution)/shard_map/dot_general | solution.py:205
  93.4 2.8 %fusion.43 = f32[1024,1024]{1,0:T(8,128)S(1)} fusion(bf16[1024,512]{1,0:T(8,128)(2,1)} %collective-permute-done.9, bf16[4096,1024]{1,0:T(8,128)(2,1)} %param.11, s32[]{:T(128)S(6)} %select_n.24), kind=kOutput, calls=%fused_computation.68 | convolution fusion | flops 1073741824 | bytes 6291460 | tf_op jit(solution)/shard_map/dot_general | solution.py:205
  96.2 6.6 %add_add_fusion = f32[1024,1024]{1,0:T(8,128)} fusion(f32[1024,1024]{1,0:T(8,128)S(1)} %fusion.24, f32[1024,1024]{1,0:T(8,128)S(1)} %fusion.43, bf16[1024,1024]{1,0:T(8,128)(2,1)} %collective-permute-done.10, bf16[4096,1024]{1,0:T(8,128)(2,1)} %param.11, s32[]{:T(128)S(6)} %select_n.25), kind=kOutput, calls=%fused_computation.21 | convolution fusion | flops 2149580800 | bytes 16777220 | tf_op jit(solution)/shard_map/dot_general | solution.py:205
  102.8 10.1 %collective-permute-done.8 = bf16[1024,512]{1,0:T(8,128)(2,1)} collective-permute-done((bf16[1024,512]{1,0:T(8,128)(2,1)S(1)}, bf16[1024,512]{1,0:T(8,128)(2,1)}, u32[]{:S(2)}, u32[]{:S(2)}) %collective-permute-start.8) | collective-permute-done | bytes 1048608 | tf_op jit(solution)/shard_map/ppermute | solution.py:207
  113.7 2.8 %fusion.39 = f32[1024,1024]{1,0:T(8,128)S(1)} fusion(bf16[1024,512]{1,0:T(8,128)(2,1)} %collective-permute-done.11, bf16[4096,1024]{1,0:T(8,128)(2,1)} %param.11, s32[]{:T(128)S(6)} %select_n.27), kind=kOutput, calls=%fused_computation.64 | convolution fusion | flops 1073741824 | bytes 6291460 | tf_op jit(solution)/shard_map/dot_general | solution.py:205
  116.5 2.9 %fusion.41 = f32[1024,1024]{1,0:T(8,128)S(1)} fusion(bf16[1024,512]{1,0:T(8,128)(2,1)} %collective-permute-done.8, bf16[4096,1024]{1,0:T(8,128)(2,1)} %param.11, s32[]{:T(128)S(6)} %select_n.26), kind=kOutput, calls=%fused_computation.66 | convolution fusion | flops 1073741824 | bytes 6291460 | tf_op jit(solution)/shard_map/dot_general | solution.py:205
  119.4 3.9 %add_convert_fusion = bf16[1024,1024]{1,0:T(8,128)(2,1)} fusion(f32[1024,1024]{1,0:T(8,128)S(1)} %fusion.39, f32[1024,1024]{1,0:T(8,128)S(1)} %copy-done, f32[1024,1024]{1,0:T(8,128)S(1)} %fusion.41, bf16[1024,512]{1,0:T(8,128)(2,1)S(1)} %collective-permute-done.12, bf16[4096,1024]{1,0:T(8,128)(2,1)} %param.11, s32[]{:T(128)S(6)} %select_n.28), kind=kOutput, calls=%fused_computation.20 | convolution fusion | flops 1077936128 | bytes 16777220 | tf_op jit(solution)/shard_map/dot_general | solution.py:205
  (26 shorter events, 3.6 us)
Async XLA Ops:
  0.8 7.9 %collective-permute-start = (bf16[3,2,1024]{2,1,0:T(2,128)(2,1)S(1)}, bf16[3,2,1024]{2,1,0:T(2,128)(2,1)S(1)}, u32[]{:S(2)}, u32[]{:S(2)}) collective-permute-start(bf16[3,2,1024]{2,1,0:T(2,128)(2,1)S(1)} %slice.108), channel_id=1, source_target_pairs={{0,4},{4,8},{8,12},{12,16},{16,20},{20,24},{24,28},{1,5},{5,9},{9,... | collective-permute-start | bytes 36872 | tf_op jit(solution)/shard_map/ppermute | solution.py:15
  17.5 29.4 %copy-start.1 = (f32[16,1024]{1,0:T(8,128)S(1)}, f32[16,1024]{1,0:T(8,128)}, u32[]{:S(2)}) copy-start(f32[16,1024]{1,0:T(8,128)} %param.8) | copy-start | bytes 196612
  28.3 14.5 %collective-permute-start.1 = (f32[16,1024]{1,0:T(8,128)S(1)}, f32[16,1024]{1,0:T(8,128)S(1)}, u32[]{:S(2)}, u32[]{:S(2)}) collective-permute-start(f32[16,1024]{1,0:T(8,128)S(1)} %multiply_reduce_fusion.1), channel_id=1, source_target_pairs={{0,4},{4,8},{8,12},{12,16},{16,20},{20,24},{24,28},{1,5},{5,9},{9,... | collective-permute-start | bytes 196616 | tf_op jit(solution)/shard_map/ppermute | solution.py:15
  31.4 12.7 %collective-permute-start.2 = (f32[16,1024]{1,0:T(8,128)S(1)}, f32[16,1024]{1,0:T(8,128)S(1)}, u32[]{:S(2)}, u32[]{:S(2)}) collective-permute-start(f32[16,1024]{1,0:T(8,128)S(1)} %multiply_reduce_fusion.1), channel_id=1, source_target_pairs={{0,8},{4,12},{8,16},{12,20},{16,24},{20,28},{1,9},{5,13},{9,17},{1... | collective-permute-start | bytes 196616 | tf_op jit(solution)/shard_map/ppermute | solution.py:15
  34.7 12.2 %collective-permute-start.3 = (f32[16,1024]{1,0:T(8,128)S(1)}, f32[16,1024]{1,0:T(8,128)S(1)}, u32[]{:S(2)}, u32[]{:S(2)}) collective-permute-start(f32[16,1024]{1,0:T(8,128)S(1)} %multiply_reduce_fusion.1), channel_id=1, source_target_pairs={{0,12},{4,16},{8,20},{12,24},{16,28},{1,13},{5,17},{9,21},{13,25},... | collective-permute-start | bytes 196616 | tf_op jit(solution)/shard_map/ppermute | solution.py:15
  38.8 8.0 %collective-permute-start.4 = (f32[16,1024]{1,0:T(8,128)S(1)}, f32[16,1024]{1,0:T(8,128)S(1)}, u32[]{:S(2)}, u32[]{:S(2)}) collective-permute-start(f32[16,1024]{1,0:T(8,128)S(1)} %multiply_reduce_fusion.1), channel_id=1, source_target_pairs={{0,16},{4,20},{8,24},{12,28},{1,17},{5,21},{9,25},{13,29},{2,18},{... | collective-permute-start | bytes 196616 | tf_op jit(solution)/shard_map/ppermute | solution.py:15
  40.1 6.7 %collective-permute-start.5 = (f32[16,1024]{1,0:T(8,128)S(1)}, f32[16,1024]{1,0:T(8,128)S(1)}, u32[]{:S(2)}, u32[]{:S(2)}) collective-permute-start(f32[16,1024]{1,0:T(8,128)S(1)} %multiply_reduce_fusion.1), channel_id=1, source_target_pairs={{0,20},{4,24},{8,28},{1,21},{5,25},{9,29},{2,22},{6,26},{10,30},{3... | collective-permute-start | bytes 196616 | tf_op jit(solution)/shard_map/ppermute | solution.py:15
  42.8 4.0 %collective-permute-start.6 = (f32[16,1024]{1,0:T(8,128)S(1)}, f32[16,1024]{1,0:T(8,128)S(1)}, u32[]{:S(2)}, u32[]{:S(2)}) collective-permute-start(f32[16,1024]{1,0:T(8,128)S(1)} %multiply_reduce_fusion.1), channel_id=1, source_target_pairs={{0,24},{4,28},{1,25},{5,29},{2,26},{6,30},{3,27},{7,31}} | collective-permute-start | bytes 196616 | tf_op jit(solution)/shard_map/ppermute | solution.py:15
  44.1 2.7 %collective-permute-start.7 = (f32[16,1024]{1,0:T(8,128)S(1)}, f32[16,1024]{1,0:T(8,128)S(1)}, u32[]{:S(2)}, u32[]{:S(2)}) collective-permute-start(f32[16,1024]{1,0:T(8,128)S(1)} %multiply_reduce_fusion.1), channel_id=1, source_target_pairs={{0,28},{1,29},{2,30},{3,31}} | collective-permute-start | bytes 196616 | tf_op jit(solution)/shard_map/ppermute | solution.py:15
  62.1 22.8 %collective-permute-start.9 = (bf16[1024,512]{1,0:T(8,128)(2,1)}, bf16[1024,512]{1,0:T(8,128)(2,1)}, u32[]{:S(2)}, u32[]{:S(2)}) collective-permute-start(bf16[1024,512]{1,0:T(8,128)(2,1)} %fusion.16), channel_id=1, source_target_pairs={{0,2},{1,3},{2,0},{3,1},{4,6},{5,7},{6,4},{7,5},{8,10},{9,11},{10,... | collective-permute-start | bytes 3145736 | tf_op jit(solution)/shard_map/ppermute | solution.py:207
  84.9 11.4 %collective-permute-start.10 = (bf16[1024,1024]{1,0:T(8,128)(2,1)S(1)}, bf16[1024,1024]{1,0:T(8,128)(2,1)}, u32[]{:S(2)}, u32[]{:S(2)}) collective-permute-start(bf16[1024,1024]{1,0:T(8,128)(2,1)S(1)} %pad_maximum_fusion), channel_id=1, source_target_pairs={{0,1},{1,0},{2,3},{3,2},{4,5},{5,4},{6,7},{7,6},{8,9},{9,8},{10,11... | collective-permute-start | bytes 6291464 | tf_op jit(solution)/shard_map/ppermute | solution.py:210
  88.0 24.9 %collective-permute-start.8 = (bf16[1024,512]{1,0:T(8,128)(2,1)S(1)}, bf16[1024,512]{1,0:T(8,128)(2,1)}, u32[]{:S(2)}, u32[]{:S(2)}) collective-permute-start(bf16[1024,512]{1,0:T(8,128)(2,1)S(1)} %fusion.20), channel_id=1, source_target_pairs={{0,2},{1,3},{2,0},{3,1},{4,6},{5,7},{6,4},{7,5},{8,10},{9,11},{10,... | collective-permute-start | bytes 3145736 | tf_op jit(solution)/shard_map/ppermute | solution.py:207
  89.2 24.5 %collective-permute-start.11 = (bf16[1024,512]{1,0:T(8,128)(2,1)}, bf16[1024,512]{1,0:T(8,128)(2,1)}, u32[]{:S(2)}, u32[]{:S(2)}) collective-permute-start(bf16[1024,512]{1,0:T(8,128)(2,1)} %collective-permute-done.9), channel_id=1, source_target_pairs={{0,1},{1,0},{2,3},{3,2},{4,5},{5,4},{6,7},{7,6},{8,9},{9,8},{10,11... | collective-permute-start | bytes 3145736 | tf_op jit(solution)/shard_map/ppermute | solution.py:211
  112.9 6.5 %collective-permute-start.12 = (bf16[1024,512]{1,0:T(8,128)(2,1)}, bf16[1024,512]{1,0:T(8,128)(2,1)S(1)}, u32[]{:S(2)}, u32[]{:S(2)}) collective-permute-start(bf16[1024,512]{1,0:T(8,128)(2,1)} %collective-permute-done.8), channel_id=1, source_target_pairs={{0,1},{1,0},{2,3},{3,2},{4,5},{5,4},{6,7},{7,6},{8,9},{9,8},{10,11... | collective-permute-start | bytes 3145736 | tf_op jit(solution)/shard_map/ppermute | solution.py:216
  116.5 3.0 %copy-start = (f32[1024,1024]{1,0:T(8,128)S(1)}, f32[1024,1024]{1,0:T(8,128)}, u32[]{:S(2)}) copy-start(f32[1024,1024]{1,0:T(8,128)} %add_add_fusion) | copy-start | bytes 12582916

commit v10 on v9

--- a/solution.py
+++ b/solution.py
@@ -171,13 +171,16 @@
     start = incoming_state(device_end(ends, pole_rates, span), pole_rates, row_count)
     starts = segment_starts(ends, start, pole_rates, span)
     ch_count = lax.axis_size("ch")
-    pieces = 2 if (ch_count == 4 and width % (2 * LANES) == 0) else 1
-    piece = width // pieces
+    groups = width // LANES
+    lead_groups = (3 * groups) // 8 if ch_count == 4 else 0
+    bounds = [0, lead_groups * LANES, width] if lead_groups > 0 else [0, width]
+    pieces = len(bounds) - 1
     gated = []
     x_next = x
     for index in range(pieces):
-        cols = slice(index * piece, (index + 1) * piece)
-        long_part = run_recurrence(x_next, decay, residues, starts, index * piece // LANES, piece // LANES)
+        cols = slice(bounds[index], bounds[index + 1])
+        group_count = (cols.stop - cols.start) // LANES
+        long_part = run_recurrence(x_next, decay, residues, starts, cols.start // LANES, group_count)
         long_mix = long_part.astype(jnp.bfloat16)
         stream0 = featurize(extended[:, :, cols], tap_weights[:, :, cols], 0, row_count)
         gated_mix = stream0 * (
@@ -194,14 +197,16 @@
 
 def project_pieces(gated, out_weight):
     ch_count = lax.axis_size("ch")
-    piece = gated[0].shape[1]
-    width = piece * len(gated)
+    offsets = [0]
+    for value in gated:
+        offsets.append(offsets[-1] + value.shape[1])
+    width = offsets[-1]
     here = lax.axis_index("ch")
     other_core = [(i, i ^ 1) for i in range(ch_count)]
     other_chip = [(i, i ^ 2) for i in range(ch_count)]
 
     def part(value, owner, index):
-        rows = lax.dynamic_slice_in_dim(out_weight, owner * width + index * piece, value.shape[1], 0)
+        rows = lax.dynamic_slice_in_dim(out_weight, owner * width + offsets[index], value.shape[1], 0)
         return jnp.dot(value, rows, preferred_element_type=jnp.float32)
 
     far = [lax.ppermute(g, "ch", other_chip) for g in gated]
@@ -209,13 +214,16 @@
     own, far[0] = lax.optimization_barrier((own, far[0]))
     near = lax.ppermute(own, "ch", other_core)
     near_far = [lax.ppermute(far[0], "ch", other_core)]
-    total = part(own, here, 0) + part(far[0], here ^ 2, 0)
-    total = total + part(near, here ^ 1, 0)
+    rows_own = lax.dynamic_slice_in_dim(out_weight, here * width, width, 0)
+    rows_near = lax.dynamic_slice_in_dim(out_weight, (here ^ 1) * width, width, 0)
+    total = jnp.dot(own, rows_own, preferred_element_type=jnp.float32) + part(far[0], here ^ 2, 0)
+    total = total + jnp.dot(near, rows_near, preferred_element_type=jnp.float32)
+    total = total + part(near_far[0], here ^ 3, 0)
     for index in range(1, len(far)):
         far[index], total = lax.optimization_barrier((far[index], total))
         near_far.append(lax.ppermute(far[index], "ch", other_core))
         total = total + part(far[index], here ^ 2, index)
-    for index in range(len(far)):
+    for index in range(1, len(far)):
         total = total + part(near_far[index], here ^ 3, index)
     return total
 

time: 124 us -> 120 us (0.968)
  waiting for transfers between devices: 17.2 us -> 14.3 us
  starting transfers between devices: 26.5 us -> 24.8 us
    dot_general x0 -> x2, matrix products: none -> 8.47 us  [the longest x1 4.55 us: project_pieces(): total = total + jnp.dot(near, rows_near, preferred_element_type=jnp.float32)]
    dot_general x6 -> x4, matrix products: 22.9 us -> 15.1 us  [part(): return jnp.dot(value, rows, preferred_element_type=jnp.float32)]
    ppermute x2, waiting for transfers between devices: 17.2 us -> 14.3 us  [project_pieces(): far = [lax.ppermute(g, 'ch', other_chip) for g in gated]]
  transfers between devices with their start and end apart: 13 -> 13, of which waited for: 2 -> 1; matrix products, arithmetic and copies ran while one was open for 25% -> 26% of each run, Pallas kernels for 7% -> 9%
where the time goes in v10:
time: 120 us; the launch traced here: 119 us
  Pallas kernels  27.9 us (23%)
  other arithmetic  25.7 us (21%)
  starting transfers between devices  24.8 us (21%)
  matrix products  23.6 us (20%)
  waiting for transfers between devices  14.3 us (12%)
  local copies, waits for them, and re-layouts  2.18 us (2%)
    ppermute x8, starting transfers between devices, shifted(): lax.ppermute(value, axis, [(source, source + steps) for source in range(i...  19.2 us
    pallas_call x2, Pallas kernels, run_recurrence(): pl.pallas_call(recurrence_kernel, grid=(group_count,), in_specs=[pl.Block...  18.4 us
    dot_general x4, matrix products, part(): return jnp.dot(value, rows, preferred_element_type=jnp.float32)  15.1 us
    ppermute x2, waiting for transfers between devices, project_pieces(): far = [lax.ppermute(g, 'ch', other_chip) for g in gated]  14.3 us
    pallas_call x1, Pallas kernels, run_end_state(): pl.pallas_call(end_state_kernel, grid=(width // LANES,), in_specs=[pl.Blo...  9.44 us
    convert_element_type x1, other arithmetic, shards(): x = mixed_input.astype(jnp.float32)  8.74 us
    convert_element_type x2, other arithmetic, shards(): gated_mix = gated_mix.astype(jnp.bfloat16)  7.81 us
    dot_general x1, matrix products, project_pieces(): total = total + jnp.dot(near, rows_near, preferred_element_type=jnp.float32)  4.55 us
  transfers between devices with their start and end apart: 13, of which 1 were waited for; matrix products, arithmetic and copies ran while one was open for 26% of the time, Pallas kernels for 9%

profile of v10, /device:TPU:1, one launch (start us, length us, event | category | flops | bytes accessed | tf_op | source)
XLA Modules:
  0.0 118.8 jit_solution(17471942647143863290)
XLA Ops:
  0.0 0.8 slice.108
  0.8 4.0 %collective-permute-start = (bf16[3,2,1024]{2,1,0:T(2,128)(2,1)S(1)}, bf16[3,2,1024]{2,1,0:T(2,128)(2,1)S(1)}, u32[]{:S(2)}, u32[]{:S(2)}) collective-permute-start(bf16[3,2,1024]{2,1,0:T(2,128)(2,1)S(1)} %slice.108), channel_id=1, source_target_pairs={{0,4},{4,8},{8,12},{12,16},{16,20},{20,24},{24,28},{1,5},{5,9},{9,... | collective-permute-start | bytes 36872 | tf_op jit(solution)/shard_map/ppermute | solution.py:15
  5.6 0.8 slice_convert_fusion.5
  6.5 1.5 %fusion.52 = (f32[16,1024]{1,0:T(8,128)S(1)}, f32[16,1024]{1,0:T(8,128)}) fusion(f32[16,1024]{1,0:T(8,128)} %param.8), kind=kLoop, calls=%fused_computation.97 | loop fusion | flops 16384 | bytes 196608 | tf_op jit(solution)/shard_map/neg | solution.py:169
  7.9 8.7 %fusion.50 = (f32[1024,1024]{1,0:T(8,128)}, bf16[1024,1024]{1,0:T(8,128)(2,1)S(1)}) fusion(f32[1024]{0:T(1024)S(1)} %bitcast.77, f32[1024]{0:T(1024)S(1)} %bitcast.78, bf16[3,1024,1024]{2,1,0:T(8,128)(2,1)} %param.6, f32[1024]{0:T(1024)S(1)} %bitcast.79, f32[1024]{0:T(1024)S(1)} %bitcast.75, bf16[3,2,1024]{2,1,0:T(2,128)(2,1)S(1)} %collective-permute-done, ...), kind=kLoop, calls=%fused_computation.96 | loop fusion | flops 36700160 | bytes 16814080 | tf_op jit(solution)/shard_map/convert_element_type | solution.py:166
  16.7 9.4 %shard_map.64 = f32[16,8,1024]{2,1,0:T(8,128)} custom-call(f32[1024,1024]{1,0:T(8,128)} %get-tuple-element.11.x_ref, f32[16,1024]{1,0:T(8,128)} %get-tuple-element.26.decay_ref), custom_call_target="tpu_custom_call" | custom-call | tf_op jit(solution)/shard_map/pallas_call | solution.py:62
  26.1 1.3 %multiply_reduce_fusion.1 = f32[16,1024]{1,0:T(8,128)S(1)} fusion(f32[16,8,1024]{2,1,0:T(8,128)} %shard_map.64, f32[8]{0:T(128)S(1)} %subtract_multiply_fusion, f32[16,1024]{1,0:T(8,128)S(1)} %get-tuple-element.25), kind=kLoop, calls=%fused_computation.70 | loop fusion | flops 376832 | bytes 655392 | tf_op jit(solution)/shard_map/reduce_sum | solution.py:110
  27.5 4.3 %collective-permute-start.7 = (f32[16,1024]{1,0:T(8,128)S(1)}, f32[16,1024]{1,0:T(8,128)S(1)}, u32[]{:S(2)}, u32[]{:S(2)}) collective-permute-start(f32[16,1024]{1,0:T(8,128)S(1)} %multiply_reduce_fusion.1), channel_id=1, source_target_pairs={{0,28},{1,29},{2,30},{3,31}} | collective-permute-start | bytes 196616 | tf_op jit(solution)/shard_map/ppermute | solution.py:15
  31.8 1.6 %collective-permute-start.6 = (f32[16,1024]{1,0:T(8,128)S(1)}, f32[16,1024]{1,0:T(8,128)S(1)}, u32[]{:S(2)}, u32[]{:S(2)}) collective-permute-start(f32[16,1024]{1,0:T(8,128)S(1)} %multiply_reduce_fusion.1), channel_id=1, source_target_pairs={{0,24},{4,28},{1,25},{5,29},{2,26},{6,30},{3,27},{7,31}} | collective-permute-start | bytes 196616 | tf_op jit(solution)/shard_map/ppermute | solution.py:15
  33.4 1.3 %collective-permute-start.5 = (f32[16,1024]{1,0:T(8,128)S(1)}, f32[16,1024]{1,0:T(8,128)S(1)}, u32[]{:S(2)}, u32[]{:S(2)}) collective-permute-start(f32[16,1024]{1,0:T(8,128)S(1)} %multiply_reduce_fusion.1), channel_id=1, source_target_pairs={{0,20},{4,24},{8,28},{1,21},{5,25},{9,29},{2,22},{6,26},{10,30},{3... | collective-permute-start | bytes 196616 | tf_op jit(solution)/shard_map/ppermute | solution.py:15
  34.7 1.3 %collective-permute-start.4 = (f32[16,1024]{1,0:T(8,128)S(1)}, f32[16,1024]{1,0:T(8,128)S(1)}, u32[]{:S(2)}, u32[]{:S(2)}) collective-permute-start(f32[16,1024]{1,0:T(8,128)S(1)} %multiply_reduce_fusion.1), channel_id=1, source_target_pairs={{0,16},{4,20},{8,24},{12,28},{1,17},{5,21},{9,25},{13,29},{2,18},{... | collective-permute-start | bytes 196616 | tf_op jit(solution)/shard_map/ppermute | solution.py:15
  36.0 1.9 %collective-permute-start.3 = (f32[16,1024]{1,0:T(8,128)S(1)}, f32[16,1024]{1,0:T(8,128)S(1)}, u32[]{:S(2)}, u32[]{:S(2)}) collective-permute-start(f32[16,1024]{1,0:T(8,128)S(1)} %multiply_reduce_fusion.1), channel_id=1, source_target_pairs={{0,12},{4,16},{8,20},{12,24},{16,28},{1,13},{5,17},{9,21},{13,25},... | collective-permute-start | bytes 196616 | tf_op jit(solution)/shard_map/ppermute | solution.py:15
  37.9 1.4 %copy.15 = f32[16,1024,8]{1,0,2:T(8,128)S(1)} copy(f32[16,1024,8]{1,2,0:T(8,128)} %bitcast.73) | data formatting | bytes 1048576
  39.3 1.6 %collective-permute-start.2 = (f32[16,1024]{1,0:T(8,128)S(1)}, f32[16,1024]{1,0:T(8,128)S(1)}, u32[]{:S(2)}, u32[]{:S(2)}) collective-permute-start(f32[16,1024]{1,0:T(8,128)S(1)} %multiply_reduce_fusion.1), channel_id=1, source_target_pairs={{0,8},{4,12},{8,16},{12,20},{16,24},{20,28},{1,9},{5,13},{9,17},{1... | collective-permute-start | bytes 196616 | tf_op jit(solution)/shard_map/ppermute | solution.py:15
  40.9 3.3 %collective-permute-start.1 = (f32[16,1024]{1,0:T(8,128)S(1)}, f32[16,1024]{1,0:T(8,128)S(1)}, u32[]{:S(2)}, u32[]{:S(2)}) collective-permute-start(f32[16,1024]{1,0:T(8,128)S(1)} %multiply_reduce_fusion.1), channel_id=1, source_target_pairs={{0,4},{4,8},{8,12},{12,16},{16,20},{20,24},{24,28},{1,5},{5,9},{9,... | collective-permute-start | bytes 196616 | tf_op jit(solution)/shard_map/ppermute | solution.py:15
  44.1 1.2 %multiply_reduce_fusion = f32[16,1024,8]{1,0,2:T(8,128)S(1)} fusion(f32[16,1024,8]{1,0,2:T(8,128)S(1)} %copy.15, f32[8,8]{1,0:T(8,128)S(1)} %maximum_multiply_fusion, f32[16,1024]{1,0:T(8,128)S(1)} %get-tuple-element.25, pred[8,8]{1,0:T(8,128)(4,1)S(1)} %iota_compare_fusion), kind=kLoop, calls=%fused_computation.19 | loop fusion | flops 4063232 | bytes 1114432
  45.5 1.2 %bitcast_add_fusion.start_ref = f32[16,8,1024]{2,1,0:T(8,128)} fusion(f32[16,1024,8]{1,0,2:T(8,128)S(1)} %multiply_reduce_fusion, f32[16,1024]{1,0:T(8,128)S(1)} %multiply_add_fusion, f32[8]{0:T(128)S(1)} %convert_multiply_fusion.12, f32[16,1024]{1,0:T(8,128)S(1)} %get-tuple-element.25), kind=kLoop, calls=%fused_computation.69 | loop fusion | flops 393216 | bytes 1179680 | tf_op jit(solution)/shard_map/add | solution.py:103
  46.7 7.4 %shard_map.65 = f32[1024,384]{1,0:T(8,128)} custom-call(f32[1024,1024]{1,0:T(8,128)} %get-tuple-element.11.x_ref, f32[16,1024]{1,0:T(8,128)} %get-tuple-element.26.decay_ref, f32[16,1024]{1,0:T(8,128)} %residue_ref.3, f32[16,8,1024]{2,1,0:T(8,128)} %bitcast_add_fusion.start_ref), custom_call_target="tpu_custom_call" | custom-call | tf_op jit(solution)/shard_map/pallas_call | solution.py:78
  54.1 4.0 %fusion.24 = bf16[1024,384]{1,0:T(8,128)(2,1)} fusion(bf16[1024,1024]{1,0:T(8,128)(2,1)S(1)} %get-tuple-element.24, bf16[3,1024,1024]{2,1,0:T(8,128)(2,1)} %param.6, bf16[3,2,1024]{2,1,0:T(2,128)(2,1)S(1)} %collective-permute-done, f32[384]{0:T(512)S(1)} %slice-done, f32[1024,384]{1,0:T(8,128)} %shard_map.65, f32[384]{0:T(512)S(1)} %get-tuple-element.21, ...), kind=kLoop, calls=%fused_computation.50 | loop fusion | flops 9043968 | bytes 10242048 | tf_op jit(solution)/shard_map/convert_element_type | solution.py:189
  58.1 1.2 %collective-permute-start.9 = (bf16[1024,384]{1,0:T(8,128)(2,1)}, bf16[1024,384]{1,0:T(8,128)(2,1)}, u32[]{:S(2)}, u32[]{:S(2)}) collective-permute-start(bf16[1024,384]{1,0:T(8,128)(2,1)} %fusion.24), channel_id=1, source_target_pairs={{0,2},{1,3},{2,0},{3,1},{4,6},{5,7},{6,4},{7,5},{8,10},{9,11},{10,... | collective-permute-start | bytes 2359304 | tf_op jit(solution)/shard_map/ppermute | solution.py:212
  60.1 11.1 %shard_map.66 = f32[1024,640]{1,0:T(8,128)} custom-call(f32[1024,1024]{1,0:T(8,128)} %get-tuple-element.11.x_ref, f32[16,1024]{1,0:T(8,128)} %get-tuple-element.26.decay_ref, f32[16,1024]{1,0:T(8,128)} %residue_ref.3, f32[16,8,1024]{2,1,0:T(8,128)} %bitcast_add_fusion.start_ref), custom_call_target="tpu_custom_call" | custom-call | tf_op jit(solution)/shard_map/pallas_call | solution.py:78
  71.2 3.8 %fusion.8 = bf16[1024,640]{1,0:T(8,128)(2,1)S(1)} fusion(bf16[3,1024,1024]{2,1,0:T(8,128)(2,1)} %param.6, bf16[3,2,1024]{2,1,0:T(2,128)(2,1)S(1)} %collective-permute-done, bf16[1024,1024]{1,0:T(8,128)(2,1)S(1)} %get-tuple-element.24, f32[640]{0:T(1024)S(1)} %slice.132, f32[1024,640]{1,0:T(8,128)} %shard_map.66, f32[640]{0:T(1024)S(1)} %get-tuple-element.18, ...), kind=kLoop, calls=%fused_computation.25 | loop fusion | flops 15073280 | bytes 12867584 | tf_op jit(solution)/shard_map/convert_element_type | solution.py:189
  75.0 1.4 %pad_maximum_fusion = bf16[1024,1024]{1,0:T(8,128)(2,1)S(1)} fusion(bf16[1024,640]{1,0:T(8,128)(2,1)S(1)} %fusion.8, bf16[1024,384]{1,0:T(8,128)(2,1)} %fusion.24), kind=kLoop, calls=%fused_computation.42 | loop fusion | flops 4194304 | bytes 4194304 | tf_op jit(solution)/shard_map/concatenate | solution.py:213
  76.4 2.9 %collective-permute-start.10 = (bf16[1024,1024]{1,0:T(8,128)(2,1)S(1)}, bf16[1024,1024]{1,0:T(8,128)(2,1)}, u32[]{:S(2)}, u32[]{:S(2)}) collective-permute-start(bf16[1024,1024]{1,0:T(8,128)(2,1)S(1)} %pad_maximum_fusion), channel_id=1, source_target_pairs={{0,1},{1,0},{2,3},{3,2},{4,5},{5,4},{6,7},{7,6},{8,9},{9,8},{10,11... | collective-permute-start | bytes 6291464 | tf_op jit(solution)/shard_map/ppermute | solution.py:215
  80.0 3.9 %fusion.20 = f32[1024,1024]{1,0:T(8,128)S(1)} fusion(bf16[1024,1024]{1,0:T(8,128)(2,1)S(1)} %pad_maximum_fusion, bf16[4096,1024]{1,0:T(8,128)(2,1)} %param.11, s32[]{:T(128)S(6)} %select_n.23), kind=kOutput, calls=%fused_computation.45 | convolution fusion | flops 2147483648 | bytes 8388612 | tf_op jit(solution)/shard_map/dot_general | solution.py:219
  83.9 2.6 %fusion.42 = f32[1024,1024]{1,0:T(8,128)S(1)} fusion(bf16[1024,384]{1,0:T(8,128)(2,1)} %collective-permute-done.9, bf16[4096,1024]{1,0:T(8,128)(2,1)} %param.11, s32[]{:T(128)S(6)} %select_n.24), kind=kOutput, calls=%fused_computation.67 | convolution fusion | flops 805306368 | bytes 5767172 | tf_op jit(solution)/shard_map/dot_general | solution.py:210
  86.5 4.6 %fusion.18 = f32[1024,1024]{1,0:T(8,128)S(1)} fusion(bf16[1024,1024]{1,0:T(8,128)(2,1)} %collective-permute-done.10, bf16[4096,1024]{1,0:T(8,128)(2,1)} %param.11, s32[]{:T(128)S(6)} %select_n.25), kind=kOutput, calls=%fused_computation.43 | convolution fusion | flops 2147483648 | bytes 8388612 | tf_op jit(solution)/shard_map/dot_general | solution.py:220
  91.1 4.4 %add_add_fusion = f32[1024,1024]{1,0:T(8,128)} fusion(f32[1024,1024]{1,0:T(8,128)S(1)} %fusion.18, f32[1024,1024]{1,0:T(8,128)S(1)} %fusion.20, f32[1024,1024]{1,0:T(8,128)S(1)} %fusion.42, bf16[1024,384]{1,0:T(8,128)(2,1)S(1)} %collective-permute-done.11, bf16[4096,1024]{1,0:T(8,128)(2,1)} %param.11, s32[]{:T(128)S(6)} %select_n.26), kind=kOutput, calls=%fused_computation.21 | convolution fusion | flops 808452096 | bytes 18350084 | tf_op jit(solution)/shard_map/dot_general | solution.py:210
  95.5 14.3 %collective-permute-done.8 = bf16[1024,640]{1,0:T(8,128)(2,1)} collective-permute-done((bf16[1024,640]{1,0:T(8,128)(2,1)S(1)}, bf16[1024,640]{1,0:T(8,128)(2,1)}, u32[]{:S(2)}, u32[]{:S(2)}) %collective-permute-start.8) | collective-permute-done | bytes 1310752 | tf_op jit(solution)/shard_map/ppermute | solution.py:212
  109.8 0.9 collective-permute-start.12
  110.6 3.6 %fusion.34 = f32[1024,1024]{1,0:T(8,128)S(1)} fusion(bf16[1024,640]{1,0:T(8,128)(2,1)} %collective-permute-done.8, bf16[4096,1024]{1,0:T(8,128)(2,1)} %param.11, s32[]{:T(128)S(6)} %select_n.27), kind=kOutput, calls=%fused_computation.60 | convolution fusion | flops 1342177280 | bytes 6815748 | tf_op jit(solution)/shard_map/dot_general | solution.py:210
  114.3 4.4 %add_convert_fusion = bf16[1024,1024]{1,0:T(8,128)(2,1)} fusion(f32[1024,1024]{1,0:T(8,128)S(1)} %copy-done, f32[1024,1024]{1,0:T(8,128)S(1)} %fusion.34, bf16[1024,640]{1,0:T(8,128)(2,1)S(1)} %collective-permute-done.12, bf16[4096,1024]{1,0:T(8,128)(2,1)} %param.11, s32[]{:T(128)S(6)} %select_n.28), kind=kOutput, calls=%fused_computation.20 | convolution fusion | flops 1345323008 | bytes 13107204 | tf_op jit(solution)/shard_map/dot_general | solution.py:210
  (31 shorter events, 2.4 us)
Async XLA Ops:
  0.8 7.1 %collective-permute-start = (bf16[3,2,1024]{2,1,0:T(2,128)(2,1)S(1)}, bf16[3,2,1024]{2,1,0:T(2,128)(2,1)S(1)}, u32[]{:S(2)}, u32[]{:S(2)}) collective-permute-start(bf16[3,2,1024]{2,1,0:T(2,128)(2,1)S(1)} %slice.108), channel_id=1, source_target_pairs={{0,4},{4,8},{8,12},{12,16},{16,20},{20,24},{24,28},{1,5},{5,9},{9,... | collective-permute-start | bytes 36872 | tf_op jit(solution)/shard_map/ppermute | solution.py:15
  26.1 19.3 %copy-start.1 = (f32[16,1024]{1,0:T(8,128)S(1)}, f32[16,1024]{1,0:T(8,128)}, u32[]{:S(2)}) copy-start(f32[16,1024]{1,0:T(8,128)} %param.8) | copy-start | bytes 196612
  27.5 11.8 %collective-permute-start.7 = (f32[16,1024]{1,0:T(8,128)S(1)}, f32[16,1024]{1,0:T(8,128)S(1)}, u32[]{:S(2)}, u32[]{:S(2)}) collective-permute-start(f32[16,1024]{1,0:T(8,128)S(1)} %multiply_reduce_fusion.1), channel_id=1, source_target_pairs={{0,28},{1,29},{2,30},{3,31}} | collective-permute-start | bytes 196616 | tf_op jit(solution)/shard_map/ppermute | solution.py:15
  31.8 9.1 %collective-permute-start.6 = (f32[16,1024]{1,0:T(8,128)S(1)}, f32[16,1024]{1,0:T(8,128)S(1)}, u32[]{:S(2)}, u32[]{:S(2)}) collective-permute-start(f32[16,1024]{1,0:T(8,128)S(1)} %multiply_reduce_fusion.1), channel_id=1, source_target_pairs={{0,24},{4,28},{1,25},{5,29},{2,26},{6,30},{3,27},{7,31}} | collective-permute-start | bytes 196616 | tf_op jit(solution)/shard_map/ppermute | solution.py:15
  33.4 12.0 %collective-permute-start.5 = (f32[16,1024]{1,0:T(8,128)S(1)}, f32[16,1024]{1,0:T(8,128)S(1)}, u32[]{:S(2)}, u32[]{:S(2)}) collective-permute-start(f32[16,1024]{1,0:T(8,128)S(1)} %multiply_reduce_fusion.1), channel_id=1, source_target_pairs={{0,20},{4,24},{8,28},{1,21},{5,25},{9,29},{2,22},{6,26},{10,30},{3... | collective-permute-start | bytes 196616 | tf_op jit(solution)/shard_map/ppermute | solution.py:15
  34.7 10.7 %collective-permute-start.4 = (f32[16,1024]{1,0:T(8,128)S(1)}, f32[16,1024]{1,0:T(8,128)S(1)}, u32[]{:S(2)}, u32[]{:S(2)}) collective-permute-start(f32[16,1024]{1,0:T(8,128)S(1)} %multiply_reduce_fusion.1), channel_id=1, source_target_pairs={{0,16},{4,20},{8,24},{12,28},{1,17},{5,21},{9,25},{13,29},{2,18},{... | collective-permute-start | bytes 196616 | tf_op jit(solution)/shard_map/ppermute | solution.py:15
  36.0 9.4 %collective-permute-start.3 = (f32[16,1024]{1,0:T(8,128)S(1)}, f32[16,1024]{1,0:T(8,128)S(1)}, u32[]{:S(2)}, u32[]{:S(2)}) collective-permute-start(f32[16,1024]{1,0:T(8,128)S(1)} %multiply_reduce_fusion.1), channel_id=1, source_target_pairs={{0,12},{4,16},{8,20},{12,24},{16,28},{1,13},{5,17},{9,21},{13,25},... | collective-permute-start | bytes 196616 | tf_op jit(solution)/shard_map/ppermute | solution.py:15
  39.3 6.1 %collective-permute-start.2 = (f32[16,1024]{1,0:T(8,128)S(1)}, f32[16,1024]{1,0:T(8,128)S(1)}, u32[]{:S(2)}, u32[]{:S(2)}) collective-permute-start(f32[16,1024]{1,0:T(8,128)S(1)} %multiply_reduce_fusion.1), channel_id=1, source_target_pairs={{0,8},{4,12},{8,16},{12,20},{16,24},{20,28},{1,9},{5,13},{9,17},{1... | collective-permute-start | bytes 196616 | tf_op jit(solution)/shard_map/ppermute | solution.py:15
  40.9 4.5 %collective-permute-start.1 = (f32[16,1024]{1,0:T(8,128)S(1)}, f32[16,1024]{1,0:T(8,128)S(1)}, u32[]{:S(2)}, u32[]{:S(2)}) collective-permute-start(f32[16,1024]{1,0:T(8,128)S(1)} %multiply_reduce_fusion.1), channel_id=1, source_target_pairs={{0,4},{4,8},{8,12},{12,16},{16,20},{20,24},{24,28},{1,5},{5,9},{9,... | collective-permute-start | bytes 196616 | tf_op jit(solution)/shard_map/ppermute | solution.py:15
  46.7 7.4 %slice-start = ((f32[1024]{0:T(1024)}), f32[384]{0:T(512)S(1)}, s32[]{:S(2)}) async-start(f32[1024]{0:T(1024)} %param.10), calls=%async_computation | async-start | bytes 4096 | tf_op jit(solution)/shard_map/slice | solution.py:187
  54.1 5.9 %copy-start.2 = (f32[1024]{0:T(1024)S(1)}, f32[1024]{0:T(1024)}, u32[]{:S(2)}) copy-start(f32[1024]{0:T(1024)} %param.10) | copy-start | bytes 12292
  58.1 18.4 %collective-permute-start.9 = (bf16[1024,384]{1,0:T(8,128)(2,1)}, bf16[1024,384]{1,0:T(8,128)(2,1)}, u32[]{:S(2)}, u32[]{:S(2)}) collective-permute-start(bf16[1024,384]{1,0:T(8,128)(2,1)} %fusion.24), channel_id=1, source_target_pairs={{0,2},{1,3},{2,0},{3,1},{4,6},{5,7},{6,4},{7,5},{8,10},{9,11},{10,... | collective-permute-start | bytes 2359304 | tf_op jit(solution)/shard_map/ppermute | solution.py:212
  76.4 10.1 %collective-permute-start.10 = (bf16[1024,1024]{1,0:T(8,128)(2,1)S(1)}, bf16[1024,1024]{1,0:T(8,128)(2,1)}, u32[]{:S(2)}, u32[]{:S(2)}) collective-permute-start(bf16[1024,1024]{1,0:T(8,128)(2,1)S(1)} %pad_maximum_fusion), channel_id=1, source_target_pairs={{0,1},{1,0},{2,3},{3,2},{4,5},{5,4},{6,7},{7,6},{8,9},{9,8},{10,11... | collective-permute-start | bytes 6291464 | tf_op jit(solution)/shard_map/ppermute | solution.py:215
  79.3 30.4 %collective-permute-start.8 = (bf16[1024,640]{1,0:T(8,128)(2,1)S(1)}, bf16[1024,640]{1,0:T(8,128)(2,1)}, u32[]{:S(2)}, u32[]{:S(2)}) collective-permute-start(bf16[1024,640]{1,0:T(8,128)(2,1)S(1)} %fusion.8), channel_id=1, source_target_pairs={{0,2},{1,3},{2,0},{3,1},{4,6},{5,7},{6,4},{7,5},{8,10},{9,11},{10,... | collective-permute-start | bytes 3932168 | tf_op jit(solution)/shard_map/ppermute | solution.py:212
  79.6 11.5 %collective-permute-start.11 = (bf16[1024,384]{1,0:T(8,128)(2,1)}, bf16[1024,384]{1,0:T(8,128)(2,1)S(1)}, u32[]{:S(2)}, u32[]{:S(2)}) collective-permute-start(bf16[1024,384]{1,0:T(8,128)(2,1)} %collective-permute-done.9), channel_id=1, source_target_pairs={{0,1},{1,0},{2,3},{3,2},{4,5},{5,4},{6,7},{7,6},{8,9},{9,8},{10,11... | collective-permute-start | bytes 2359304 | tf_op jit(solution)/shard_map/ppermute | solution.py:216
  109.8 4.5 %collective-permute-start.12 = (bf16[1024,640]{1,0:T(8,128)(2,1)}, bf16[1024,640]{1,0:T(8,128)(2,1)S(1)}, u32[]{:S(2)}, u32[]{:S(2)}) collective-permute-start(bf16[1024,640]{1,0:T(8,128)(2,1)} %collective-permute-done.8), channel_id=1, source_target_pairs={{0,1},{1,0},{2,3},{3,2},{4,5},{5,4},{6,7},{7,6},{8,9},{9,8},{10,11... | collective-permute-start | bytes 3932168 | tf_op jit(solution)/shard_map/ppermute | solution.py:224
  110.6 3.7 %copy-start = (f32[1024,1024]{1,0:T(8,128)S(1)}, f32[1024,1024]{1,0:T(8,128)}, u32[]{:S(2)}) copy-start(f32[1024,1024]{1,0:T(8,128)} %add_add_fusion) | copy-start | bytes 12582916

commit v11 on v10

--- a/solution.py
+++ b/solution.py
@@ -172,10 +172,13 @@
     starts = segment_starts(ends, start, pole_rates, span)
     ch_count = lax.axis_size("ch")
     groups = width // LANES
-    lead_groups = (3 * groups) // 8 if ch_count == 4 else 0
-    bounds = [0, lead_groups * LANES, width] if lead_groups > 0 else [0, width]
+    if ch_count == 4 and groups >= 8:
+        bounds = [0, (2 * groups) // 8 * LANES, (5 * groups) // 8 * LANES, width]
+    else:
+        bounds = [0, width]
     pieces = len(bounds) - 1
     gated = []
+    far = []
     x_next = x
     for index in range(pieces):
         cols = slice(bounds[index], bounds[index + 1])
@@ -190,12 +193,16 @@
         if index + 1 < pieces:
             x_next, gated_mix = lax.optimization_barrier((x, gated_mix))
         gated.append(gated_mix)
+        if pieces > 1:
+            far.append(lax.ppermute(gated_mix, "ch", [(i, i ^ 2) for i in range(ch_count)]))
+        if index + 1 < pieces and index >= 1:
+            x_next, far[index - 1] = lax.optimization_barrier((x_next, far[index - 1]))
     if pieces == 1:
         return project(gated[0], out_weight).astype(jnp.bfloat16)
-    return project_pieces(gated, out_weight).astype(jnp.bfloat16)
-
-
-def project_pieces(gated, out_weight):
+    return project_pieces(gated, far, out_weight).astype(jnp.bfloat16)
+
+
+def project_pieces(gated, far, out_weight):
     ch_count = lax.axis_size("ch")
     offsets = [0]
     for value in gated:
@@ -209,22 +216,26 @@
         rows = lax.dynamic_slice_in_dim(out_weight, owner * width + offsets[index], value.shape[1], 0)
         return jnp.dot(value, rows, preferred_element_type=jnp.float32)
 
-    far = [lax.ppermute(g, "ch", other_chip) for g in gated]
+    far = list(far)
     own = jnp.concatenate(gated, 1)
-    own, far[0] = lax.optimization_barrier((own, far[0]))
+    early = len(far) - 1
+    own, early_far = lax.optimization_barrier((own, far[:early]))
+    far[:early] = early_far
     near = lax.ppermute(own, "ch", other_core)
-    near_far = [lax.ppermute(far[0], "ch", other_core)]
+    near_far = [lax.ppermute(f, "ch", other_core) for f in far[:early]]
     rows_own = lax.dynamic_slice_in_dim(out_weight, here * width, width, 0)
     rows_near = lax.dynamic_slice_in_dim(out_weight, (here ^ 1) * width, width, 0)
-    total = jnp.dot(own, rows_own, preferred_element_type=jnp.float32) + part(far[0], here ^ 2, 0)
+    total = jnp.dot(own, rows_own, preferred_element_type=jnp.float32)
+    for index in range(early):
+        total = total + part(far[index], here ^ 2, index)
     total = total + jnp.dot(near, rows_near, preferred_element_type=jnp.float32)
-    total = total + part(near_far[0], here ^ 3, 0)
-    for index in range(1, len(far)):
-        far[index], total = lax.optimization_barrier((far[index], total))
-        near_far.append(lax.ppermute(far[index], "ch", other_core))
-        total = total + part(far[index], here ^ 2, index)
-    for index in range(1, len(far)):
+    for index in range(early):
         total = total + part(near_far[index], here ^ 3, index)
+    last = far[early]
+    last, total = lax.optimization_barrier((last, total))
+    near_last = lax.ppermute(last, "ch", other_core)
+    total = total + part(last, here ^ 2, early)
+    total = total + part(near_last, here ^ 3, early)
     return total
 
 

time: 120 us -> 117 us (0.975)
  waiting for transfers between devices: 14.3 us -> 5.96 us
  Pallas kernels: 27.9 us -> 29.8 us
  other arithmetic: 25.7 us -> 27.4 us
    ppermute x4 -> x6, waiting for transfers between devices: 14.3 us -> 5.91 us  [the longest x3 5.9 us: shards(): lax.ppermute(gated_mix, 'ch', [(i, i ^ 2) for i in range(ch_count)])]
    pallas_call x2 -> x3, Pallas kernels: 18.4 us -> 20.4 us  [run_recurrence(): pl.pallas_call(recurrence_kernel, grid=(group_count,), in_specs=[pl.Block...]
    convert_element_type x2 -> x3, other arithmetic: 7.81 us -> 9.51 us  [shards(): gated_mix = gated_mix.astype(jnp.bfloat16)]
    dot_general x1, matrix products: 3.92 us -> 2.34 us  [project_pieces(): total = jnp.dot(own, rows_own, preferred_element_type=jnp.float32)]
    dot_general x4 -> x6, matrix products: 15.1 us -> 16.6 us  [part(): return jnp.dot(value, rows, preferred_element_type=jnp.float32)]
    ppermute x4 -> x6, starting transfers between devices: 2.72 us -> 3.08 us  [the longest x3 1.79 us: shards(): lax.ppermute(gated_mix, 'ch', [(i, i ^ 2) for i in range(ch_count)])]
  transfers between devices with their start and end apart: 13 -> 15, of which waited for: 1 -> 2; matrix products, arithmetic and copies ran while one was open for 26% -> 30% of each run, Pallas kernels for 9% -> 13%
where the time goes in v11:
time: 117 us; the launch traced here: 115 us
  Pallas kernels  29.8 us (25%)
  other arithmetic  27.4 us (23%)
  starting transfers between devices  25.7 us (22%)
  matrix products  22.9 us (20%)
  waiting for transfers between devices  5.96 us (5%)
  local copies, waits for them, and re-layouts  3.38 us (3%)
    pallas_call x3, Pallas kernels, run_recurrence(): pl.pallas_call(recurrence_kernel, grid=(group_count,), in_specs=[pl.Block...  20.4 us
    ppermute x8, starting transfers between devices, shifted(): lax.ppermute(value, axis, [(source, source + steps) for source in range(i...  19 us
    dot_general x6, matrix products, part(): return jnp.dot(value, rows, preferred_element_type=jnp.float32)  16.6 us
    convert_element_type x3, other arithmetic, shards(): gated_mix = gated_mix.astype(jnp.bfloat16)  9.51 us
    pallas_call x1, Pallas kernels, run_end_state(): pl.pallas_call(end_state_kernel, grid=(width // LANES,), in_specs=[pl.Blo...  9.47 us
    convert_element_type x1, other arithmetic, shards(): x = mixed_input.astype(jnp.float32)  8.74 us
    ppermute x3, waiting for transfers between devices, shards(): lax.ppermute(gated_mix, 'ch', [(i, i ^ 2) for i in range(ch_count)])  5.9 us
    dot_general x1, matrix products, project_pieces(): total = total + jnp.dot(near, rows_near, preferred_element_type=jnp.float32)  3.94 us
  transfers between devices with their start and end apart: 15, of which 2 were waited for; matrix products, arithmetic and copies ran while one was open for 30% of the time, Pallas kernels for 13%

profile of v11, /device:TPU:1, one launch (start us, length us, event | category | flops | bytes accessed | tf_op | source)
XLA Modules:
  0.0 115.4 jit_solution(13571482879250190101)
XLA Ops:
  0.8 4.0 %collective-permute-start = (bf16[3,2,1024]{2,1,0:T(2,128)(2,1)S(1)}, bf16[3,2,1024]{2,1,0:T(2,128)(2,1)S(1)}, u32[]{:S(2)}, u32[]{:S(2)}) collective-permute-start(bf16[3,2,1024]{2,1,0:T(2,128)(2,1)S(1)} %slice.141), channel_id=1, source_target_pairs={{0,4},{4,8},{8,12},{12,16},{16,20},{20,24},{24,28},{1,5},{5,9},{9,... | collective-permute-start | bytes 36872 | tf_op jit(solution)/shard_map/ppermute | solution.py:15
  8.0 1.5 %fusion.62 = (f32[16,1024]{1,0:T(8,128)S(1)}, f32[16,1024]{1,0:T(8,128)}) fusion(f32[16,1024]{1,0:T(8,128)} %param.8), kind=kLoop, calls=%fused_computation.115 | loop fusion | flops 16384 | bytes 196608 | tf_op jit(solution)/shard_map/neg | solution.py:169
  9.5 8.7 %fusion.60 = (f32[1024,1024]{1,0:T(8,128)}, bf16[1024,1024]{1,0:T(8,128)(2,1)S(1)}) fusion(f32[1024]{0:T(1024)S(1)} %bitcast.91, f32[1024]{0:T(1024)S(1)} %bitcast.87, bf16[3,1024,1024]{2,1,0:T(8,128)(2,1)} %param.6, f32[1024]{0:T(1024)S(1)} %bitcast.88, f32[1024]{0:T(1024)S(1)} %bitcast.89, bf16[3,2,1024]{2,1,0:T(2,128)(2,1)S(1)} %collective-permute-done, ...), kind=kLoop, calls=%fused_computation.114 | loop fusion | flops 36700160 | bytes 16814080 | tf_op jit(solution)/shard_map/convert_element_type | solution.py:166
  18.2 9.5 %shard_map.64 = f32[16,8,1024]{2,1,0:T(8,128)} custom-call(f32[1024,1024]{1,0:T(8,128)} %get-tuple-element.19.x_ref, f32[16,1024]{1,0:T(8,128)} %get-tuple-element.36.decay_ref), custom_call_target="tpu_custom_call" | custom-call | tf_op jit(solution)/shard_map/pallas_call | solution.py:62
  27.7 1.3 %multiply_reduce_fusion.1 = f32[16,1024]{1,0:T(8,128)S(1)} fusion(f32[16,8,1024]{2,1,0:T(8,128)} %shard_map.64, f32[8]{0:T(128)S(1)} %subtract_multiply_fusion, f32[16,1024]{1,0:T(8,128)S(1)} %get-tuple-element.35), kind=kLoop, calls=%fused_computation.83 | loop fusion | flops 376832 | bytes 655392 | tf_op jit(solution)/shard_map/reduce_sum | solution.py:110
  29.0 4.3 %collective-permute-start.7 = (f32[16,1024]{1,0:T(8,128)S(1)}, f32[16,1024]{1,0:T(8,128)S(1)}, u32[]{:S(2)}, u32[]{:S(2)}) collective-permute-start(f32[16,1024]{1,0:T(8,128)S(1)} %multiply_reduce_fusion.1), channel_id=1, source_target_pairs={{0,28},{1,29},{2,30},{3,31}} | collective-permute-start | bytes 196616 | tf_op jit(solution)/shard_map/ppermute | solution.py:15
  33.4 1.6 %collective-permute-start.6 = (f32[16,1024]{1,0:T(8,128)S(1)}, f32[16,1024]{1,0:T(8,128)S(1)}, u32[]{:S(2)}, u32[]{:S(2)}) collective-permute-start(f32[16,1024]{1,0:T(8,128)S(1)} %multiply_reduce_fusion.1), channel_id=1, source_target_pairs={{0,24},{4,28},{1,25},{5,29},{2,26},{6,30},{3,27},{7,31}} | collective-permute-start | bytes 196616 | tf_op jit(solution)/shard_map/ppermute | solution.py:15
  34.9 1.3 %collective-permute-start.5 = (f32[16,1024]{1,0:T(8,128)S(1)}, f32[16,1024]{1,0:T(8,128)S(1)}, u32[]{:S(2)}, u32[]{:S(2)}) collective-permute-start(f32[16,1024]{1,0:T(8,128)S(1)} %multiply_reduce_fusion.1), channel_id=1, source_target_pairs={{0,20},{4,24},{8,28},{1,21},{5,25},{9,29},{2,22},{6,26},{10,30},{3... | collective-permute-start | bytes 196616 | tf_op jit(solution)/shard_map/ppermute | solution.py:15
  36.2 1.3 %collective-permute-start.4 = (f32[16,1024]{1,0:T(8,128)S(1)}, f32[16,1024]{1,0:T(8,128)S(1)}, u32[]{:S(2)}, u32[]{:S(2)}) collective-permute-start(f32[16,1024]{1,0:T(8,128)S(1)} %multiply_reduce_fusion.1), channel_id=1, source_target_pairs={{0,16},{4,20},{8,24},{12,28},{1,17},{5,21},{9,25},{13,29},{2,18},{... | collective-permute-start | bytes 196616 | tf_op jit(solution)/shard_map/ppermute | solution.py:15
  37.5 1.9 %collective-permute-start.3 = (f32[16,1024]{1,0:T(8,128)S(1)}, f32[16,1024]{1,0:T(8,128)S(1)}, u32[]{:S(2)}, u32[]{:S(2)}) collective-permute-start(f32[16,1024]{1,0:T(8,128)S(1)} %multiply_reduce_fusion.1), channel_id=1, source_target_pairs={{0,12},{4,16},{8,20},{12,24},{16,28},{1,13},{5,17},{9,21},{13,25},... | collective-permute-start | bytes 196616 | tf_op jit(solution)/shard_map/ppermute | solution.py:15
  39.5 1.4 %copy.15 = f32[16,1024,8]{1,0,2:T(8,128)S(1)} copy(f32[16,1024,8]{1,2,0:T(8,128)} %bitcast.83) | data formatting | bytes 1048576
  40.8 1.6 %collective-permute-start.2 = (f32[16,1024]{1,0:T(8,128)S(1)}, f32[16,1024]{1,0:T(8,128)S(1)}, u32[]{:S(2)}, u32[]{:S(2)}) collective-permute-start(f32[16,1024]{1,0:T(8,128)S(1)} %multiply_reduce_fusion.1), channel_id=1, source_target_pairs={{0,8},{4,12},{8,16},{12,20},{16,24},{20,28},{1,9},{5,13},{9,17},{1... | collective-permute-start | bytes 196616 | tf_op jit(solution)/shard_map/ppermute | solution.py:15
  42.4 3.1 %collective-permute-start.1 = (f32[16,1024]{1,0:T(8,128)S(1)}, f32[16,1024]{1,0:T(8,128)S(1)}, u32[]{:S(2)}, u32[]{:S(2)}) collective-permute-start(f32[16,1024]{1,0:T(8,128)S(1)} %multiply_reduce_fusion.1), channel_id=1, source_target_pairs={{0,4},{4,8},{8,12},{12,16},{16,20},{20,24},{24,28},{1,5},{5,9},{9,... | collective-permute-start | bytes 196616 | tf_op jit(solution)/shard_map/ppermute | solution.py:15
  45.5 1.2 %multiply_reduce_fusion = f32[16,1024,8]{1,0,2:T(8,128)S(1)} fusion(f32[16,1024,8]{1,0,2:T(8,128)S(1)} %copy.15, f32[8,8]{1,0:T(8,128)S(1)} %maximum_multiply_fusion, f32[16,1024]{1,0:T(8,128)S(1)} %get-tuple-element.35, pred[8,8]{1,0:T(8,128)(4,1)S(1)} %iota_compare_fusion), kind=kLoop, calls=%fused_computation.21 | loop fusion | flops 4063232 | bytes 1114432
  48.1 5.5 %shard_map.65 = f32[1024,256]{1,0:T(8,128)} custom-call(f32[1024,1024]{1,0:T(8,128)} %get-tuple-element.19.x_ref, f32[16,1024]{1,0:T(8,128)} %get-tuple-element.36.decay_ref, f32[16,1024]{1,0:T(8,128)} %residue_ref.5, f32[16,8,1024]{2,1,0:T(8,128)} %bitcast_add_fusion.start_ref), custom_call_target="tpu_custom_call" | custom-call | tf_op jit(solution)/shard_map/pallas_call | solution.py:78
  53.6 2.4 %fusion.28 = bf16[1024,256]{1,0:T(8,128)(2,1)S(1)} fusion(bf16[1024,1024]{1,0:T(8,128)(2,1)S(1)} %get-tuple-element.34, bf16[3,1024,1024]{2,1,0:T(8,128)(2,1)} %param.6, bf16[3,2,1024]{2,1,0:T(2,128)(2,1)S(1)} %collective-permute-done, f32[256]{0:T(256)S(1)} %slice-done.2, f32[1024,256]{1,0:T(8,128)} %shard_map.65, f32[256]{0:T(256)S(1)} %bitcast.93, ...), kind=kLoop, calls=%fused_computation.59 | loop fusion | flops 6029312 | bytes 8929280 | tf_op jit(solution)/shard_map/convert_element_type | solution.py:192
  56.0 1.3 %collective-permute-start.8 = (bf16[1024,256]{1,0:T(8,128)(2,1)S(1)}, bf16[1024,256]{1,0:T(8,128)(2,1)S(1)}, u32[]{:S(2)}, u32[]{:S(2)}) collective-permute-start(bf16[1024,256]{1,0:T(8,128)(2,1)S(1)} %fusion.28), channel_id=1, source_target_pairs={{0,2},{1,3},{2,0},{3,1},{4,6},{5,7},{6,4},{7,5},{8,10},{9,11},{10,... | collective-permute-start | bytes 1572872 | tf_op jit(solution)/shard_map/ppermute | solution.py:197
  57.3 7.3 %shard_map.66 = f32[1024,384]{1,0:T(8,128)} custom-call(f32[1024,1024]{1,0:T(8,128)} %get-tuple-element.19.x_ref, f32[16,1024]{1,0:T(8,128)} %get-tuple-element.36.decay_ref, f32[16,1024]{1,0:T(8,128)} %residue_ref.5, f32[16,8,1024]{2,1,0:T(8,128)} %bitcast_add_fusion.start_ref), custom_call_target="tpu_custom_call" | custom-call | tf_op jit(solution)/shard_map/pallas_call | solution.py:78
  64.6 4.0 %fusion.20 = bf16[1024,384]{1,0:T(8,128)(2,1)} fusion(bf16[1024,1024]{1,0:T(8,128)(2,1)S(1)} %get-tuple-element.34, f32[384]{0:T(512)S(1)} %get-tuple-element.46, f32[1024,384]{1,0:T(8,128)} %shard_map.66, f32[384]{0:T(512)S(1)} %get-tuple-element.28, f32[384]{0:T(512)S(1)} %get-tuple-element.29, bf16[3,1024,1024]{2,1,0:T(8,128)(2,1)} %param.6, ...), kind=kLoop, calls=%fused_computation.45 | loop fusion | flops 9043968 | bytes 10242048 | tf_op jit(solution)/shard_map/convert_element_type | solution.py:192
  68.9 7.5 %shard_map.67 = f32[1024,384]{1,0:T(8,128)} custom-call(f32[1024,1024]{1,0:T(8,128)} %get-tuple-element.19.x_ref, f32[16,1024]{1,0:T(8,128)} %get-tuple-element.36.decay_ref, f32[16,1024]{1,0:T(8,128)} %residue_ref.5, f32[16,8,1024]{2,1,0:T(8,128)} %bitcast_add_fusion.start_ref), custom_call_target="tpu_custom_call" | custom-call | tf_op jit(solution)/shard_map/pallas_call | solution.py:78
  76.4 3.1 %fusion.24 = bf16[1024,384]{1,0:T(8,128)(2,1)S(1)} fusion(bf16[1024,1024]{1,0:T(8,128)(2,1)S(1)} %get-tuple-element.34, f32[384]{0:T(512)S(1)} %get-tuple-element.47, f32[1024,384]{1,0:T(8,128)} %shard_map.67, f32[384]{0:T(512)S(1)} %get-tuple-element.31, f32[384]{0:T(512)S(1)} %get-tuple-element.32, bf16[3,1024,1024]{2,1,0:T(8,128)(2,1)} %param.6, ...), kind=kLoop, calls=%fused_computation.52 | loop fusion | flops 9043968 | bytes 10242048 | tf_op jit(solution)/shard_map/convert_element_type | solution.py:192
  79.5 1.4 %pad_maximum_fusion = bf16[1024,1024]{1,0:T(8,128)(2,1)S(1)} fusion(bf16[1024,384]{1,0:T(8,128)(2,1)S(1)} %fusion.24, bf16[1024,384]{1,0:T(8,128)(2,1)} %fusion.20, bf16[1024,256]{1,0:T(8,128)(2,1)S(1)} %fusion.28), kind=kLoop, calls=%fused_computation.37 | loop fusion | flops 6291456 | bytes 4194304 | tf_op jit(solution)/shard_map/concatenate | solution.py:220
  81.0 4.4 %collective-permute-done.10 = bf16[1024,384]{1,0:T(8,128)(2,1)} collective-permute-done((bf16[1024,384]{1,0:T(8,128)(2,1)}, bf16[1024,384]{1,0:T(8,128)(2,1)}, u32[]{:S(2)}, u32[]{:S(2)}) %collective-permute-start.10) | collective-permute-done | bytes 786464 | tf_op jit(solution)/shard_map/ppermute | solution.py:197
  85.3 3.6 %collective-permute-start.11 = (bf16[1024,1024]{1,0:T(8,128)(2,1)S(1)}, bf16[1024,1024]{1,0:T(8,128)(2,1)}, u32[]{:S(2)}, u32[]{:S(2)}) collective-permute-start(bf16[1024,1024]{1,0:T(8,128)(2,1)S(1)} %pad_maximum_fusion), channel_id=1, source_target_pairs={{0,1},{1,0},{2,3},{3,2},{4,5},{5,4},{6,7},{7,6},{8,9},{9,8},{10,11... | collective-permute-start | bytes 6291464 | tf_op jit(solution)/shard_map/ppermute | solution.py:224
  89.7 2.8 %fusion.44 = f32[1024,1024]{1,0:T(8,128)S(1)} fusion(bf16[1024,384]{1,0:T(8,128)(2,1)} %collective-permute-done.10, bf16[4096,1024]{1,0:T(8,128)(2,1)} %param.11, s32[]{:T(128)S(6)} %select_n.31), kind=kOutput, calls=%fused_computation.73 | convolution fusion | flops 805306368 | bytes 5767172 | tf_op jit(solution)/shard_map/dot_general | solution.py:217
  92.5 1.9 %fusion.50 = f32[1024,1024]{1,0:T(8,128)S(1)} fusion(bf16[1024,256]{1,0:T(8,128)(2,1)S(1)} %copy-done.2, bf16[4096,1024]{1,0:T(8,128)(2,1)} %param.11, s32[]{:T(128)S(6)} %select_n.30), kind=kOutput, calls=%fused_computation.81 | convolution fusion | flops 536870912 | bytes 5242884 | tf_op jit(solution)/shard_map/dot_general | solution.py:217
  94.8 2.3 %fusion.16 = f32[1024,1024]{1,0:T(8,128)S(1)} fusion(bf16[1024,1024]{1,0:T(8,128)(2,1)S(1)} %pad_maximum_fusion, bf16[4096,1024]{1,0:T(8,128)(2,1)S(1)} %bitcast.85, s32[]{:T(128)S(6)} %select_n.29), kind=kOutput, calls=%fused_computation.40 | convolution fusion | flops 2147483648 | bytes 8388612 | tf_op jit(solution)/shard_map/dot_general | solution.py:228
  97.9 3.9 %fusion.14 = f32[1024,1024]{1,0:T(8,128)S(1)} fusion(bf16[1024,1024]{1,0:T(8,128)(2,1)} %collective-permute-done.11, bf16[4096,1024]{1,0:T(8,128)(2,1)S(1)} %bitcast.85, s32[]{:T(128)S(6)} %select_n.32), kind=kOutput, calls=%fused_computation.38 | convolution fusion | flops 2147483648 | bytes 8388612 | tf_op jit(solution)/shard_map/dot_general | solution.py:231
  101.8 4.8 %add_add_fusion = f32[1024,1024]{1,0:T(8,128)} fusion(f32[1024,1024]{1,0:T(8,128)S(1)} %fusion.48, f32[1024,1024]{1,0:T(8,128)S(1)} %fusion.14, f32[1024,1024]{1,0:T(8,128)S(1)} %fusion.44, f32[1024,1024]{1,0:T(8,128)S(1)} %fusion.16, f32[1024,1024]{1,0:T(8,128)S(1)} %fusion.50, bf16[1024,384]{1,0:T(8,128)(2,1)S(1)} %collective-permute-done.13, ...), kind=kOutput, calls=%fused_computation.23 | convolution fusion | flops 810549248 | bytes 26738692 | tf_op jit(solution)/shard_map/dot_general | solution.py:217
  106.6 1.5 %collective-permute-done.9 = bf16[1024,384]{1,0:T(8,128)(2,1)} collective-permute-done((bf16[1024,384]{1,0:T(8,128)(2,1)S(1)}, bf16[1024,384]{1,0:T(8,128)(2,1)}, u32[]{:S(2)}, u32[]{:S(2)}) %collective-permute-start.9) | collective-permute-done | bytes 786464 | tf_op jit(solution)/shard_map/ppermute | solution.py:197
  109.0 2.8 %fusion.38 = f32[1024,1024]{1,0:T(8,128)S(1)} fusion(bf16[1024,384]{1,0:T(8,128)(2,1)} %collective-permute-done.9, bf16[4096,1024]{1,0:T(8,128)(2,1)} %param.11, s32[]{:T(128)S(6)} %select_n.35), kind=kOutput, calls=%fused_computation.69 | convolution fusion | flops 805306368 | bytes 5767172 | tf_op jit(solution)/shard_map/dot_general | solution.py:217
  111.7 3.7 %add_convert_fusion = bf16[1024,1024]{1,0:T(8,128)(2,1)} fusion(f32[1024,1024]{1,0:T(8,128)S(1)} %copy-done, f32[1024,1024]{1,0:T(8,128)S(1)} %fusion.38, bf16[1024,384]{1,0:T(8,128)(2,1)S(1)} %collective-permute-done.14, bf16[4096,1024]{1,0:T(8,128)(2,1)} %param.11, s32[]{:T(128)S(6)} %select_n.36), kind=kOutput, calls=%fused_computation.22 | convolution fusion | flops 808452096 | bytes 12058628 | tf_op jit(solution)/shard_map/dot_general | solution.py:217
  (46 shorter events, 8.3 us)
Async XLA Ops:
  0.8 8.7 %collective-permute-start = (bf16[3,2,1024]{2,1,0:T(2,128)(2,1)S(1)}, bf16[3,2,1024]{2,1,0:T(2,128)(2,1)S(1)}, u32[]{:S(2)}, u32[]{:S(2)}) collective-permute-start(bf16[3,2,1024]{2,1,0:T(2,128)(2,1)S(1)} %slice.141), channel_id=1, source_target_pairs={{0,4},{4,8},{8,12},{12,16},{16,20},{20,24},{24,28},{1,5},{5,9},{9,... | collective-permute-start | bytes 36872 | tf_op jit(solution)/shard_map/ppermute | solution.py:15
  18.2 28.6 %copy-start.3 = (f32[16,1024]{1,0:T(8,128)S(1)}, f32[16,1024]{1,0:T(8,128)}, u32[]{:S(2)}) copy-start(f32[16,1024]{1,0:T(8,128)} %param.8) | copy-start | bytes 196612
  29.0 11.8 %collective-permute-start.7 = (f32[16,1024]{1,0:T(8,128)S(1)}, f32[16,1024]{1,0:T(8,128)S(1)}, u32[]{:S(2)}, u32[]{:S(2)}) collective-permute-start(f32[16,1024]{1,0:T(8,128)S(1)} %multiply_reduce_fusion.1), channel_id=1, source_target_pairs={{0,28},{1,29},{2,30},{3,31}} | collective-permute-start | bytes 196616 | tf_op jit(solution)/shard_map/ppermute | solution.py:15
  33.4 9.1 %collective-permute-start.6 = (f32[16,1024]{1,0:T(8,128)S(1)}, f32[16,1024]{1,0:T(8,128)S(1)}, u32[]{:S(2)}, u32[]{:S(2)}) collective-permute-start(f32[16,1024]{1,0:T(8,128)S(1)} %multiply_reduce_fusion.1), channel_id=1, source_target_pairs={{0,24},{4,28},{1,25},{5,29},{2,26},{6,30},{3,27},{7,31}} | collective-permute-start | bytes 196616 | tf_op jit(solution)/shard_map/ppermute | solution.py:15
  34.9 11.8 %collective-permute-start.5 = (f32[16,1024]{1,0:T(8,128)S(1)}, f32[16,1024]{1,0:T(8,128)S(1)}, u32[]{:S(2)}, u32[]{:S(2)}) collective-permute-start(f32[16,1024]{1,0:T(8,128)S(1)} %multiply_reduce_fusion.1), channel_id=1, source_target_pairs={{0,20},{4,24},{8,28},{1,21},{5,25},{9,29},{2,22},{6,26},{10,30},{3... | collective-permute-start | bytes 196616 | tf_op jit(solution)/shard_map/ppermute | solution.py:15
  36.2 10.5 %collective-permute-start.4 = (f32[16,1024]{1,0:T(8,128)S(1)}, f32[16,1024]{1,0:T(8,128)S(1)}, u32[]{:S(2)}, u32[]{:S(2)}) collective-permute-start(f32[16,1024]{1,0:T(8,128)S(1)} %multiply_reduce_fusion.1), channel_id=1, source_target_pairs={{0,16},{4,20},{8,24},{12,28},{1,17},{5,21},{9,25},{13,29},{2,18},{... | collective-permute-start | bytes 196616 | tf_op jit(solution)/shard_map/ppermute | solution.py:15
  37.5 9.2 %collective-permute-start.3 = (f32[16,1024]{1,0:T(8,128)S(1)}, f32[16,1024]{1,0:T(8,128)S(1)}, u32[]{:S(2)}, u32[]{:S(2)}) collective-permute-start(f32[16,1024]{1,0:T(8,128)S(1)} %multiply_reduce_fusion.1), channel_id=1, source_target_pairs={{0,12},{4,16},{8,20},{12,24},{16,28},{1,13},{5,17},{9,21},{13,25},... | collective-permute-start | bytes 196616 | tf_op jit(solution)/shard_map/ppermute | solution.py:15
  40.8 6.0 %collective-permute-start.2 = (f32[16,1024]{1,0:T(8,128)S(1)}, f32[16,1024]{1,0:T(8,128)S(1)}, u32[]{:S(2)}, u32[]{:S(2)}) collective-permute-start(f32[16,1024]{1,0:T(8,128)S(1)} %multiply_reduce_fusion.1), channel_id=1, source_target_pairs={{0,8},{4,12},{8,16},{12,20},{16,24},{20,28},{1,9},{5,13},{9,17},{1... | collective-permute-start | bytes 196616 | tf_op jit(solution)/shard_map/ppermute | solution.py:15
  42.4 4.4 %collective-permute-start.1 = (f32[16,1024]{1,0:T(8,128)S(1)}, f32[16,1024]{1,0:T(8,128)S(1)}, u32[]{:S(2)}, u32[]{:S(2)}) collective-permute-start(f32[16,1024]{1,0:T(8,128)S(1)} %multiply_reduce_fusion.1), channel_id=1, source_target_pairs={{0,4},{4,8},{8,12},{12,16},{16,20},{20,24},{24,28},{1,5},{5,9},{9,... | collective-permute-start | bytes 196616 | tf_op jit(solution)/shard_map/ppermute | solution.py:15
  46.7 6.9 %slice-start.2 = ((f32[1024]{0:T(1024)}), f32[256]{0:T(256)S(1)}, s32[]{:S(2)}) async-start(f32[1024]{0:T(1024)} %param.10), calls=%async_computation.2 | async-start | bytes 2048 | tf_op jit(solution)/shard_map/slice | solution.py:190
  56.0 12.8 %collective-permute-start.8 = (bf16[1024,256]{1,0:T(8,128)(2,1)S(1)}, bf16[1024,256]{1,0:T(8,128)(2,1)S(1)}, u32[]{:S(2)}, u32[]{:S(2)}) collective-permute-start(bf16[1024,256]{1,0:T(8,128)(2,1)S(1)} %fusion.28), channel_id=1, source_target_pairs={{0,2},{1,3},{2,0},{3,1},{4,6},{5,7},{6,4},{7,5},{8,10},{9,11},{10,... | collective-permute-start | bytes 1572872 | tf_op jit(solution)/shard_map/ppermute | solution.py:197
  68.6 16.7 %collective-permute-start.10 = (bf16[1024,384]{1,0:T(8,128)(2,1)}, bf16[1024,384]{1,0:T(8,128)(2,1)}, u32[]{:S(2)}, u32[]{:S(2)}) collective-permute-start(bf16[1024,384]{1,0:T(8,128)(2,1)} %fusion.20), channel_id=1, source_target_pairs={{0,2},{1,3},{2,0},{3,1},{4,6},{5,7},{6,4},{7,5},{8,10},{9,11},{10,... | collective-permute-start | bytes 2359304 | tf_op jit(solution)/shard_map/ppermute | solution.py:197
  68.9 7.5 %copy-start.1 = (bf16[1024,256]{1,0:T(8,128)(2,1)}, bf16[1024,256]{1,0:T(8,128)(2,1)S(1)}, u32[]{:S(2)}) copy-start(bf16[1024,256]{1,0:T(8,128)(2,1)S(1)} %collective-permute-done.8) | copy-start | bytes 1572868
  81.0 11.5 %copy-start.2 = (bf16[1024,256]{1,0:T(8,128)(2,1)S(1)}, bf16[1024,256]{1,0:T(8,128)(2,1)}, u32[]{:S(2)}) copy-start(bf16[1024,256]{1,0:T(8,128)(2,1)} %copy-done.1) | copy-start | bytes 1572868
  85.3 12.6 %collective-permute-start.11 = (bf16[1024,1024]{1,0:T(8,128)(2,1)S(1)}, bf16[1024,1024]{1,0:T(8,128)(2,1)}, u32[]{:S(2)}, u32[]{:S(2)}) collective-permute-start(bf16[1024,1024]{1,0:T(8,128)(2,1)S(1)} %pad_maximum_fusion), channel_id=1, source_target_pairs={{0,1},{1,0},{2,3},{3,2},{4,5},{5,4},{6,7},{7,6},{8,9},{9,8},{10,11... | collective-permute-start | bytes 6291464 | tf_op jit(solution)/shard_map/ppermute | solution.py:224
  88.9 19.3 %collective-permute-start.9 = (bf16[1024,384]{1,0:T(8,128)(2,1)S(1)}, bf16[1024,384]{1,0:T(8,128)(2,1)}, u32[]{:S(2)}, u32[]{:S(2)}) collective-permute-start(bf16[1024,384]{1,0:T(8,128)(2,1)S(1)} %fusion.24), channel_id=1, source_target_pairs={{0,2},{1,3},{2,0},{3,1},{4,6},{5,7},{6,4},{7,5},{8,10},{9,11},{10,... | collective-permute-start | bytes 2359304 | tf_op jit(solution)/shard_map/ppermute | solution.py:197
  89.1 8.0 %collective-permute-start.12 = (bf16[1024,256]{1,0:T(8,128)(2,1)}, bf16[1024,256]{1,0:T(8,128)(2,1)S(1)}, u32[]{:S(2)}, u32[]{:S(2)}) collective-permute-start(bf16[1024,256]{1,0:T(8,128)(2,1)} %copy-done.1), channel_id=1, source_target_pairs={{0,1},{1,0},{2,3},{3,2},{4,5},{5,4},{6,7},{7,6},{8,9},{9,8},{10,11... | collective-permute-start | bytes 1572872 | tf_op jit(solution)/shard_map/ppermute | solution.py:225
  89.4 12.4 %collective-permute-start.13 = (bf16[1024,384]{1,0:T(8,128)(2,1)}, bf16[1024,384]{1,0:T(8,128)(2,1)S(1)}, u32[]{:S(2)}, u32[]{:S(2)}) collective-permute-start(bf16[1024,384]{1,0:T(8,128)(2,1)} %collective-permute-done.10), channel_id=1, source_target_pairs={{0,1},{1,0},{2,3},{3,2},{4,5},{5,4},{6,7},{7,6},{8,9},{9,8},{10,11... | collective-permute-start | bytes 2359304 | tf_op jit(solution)/shard_map/ppermute | solution.py:225
  89.7 4.7 %slice-start = ((s8[8388608]{0:T(1024)(128)(4,1)}), s8[4194304]{0:T(1024)(128)(4,1)S(1)}, s32[]{:S(2)}) async-start(s8[8388608]{0:T(1024)(128)(4,1)} %bitcast.84), calls=%async_computation | async-start | bytes 8388608
  92.4 2.4 %slice-start.1 = ((s8[8388608]{0:T(1024)(128)(4,1)}), s8[4194304]{0:T(1024)(128)(4,1)S(1)}, s32[]{:S(2)}) async-start(s8[8388608]{0:T(1024)(128)(4,1)} %bitcast.84), calls=%async_computation.1 | async-start | bytes 8388608
  108.2 3.6 %collective-permute-start.14 = (bf16[1024,384]{1,0:T(8,128)(2,1)}, bf16[1024,384]{1,0:T(8,128)(2,1)S(1)}, u32[]{:S(2)}, u32[]{:S(2)}) collective-permute-start(bf16[1024,384]{1,0:T(8,128)(2,1)} %collective-permute-done.9), channel_id=1, source_target_pairs={{0,1},{1,0},{2,3},{3,2},{4,5},{5,4},{6,7},{7,6},{8,9},{9,8},{10,11... | collective-permute-start | bytes 2359304 | tf_op jit(solution)/shard_map/ppermute | solution.py:236
  109.0 2.8 %copy-start = (f32[1024,1024]{1,0:T(8,128)S(1)}, f32[1024,1024]{1,0:T(8,128)}, u32[]{:S(2)}) copy-start(f32[1024,1024]{1,0:T(8,128)} %add_add_fusion) | copy-start | bytes 12582916

commit v12 on v11

--- a/solution.py
+++ b/solution.py
@@ -173,7 +173,7 @@
     ch_count = lax.axis_size("ch")
     groups = width // LANES
     if ch_count == 4 and groups >= 8:
-        bounds = [0, (2 * groups) // 8 * LANES, (5 * groups) // 8 * LANES, width]
+        bounds = [split * groups // 8 * LANES for split in (0, 1, 3, 5, 8)]
     else:
         bounds = [0, width]
     pieces = len(bounds) - 1

time: 117 us -> 124 us (1.060)
  matrix products: 22.9 us -> 29 us
  waiting for transfers between devices: 5.96 us -> 0.52 us
  starting transfers between devices: 25.7 us -> 28.5 us
  other arithmetic: 27.4 us -> 29.4 us
  Pallas kernels: 29.8 us -> 31.6 us
    ppermute x3 -> x4, waiting for transfers between devices: 5.9 us -> 0.45 us  [shards(): lax.ppermute(gated_mix, 'ch', [(i, i ^ 2) for i in range(ch_count)])]
    ppermute x2 -> x3, starting transfers between devices: 0.51 us -> 5.83 us  [project_pieces(): near_far = [lax.ppermute(f, 'ch', other_core) for f in far[:early]]]
    dot_general x6 -> x8, matrix products: 16.6 us -> 20.4 us  [part(): return jnp.dot(value, rows, preferred_element_type=jnp.float32)]
    ppermute x1, starting transfers between devices: 3.57 us -> 0.08 us  [project_pieces(): near = lax.ppermute(own, 'ch', other_core)]
    dot_general x1, matrix products: 2.34 us -> 4.29 us  [project_pieces(): total = jnp.dot(own, rows_own, preferred_element_type=jnp.float32)]
    pallas_call x3 -> x4, Pallas kernels: 20.4 us -> 22.1 us  [run_recurrence(): pl.pallas_call(recurrence_kernel, grid=(group_count,), in_specs=[pl.Block...]
    ppermute x3 -> x4, starting transfers between devices: 1.79 us -> 3.13 us  [shards(): lax.ppermute(gated_mix, 'ch', [(i, i ^ 2) for i in range(ch_count)])]
    convert_element_type x3 -> x4, other arithmetic: 9.51 us -> 10.7 us  [shards(): gated_mix = gated_mix.astype(jnp.bfloat16)]
  transfers between devices with their start and end apart: 15 -> 17, of which waited for: 2 -> 1; matrix products, arithmetic and copies ran while one was open for 30% -> 36% of each run, Pallas kernels for 13% -> 15%
where the time goes in v12:
time: 124 us; the launch traced here: 122 us
  Pallas kernels  31.6 us (25%)
  other arithmetic  29.4 us (24%)
  matrix products  29 us (23%)
  starting transfers between devices  28.5 us (23%)
  local copies, waits for them, and re-layouts  2.97 us (2%)
    pallas_call x4, Pallas kernels, run_recurrence(): pl.pallas_call(recurrence_kernel, grid=(group_count,), in_specs=[pl.Block...  22.1 us
    dot_general x8, matrix products, part(): return jnp.dot(value, rows, preferred_element_type=jnp.float32)  20.4 us
    ppermute x8, starting transfers between devices, shifted(): lax.ppermute(value, axis, [(source, source + steps) for source in range(i...  19 us
    convert_element_type x4, other arithmetic, shards(): gated_mix = gated_mix.astype(jnp.bfloat16)  10.7 us
    pallas_call x1, Pallas kernels, run_end_state(): pl.pallas_call(end_state_kernel, grid=(width // LANES,), in_specs=[pl.Blo...  9.47 us
    convert_element_type x1, other arithmetic, shards(): x = mixed_input.astype(jnp.float32)  8.73 us
    ppermute x3, starting transfers between devices, project_pieces(): near_far = [lax.ppermute(f, 'ch', other_core) for f in far[:early]]  5.83 us
    dot_general x1, matrix products, project_pieces(): total = total + jnp.dot(near, rows_near, preferred_element_type=jnp.float32)  4.33 us
  transfers between devices with their start and end apart: 17, of which 1 were waited for; matrix products, arithmetic and copies ran while one was open for 36% of the time, Pallas kernels for 15%

profile of v12, /device:TPU:1, one launch (start us, length us, event | category | flops | bytes accessed | tf_op | source)
XLA Modules:
  0.0 122.3 jit_solution(12187828637062361360)
XLA Ops:
  0.8 4.0 %collective-permute-start = (bf16[3,2,1024]{2,1,0:T(2,128)(2,1)S(1)}, bf16[3,2,1024]{2,1,0:T(2,128)(2,1)S(1)}, u32[]{:S(2)}, u32[]{:S(2)}) collective-permute-start(bf16[3,2,1024]{2,1,0:T(2,128)(2,1)S(1)} %slice.174), channel_id=1, source_target_pairs={{0,4},{4,8},{8,12},{12,16},{16,20},{20,24},{24,28},{1,5},{5,9},{9,... | collective-permute-start | bytes 36872 | tf_op jit(solution)/shard_map/ppermute | solution.py:15
  8.0 1.5 %fusion.74 = (f32[16,1024]{1,0:T(8,128)S(1)}, f32[16,1024]{1,0:T(8,128)}) fusion(f32[16,1024]{1,0:T(8,128)} %param.8), kind=kLoop, calls=%fused_computation.137 | loop fusion | flops 16384 | bytes 196608 | tf_op jit(solution)/shard_map/neg | solution.py:169
  9.5 8.7 %fusion.72 = (f32[1024,1024]{1,0:T(8,128)}, bf16[1024,1024]{1,0:T(8,128)(2,1)S(1)}) fusion(f32[1024]{0:T(1024)S(1)} %bitcast.110, f32[1024]{0:T(1024)S(1)} %bitcast.111, bf16[3,1024,1024]{2,1,0:T(8,128)(2,1)} %param.6, f32[1024]{0:T(1024)S(1)} %bitcast.112, f32[1024]{0:T(1024)S(1)} %bitcast.113, bf16[3,2,1024]{2,1,0:T(2,128)(2,1)S(1)} %collective-permute-done, ...), kind=kLoop, calls=%fused_computation.136 | loop fusion | flops 36700160 | bytes 16814080 | tf_op jit(solution)/shard_map/convert_element_type | solution.py:166
  18.2 9.5 %shard_map.64 = f32[16,8,1024]{2,1,0:T(8,128)} custom-call(f32[1024,1024]{1,0:T(8,128)} %get-tuple-element.27.x_ref, f32[16,1024]{1,0:T(8,128)} %get-tuple-element.43.decay_ref), custom_call_target="tpu_custom_call" | custom-call | tf_op jit(solution)/shard_map/pallas_call | solution.py:62
  27.7 1.3 %multiply_reduce_fusion.1 = f32[16,1024]{1,0:T(8,128)S(1)} fusion(f32[16,8,1024]{2,1,0:T(8,128)} %shard_map.64, f32[8]{0:T(128)S(1)} %subtract_multiply_fusion, f32[16,1024]{1,0:T(8,128)S(1)} %get-tuple-element.42), kind=kLoop, calls=%fused_computation.93 | loop fusion | flops 376832 | bytes 655392 | tf_op jit(solution)/shard_map/reduce_sum | solution.py:110
  29.0 4.3 %collective-permute-start.7 = (f32[16,1024]{1,0:T(8,128)S(1)}, f32[16,1024]{1,0:T(8,128)S(1)}, u32[]{:S(2)}, u32[]{:S(2)}) collective-permute-start(f32[16,1024]{1,0:T(8,128)S(1)} %multiply_reduce_fusion.1), channel_id=1, source_target_pairs={{0,28},{1,29},{2,30},{3,31}} | collective-permute-start | bytes 196616 | tf_op jit(solution)/shard_map/ppermute | solution.py:15
  33.3 1.6 %collective-permute-start.6 = (f32[16,1024]{1,0:T(8,128)S(1)}, f32[16,1024]{1,0:T(8,128)S(1)}, u32[]{:S(2)}, u32[]{:S(2)}) collective-permute-start(f32[16,1024]{1,0:T(8,128)S(1)} %multiply_reduce_fusion.1), channel_id=1, source_target_pairs={{0,24},{4,28},{1,25},{5,29},{2,26},{6,30},{3,27},{7,31}} | collective-permute-start | bytes 196616 | tf_op jit(solution)/shard_map/ppermute | solution.py:15
  34.9 1.3 %collective-permute-start.5 = (f32[16,1024]{1,0:T(8,128)S(1)}, f32[16,1024]{1,0:T(8,128)S(1)}, u32[]{:S(2)}, u32[]{:S(2)}) collective-permute-start(f32[16,1024]{1,0:T(8,128)S(1)} %multiply_reduce_fusion.1), channel_id=1, source_target_pairs={{0,20},{4,24},{8,28},{1,21},{5,25},{9,29},{2,22},{6,26},{10,30},{3... | collective-permute-start | bytes 196616 | tf_op jit(solution)/shard_map/ppermute | solution.py:15
  36.2 1.3 %collective-permute-start.4 = (f32[16,1024]{1,0:T(8,128)S(1)}, f32[16,1024]{1,0:T(8,128)S(1)}, u32[]{:S(2)}, u32[]{:S(2)}) collective-permute-start(f32[16,1024]{1,0:T(8,128)S(1)} %multiply_reduce_fusion.1), channel_id=1, source_target_pairs={{0,16},{4,20},{8,24},{12,28},{1,17},{5,21},{9,25},{13,29},{2,18},{... | collective-permute-start | bytes 196616 | tf_op jit(solution)/shard_map/ppermute | solution.py:15
  37.5 1.9 %collective-permute-start.3 = (f32[16,1024]{1,0:T(8,128)S(1)}, f32[16,1024]{1,0:T(8,128)S(1)}, u32[]{:S(2)}, u32[]{:S(2)}) collective-permute-start(f32[16,1024]{1,0:T(8,128)S(1)} %multiply_reduce_fusion.1), channel_id=1, source_target_pairs={{0,12},{4,16},{8,20},{12,24},{16,28},{1,13},{5,17},{9,21},{13,25},... | collective-permute-start | bytes 196616 | tf_op jit(solution)/shard_map/ppermute | solution.py:15
  39.4 1.4 %copy.15 = f32[16,1024,8]{1,0,2:T(8,128)S(1)} copy(f32[16,1024,8]{1,2,0:T(8,128)} %bitcast.106) | data formatting | bytes 1048576
  40.8 1.6 %collective-permute-start.2 = (f32[16,1024]{1,0:T(8,128)S(1)}, f32[16,1024]{1,0:T(8,128)S(1)}, u32[]{:S(2)}, u32[]{:S(2)}) collective-permute-start(f32[16,1024]{1,0:T(8,128)S(1)} %multiply_reduce_fusion.1), channel_id=1, source_target_pairs={{0,8},{4,12},{8,16},{12,20},{16,24},{20,28},{1,9},{5,13},{9,17},{1... | collective-permute-start | bytes 196616 | tf_op jit(solution)/shard_map/ppermute | solution.py:15
  42.4 3.1 %collective-permute-start.1 = (f32[16,1024]{1,0:T(8,128)S(1)}, f32[16,1024]{1,0:T(8,128)S(1)}, u32[]{:S(2)}, u32[]{:S(2)}) collective-permute-start(f32[16,1024]{1,0:T(8,128)S(1)} %multiply_reduce_fusion.1), channel_id=1, source_target_pairs={{0,4},{4,8},{8,12},{12,16},{16,20},{20,24},{24,28},{1,5},{5,9},{9,... | collective-permute-start | bytes 196616 | tf_op jit(solution)/shard_map/ppermute | solution.py:15
  48.1 3.7 %shard_map.65 = f32[1024,128]{1,0:T(8,128)} custom-call(f32[1024,1024]{1,0:T(8,128)} %get-tuple-element.27.x_ref, f32[16,1024]{1,0:T(8,128)} %get-tuple-element.43.decay_ref, f32[16,1024]{1,0:T(8,128)} %residue_ref.7, f32[16,8,1024]{2,1,0:T(8,128)} %bitcast_add_fusion.start_ref), custom_call_target="tpu_custom_call" | custom-call | tf_op jit(solution)/shard_map/pallas_call | solution.py:78
  51.7 1.7 %fusion.44 = bf16[1024,128]{1,0:T(8,128)(2,1)S(1)} fusion(bf16[1024,1024]{1,0:T(8,128)(2,1)S(1)} %get-tuple-element.41, bf16[3,1024,1024]{2,1,0:T(8,128)(2,1)} %param.6, bf16[3,2,1024]{2,1,0:T(2,128)(2,1)S(1)} %collective-permute-done, f32[128]{0:T(128)S(1)} %slice-done.2, f32[1024,128]{1,0:T(8,128)} %shard_map.65, f32[128]{0:T(128)S(1)} %get-tuple-element.51, ...), kind=kLoop, calls=%fused_computation.80 | loop fusion | flops 3014656 | bytes 7616512 | tf_op jit(solution)/shard_map/convert_element_type | solution.py:192
  53.4 1.3 %collective-permute-start.8 = (bf16[1024,128]{1,0:T(8,128)(2,1)S(1)}, bf16[1024,128]{1,0:T(8,128)(2,1)S(1)}, u32[]{:S(2)}, u32[]{:S(2)}) collective-permute-start(bf16[1024,128]{1,0:T(8,128)(2,1)S(1)} %fusion.44), channel_id=1, source_target_pairs={{0,2},{1,3},{2,0},{3,1},{4,6},{5,7},{6,4},{7,5},{8,10},{9,11},{10,... | collective-permute-start | bytes 786440 | tf_op jit(solution)/shard_map/ppermute | solution.py:197
  54.7 5.5 %shard_map.66 = f32[1024,256]{1,0:T(8,128)} custom-call(f32[1024,1024]{1,0:T(8,128)} %get-tuple-element.27.x_ref, f32[16,1024]{1,0:T(8,128)} %get-tuple-element.43.decay_ref, f32[16,1024]{1,0:T(8,128)} %residue_ref.7, f32[16,8,1024]{2,1,0:T(8,128)} %bitcast_add_fusion.start_ref), custom_call_target="tpu_custom_call" | custom-call | tf_op jit(solution)/shard_map/pallas_call | solution.py:78
  60.2 2.4 %fusion.24 = bf16[1024,256]{1,0:T(8,128)(2,1)S(1)} fusion(bf16[1024,1024]{1,0:T(8,128)(2,1)S(1)} %get-tuple-element.41, f32[256]{0:T(256)S(1)} %get-tuple-element.59, f32[1024,256]{1,0:T(8,128)} %shard_map.66, f32[256]{0:T(256)S(1)} %bitcast.120, f32[256]{0:T(256)S(1)} %bitcast.118, bf16[3,1024,1024]{2,1,0:T(8,128)(2,1)} %param.6, f32[256]{0:T(256)S(1)} %bitcast.119, ...), kind=kLoop, calls=%fused_computation.56 | loop fusion | flops 6029312 | bytes 8929280 | tf_op jit(solution)/shard_map/convert_element_type | solution.py:192
  63.7 5.6 %shard_map.67 = f32[1024,256]{1,0:T(8,128)} custom-call(f32[1024,1024]{1,0:T(8,128)} %get-tuple-element.27.x_ref, f32[16,1024]{1,0:T(8,128)} %get-tuple-element.43.decay_ref, f32[16,1024]{1,0:T(8,128)} %residue_ref.7, f32[16,8,1024]{2,1,0:T(8,128)} %bitcast_add_fusion.start_ref), custom_call_target="tpu_custom_call" | custom-call | tf_op jit(solution)/shard_map/pallas_call | solution.py:78
  69.3 2.5 %fusion.28 = bf16[1024,256]{1,0:T(8,128)(2,1)S(1)} fusion(bf16[1024,1024]{1,0:T(8,128)(2,1)S(1)} %get-tuple-element.41, f32[256]{0:T(256)S(1)} %get-tuple-element.60, f32[1024,256]{1,0:T(8,128)} %shard_map.67, f32[256]{0:T(256)S(1)} %bitcast.116, f32[256]{0:T(256)S(1)} %bitcast.117, bf16[3,1024,1024]{2,1,0:T(8,128)(2,1)} %param.6, f32[256]{0:T(256)S(1)} %bitcast.115, ...), kind=kLoop, calls=%fused_computation.63 | loop fusion | flops 6029312 | bytes 8929280 | tf_op jit(solution)/shard_map/convert_element_type | solution.py:192
  71.8 1.3 %collective-permute-start.11 = (bf16[1024,256]{1,0:T(8,128)(2,1)S(1)}, bf16[1024,256]{1,0:T(8,128)(2,1)}, u32[]{:S(2)}, u32[]{:S(2)}) collective-permute-start(bf16[1024,256]{1,0:T(8,128)(2,1)S(1)} %fusion.28), channel_id=1, source_target_pairs={{0,2},{1,3},{2,0},{3,1},{4,6},{5,7},{6,4},{7,5},{8,10},{9,11},{10,... | collective-permute-start | bytes 1572872 | tf_op jit(solution)/shard_map/ppermute | solution.py:197
  73.5 7.3 %shard_map.68 = f32[1024,384]{1,0:T(8,128)} custom-call(f32[1024,1024]{1,0:T(8,128)} %get-tuple-element.27.x_ref, f32[16,1024]{1,0:T(8,128)} %get-tuple-element.43.decay_ref, f32[16,1024]{1,0:T(8,128)} %residue_ref.7, f32[16,8,1024]{2,1,0:T(8,128)} %bitcast_add_fusion.start_ref), custom_call_target="tpu_custom_call" | custom-call | tf_op jit(solution)/shard_map/pallas_call | solution.py:78
  80.9 4.1 %fusion.20 = bf16[1024,384]{1,0:T(8,128)(2,1)} fusion(bf16[1024,1024]{1,0:T(8,128)(2,1)S(1)} %get-tuple-element.41, f32[384]{0:T(512)S(1)} %slice.214, f32[1024,384]{1,0:T(8,128)} %shard_map.68, f32[384]{0:T(512)S(1)} %get-tuple-element.38, f32[384]{0:T(512)S(1)} %get-tuple-element.39, bf16[3,1024,1024]{2,1,0:T(8,128)(2,1)} %param.6, ...), kind=kLoop, calls=%fused_computation.42 | loop fusion | flops 9043968 | bytes 10242048 | tf_op jit(solution)/shard_map/convert_element_type | solution.py:192
  85.2 1.6 %pad_maximum_fusion = bf16[1024,1024]{1,0:T(8,128)(2,1)S(1)} fusion(bf16[1024,384]{1,0:T(8,128)(2,1)} %fusion.20, bf16[1024,256]{1,0:T(8,128)(2,1)S(1)} %fusion.28, bf16[1024,256]{1,0:T(8,128)(2,1)S(1)} %fusion.24, bf16[1024,128]{1,0:T(8,128)(2,1)S(1)} %fusion.44), kind=kLoop, calls=%fused_computation.34 | loop fusion | flops 8388608 | bytes 4194304 | tf_op jit(solution)/shard_map/concatenate | solution.py:220
  86.8 5.3 %collective-permute-start.13 = (bf16[1024,128]{1,0:T(8,128)(2,1)S(1)}, bf16[1024,128]{1,0:T(8,128)(2,1)S(1)}, u32[]{:S(2)}, u32[]{:S(2)}) collective-permute-start(bf16[1024,128]{1,0:T(8,128)(2,1)S(1)} %copy-done.2), channel_id=1, source_target_pairs={{0,1},{1,0},{2,3},{3,2},{4,5},{5,4},{6,7},{7,6},{8,9},{9,8},{10,11... | collective-permute-start | bytes 786440 | tf_op jit(solution)/shard_map/ppermute | solution.py:225
  92.7 1.9 %fusion.54 = f32[1024,1024]{1,0:T(8,128)S(1)} fusion(bf16[1024,256]{1,0:T(8,128)(2,1)} %collective-permute-done.9, bf16[4096,1024]{1,0:T(8,128)(2,1)} %param.11, s32[]{:T(128)S(6)} %select_n.37), kind=kOutput, calls=%fused_computation.91 | convolution fusion | flops 536870912 | bytes 5242884 | tf_op jit(solution)/shard_map/dot_general | solution.py:217
  94.7 1.8 %fusion.52 = f32[1024,1024]{1,0:T(8,128)S(1)} fusion(bf16[1024,256]{1,0:T(8,128)(2,1)} %collective-permute-done.11, bf16[4096,1024]{1,0:T(8,128)(2,1)S(1)} %bitcast.108, s32[]{:T(128)S(6)} %select_n.38), kind=kOutput, calls=%fused_computation.89 | convolution fusion | flops 536870912 | bytes 5242884 | tf_op jit(solution)/shard_map/dot_general | solution.py:217
  96.4 4.3 %fusion.16 = f32[1024,1024]{1,0:T(8,128)} fusion(bf16[1024,1024]{1,0:T(8,128)(2,1)S(1)} %pad_maximum_fusion, bf16[4096,1024]{1,0:T(8,128)(2,1)S(1)} %bitcast.108, s32[]{:T(128)S(6)} %select_n.35), kind=kOutput, calls=%fused_computation.37 | convolution fusion | flops 2147483648 | bytes 8388612 | tf_op jit(solution)/shard_map/dot_general | solution.py:228
  102.9 4.3 %fusion.14 = f32[1024,1024]{1,0:T(8,128)} fusion(bf16[1024,1024]{1,0:T(8,128)(2,1)S(1)} %collective-permute-done.12, bf16[4096,1024]{1,0:T(8,128)(2,1)S(1)} %bitcast.108, s32[]{:T(128)S(6)} %select_n.39), kind=kOutput, calls=%fused_computation.35 | convolution fusion | flops 2147483648 | bytes 8388612 | tf_op jit(solution)/shard_map/dot_general | solution.py:231
  107.2 8.2 %add_add_fusion = f32[1024,1024]{1,0:T(8,128)} fusion(f32[1024,1024]{1,0:T(8,128)S(1)} %fusion.50, f32[1024,1024]{1,0:T(8,128)S(1)} %fusion.58, f32[1024,1024]{1,0:T(8,128)} %fusion.14, f32[1024,1024]{1,0:T(8,128)S(1)} %fusion.52, f32[1024,1024]{1,0:T(8,128)S(1)} %fusion.54, f32[1024,1024]{1,0:T(8,128)} %fusion.16, f32[1024,1024]{1,0:T(8,128)S(1)} %fusion.60, ...), kind=kOutput, calls=%fused_computation.25 | convolution fusion | flops 544210944 | bytes 34603012 | tf_op jit(solution)/shard_map/dot_general | solution.py:217
  115.8 2.8 %fusion.36 = f32[1024,1024]{1,0:T(8,128)S(1)} fusion(bf16[1024,384]{1,0:T(8,128)(2,1)} %collective-permute-done.10, bf16[4096,1024]{1,0:T(8,128)(2,1)} %param.11, s32[]{:T(128)S(6)} %select_n.43), kind=kOutput, calls=%fused_computation.71 | convolution fusion | flops 805306368 | bytes 5767172 | tf_op jit(solution)/shard_map/dot_general | solution.py:217
  118.6 3.7 %add_convert_fusion = bf16[1024,1024]{1,0:T(8,128)(2,1)} fusion(f32[1024,1024]{1,0:T(8,128)S(1)} %copy-done, f32[1024,1024]{1,0:T(8,128)S(1)} %fusion.36, bf16[1024,384]{1,0:T(8,128)(2,1)S(1)} %collective-permute-done.16, bf16[4096,1024]{1,0:T(8,128)(2,1)} %param.11, s32[]{:T(128)S(6)} %select_n.44), kind=kOutput, calls=%fused_computation.24 | convolution fusion | flops 808452096 | bytes 12058628 | tf_op jit(solution)/shard_map/dot_general | solution.py:217
  (58 shorter events, 11.5 us)
Async XLA Ops:
  0.8 8.6 %collective-permute-start = (bf16[3,2,1024]{2,1,0:T(2,128)(2,1)S(1)}, bf16[3,2,1024]{2,1,0:T(2,128)(2,1)S(1)}, u32[]{:S(2)}, u32[]{:S(2)}) collective-permute-start(bf16[3,2,1024]{2,1,0:T(2,128)(2,1)S(1)} %slice.174), channel_id=1, source_target_pairs={{0,4},{4,8},{8,12},{12,16},{16,20},{20,24},{24,28},{1,5},{5,9},{9,... | collective-permute-start | bytes 36872 | tf_op jit(solution)/shard_map/ppermute | solution.py:15
  18.2 28.6 %copy-start.3 = (f32[16,1024]{1,0:T(8,128)S(1)}, f32[16,1024]{1,0:T(8,128)}, u32[]{:S(2)}) copy-start(f32[16,1024]{1,0:T(8,128)} %param.8) | copy-start | bytes 196612
  29.0 11.8 %collective-permute-start.7 = (f32[16,1024]{1,0:T(8,128)S(1)}, f32[16,1024]{1,0:T(8,128)S(1)}, u32[]{:S(2)}, u32[]{:S(2)}) collective-permute-start(f32[16,1024]{1,0:T(8,128)S(1)} %multiply_reduce_fusion.1), channel_id=1, source_target_pairs={{0,28},{1,29},{2,30},{3,31}} | collective-permute-start | bytes 196616 | tf_op jit(solution)/shard_map/ppermute | solution.py:15
  33.3 9.1 %collective-permute-start.6 = (f32[16,1024]{1,0:T(8,128)S(1)}, f32[16,1024]{1,0:T(8,128)S(1)}, u32[]{:S(2)}, u32[]{:S(2)}) collective-permute-start(f32[16,1024]{1,0:T(8,128)S(1)} %multiply_reduce_fusion.1), channel_id=1, source_target_pairs={{0,24},{4,28},{1,25},{5,29},{2,26},{6,30},{3,27},{7,31}} | collective-permute-start | bytes 196616 | tf_op jit(solution)/shard_map/ppermute | solution.py:15
  34.9 11.8 %collective-permute-start.5 = (f32[16,1024]{1,0:T(8,128)S(1)}, f32[16,1024]{1,0:T(8,128)S(1)}, u32[]{:S(2)}, u32[]{:S(2)}) collective-permute-start(f32[16,1024]{1,0:T(8,128)S(1)} %multiply_reduce_fusion.1), channel_id=1, source_target_pairs={{0,20},{4,24},{8,28},{1,21},{5,25},{9,29},{2,22},{6,26},{10,30},{3... | collective-permute-start | bytes 196616 | tf_op jit(solution)/shard_map/ppermute | solution.py:15
  36.2 10.5 %collective-permute-start.4 = (f32[16,1024]{1,0:T(8,128)S(1)}, f32[16,1024]{1,0:T(8,128)S(1)}, u32[]{:S(2)}, u32[]{:S(2)}) collective-permute-start(f32[16,1024]{1,0:T(8,128)S(1)} %multiply_reduce_fusion.1), channel_id=1, source_target_pairs={{0,16},{4,20},{8,24},{12,28},{1,17},{5,21},{9,25},{13,29},{2,18},{... | collective-permute-start | bytes 196616 | tf_op jit(solution)/shard_map/ppermute | solution.py:15
  37.5 9.2 %collective-permute-start.3 = (f32[16,1024]{1,0:T(8,128)S(1)}, f32[16,1024]{1,0:T(8,128)S(1)}, u32[]{:S(2)}, u32[]{:S(2)}) collective-permute-start(f32[16,1024]{1,0:T(8,128)S(1)} %multiply_reduce_fusion.1), channel_id=1, source_target_pairs={{0,12},{4,16},{8,20},{12,24},{16,28},{1,13},{5,17},{9,21},{13,25},... | collective-permute-start | bytes 196616 | tf_op jit(solution)/shard_map/ppermute | solution.py:15
  40.8 10.9 %slice-start.2 = ((f32[1024]{0:T(1024)}), f32[128]{0:T(128)S(1)}, s32[]{:S(2)}) async-start(f32[1024]{0:T(1024)} %param.10), calls=%async_computation.2 | async-start | bytes 1024 | tf_op jit(solution)/shard_map/slice | solution.py:190
  40.8 5.9 %collective-permute-start.2 = (f32[16,1024]{1,0:T(8,128)S(1)}, f32[16,1024]{1,0:T(8,128)S(1)}, u32[]{:S(2)}, u32[]{:S(2)}) collective-permute-start(f32[16,1024]{1,0:T(8,128)S(1)} %multiply_reduce_fusion.1), channel_id=1, source_target_pairs={{0,8},{4,12},{8,16},{12,20},{16,24},{20,28},{1,9},{5,13},{9,17},{1... | collective-permute-start | bytes 196616 | tf_op jit(solution)/shard_map/ppermute | solution.py:15
  42.4 4.4 %collective-permute-start.1 = (f32[16,1024]{1,0:T(8,128)S(1)}, f32[16,1024]{1,0:T(8,128)S(1)}, u32[]{:S(2)}, u32[]{:S(2)}) collective-permute-start(f32[16,1024]{1,0:T(8,128)S(1)} %multiply_reduce_fusion.1), channel_id=1, source_target_pairs={{0,4},{4,8},{8,12},{12,16},{16,20},{20,24},{24,28},{1,5},{5,9},{9,... | collective-permute-start | bytes 196616 | tf_op jit(solution)/shard_map/ppermute | solution.py:15
  53.4 10.3 %collective-permute-start.8 = (bf16[1024,128]{1,0:T(8,128)(2,1)S(1)}, bf16[1024,128]{1,0:T(8,128)(2,1)S(1)}, u32[]{:S(2)}, u32[]{:S(2)}) collective-permute-start(bf16[1024,128]{1,0:T(8,128)(2,1)S(1)} %fusion.44), channel_id=1, source_target_pairs={{0,2},{1,3},{2,0},{3,1},{4,6},{5,7},{6,4},{7,5},{8,10},{9,11},{10,... | collective-permute-start | bytes 786440 | tf_op jit(solution)/shard_map/ppermute | solution.py:197
  60.2 2.7 %copy-start.4 = (f32[1024]{0:T(1024)S(1)}, f32[1024]{0:T(1024)}, u32[]{:S(2)}) copy-start(f32[1024]{0:T(1024)} %param.10) | copy-start | bytes 12292
  62.6 10.9 %collective-permute-start.9 = (bf16[1024,256]{1,0:T(8,128)(2,1)S(1)}, bf16[1024,256]{1,0:T(8,128)(2,1)}, u32[]{:S(2)}, u32[]{:S(2)}) collective-permute-start(bf16[1024,256]{1,0:T(8,128)(2,1)S(1)} %fusion.24), channel_id=1, source_target_pairs={{0,2},{1,3},{2,0},{3,1},{4,6},{5,7},{6,4},{7,5},{8,10},{9,11},{10,... | collective-permute-start | bytes 1572872 | tf_op jit(solution)/shard_map/ppermute | solution.py:197
  63.7 5.6 %copy-start.1 = (bf16[1024,128]{1,0:T(8,128)(2,1)}, bf16[1024,128]{1,0:T(8,128)(2,1)S(1)}, u32[]{:S(2)}) copy-start(bf16[1024,128]{1,0:T(8,128)(2,1)S(1)} %collective-permute-done.8) | copy-start | bytes 786436
  71.8 15.0 %collective-permute-start.11 = (bf16[1024,256]{1,0:T(8,128)(2,1)S(1)}, bf16[1024,256]{1,0:T(8,128)(2,1)}, u32[]{:S(2)}, u32[]{:S(2)}) collective-permute-start(bf16[1024,256]{1,0:T(8,128)(2,1)S(1)} %fusion.28), channel_id=1, source_target_pairs={{0,2},{1,3},{2,0},{3,1},{4,6},{5,7},{6,4},{7,5},{8,10},{9,11},{10,... | collective-permute-start | bytes 1572872 | tf_op jit(solution)/shard_map/ppermute | solution.py:197
  80.9 6.0 %copy-start.2 = (bf16[1024,128]{1,0:T(8,128)(2,1)S(1)}, bf16[1024,128]{1,0:T(8,128)(2,1)}, u32[]{:S(2)}) copy-start(bf16[1024,128]{1,0:T(8,128)(2,1)} %copy-done.1) | copy-start | bytes 786436
  80.9 13.8 %slice-start = ((s8[8388608]{0:T(1024)(128)(4,1)}), s8[4194304]{0:T(1024)(128)(4,1)S(1)}, s32[]{:S(2)}) async-start(s8[8388608]{0:T(1024)(128)(4,1)} %bitcast.107), calls=%async_computation | async-start | bytes 8388608
  85.0 9.7 %slice-start.1 = ((s8[8388608]{0:T(1024)(128)(4,1)}), s8[4194304]{0:T(1024)(128)(4,1)S(1)}, s32[]{:S(2)}) async-start(s8[8388608]{0:T(1024)(128)(4,1)} %bitcast.107), calls=%async_computation.1 | async-start | bytes 8388608
  85.0 30.4 %collective-permute-start.10 = (bf16[1024,384]{1,0:T(8,128)(2,1)}, bf16[1024,384]{1,0:T(8,128)(2,1)}, u32[]{:S(2)}, u32[]{:S(2)}) collective-permute-start(bf16[1024,384]{1,0:T(8,128)(2,1)} %fusion.20), channel_id=1, source_target_pairs={{0,2},{1,3},{2,0},{3,1},{4,6},{5,7},{6,4},{7,5},{8,10},{9,11},{10,... | collective-permute-start | bytes 2359304 | tf_op jit(solution)/shard_map/ppermute | solution.py:197
  86.8 14.6 %collective-permute-start.13 = (bf16[1024,128]{1,0:T(8,128)(2,1)S(1)}, bf16[1024,128]{1,0:T(8,128)(2,1)S(1)}, u32[]{:S(2)}, u32[]{:S(2)}) collective-permute-start(bf16[1024,128]{1,0:T(8,128)(2,1)S(1)} %copy-done.2), channel_id=1, source_target_pairs={{0,1},{1,0},{2,3},{3,2},{4,5},{5,4},{6,7},{7,6},{8,9},{9,8},{10,11... | collective-permute-start | bytes 786440 | tf_op jit(solution)/shard_map/ppermute | solution.py:225
  92.2 10.0 %collective-permute-start.14 = (bf16[1024,256]{1,0:T(8,128)(2,1)}, bf16[1024,256]{1,0:T(8,128)(2,1)S(1)}, u32[]{:S(2)}, u32[]{:S(2)}) collective-permute-start(bf16[1024,256]{1,0:T(8,128)(2,1)} %collective-permute-done.9), channel_id=1, source_target_pairs={{0,1},{1,0},{2,3},{3,2},{4,5},{5,4},{6,7},{7,6},{8,9},{9,8},{10,11... | collective-permute-start | bytes 1572872 | tf_op jit(solution)/shard_map/ppermute | solution.py:225
  92.2 15.0 %collective-permute-start.15 = (bf16[1024,256]{1,0:T(8,128)(2,1)}, bf16[1024,256]{1,0:T(8,128)(2,1)}, u32[]{:S(2)}, u32[]{:S(2)}) collective-permute-start(bf16[1024,256]{1,0:T(8,128)(2,1)} %collective-permute-done.11), channel_id=1, source_target_pairs={{0,1},{1,0},{2,3},{3,2},{4,5},{5,4},{6,7},{7,6},{8,9},{9,8},{10,11... | collective-permute-start | bytes 1572872 | tf_op jit(solution)/shard_map/ppermute | solution.py:225
  92.7 10.2 %collective-permute-start.12 = (bf16[1024,1024]{1,0:T(8,128)(2,1)S(1)}, bf16[1024,1024]{1,0:T(8,128)(2,1)S(1)}, u32[]{:S(2)}, u32[]{:S(2)}) collective-permute-start(bf16[1024,1024]{1,0:T(8,128)(2,1)S(1)} %pad_maximum_fusion), channel_id=1, source_target_pairs={{0,1},{1,0},{2,3},{3,2},{4,5},{5,4},{6,7},{7,6},{8,9},{9,8},{10,11... | collective-permute-start | bytes 6291464 | tf_op jit(solution)/shard_map/ppermute | solution.py:224
  115.4 3.2 %collective-permute-start.16 = (bf16[1024,384]{1,0:T(8,128)(2,1)}, bf16[1024,384]{1,0:T(8,128)(2,1)S(1)}, u32[]{:S(2)}, u32[]{:S(2)}) collective-permute-start(bf16[1024,384]{1,0:T(8,128)(2,1)} %collective-permute-done.10), channel_id=1, source_target_pairs={{0,1},{1,0},{2,3},{3,2},{4,5},{5,4},{6,7},{7,6},{8,9},{9,8},{10,11... | collective-permute-start | bytes 2359304 | tf_op jit(solution)/shard_map/ppermute | solution.py:236
  115.8 2.8 %copy-start = (f32[1024,1024]{1,0:T(8,128)S(1)}, f32[1024,1024]{1,0:T(8,128)}, u32[]{:S(2)}) copy-start(f32[1024,1024]{1,0:T(8,128)} %add_add_fusion) | copy-start | bytes 12582916

commit v13 on v11

--- a/solution.py
+++ b/solution.py
@@ -42,7 +42,7 @@
             y_ref[pl.ds(t, segments, stride=span), :] = total
         return tuple(updated)
 
-    states = lax.fori_loop(0, span, body, states, unroll=4)
+    states = lax.fori_loop(0, span, body, states, unroll=8)
     if end_ref is not None:
         for p in range(pole_count):
             end_ref[p] = states[p]

time: 117 us -> 115 us (0.983)
  Pallas kernels: 29.8 us -> 27.2 us
    pallas_call x3, Pallas kernels: 20.4 us -> 18.3 us  [run_recurrence(): pl.pallas_call(recurrence_kernel, grid=(group_count,), in_specs=[pl.Block...]
  transfers between devices with their start and end apart: 15 -> 15, of which waited for: 2 -> 2; matrix products, arithmetic and copies ran while one was open for 30% -> 31% of each run, Pallas kernels for 13% -> 12%
where the time goes in v13:
time: 115 us; the launch traced here: 114 us
  other arithmetic  27.4 us (24%)
  Pallas kernels  27.2 us (24%)
  starting transfers between devices  25.9 us (23%)
  matrix products  22.9 us (20%)
  waiting for transfers between devices  6.5 us (6%)
  local copies, waits for them, and re-layouts  3.38 us (3%)
    ppermute x8, starting transfers between devices, shifted(): lax.ppermute(value, axis, [(source, source + steps) for source in range(i...  19 us
    pallas_call x3, Pallas kernels, run_recurrence(): pl.pallas_call(recurrence_kernel, grid=(group_count,), in_specs=[pl.Block...  18.3 us
    dot_general x6, matrix products, part(): return jnp.dot(value, rows, preferred_element_type=jnp.float32)  16.7 us
    convert_element_type x3, other arithmetic, shards(): gated_mix = gated_mix.astype(jnp.bfloat16)  9.51 us
    pallas_call x1, Pallas kernels, run_end_state(): pl.pallas_call(end_state_kernel, grid=(width // LANES,), in_specs=[pl.Blo...  8.94 us
    convert_element_type x1, other arithmetic, shards(): x = mixed_input.astype(jnp.float32)  8.74 us
    ppermute x3, waiting for transfers between devices, shards(): lax.ppermute(gated_mix, 'ch', [(i, i ^ 2) for i in range(ch_count)])  6.44 us
    dot_general x1, matrix products, project_pieces(): total = total + jnp.dot(near, rows_near, preferred_element_type=jnp.float32)  3.94 us
  transfers between devices with their start and end apart: 15, of which 2 were waited for; matrix products, arithmetic and copies ran while one was open for 31% of the time, Pallas kernels for 12%

profile of v13, /device:TPU:1, one launch (start us, length us, event | category | flops | bytes accessed | tf_op | source)
XLA Modules:
  0.0 113.6 jit_solution(431879828401965497)
XLA Ops:
  0.8 4.0 %collective-permute-start = (bf16[3,2,1024]{2,1,0:T(2,128)(2,1)S(1)}, bf16[3,2,1024]{2,1,0:T(2,128)(2,1)S(1)}, u32[]{:S(2)}, u32[]{:S(2)}) collective-permute-start(bf16[3,2,1024]{2,1,0:T(2,128)(2,1)S(1)} %slice.141), channel_id=1, source_target_pairs={{0,4},{4,8},{8,12},{12,16},{16,20},{20,24},{24,28},{1,5},{5,9},{9,... | collective-permute-start | bytes 36872 | tf_op jit(solution)/shard_map/ppermute | solution.py:15
  8.0 1.5 %fusion.62 = (f32[16,1024]{1,0:T(8,128)S(1)}, f32[16,1024]{1,0:T(8,128)}) fusion(f32[16,1024]{1,0:T(8,128)} %param.8), kind=kLoop, calls=%fused_computation.115 | loop fusion | flops 16384 | bytes 196608 | tf_op jit(solution)/shard_map/neg | solution.py:169
  9.5 8.7 %fusion.60 = (f32[1024,1024]{1,0:T(8,128)}, bf16[1024,1024]{1,0:T(8,128)(2,1)S(1)}) fusion(f32[1024]{0:T(1024)S(1)} %bitcast.91, f32[1024]{0:T(1024)S(1)} %bitcast.87, bf16[3,1024,1024]{2,1,0:T(8,128)(2,1)} %param.6, f32[1024]{0:T(1024)S(1)} %bitcast.88, f32[1024]{0:T(1024)S(1)} %bitcast.89, bf16[3,2,1024]{2,1,0:T(2,128)(2,1)S(1)} %collective-permute-done, ...), kind=kLoop, calls=%fused_computation.114 | loop fusion | flops 36700160 | bytes 16814080 | tf_op jit(solution)/shard_map/convert_element_type | solution.py:166
  18.2 8.9 %shard_map.64 = f32[16,8,1024]{2,1,0:T(8,128)} custom-call(f32[1024,1024]{1,0:T(8,128)} %get-tuple-element.19.x_ref, f32[16,1024]{1,0:T(8,128)} %get-tuple-element.36.decay_ref), custom_call_target="tpu_custom_call" | custom-call | tf_op jit(solution)/shard_map/pallas_call | solution.py:62
  27.2 1.3 %multiply_reduce_fusion.1 = f32[16,1024]{1,0:T(8,128)S(1)} fusion(f32[16,8,1024]{2,1,0:T(8,128)} %shard_map.64, f32[8]{0:T(128)S(1)} %subtract_multiply_fusion, f32[16,1024]{1,0:T(8,128)S(1)} %get-tuple-element.35), kind=kLoop, calls=%fused_computation.83 | loop fusion | flops 376832 | bytes 655392 | tf_op jit(solution)/shard_map/reduce_sum | solution.py:110
  28.5 4.3 %collective-permute-start.7 = (f32[16,1024]{1,0:T(8,128)S(1)}, f32[16,1024]{1,0:T(8,128)S(1)}, u32[]{:S(2)}, u32[]{:S(2)}) collective-permute-start(f32[16,1024]{1,0:T(8,128)S(1)} %multiply_reduce_fusion.1), channel_id=1, source_target_pairs={{0,28},{1,29},{2,30},{3,31}} | collective-permute-start | bytes 196616 | tf_op jit(solution)/shard_map/ppermute | solution.py:15
  32.8 1.6 %collective-permute-start.6 = (f32[16,1024]{1,0:T(8,128)S(1)}, f32[16,1024]{1,0:T(8,128)S(1)}, u32[]{:S(2)}, u32[]{:S(2)}) collective-permute-start(f32[16,1024]{1,0:T(8,128)S(1)} %multiply_reduce_fusion.1), channel_id=1, source_target_pairs={{0,24},{4,28},{1,25},{5,29},{2,26},{6,30},{3,27},{7,31}} | collective-permute-start | bytes 196616 | tf_op jit(solution)/shard_map/ppermute | solution.py:15
  34.4 1.3 %collective-permute-start.5 = (f32[16,1024]{1,0:T(8,128)S(1)}, f32[16,1024]{1,0:T(8,128)S(1)}, u32[]{:S(2)}, u32[]{:S(2)}) collective-permute-start(f32[16,1024]{1,0:T(8,128)S(1)} %multiply_reduce_fusion.1), channel_id=1, source_target_pairs={{0,20},{4,24},{8,28},{1,21},{5,25},{9,29},{2,22},{6,26},{10,30},{3... | collective-permute-start | bytes 196616 | tf_op jit(solution)/shard_map/ppermute | solution.py:15
  35.7 1.3 %collective-permute-start.4 = (f32[16,1024]{1,0:T(8,128)S(1)}, f32[16,1024]{1,0:T(8,128)S(1)}, u32[]{:S(2)}, u32[]{:S(2)}) collective-permute-start(f32[16,1024]{1,0:T(8,128)S(1)} %multiply_reduce_fusion.1), channel_id=1, source_target_pairs={{0,16},{4,20},{8,24},{12,28},{1,17},{5,21},{9,25},{13,29},{2,18},{... | collective-permute-start | bytes 196616 | tf_op jit(solution)/shard_map/ppermute | solution.py:15
  37.0 1.9 %collective-permute-start.3 = (f32[16,1024]{1,0:T(8,128)S(1)}, f32[16,1024]{1,0:T(8,128)S(1)}, u32[]{:S(2)}, u32[]{:S(2)}) collective-permute-start(f32[16,1024]{1,0:T(8,128)S(1)} %multiply_reduce_fusion.1), channel_id=1, source_target_pairs={{0,12},{4,16},{8,20},{12,24},{16,28},{1,13},{5,17},{9,21},{13,25},... | collective-permute-start | bytes 196616 | tf_op jit(solution)/shard_map/ppermute | solution.py:15
  38.9 1.4 %copy.15 = f32[16,1024,8]{1,0,2:T(8,128)S(1)} copy(f32[16,1024,8]{1,2,0:T(8,128)} %bitcast.83) | data formatting | bytes 1048576
  40.3 1.6 %collective-permute-start.2 = (f32[16,1024]{1,0:T(8,128)S(1)}, f32[16,1024]{1,0:T(8,128)S(1)}, u32[]{:S(2)}, u32[]{:S(2)}) collective-permute-start(f32[16,1024]{1,0:T(8,128)S(1)} %multiply_reduce_fusion.1), channel_id=1, source_target_pairs={{0,8},{4,12},{8,16},{12,20},{16,24},{20,28},{1,9},{5,13},{9,17},{1... | collective-permute-start | bytes 196616 | tf_op jit(solution)/shard_map/ppermute | solution.py:15
  41.9 3.1 %collective-permute-start.1 = (f32[16,1024]{1,0:T(8,128)S(1)}, f32[16,1024]{1,0:T(8,128)S(1)}, u32[]{:S(2)}, u32[]{:S(2)}) collective-permute-start(f32[16,1024]{1,0:T(8,128)S(1)} %multiply_reduce_fusion.1), channel_id=1, source_target_pairs={{0,4},{4,8},{8,12},{12,16},{16,20},{20,24},{24,28},{1,5},{5,9},{9,... | collective-permute-start | bytes 196616 | tf_op jit(solution)/shard_map/ppermute | solution.py:15
  45.0 1.2 %multiply_reduce_fusion = f32[16,1024,8]{1,0,2:T(8,128)S(1)} fusion(f32[16,1024,8]{1,0,2:T(8,128)S(1)} %copy.15, f32[8,8]{1,0:T(8,128)S(1)} %maximum_multiply_fusion, f32[16,1024]{1,0:T(8,128)S(1)} %get-tuple-element.35, pred[8,8]{1,0:T(8,128)(4,1)S(1)} %iota_compare_fusion), kind=kLoop, calls=%fused_computation.21 | loop fusion | flops 4063232 | bytes 1114432
  47.6 5.0 %shard_map.65 = f32[1024,256]{1,0:T(8,128)} custom-call(f32[1024,1024]{1,0:T(8,128)} %get-tuple-element.19.x_ref, f32[16,1024]{1,0:T(8,128)} %get-tuple-element.36.decay_ref, f32[16,1024]{1,0:T(8,128)} %residue_ref.5, f32[16,8,1024]{2,1,0:T(8,128)} %bitcast_add_fusion.start_ref), custom_call_target="tpu_custom_call" | custom-call | tf_op jit(solution)/shard_map/pallas_call | solution.py:78
  52.5 2.4 %fusion.28 = bf16[1024,256]{1,0:T(8,128)(2,1)S(1)} fusion(bf16[1024,1024]{1,0:T(8,128)(2,1)S(1)} %get-tuple-element.34, bf16[3,1024,1024]{2,1,0:T(8,128)(2,1)} %param.6, bf16[3,2,1024]{2,1,0:T(2,128)(2,1)S(1)} %collective-permute-done, f32[256]{0:T(256)S(1)} %slice-done.2, f32[1024,256]{1,0:T(8,128)} %shard_map.65, f32[256]{0:T(256)S(1)} %bitcast.93, ...), kind=kLoop, calls=%fused_computation.59 | loop fusion | flops 6029312 | bytes 8929280 | tf_op jit(solution)/shard_map/convert_element_type | solution.py:192
  55.0 1.3 %collective-permute-start.8 = (bf16[1024,256]{1,0:T(8,128)(2,1)S(1)}, bf16[1024,256]{1,0:T(8,128)(2,1)S(1)}, u32[]{:S(2)}, u32[]{:S(2)}) collective-permute-start(bf16[1024,256]{1,0:T(8,128)(2,1)S(1)} %fusion.28), channel_id=1, source_target_pairs={{0,2},{1,3},{2,0},{3,1},{4,6},{5,7},{6,4},{7,5},{8,10},{9,11},{10,... | collective-permute-start | bytes 1572872 | tf_op jit(solution)/shard_map/ppermute | solution.py:197
  56.3 6.6 %shard_map.66 = f32[1024,384]{1,0:T(8,128)} custom-call(f32[1024,1024]{1,0:T(8,128)} %get-tuple-element.19.x_ref, f32[16,1024]{1,0:T(8,128)} %get-tuple-element.36.decay_ref, f32[16,1024]{1,0:T(8,128)} %residue_ref.5, f32[16,8,1024]{2,1,0:T(8,128)} %bitcast_add_fusion.start_ref), custom_call_target="tpu_custom_call" | custom-call | tf_op jit(solution)/shard_map/pallas_call | solution.py:78
  62.8 4.0 %fusion.20 = bf16[1024,384]{1,0:T(8,128)(2,1)} fusion(bf16[1024,1024]{1,0:T(8,128)(2,1)S(1)} %get-tuple-element.34, f32[384]{0:T(512)S(1)} %get-tuple-element.46, f32[1024,384]{1,0:T(8,128)} %shard_map.66, f32[384]{0:T(512)S(1)} %get-tuple-element.28, f32[384]{0:T(512)S(1)} %get-tuple-element.29, bf16[3,1024,1024]{2,1,0:T(8,128)(2,1)} %param.6, ...), kind=kLoop, calls=%fused_computation.45 | loop fusion | flops 9043968 | bytes 10242048 | tf_op jit(solution)/shard_map/convert_element_type | solution.py:192
  67.0 6.8 %shard_map.67 = f32[1024,384]{1,0:T(8,128)} custom-call(f32[1024,1024]{1,0:T(8,128)} %get-tuple-element.19.x_ref, f32[16,1024]{1,0:T(8,128)} %get-tuple-element.36.decay_ref, f32[16,1024]{1,0:T(8,128)} %residue_ref.5, f32[16,8,1024]{2,1,0:T(8,128)} %bitcast_add_fusion.start_ref), custom_call_target="tpu_custom_call" | custom-call | tf_op jit(solution)/shard_map/pallas_call | solution.py:78
  73.8 3.1 %fusion.24 = bf16[1024,384]{1,0:T(8,128)(2,1)S(1)} fusion(bf16[1024,1024]{1,0:T(8,128)(2,1)S(1)} %get-tuple-element.34, f32[384]{0:T(512)S(1)} %get-tuple-element.47, f32[1024,384]{1,0:T(8,128)} %shard_map.67, f32[384]{0:T(512)S(1)} %get-tuple-element.31, f32[384]{0:T(512)S(1)} %get-tuple-element.32, bf16[3,1024,1024]{2,1,0:T(8,128)(2,1)} %param.6, ...), kind=kLoop, calls=%fused_computation.52 | loop fusion | flops 9043968 | bytes 10242048 | tf_op jit(solution)/shard_map/convert_element_type | solution.py:192
  76.9 1.4 %pad_maximum_fusion = bf16[1024,1024]{1,0:T(8,128)(2,1)S(1)} fusion(bf16[1024,384]{1,0:T(8,128)(2,1)S(1)} %fusion.24, bf16[1024,384]{1,0:T(8,128)(2,1)} %fusion.20, bf16[1024,256]{1,0:T(8,128)(2,1)S(1)} %fusion.28), kind=kLoop, calls=%fused_computation.37 | loop fusion | flops 6291456 | bytes 4194304 | tf_op jit(solution)/shard_map/concatenate | solution.py:220
  78.3 5.1 %collective-permute-done.10 = bf16[1024,384]{1,0:T(8,128)(2,1)} collective-permute-done((bf16[1024,384]{1,0:T(8,128)(2,1)}, bf16[1024,384]{1,0:T(8,128)(2,1)}, u32[]{:S(2)}, u32[]{:S(2)}) %collective-permute-start.10) | collective-permute-done | bytes 786464 | tf_op jit(solution)/shard_map/ppermute | solution.py:197
  83.5 3.6 %collective-permute-start.11 = (bf16[1024,1024]{1,0:T(8,128)(2,1)S(1)}, bf16[1024,1024]{1,0:T(8,128)(2,1)}, u32[]{:S(2)}, u32[]{:S(2)}) collective-permute-start(bf16[1024,1024]{1,0:T(8,128)(2,1)S(1)} %pad_maximum_fusion), channel_id=1, source_target_pairs={{0,1},{1,0},{2,3},{3,2},{4,5},{5,4},{6,7},{7,6},{8,9},{9,8},{10,11... | collective-permute-start | bytes 6291464 | tf_op jit(solution)/shard_map/ppermute | solution.py:224
  88.1 2.8 %fusion.44 = f32[1024,1024]{1,0:T(8,128)S(1)} fusion(bf16[1024,384]{1,0:T(8,128)(2,1)} %collective-permute-done.10, bf16[4096,1024]{1,0:T(8,128)(2,1)} %param.11, s32[]{:T(128)S(6)} %select_n.31), kind=kOutput, calls=%fused_computation.73 | convolution fusion | flops 805306368 | bytes 5767172 | tf_op jit(solution)/shard_map/dot_general | solution.py:217
  90.9 1.9 %fusion.50 = f32[1024,1024]{1,0:T(8,128)S(1)} fusion(bf16[1024,256]{1,0:T(8,128)(2,1)S(1)} %copy-done.2, bf16[4096,1024]{1,0:T(8,128)(2,1)} %param.11, s32[]{:T(128)S(6)} %select_n.30), kind=kOutput, calls=%fused_computation.81 | convolution fusion | flops 536870912 | bytes 5242884 | tf_op jit(solution)/shard_map/dot_general | solution.py:217
  93.2 2.3 %fusion.16 = f32[1024,1024]{1,0:T(8,128)S(1)} fusion(bf16[1024,1024]{1,0:T(8,128)(2,1)S(1)} %pad_maximum_fusion, bf16[4096,1024]{1,0:T(8,128)(2,1)S(1)} %bitcast.85, s32[]{:T(128)S(6)} %select_n.29), kind=kOutput, calls=%fused_computation.40 | convolution fusion | flops 2147483648 | bytes 8388612 | tf_op jit(solution)/shard_map/dot_general | solution.py:228
  96.3 3.9 %fusion.14 = f32[1024,1024]{1,0:T(8,128)S(1)} fusion(bf16[1024,1024]{1,0:T(8,128)(2,1)} %collective-permute-done.11, bf16[4096,1024]{1,0:T(8,128)(2,1)S(1)} %bitcast.85, s32[]{:T(128)S(6)} %select_n.32), kind=kOutput, calls=%fused_computation.38 | convolution fusion | flops 2147483648 | bytes 8388612 | tf_op jit(solution)/shard_map/dot_general | solution.py:231
  100.2 4.8 %add_add_fusion = f32[1024,1024]{1,0:T(8,128)} fusion(f32[1024,1024]{1,0:T(8,128)S(1)} %fusion.48, f32[1024,1024]{1,0:T(8,128)S(1)} %fusion.14, f32[1024,1024]{1,0:T(8,128)S(1)} %fusion.44, f32[1024,1024]{1,0:T(8,128)S(1)} %fusion.16, f32[1024,1024]{1,0:T(8,128)S(1)} %fusion.50, bf16[1024,384]{1,0:T(8,128)(2,1)S(1)} %collective-permute-done.13, ...), kind=kOutput, calls=%fused_computation.23 | convolution fusion | flops 810549248 | bytes 26738692 | tf_op jit(solution)/shard_map/dot_general | solution.py:217
  105.0 1.3 %collective-permute-done.9 = bf16[1024,384]{1,0:T(8,128)(2,1)} collective-permute-done((bf16[1024,384]{1,0:T(8,128)(2,1)S(1)}, bf16[1024,384]{1,0:T(8,128)(2,1)}, u32[]{:S(2)}, u32[]{:S(2)}) %collective-permute-start.9) | collective-permute-done | bytes 786464 | tf_op jit(solution)/shard_map/ppermute | solution.py:197
  107.1 2.8 %fusion.38 = f32[1024,1024]{1,0:T(8,128)S(1)} fusion(bf16[1024,384]{1,0:T(8,128)(2,1)} %collective-permute-done.9, bf16[4096,1024]{1,0:T(8,128)(2,1)} %param.11, s32[]{:T(128)S(6)} %select_n.35), kind=kOutput, calls=%fused_computation.69 | convolution fusion | flops 805306368 | bytes 5767172 | tf_op jit(solution)/shard_map/dot_general | solution.py:217
  109.9 3.7 %add_convert_fusion = bf16[1024,1024]{1,0:T(8,128)(2,1)} fusion(f32[1024,1024]{1,0:T(8,128)S(1)} %copy-done, f32[1024,1024]{1,0:T(8,128)S(1)} %fusion.38, bf16[1024,384]{1,0:T(8,128)(2,1)S(1)} %collective-permute-done.14, bf16[4096,1024]{1,0:T(8,128)(2,1)} %param.11, s32[]{:T(128)S(6)} %select_n.36), kind=kOutput, calls=%fused_computation.22 | convolution fusion | flops 808452096 | bytes 12058628 | tf_op jit(solution)/shard_map/dot_general | solution.py:217
  (46 shorter events, 8.6 us)
Async XLA Ops:
  0.8 8.7 %collective-permute-start = (bf16[3,2,1024]{2,1,0:T(2,128)(2,1)S(1)}, bf16[3,2,1024]{2,1,0:T(2,128)(2,1)S(1)}, u32[]{:S(2)}, u32[]{:S(2)}) collective-permute-start(bf16[3,2,1024]{2,1,0:T(2,128)(2,1)S(1)} %slice.141), channel_id=1, source_target_pairs={{0,4},{4,8},{8,12},{12,16},{16,20},{20,24},{24,28},{1,5},{5,9},{9,... | collective-permute-start | bytes 36872 | tf_op jit(solution)/shard_map/ppermute | solution.py:15
  18.2 28.1 %copy-start.3 = (f32[16,1024]{1,0:T(8,128)S(1)}, f32[16,1024]{1,0:T(8,128)}, u32[]{:S(2)}) copy-start(f32[16,1024]{1,0:T(8,128)} %param.8) | copy-start | bytes 196612
  28.5 11.8 %collective-permute-start.7 = (f32[16,1024]{1,0:T(8,128)S(1)}, f32[16,1024]{1,0:T(8,128)S(1)}, u32[]{:S(2)}, u32[]{:S(2)}) collective-permute-start(f32[16,1024]{1,0:T(8,128)S(1)} %multiply_reduce_fusion.1), channel_id=1, source_target_pairs={{0,28},{1,29},{2,30},{3,31}} | collective-permute-start | bytes 196616 | tf_op jit(solution)/shard_map/ppermute | solution.py:15
  32.8 9.1 %collective-permute-start.6 = (f32[16,1024]{1,0:T(8,128)S(1)}, f32[16,1024]{1,0:T(8,128)S(1)}, u32[]{:S(2)}, u32[]{:S(2)}) collective-permute-start(f32[16,1024]{1,0:T(8,128)S(1)} %multiply_reduce_fusion.1), channel_id=1, source_target_pairs={{0,24},{4,28},{1,25},{5,29},{2,26},{6,30},{3,27},{7,31}} | collective-permute-start | bytes 196616 | tf_op jit(solution)/shard_map/ppermute | solution.py:15
  34.4 11.8 %collective-permute-start.5 = (f32[16,1024]{1,0:T(8,128)S(1)}, f32[16,1024]{1,0:T(8,128)S(1)}, u32[]{:S(2)}, u32[]{:S(2)}) collective-permute-start(f32[16,1024]{1,0:T(8,128)S(1)} %multiply_reduce_fusion.1), channel_id=1, source_target_pairs={{0,20},{4,24},{8,28},{1,21},{5,25},{9,29},{2,22},{6,26},{10,30},{3... | collective-permute-start | bytes 196616 | tf_op jit(solution)/shard_map/ppermute | solution.py:15
  35.7 10.5 %collective-permute-start.4 = (f32[16,1024]{1,0:T(8,128)S(1)}, f32[16,1024]{1,0:T(8,128)S(1)}, u32[]{:S(2)}, u32[]{:S(2)}) collective-permute-start(f32[16,1024]{1,0:T(8,128)S(1)} %multiply_reduce_fusion.1), channel_id=1, source_target_pairs={{0,16},{4,20},{8,24},{12,28},{1,17},{5,21},{9,25},{13,29},{2,18},{... | collective-permute-start | bytes 196616 | tf_op jit(solution)/shard_map/ppermute | solution.py:15
  37.0 9.2 %collective-permute-start.3 = (f32[16,1024]{1,0:T(8,128)S(1)}, f32[16,1024]{1,0:T(8,128)S(1)}, u32[]{:S(2)}, u32[]{:S(2)}) collective-permute-start(f32[16,1024]{1,0:T(8,128)S(1)} %multiply_reduce_fusion.1), channel_id=1, source_target_pairs={{0,12},{4,16},{8,20},{12,24},{16,28},{1,13},{5,17},{9,21},{13,25},... | collective-permute-start | bytes 196616 | tf_op jit(solution)/shard_map/ppermute | solution.py:15
  40.3 6.0 %collective-permute-start.2 = (f32[16,1024]{1,0:T(8,128)S(1)}, f32[16,1024]{1,0:T(8,128)S(1)}, u32[]{:S(2)}, u32[]{:S(2)}) collective-permute-start(f32[16,1024]{1,0:T(8,128)S(1)} %multiply_reduce_fusion.1), channel_id=1, source_target_pairs={{0,8},{4,12},{8,16},{12,20},{16,24},{20,28},{1,9},{5,13},{9,17},{1... | collective-permute-start | bytes 196616 | tf_op jit(solution)/shard_map/ppermute | solution.py:15
  41.9 4.4 %collective-permute-start.1 = (f32[16,1024]{1,0:T(8,128)S(1)}, f32[16,1024]{1,0:T(8,128)S(1)}, u32[]{:S(2)}, u32[]{:S(2)}) collective-permute-start(f32[16,1024]{1,0:T(8,128)S(1)} %multiply_reduce_fusion.1), channel_id=1, source_target_pairs={{0,4},{4,8},{8,12},{12,16},{16,20},{20,24},{24,28},{1,5},{5,9},{9,... | collective-permute-start | bytes 196616 | tf_op jit(solution)/shard_map/ppermute | solution.py:15
  46.2 6.3 %slice-start.2 = ((f32[1024]{0:T(1024)}), f32[256]{0:T(256)S(1)}, s32[]{:S(2)}) async-start(f32[1024]{0:T(1024)} %param.10), calls=%async_computation.2 | async-start | bytes 2048 | tf_op jit(solution)/shard_map/slice | solution.py:190
  55.0 12.1 %collective-permute-start.8 = (bf16[1024,256]{1,0:T(8,128)(2,1)S(1)}, bf16[1024,256]{1,0:T(8,128)(2,1)S(1)}, u32[]{:S(2)}, u32[]{:S(2)}) collective-permute-start(bf16[1024,256]{1,0:T(8,128)(2,1)S(1)} %fusion.28), channel_id=1, source_target_pairs={{0,2},{1,3},{2,0},{3,1},{4,6},{5,7},{6,4},{7,5},{8,10},{9,11},{10,... | collective-permute-start | bytes 1572872 | tf_op jit(solution)/shard_map/ppermute | solution.py:197
  66.8 16.7 %collective-permute-start.10 = (bf16[1024,384]{1,0:T(8,128)(2,1)}, bf16[1024,384]{1,0:T(8,128)(2,1)}, u32[]{:S(2)}, u32[]{:S(2)}) collective-permute-start(bf16[1024,384]{1,0:T(8,128)(2,1)} %fusion.20), channel_id=1, source_target_pairs={{0,2},{1,3},{2,0},{3,1},{4,6},{5,7},{6,4},{7,5},{8,10},{9,11},{10,... | collective-permute-start | bytes 2359304 | tf_op jit(solution)/shard_map/ppermute | solution.py:197
  67.0 6.8 %copy-start.1 = (bf16[1024,256]{1,0:T(8,128)(2,1)}, bf16[1024,256]{1,0:T(8,128)(2,1)S(1)}, u32[]{:S(2)}) copy-start(bf16[1024,256]{1,0:T(8,128)(2,1)S(1)} %collective-permute-done.8) | copy-start | bytes 1572868
  78.3 12.5 %copy-start.2 = (bf16[1024,256]{1,0:T(8,128)(2,1)S(1)}, bf16[1024,256]{1,0:T(8,128)(2,1)}, u32[]{:S(2)}) copy-start(bf16[1024,256]{1,0:T(8,128)(2,1)} %copy-done.1) | copy-start | bytes 1572868
  83.5 12.8 %collective-permute-start.11 = (bf16[1024,1024]{1,0:T(8,128)(2,1)S(1)}, bf16[1024,1024]{1,0:T(8,128)(2,1)}, u32[]{:S(2)}, u32[]{:S(2)}) collective-permute-start(bf16[1024,1024]{1,0:T(8,128)(2,1)S(1)} %pad_maximum_fusion), channel_id=1, source_target_pairs={{0,1},{1,0},{2,3},{3,2},{4,5},{5,4},{6,7},{7,6},{8,9},{9,8},{10,11... | collective-permute-start | bytes 6291464 | tf_op jit(solution)/shard_map/ppermute | solution.py:224
  87.1 19.3 %collective-permute-start.9 = (bf16[1024,384]{1,0:T(8,128)(2,1)S(1)}, bf16[1024,384]{1,0:T(8,128)(2,1)}, u32[]{:S(2)}, u32[]{:S(2)}) collective-permute-start(bf16[1024,384]{1,0:T(8,128)(2,1)S(1)} %fusion.24), channel_id=1, source_target_pairs={{0,2},{1,3},{2,0},{3,1},{4,6},{5,7},{6,4},{7,5},{8,10},{9,11},{10,... | collective-permute-start | bytes 2359304 | tf_op jit(solution)/shard_map/ppermute | solution.py:197
  87.6 8.0 %collective-permute-start.12 = (bf16[1024,256]{1,0:T(8,128)(2,1)}, bf16[1024,256]{1,0:T(8,128)(2,1)S(1)}, u32[]{:S(2)}, u32[]{:S(2)}) collective-permute-start(bf16[1024,256]{1,0:T(8,128)(2,1)} %copy-done.1), channel_id=1, source_target_pairs={{0,1},{1,0},{2,3},{3,2},{4,5},{5,4},{6,7},{7,6},{8,9},{9,8},{10,11... | collective-permute-start | bytes 1572872 | tf_op jit(solution)/shard_map/ppermute | solution.py:225
  87.8 12.4 %collective-permute-start.13 = (bf16[1024,384]{1,0:T(8,128)(2,1)}, bf16[1024,384]{1,0:T(8,128)(2,1)S(1)}, u32[]{:S(2)}, u32[]{:S(2)}) collective-permute-start(bf16[1024,384]{1,0:T(8,128)(2,1)} %collective-permute-done.10), channel_id=1, source_target_pairs={{0,1},{1,0},{2,3},{3,2},{4,5},{5,4},{6,7},{7,6},{8,9},{9,8},{10,11... | collective-permute-start | bytes 2359304 | tf_op jit(solution)/shard_map/ppermute | solution.py:225
  88.1 4.7 %slice-start = ((s8[8388608]{0:T(1024)(128)(4,1)}), s8[4194304]{0:T(1024)(128)(4,1)S(1)}, s32[]{:S(2)}) async-start(s8[8388608]{0:T(1024)(128)(4,1)} %bitcast.84), calls=%async_computation | async-start | bytes 8388608
  90.8 2.4 %slice-start.1 = ((s8[8388608]{0:T(1024)(128)(4,1)}), s8[4194304]{0:T(1024)(128)(4,1)S(1)}, s32[]{:S(2)}) async-start(s8[8388608]{0:T(1024)(128)(4,1)} %bitcast.84), calls=%async_computation.1 | async-start | bytes 8388608
  106.3 3.6 %collective-permute-start.14 = (bf16[1024,384]{1,0:T(8,128)(2,1)}, bf16[1024,384]{1,0:T(8,128)(2,1)S(1)}, u32[]{:S(2)}, u32[]{:S(2)}) collective-permute-start(bf16[1024,384]{1,0:T(8,128)(2,1)} %collective-permute-done.9), channel_id=1, source_target_pairs={{0,1},{1,0},{2,3},{3,2},{4,5},{5,4},{6,7},{7,6},{8,9},{9,8},{10,11... | collective-permute-start | bytes 2359304 | tf_op jit(solution)/shard_map/ppermute | solution.py:236
  107.1 2.8 %copy-start = (f32[1024,1024]{1,0:T(8,128)S(1)}, f32[1024,1024]{1,0:T(8,128)}, u32[]{:S(2)}) copy-start(f32[1024,1024]{1,0:T(8,128)} %add_add_fusion) | copy-start | bytes 12582916

commit v14 on v13

--- a/solution.py
+++ b/solution.py
@@ -42,7 +42,7 @@
             y_ref[pl.ds(t, segments, stride=span), :] = total
         return tuple(updated)
 
-    states = lax.fori_loop(0, span, body, states, unroll=8)
+    states = lax.fori_loop(0, span, body, states, unroll=16)
     if end_ref is not None:
         for p in range(pole_count):
             end_ref[p] = states[p]

time: 115 us -> 114 us (level)
  Pallas kernels: 27.2 us -> 26 us
  transfers between devices with their start and end apart: 15 -> 15, of which waited for: 2 -> 2; matrix products, arithmetic and copies ran while one was open for 31% -> 31% of each run, Pallas kernels for 12% -> 11%
where the time goes in v14:
time: 114 us; the launch traced here: 113 us
  other arithmetic  27.4 us (24%)
  starting transfers between devices  26.3 us (23%)
  Pallas kernels  26 us (23%)
  matrix products  22.9 us (20%)
  waiting for transfers between devices  6.5 us (6%)
  local copies, waits for them, and re-layouts  3.37 us (3%)
    ppermute x8, starting transfers between devices, shifted(): lax.ppermute(value, axis, [(source, source + steps) for source in range(i...  19 us
    pallas_call x3, Pallas kernels, run_recurrence(): pl.pallas_call(recurrence_kernel, grid=(group_count,), in_specs=[pl.Block...  17.3 us
    dot_general x6, matrix products, part(): return jnp.dot(value, rows, preferred_element_type=jnp.float32)  16.7 us
    convert_element_type x3, other arithmetic, shards(): gated_mix = gated_mix.astype(jnp.bfloat16)  9.51 us
    convert_element_type x1, other arithmetic, shards(): x = mixed_input.astype(jnp.float32)  8.74 us
    pallas_call x1, Pallas kernels, run_end_state(): pl.pallas_call(end_state_kernel, grid=(width // LANES,), in_specs=[pl.Blo...  8.67 us
    ppermute x3, waiting for transfers between devices, shards(): lax.ppermute(gated_mix, 'ch', [(i, i ^ 2) for i in range(ch_count)])  6.44 us
    dot_general x1, matrix products, project_pieces(): total = total + jnp.dot(near, rows_near, preferred_element_type=jnp.float32)  3.94 us
  transfers between devices with their start and end apart: 15, of which 2 were waited for; matrix products, arithmetic and copies ran while one was open for 31% of the time, Pallas kernels for 11%

profile of v14, /device:TPU:1, one launch (start us, length us, event | category | flops | bytes accessed | tf_op | source)
XLA Modules:
  0.0 112.8 jit_solution(7729054474179324568)
XLA Ops:
  0.8 4.0 %collective-permute-start = (bf16[3,2,1024]{2,1,0:T(2,128)(2,1)S(1)}, bf16[3,2,1024]{2,1,0:T(2,128)(2,1)S(1)}, u32[]{:S(2)}, u32[]{:S(2)}) collective-permute-start(bf16[3,2,1024]{2,1,0:T(2,128)(2,1)S(1)} %slice.141), channel_id=1, source_target_pairs={{0,4},{4,8},{8,12},{12,16},{16,20},{20,24},{24,28},{1,5},{5,9},{9,... | collective-permute-start | bytes 36872 | tf_op jit(solution)/shard_map/ppermute | solution.py:15
  8.0 1.5 %fusion.62 = (f32[16,1024]{1,0:T(8,128)S(1)}, f32[16,1024]{1,0:T(8,128)}) fusion(f32[16,1024]{1,0:T(8,128)} %param.8), kind=kLoop, calls=%fused_computation.115 | loop fusion | flops 16384 | bytes 196608 | tf_op jit(solution)/shard_map/neg | solution.py:169
  9.5 8.7 %fusion.60 = (f32[1024,1024]{1,0:T(8,128)}, bf16[1024,1024]{1,0:T(8,128)(2,1)S(1)}) fusion(f32[1024]{0:T(1024)S(1)} %bitcast.91, f32[1024]{0:T(1024)S(1)} %bitcast.87, bf16[3,1024,1024]{2,1,0:T(8,128)(2,1)} %param.6, f32[1024]{0:T(1024)S(1)} %bitcast.88, f32[1024]{0:T(1024)S(1)} %bitcast.89, bf16[3,2,1024]{2,1,0:T(2,128)(2,1)S(1)} %collective-permute-done, ...), kind=kLoop, calls=%fused_computation.114 | loop fusion | flops 36700160 | bytes 16814080 | tf_op jit(solution)/shard_map/convert_element_type | solution.py:166
  18.2 8.7 %shard_map.64 = f32[16,8,1024]{2,1,0:T(8,128)} custom-call(f32[1024,1024]{1,0:T(8,128)} %get-tuple-element.19.x_ref, f32[16,1024]{1,0:T(8,128)} %get-tuple-element.36.decay_ref), custom_call_target="tpu_custom_call" | custom-call | tf_op jit(solution)/shard_map/pallas_call | solution.py:62
  26.9 1.3 %multiply_reduce_fusion.1 = f32[16,1024]{1,0:T(8,128)S(1)} fusion(f32[16,8,1024]{2,1,0:T(8,128)} %shard_map.64, f32[8]{0:T(128)S(1)} %subtract_multiply_fusion, f32[16,1024]{1,0:T(8,128)S(1)} %get-tuple-element.35), kind=kLoop, calls=%fused_computation.83 | loop fusion | flops 376832 | bytes 655392 | tf_op jit(solution)/shard_map/reduce_sum | solution.py:110
  28.2 4.3 %collective-permute-start.7 = (f32[16,1024]{1,0:T(8,128)S(1)}, f32[16,1024]{1,0:T(8,128)S(1)}, u32[]{:S(2)}, u32[]{:S(2)}) collective-permute-start(f32[16,1024]{1,0:T(8,128)S(1)} %multiply_reduce_fusion.1), channel_id=1, source_target_pairs={{0,28},{1,29},{2,30},{3,31}} | collective-permute-start | bytes 196616 | tf_op jit(solution)/shard_map/ppermute | solution.py:15
  32.6 1.6 %collective-permute-start.6 = (f32[16,1024]{1,0:T(8,128)S(1)}, f32[16,1024]{1,0:T(8,128)S(1)}, u32[]{:S(2)}, u32[]{:S(2)}) collective-permute-start(f32[16,1024]{1,0:T(8,128)S(1)} %multiply_reduce_fusion.1), channel_id=1, source_target_pairs={{0,24},{4,28},{1,25},{5,29},{2,26},{6,30},{3,27},{7,31}} | collective-permute-start | bytes 196616 | tf_op jit(solution)/shard_map/ppermute | solution.py:15
  34.1 1.3 %collective-permute-start.5 = (f32[16,1024]{1,0:T(8,128)S(1)}, f32[16,1024]{1,0:T(8,128)S(1)}, u32[]{:S(2)}, u32[]{:S(2)}) collective-permute-start(f32[16,1024]{1,0:T(8,128)S(1)} %multiply_reduce_fusion.1), channel_id=1, source_target_pairs={{0,20},{4,24},{8,28},{1,21},{5,25},{9,29},{2,22},{6,26},{10,30},{3... | collective-permute-start | bytes 196616 | tf_op jit(solution)/shard_map/ppermute | solution.py:15
  35.4 1.3 %collective-permute-start.4 = (f32[16,1024]{1,0:T(8,128)S(1)}, f32[16,1024]{1,0:T(8,128)S(1)}, u32[]{:S(2)}, u32[]{:S(2)}) collective-permute-start(f32[16,1024]{1,0:T(8,128)S(1)} %multiply_reduce_fusion.1), channel_id=1, source_target_pairs={{0,16},{4,20},{8,24},{12,28},{1,17},{5,21},{9,25},{13,29},{2,18},{... | collective-permute-start | bytes 196616 | tf_op jit(solution)/shard_map/ppermute | solution.py:15
  36.7 1.9 %collective-permute-start.3 = (f32[16,1024]{1,0:T(8,128)S(1)}, f32[16,1024]{1,0:T(8,128)S(1)}, u32[]{:S(2)}, u32[]{:S(2)}) collective-permute-start(f32[16,1024]{1,0:T(8,128)S(1)} %multiply_reduce_fusion.1), channel_id=1, source_target_pairs={{0,12},{4,16},{8,20},{12,24},{16,28},{1,13},{5,17},{9,21},{13,25},... | collective-permute-start | bytes 196616 | tf_op jit(solution)/shard_map/ppermute | solution.py:15
  38.7 1.4 %copy.15 = f32[16,1024,8]{1,0,2:T(8,128)S(1)} copy(f32[16,1024,8]{1,2,0:T(8,128)} %bitcast.83) | data formatting | bytes 1048576
  40.0 1.6 %collective-permute-start.2 = (f32[16,1024]{1,0:T(8,128)S(1)}, f32[16,1024]{1,0:T(8,128)S(1)}, u32[]{:S(2)}, u32[]{:S(2)}) collective-permute-start(f32[16,1024]{1,0:T(8,128)S(1)} %multiply_reduce_fusion.1), channel_id=1, source_target_pairs={{0,8},{4,12},{8,16},{12,20},{16,24},{20,28},{1,9},{5,13},{9,17},{1... | collective-permute-start | bytes 196616 | tf_op jit(solution)/shard_map/ppermute | solution.py:15
  41.6 3.1 %collective-permute-start.1 = (f32[16,1024]{1,0:T(8,128)S(1)}, f32[16,1024]{1,0:T(8,128)S(1)}, u32[]{:S(2)}, u32[]{:S(2)}) collective-permute-start(f32[16,1024]{1,0:T(8,128)S(1)} %multiply_reduce_fusion.1), channel_id=1, source_target_pairs={{0,4},{4,8},{8,12},{12,16},{16,20},{20,24},{24,28},{1,5},{5,9},{9,... | collective-permute-start | bytes 196616 | tf_op jit(solution)/shard_map/ppermute | solution.py:15
  44.7 1.2 %multiply_reduce_fusion = f32[16,1024,8]{1,0,2:T(8,128)S(1)} fusion(f32[16,1024,8]{1,0,2:T(8,128)S(1)} %copy.15, f32[8,8]{1,0:T(8,128)S(1)} %maximum_multiply_fusion, f32[16,1024]{1,0:T(8,128)S(1)} %get-tuple-element.35, pred[8,8]{1,0:T(8,128)(4,1)S(1)} %iota_compare_fusion), kind=kLoop, calls=%fused_computation.21 | loop fusion | flops 4063232 | bytes 1114432
  46.1 1.2 %bitcast_add_fusion.start_ref = f32[16,8,1024]{2,1,0:T(8,128)} fusion(f32[16,1024,8]{1,0,2:T(8,128)S(1)} %multiply_reduce_fusion, f32[16,1024]{1,0:T(8,128)S(1)} %multiply_add_fusion, f32[8]{0:T(128)S(1)} %convert_multiply_fusion.15, f32[16,1024]{1,0:T(8,128)S(1)} %get-tuple-element.35), kind=kLoop, calls=%fused_computation.78 | loop fusion | flops 393216 | bytes 1179680 | tf_op jit(solution)/shard_map/add | solution.py:103
  47.3 4.7 %shard_map.65 = f32[1024,256]{1,0:T(8,128)} custom-call(f32[1024,1024]{1,0:T(8,128)} %get-tuple-element.19.x_ref, f32[16,1024]{1,0:T(8,128)} %get-tuple-element.36.decay_ref, f32[16,1024]{1,0:T(8,128)} %residue_ref.5, f32[16,8,1024]{2,1,0:T(8,128)} %bitcast_add_fusion.start_ref), custom_call_target="tpu_custom_call" | custom-call | tf_op jit(solution)/shard_map/pallas_call | solution.py:78
  52.0 2.4 %fusion.28 = bf16[1024,256]{1,0:T(8,128)(2,1)S(1)} fusion(bf16[1024,1024]{1,0:T(8,128)(2,1)S(1)} %get-tuple-element.34, bf16[3,1024,1024]{2,1,0:T(8,128)(2,1)} %param.6, bf16[3,2,1024]{2,1,0:T(2,128)(2,1)S(1)} %collective-permute-done, f32[256]{0:T(256)S(1)} %slice-done.2, f32[1024,256]{1,0:T(8,128)} %shard_map.65, f32[256]{0:T(256)S(1)} %bitcast.93, ...), kind=kLoop, calls=%fused_computation.59 | loop fusion | flops 6029312 | bytes 8929280 | tf_op jit(solution)/shard_map/convert_element_type | solution.py:192
  54.5 1.3 %collective-permute-start.8 = (bf16[1024,256]{1,0:T(8,128)(2,1)S(1)}, bf16[1024,256]{1,0:T(8,128)(2,1)S(1)}, u32[]{:S(2)}, u32[]{:S(2)}) collective-permute-start(bf16[1024,256]{1,0:T(8,128)(2,1)S(1)} %fusion.28), channel_id=1, source_target_pairs={{0,2},{1,3},{2,0},{3,1},{4,6},{5,7},{6,4},{7,5},{8,10},{9,11},{10,... | collective-permute-start | bytes 1572872 | tf_op jit(solution)/shard_map/ppermute | solution.py:197
  55.7 6.2 %shard_map.66 = f32[1024,384]{1,0:T(8,128)} custom-call(f32[1024,1024]{1,0:T(8,128)} %get-tuple-element.19.x_ref, f32[16,1024]{1,0:T(8,128)} %get-tuple-element.36.decay_ref, f32[16,1024]{1,0:T(8,128)} %residue_ref.5, f32[16,8,1024]{2,1,0:T(8,128)} %bitcast_add_fusion.start_ref), custom_call_target="tpu_custom_call" | custom-call | tf_op jit(solution)/shard_map/pallas_call | solution.py:78
  61.9 4.0 %fusion.20 = bf16[1024,384]{1,0:T(8,128)(2,1)} fusion(bf16[1024,1024]{1,0:T(8,128)(2,1)S(1)} %get-tuple-element.34, f32[384]{0:T(512)S(1)} %get-tuple-element.46, f32[1024,384]{1,0:T(8,128)} %shard_map.66, f32[384]{0:T(512)S(1)} %get-tuple-element.28, f32[384]{0:T(512)S(1)} %get-tuple-element.29, bf16[3,1024,1024]{2,1,0:T(8,128)(2,1)} %param.6, ...), kind=kLoop, calls=%fused_computation.45 | loop fusion | flops 9043968 | bytes 10242048 | tf_op jit(solution)/shard_map/convert_element_type | solution.py:192
  66.2 6.4 %shard_map.67 = f32[1024,384]{1,0:T(8,128)} custom-call(f32[1024,1024]{1,0:T(8,128)} %get-tuple-element.19.x_ref, f32[16,1024]{1,0:T(8,128)} %get-tuple-element.36.decay_ref, f32[16,1024]{1,0:T(8,128)} %residue_ref.5, f32[16,8,1024]{2,1,0:T(8,128)} %bitcast_add_fusion.start_ref), custom_call_target="tpu_custom_call" | custom-call | tf_op jit(solution)/shard_map/pallas_call | solution.py:78
  72.6 3.1 %fusion.24 = bf16[1024,384]{1,0:T(8,128)(2,1)S(1)} fusion(bf16[1024,1024]{1,0:T(8,128)(2,1)S(1)} %get-tuple-element.34, f32[384]{0:T(512)S(1)} %get-tuple-element.47, f32[1024,384]{1,0:T(8,128)} %shard_map.67, f32[384]{0:T(512)S(1)} %get-tuple-element.31, f32[384]{0:T(512)S(1)} %get-tuple-element.32, bf16[3,1024,1024]{2,1,0:T(8,128)(2,1)} %param.6, ...), kind=kLoop, calls=%fused_computation.52 | loop fusion | flops 9043968 | bytes 10242048 | tf_op jit(solution)/shard_map/convert_element_type | solution.py:192
  75.7 1.4 %pad_maximum_fusion = bf16[1024,1024]{1,0:T(8,128)(2,1)S(1)} fusion(bf16[1024,384]{1,0:T(8,128)(2,1)S(1)} %fusion.24, bf16[1024,384]{1,0:T(8,128)(2,1)} %fusion.20, bf16[1024,256]{1,0:T(8,128)(2,1)S(1)} %fusion.28), kind=kLoop, calls=%fused_computation.37 | loop fusion | flops 6291456 | bytes 4194304 | tf_op jit(solution)/shard_map/concatenate | solution.py:220
  77.1 5.5 %collective-permute-done.10 = bf16[1024,384]{1,0:T(8,128)(2,1)} collective-permute-done((bf16[1024,384]{1,0:T(8,128)(2,1)}, bf16[1024,384]{1,0:T(8,128)(2,1)}, u32[]{:S(2)}, u32[]{:S(2)}) %collective-permute-start.10) | collective-permute-done | bytes 786464 | tf_op jit(solution)/shard_map/ppermute | solution.py:197
  82.6 3.6 %collective-permute-start.11 = (bf16[1024,1024]{1,0:T(8,128)(2,1)S(1)}, bf16[1024,1024]{1,0:T(8,128)(2,1)}, u32[]{:S(2)}, u32[]{:S(2)}) collective-permute-start(bf16[1024,1024]{1,0:T(8,128)(2,1)S(1)} %pad_maximum_fusion), channel_id=1, source_target_pairs={{0,1},{1,0},{2,3},{3,2},{4,5},{5,4},{6,7},{7,6},{8,9},{9,8},{10,11... | collective-permute-start | bytes 6291464 | tf_op jit(solution)/shard_map/ppermute | solution.py:224
  87.6 2.8 %fusion.44 = f32[1024,1024]{1,0:T(8,128)S(1)} fusion(bf16[1024,384]{1,0:T(8,128)(2,1)} %collective-permute-done.10, bf16[4096,1024]{1,0:T(8,128)(2,1)} %param.11, s32[]{:T(128)S(6)} %select_n.31), kind=kOutput, calls=%fused_computation.73 | convolution fusion | flops 805306368 | bytes 5767172 | tf_op jit(solution)/shard_map/dot_general | solution.py:217
  90.3 1.9 %fusion.50 = f32[1024,1024]{1,0:T(8,128)S(1)} fusion(bf16[1024,256]{1,0:T(8,128)(2,1)S(1)} %copy-done.2, bf16[4096,1024]{1,0:T(8,128)(2,1)} %param.11, s32[]{:T(128)S(6)} %select_n.30), kind=kOutput, calls=%fused_computation.81 | convolution fusion | flops 536870912 | bytes 5242884 | tf_op jit(solution)/shard_map/dot_general | solution.py:217
  92.7 2.3 %fusion.16 = f32[1024,1024]{1,0:T(8,128)S(1)} fusion(bf16[1024,1024]{1,0:T(8,128)(2,1)S(1)} %pad_maximum_fusion, bf16[4096,1024]{1,0:T(8,128)(2,1)S(1)} %bitcast.85, s32[]{:T(128)S(6)} %select_n.29), kind=kOutput, calls=%fused_computation.40 | convolution fusion | flops 2147483648 | bytes 8388612 | tf_op jit(solution)/shard_map/dot_general | solution.py:228
  95.8 3.9 %fusion.14 = f32[1024,1024]{1,0:T(8,128)S(1)} fusion(bf16[1024,1024]{1,0:T(8,128)(2,1)} %collective-permute-done.11, bf16[4096,1024]{1,0:T(8,128)(2,1)S(1)} %bitcast.85, s32[]{:T(128)S(6)} %select_n.32), kind=kOutput, calls=%fused_computation.38 | convolution fusion | flops 2147483648 | bytes 8388612 | tf_op jit(solution)/shard_map/dot_general | solution.py:231
  99.7 4.8 %add_add_fusion = f32[1024,1024]{1,0:T(8,128)} fusion(f32[1024,1024]{1,0:T(8,128)S(1)} %fusion.48, f32[1024,1024]{1,0:T(8,128)S(1)} %fusion.14, f32[1024,1024]{1,0:T(8,128)S(1)} %fusion.44, f32[1024,1024]{1,0:T(8,128)S(1)} %fusion.16, f32[1024,1024]{1,0:T(8,128)S(1)} %fusion.50, bf16[1024,384]{1,0:T(8,128)(2,1)S(1)} %collective-permute-done.13, ...), kind=kOutput, calls=%fused_computation.23 | convolution fusion | flops 810549248 | bytes 26738692 | tf_op jit(solution)/shard_map/dot_general | solution.py:217
  106.3 2.8 %fusion.38 = f32[1024,1024]{1,0:T(8,128)S(1)} fusion(bf16[1024,384]{1,0:T(8,128)(2,1)} %collective-permute-done.9, bf16[4096,1024]{1,0:T(8,128)(2,1)} %param.11, s32[]{:T(128)S(6)} %select_n.35), kind=kOutput, calls=%fused_computation.69 | convolution fusion | flops 805306368 | bytes 5767172 | tf_op jit(solution)/shard_map/dot_general | solution.py:217
  109.0 3.7 %add_convert_fusion = bf16[1024,1024]{1,0:T(8,128)(2,1)} fusion(f32[1024,1024]{1,0:T(8,128)S(1)} %copy-done, f32[1024,1024]{1,0:T(8,128)S(1)} %fusion.38, bf16[1024,384]{1,0:T(8,128)(2,1)S(1)} %collective-permute-done.14, bf16[4096,1024]{1,0:T(8,128)(2,1)} %param.11, s32[]{:T(128)S(6)} %select_n.36), kind=kOutput, calls=%fused_computation.22 | convolution fusion | flops 808452096 | bytes 12058628 | tf_op jit(solution)/shard_map/dot_general | solution.py:217
  (46 shorter events, 8.7 us)
Async XLA Ops:
  0.8 8.7 %collective-permute-start = (bf16[3,2,1024]{2,1,0:T(2,128)(2,1)S(1)}, bf16[3,2,1024]{2,1,0:T(2,128)(2,1)S(1)}, u32[]{:S(2)}, u32[]{:S(2)}) collective-permute-start(bf16[3,2,1024]{2,1,0:T(2,128)(2,1)S(1)} %slice.141), channel_id=1, source_target_pairs={{0,4},{4,8},{8,12},{12,16},{16,20},{20,24},{24,28},{1,5},{5,9},{9,... | collective-permute-start | bytes 36872 | tf_op jit(solution)/shard_map/ppermute | solution.py:15
  18.2 27.8 %copy-start.3 = (f32[16,1024]{1,0:T(8,128)S(1)}, f32[16,1024]{1,0:T(8,128)}, u32[]{:S(2)}) copy-start(f32[16,1024]{1,0:T(8,128)} %param.8) | copy-start | bytes 196612
  28.2 11.8 %collective-permute-start.7 = (f32[16,1024]{1,0:T(8,128)S(1)}, f32[16,1024]{1,0:T(8,128)S(1)}, u32[]{:S(2)}, u32[]{:S(2)}) collective-permute-start(f32[16,1024]{1,0:T(8,128)S(1)} %multiply_reduce_fusion.1), channel_id=1, source_target_pairs={{0,28},{1,29},{2,30},{3,31}} | collective-permute-start | bytes 196616 | tf_op jit(solution)/shard_map/ppermute | solution.py:15
  32.6 9.1 %collective-permute-start.6 = (f32[16,1024]{1,0:T(8,128)S(1)}, f32[16,1024]{1,0:T(8,128)S(1)}, u32[]{:S(2)}, u32[]{:S(2)}) collective-permute-start(f32[16,1024]{1,0:T(8,128)S(1)} %multiply_reduce_fusion.1), channel_id=1, source_target_pairs={{0,24},{4,28},{1,25},{5,29},{2,26},{6,30},{3,27},{7,31}} | collective-permute-start | bytes 196616 | tf_op jit(solution)/shard_map/ppermute | solution.py:15
  34.1 11.8 %collective-permute-start.5 = (f32[16,1024]{1,0:T(8,128)S(1)}, f32[16,1024]{1,0:T(8,128)S(1)}, u32[]{:S(2)}, u32[]{:S(2)}) collective-permute-start(f32[16,1024]{1,0:T(8,128)S(1)} %multiply_reduce_fusion.1), channel_id=1, source_target_pairs={{0,20},{4,24},{8,28},{1,21},{5,25},{9,29},{2,22},{6,26},{10,30},{3... | collective-permute-start | bytes 196616 | tf_op jit(solution)/shard_map/ppermute | solution.py:15
  35.4 10.5 %collective-permute-start.4 = (f32[16,1024]{1,0:T(8,128)S(1)}, f32[16,1024]{1,0:T(8,128)S(1)}, u32[]{:S(2)}, u32[]{:S(2)}) collective-permute-start(f32[16,1024]{1,0:T(8,128)S(1)} %multiply_reduce_fusion.1), channel_id=1, source_target_pairs={{0,16},{4,20},{8,24},{12,28},{1,17},{5,21},{9,25},{13,29},{2,18},{... | collective-permute-start | bytes 196616 | tf_op jit(solution)/shard_map/ppermute | solution.py:15
  36.7 9.2 %collective-permute-start.3 = (f32[16,1024]{1,0:T(8,128)S(1)}, f32[16,1024]{1,0:T(8,128)S(1)}, u32[]{:S(2)}, u32[]{:S(2)}) collective-permute-start(f32[16,1024]{1,0:T(8,128)S(1)} %multiply_reduce_fusion.1), channel_id=1, source_target_pairs={{0,12},{4,16},{8,20},{12,24},{16,28},{1,13},{5,17},{9,21},{13,25},... | collective-permute-start | bytes 196616 | tf_op jit(solution)/shard_map/ppermute | solution.py:15
  40.0 6.0 %collective-permute-start.2 = (f32[16,1024]{1,0:T(8,128)S(1)}, f32[16,1024]{1,0:T(8,128)S(1)}, u32[]{:S(2)}, u32[]{:S(2)}) collective-permute-start(f32[16,1024]{1,0:T(8,128)S(1)} %multiply_reduce_fusion.1), channel_id=1, source_target_pairs={{0,8},{4,12},{8,16},{12,20},{16,24},{20,28},{1,9},{5,13},{9,17},{1... | collective-permute-start | bytes 196616 | tf_op jit(solution)/shard_map/ppermute | solution.py:15
  41.6 4.4 %collective-permute-start.1 = (f32[16,1024]{1,0:T(8,128)S(1)}, f32[16,1024]{1,0:T(8,128)S(1)}, u32[]{:S(2)}, u32[]{:S(2)}) collective-permute-start(f32[16,1024]{1,0:T(8,128)S(1)} %multiply_reduce_fusion.1), channel_id=1, source_target_pairs={{0,4},{4,8},{8,12},{12,16},{16,20},{20,24},{24,28},{1,5},{5,9},{9,... | collective-permute-start | bytes 196616 | tf_op jit(solution)/shard_map/ppermute | solution.py:15
  45.9 6.1 %slice-start.2 = ((f32[1024]{0:T(1024)}), f32[256]{0:T(256)S(1)}, s32[]{:S(2)}) async-start(f32[1024]{0:T(1024)} %param.10), calls=%async_computation.2 | async-start | bytes 2048 | tf_op jit(solution)/shard_map/slice | solution.py:190
  54.5 11.7 %collective-permute-start.8 = (bf16[1024,256]{1,0:T(8,128)(2,1)S(1)}, bf16[1024,256]{1,0:T(8,128)(2,1)S(1)}, u32[]{:S(2)}, u32[]{:S(2)}) collective-permute-start(bf16[1024,256]{1,0:T(8,128)(2,1)S(1)} %fusion.28), channel_id=1, source_target_pairs={{0,2},{1,3},{2,0},{3,1},{4,6},{5,7},{6,4},{7,5},{8,10},{9,11},{10,... | collective-permute-start | bytes 1572872 | tf_op jit(solution)/shard_map/ppermute | solution.py:197
  65.9 16.7 %collective-permute-start.10 = (bf16[1024,384]{1,0:T(8,128)(2,1)}, bf16[1024,384]{1,0:T(8,128)(2,1)}, u32[]{:S(2)}, u32[]{:S(2)}) collective-permute-start(bf16[1024,384]{1,0:T(8,128)(2,1)} %fusion.20), channel_id=1, source_target_pairs={{0,2},{1,3},{2,0},{3,1},{4,6},{5,7},{6,4},{7,5},{8,10},{9,11},{10,... | collective-permute-start | bytes 2359304 | tf_op jit(solution)/shard_map/ppermute | solution.py:197
  66.2 6.4 %copy-start.1 = (bf16[1024,256]{1,0:T(8,128)(2,1)}, bf16[1024,256]{1,0:T(8,128)(2,1)S(1)}, u32[]{:S(2)}) copy-start(bf16[1024,256]{1,0:T(8,128)(2,1)S(1)} %collective-permute-done.8) | copy-start | bytes 1572868
  77.1 13.2 %copy-start.2 = (bf16[1024,256]{1,0:T(8,128)(2,1)S(1)}, bf16[1024,256]{1,0:T(8,128)(2,1)}, u32[]{:S(2)}) copy-start(bf16[1024,256]{1,0:T(8,128)(2,1)} %copy-done.1) | copy-start | bytes 1572868
  82.6 13.2 %collective-permute-start.11 = (bf16[1024,1024]{1,0:T(8,128)(2,1)S(1)}, bf16[1024,1024]{1,0:T(8,128)(2,1)}, u32[]{:S(2)}, u32[]{:S(2)}) collective-permute-start(bf16[1024,1024]{1,0:T(8,128)(2,1)S(1)} %pad_maximum_fusion), channel_id=1, source_target_pairs={{0,1},{1,0},{2,3},{3,2},{4,5},{5,4},{6,7},{7,6},{8,9},{9,8},{10,11... | collective-permute-start | bytes 6291464 | tf_op jit(solution)/shard_map/ppermute | solution.py:224
  86.2 19.3 %collective-permute-start.9 = (bf16[1024,384]{1,0:T(8,128)(2,1)S(1)}, bf16[1024,384]{1,0:T(8,128)(2,1)}, u32[]{:S(2)}, u32[]{:S(2)}) collective-permute-start(bf16[1024,384]{1,0:T(8,128)(2,1)S(1)} %fusion.24), channel_id=1, source_target_pairs={{0,2},{1,3},{2,0},{3,1},{4,6},{5,7},{6,4},{7,5},{8,10},{9,11},{10,... | collective-permute-start | bytes 2359304 | tf_op jit(solution)/shard_map/ppermute | solution.py:197
  87.0 8.0 %collective-permute-start.12 = (bf16[1024,256]{1,0:T(8,128)(2,1)}, bf16[1024,256]{1,0:T(8,128)(2,1)S(1)}, u32[]{:S(2)}, u32[]{:S(2)}) collective-permute-start(bf16[1024,256]{1,0:T(8,128)(2,1)} %copy-done.1), channel_id=1, source_target_pairs={{0,1},{1,0},{2,3},{3,2},{4,5},{5,4},{6,7},{7,6},{8,9},{9,8},{10,11... | collective-permute-start | bytes 1572872 | tf_op jit(solution)/shard_map/ppermute | solution.py:225
  87.3 12.4 %collective-permute-start.13 = (bf16[1024,384]{1,0:T(8,128)(2,1)}, bf16[1024,384]{1,0:T(8,128)(2,1)S(1)}, u32[]{:S(2)}, u32[]{:S(2)}) collective-permute-start(bf16[1024,384]{1,0:T(8,128)(2,1)} %collective-permute-done.10), channel_id=1, source_target_pairs={{0,1},{1,0},{2,3},{3,2},{4,5},{5,4},{6,7},{7,6},{8,9},{9,8},{10,11... | collective-permute-start | bytes 2359304 | tf_op jit(solution)/shard_map/ppermute | solution.py:225
  87.6 4.7 %slice-start = ((s8[8388608]{0:T(1024)(128)(4,1)}), s8[4194304]{0:T(1024)(128)(4,1)S(1)}, s32[]{:S(2)}) async-start(s8[8388608]{0:T(1024)(128)(4,1)} %bitcast.84), calls=%async_computation | async-start | bytes 8388608
  90.3 2.4 %slice-start.1 = ((s8[8388608]{0:T(1024)(128)(4,1)}), s8[4194304]{0:T(1024)(128)(4,1)S(1)}, s32[]{:S(2)}) async-start(s8[8388608]{0:T(1024)(128)(4,1)} %bitcast.84), calls=%async_computation.1 | async-start | bytes 8388608
  105.5 3.6 %collective-permute-start.14 = (bf16[1024,384]{1,0:T(8,128)(2,1)}, bf16[1024,384]{1,0:T(8,128)(2,1)S(1)}, u32[]{:S(2)}, u32[]{:S(2)}) collective-permute-start(bf16[1024,384]{1,0:T(8,128)(2,1)} %collective-permute-done.9), channel_id=1, source_target_pairs={{0,1},{1,0},{2,3},{3,2},{4,5},{5,4},{6,7},{7,6},{8,9},{9,8},{10,11... | collective-permute-start | bytes 2359304 | tf_op jit(solution)/shard_map/ppermute | solution.py:236
  106.3 2.8 %copy-start = (f32[1024,1024]{1,0:T(8,128)S(1)}, f32[1024,1024]{1,0:T(8,128)}, u32[]{:S(2)}) copy-start(f32[1024,1024]{1,0:T(8,128)} %add_add_fusion) | copy-start | bytes 12582916

commit v15 on v14

--- a/solution.py
+++ b/solution.py
@@ -31,15 +31,16 @@
     def body(t, states):
         x = x_ref[pl.ds(t, segments, stride=span), :]
         updated = []
-        total = None
+        terms = []
         for p in range(pole_count):
             h = decays[p] * states[p] + x
             updated.append(h)
             if y_ref is not None:
-                term = residues[p] * h
-                total = term if total is None else total + term
+                terms.append(residues[p] * h)
         if y_ref is not None:
-            y_ref[pl.ds(t, segments, stride=span), :] = total
+            while len(terms) > 1:
+                terms = [terms[i] + terms[i + 1] if i + 1 < len(terms) else terms[i] for i in range(0, len(terms), 2)]
+            y_ref[pl.ds(t, segments, stride=span), :] = terms[0]
         return tuple(updated)
 
     states = lax.fori_loop(0, span, body, states, unroll=16)

time: 114 us -> 114 us (level)
  transfers between devices with their start and end apart: 15 -> 15, of which waited for: 2 -> 2; matrix products, arithmetic and copies ran while one was open for 31% -> 31% of each run, Pallas kernels for 11% -> 12%
where the time goes in v15:
time: 114 us; the launch traced here: 113 us
  other arithmetic  27.4 us (24%)
  Pallas kernels  26.9 us (24%)
  starting transfers between devices  25.9 us (23%)
  matrix products  22.9 us (20%)
  waiting for transfers between devices  6.5 us (6%)
  local copies, waits for them, and re-layouts  3.38 us (3%)
    ppermute x8, starting transfers between devices, shifted(): lax.ppermute(value, axis, [(source, source + steps) for source in range(i...  19 us
    pallas_call x3, Pallas kernels, run_recurrence(): pl.pallas_call(recurrence_kernel, grid=(group_count,), in_specs=[pl.Block...  18.3 us
    dot_general x6, matrix products, part(): return jnp.dot(value, rows, preferred_element_type=jnp.float32)  16.7 us
    convert_element_type x3, other arithmetic, shards(): gated_mix = gated_mix.astype(jnp.bfloat16)  9.51 us
    convert_element_type x1, other arithmetic, shards(): x = mixed_input.astype(jnp.float32)  8.74 us
    pallas_call x1, Pallas kernels, run_end_state(): pl.pallas_call(end_state_kernel, grid=(width // LANES,), in_specs=[pl.Blo...  8.67 us
    ppermute x3, waiting for transfers between devices, shards(): lax.ppermute(gated_mix, 'ch', [(i, i ^ 2) for i in range(ch_count)])  6.44 us
    dot_general x1, matrix products, project_pieces(): total = total + jnp.dot(near, rows_near, preferred_element_type=jnp.float32)  3.94 us
  transfers between devices with their start and end apart: 15, of which 2 were waited for; matrix products, arithmetic and copies ran while one was open for 31% of the time, Pallas kernels for 12%

profile of v15, /device:TPU:1, one launch (start us, length us, event | category | flops | bytes accessed | tf_op | source)
XLA Modules:
  0.0 113.3 jit_solution(11111754705069263952)
XLA Ops:
  0.8 4.0 %collective-permute-start = (bf16[3,2,1024]{2,1,0:T(2,128)(2,1)S(1)}, bf16[3,2,1024]{2,1,0:T(2,128)(2,1)S(1)}, u32[]{:S(2)}, u32[]{:S(2)}) collective-permute-start(bf16[3,2,1024]{2,1,0:T(2,128)(2,1)S(1)} %slice.141), channel_id=1, source_target_pairs={{0,4},{4,8},{8,12},{12,16},{16,20},{20,24},{24,28},{1,5},{5,9},{9,... | collective-permute-start | bytes 36872 | tf_op jit(solution)/shard_map/ppermute | solution.py:15
  8.0 1.5 %fusion.62 = (f32[16,1024]{1,0:T(8,128)S(1)}, f32[16,1024]{1,0:T(8,128)}) fusion(f32[16,1024]{1,0:T(8,128)} %param.8), kind=kLoop, calls=%fused_computation.115 | loop fusion | flops 16384 | bytes 196608 | tf_op jit(solution)/shard_map/neg | solution.py:170
  9.5 8.7 %fusion.60 = (f32[1024,1024]{1,0:T(8,128)}, bf16[1024,1024]{1,0:T(8,128)(2,1)S(1)}) fusion(f32[1024]{0:T(1024)S(1)} %bitcast.91, f32[1024]{0:T(1024)S(1)} %bitcast.87, bf16[3,1024,1024]{2,1,0:T(8,128)(2,1)} %param.6, f32[1024]{0:T(1024)S(1)} %bitcast.88, f32[1024]{0:T(1024)S(1)} %bitcast.89, bf16[3,2,1024]{2,1,0:T(2,128)(2,1)S(1)} %collective-permute-done, ...), kind=kLoop, calls=%fused_computation.114 | loop fusion | flops 36700160 | bytes 16814080 | tf_op jit(solution)/shard_map/convert_element_type | solution.py:167
  18.2 8.7 %shard_map.64 = f32[16,8,1024]{2,1,0:T(8,128)} custom-call(f32[1024,1024]{1,0:T(8,128)} %get-tuple-element.19.x_ref, f32[16,1024]{1,0:T(8,128)} %get-tuple-element.36.decay_ref), custom_call_target="tpu_custom_call" | custom-call | tf_op jit(solution)/shard_map/pallas_call | solution.py:63
  26.9 1.3 %multiply_reduce_fusion.1 = f32[16,1024]{1,0:T(8,128)S(1)} fusion(f32[16,8,1024]{2,1,0:T(8,128)} %shard_map.64, f32[8]{0:T(128)S(1)} %subtract_multiply_fusion, f32[16,1024]{1,0:T(8,128)S(1)} %get-tuple-element.35), kind=kLoop, calls=%fused_computation.83 | loop fusion | flops 376832 | bytes 655392 | tf_op jit(solution)/shard_map/reduce_sum | solution.py:111
  28.2 4.3 %collective-permute-start.7 = (f32[16,1024]{1,0:T(8,128)S(1)}, f32[16,1024]{1,0:T(8,128)S(1)}, u32[]{:S(2)}, u32[]{:S(2)}) collective-permute-start(f32[16,1024]{1,0:T(8,128)S(1)} %multiply_reduce_fusion.1), channel_id=1, source_target_pairs={{0,28},{1,29},{2,30},{3,31}} | collective-permute-start | bytes 196616 | tf_op jit(solution)/shard_map/ppermute | solution.py:15
  32.6 1.6 %collective-permute-start.6 = (f32[16,1024]{1,0:T(8,128)S(1)}, f32[16,1024]{1,0:T(8,128)S(1)}, u32[]{:S(2)}, u32[]{:S(2)}) collective-permute-start(f32[16,1024]{1,0:T(8,128)S(1)} %multiply_reduce_fusion.1), channel_id=1, source_target_pairs={{0,24},{4,28},{1,25},{5,29},{2,26},{6,30},{3,27},{7,31}} | collective-permute-start | bytes 196616 | tf_op jit(solution)/shard_map/ppermute | solution.py:15
  34.1 1.3 %collective-permute-start.5 = (f32[16,1024]{1,0:T(8,128)S(1)}, f32[16,1024]{1,0:T(8,128)S(1)}, u32[]{:S(2)}, u32[]{:S(2)}) collective-permute-start(f32[16,1024]{1,0:T(8,128)S(1)} %multiply_reduce_fusion.1), channel_id=1, source_target_pairs={{0,20},{4,24},{8,28},{1,21},{5,25},{9,29},{2,22},{6,26},{10,30},{3... | collective-permute-start | bytes 196616 | tf_op jit(solution)/shard_map/ppermute | solution.py:15
  35.4 1.3 %collective-permute-start.4 = (f32[16,1024]{1,0:T(8,128)S(1)}, f32[16,1024]{1,0:T(8,128)S(1)}, u32[]{:S(2)}, u32[]{:S(2)}) collective-permute-start(f32[16,1024]{1,0:T(8,128)S(1)} %multiply_reduce_fusion.1), channel_id=1, source_target_pairs={{0,16},{4,20},{8,24},{12,28},{1,17},{5,21},{9,25},{13,29},{2,18},{... | collective-permute-start | bytes 196616 | tf_op jit(solution)/shard_map/ppermute | solution.py:15
  36.7 1.9 %collective-permute-start.3 = (f32[16,1024]{1,0:T(8,128)S(1)}, f32[16,1024]{1,0:T(8,128)S(1)}, u32[]{:S(2)}, u32[]{:S(2)}) collective-permute-start(f32[16,1024]{1,0:T(8,128)S(1)} %multiply_reduce_fusion.1), channel_id=1, source_target_pairs={{0,12},{4,16},{8,20},{12,24},{16,28},{1,13},{5,17},{9,21},{13,25},... | collective-permute-start | bytes 196616 | tf_op jit(solution)/shard_map/ppermute | solution.py:15
  38.7 1.4 %copy.15 = f32[16,1024,8]{1,0,2:T(8,128)S(1)} copy(f32[16,1024,8]{1,2,0:T(8,128)} %bitcast.83) | data formatting | bytes 1048576
  40.0 1.6 %collective-permute-start.2 = (f32[16,1024]{1,0:T(8,128)S(1)}, f32[16,1024]{1,0:T(8,128)S(1)}, u32[]{:S(2)}, u32[]{:S(2)}) collective-permute-start(f32[16,1024]{1,0:T(8,128)S(1)} %multiply_reduce_fusion.1), channel_id=1, source_target_pairs={{0,8},{4,12},{8,16},{12,20},{16,24},{20,28},{1,9},{5,13},{9,17},{1... | collective-permute-start | bytes 196616 | tf_op jit(solution)/shard_map/ppermute | solution.py:15
  41.6 3.1 %collective-permute-start.1 = (f32[16,1024]{1,0:T(8,128)S(1)}, f32[16,1024]{1,0:T(8,128)S(1)}, u32[]{:S(2)}, u32[]{:S(2)}) collective-permute-start(f32[16,1024]{1,0:T(8,128)S(1)} %multiply_reduce_fusion.1), channel_id=1, source_target_pairs={{0,4},{4,8},{8,12},{12,16},{16,20},{20,24},{24,28},{1,5},{5,9},{9,... | collective-permute-start | bytes 196616 | tf_op jit(solution)/shard_map/ppermute | solution.py:15
  44.7 1.2 %multiply_reduce_fusion = f32[16,1024,8]{1,0,2:T(8,128)S(1)} fusion(f32[16,1024,8]{1,0,2:T(8,128)S(1)} %copy.15, f32[8,8]{1,0:T(8,128)S(1)} %maximum_multiply_fusion, f32[16,1024]{1,0:T(8,128)S(1)} %get-tuple-element.35, pred[8,8]{1,0:T(8,128)(4,1)S(1)} %iota_compare_fusion), kind=kLoop, calls=%fused_computation.21 | loop fusion | flops 4063232 | bytes 1114432
  47.3 5.0 %shard_map.65 = f32[1024,256]{1,0:T(8,128)} custom-call(f32[1024,1024]{1,0:T(8,128)} %get-tuple-element.19.x_ref, f32[16,1024]{1,0:T(8,128)} %get-tuple-element.36.decay_ref, f32[16,1024]{1,0:T(8,128)} %residue_ref.5, f32[16,8,1024]{2,1,0:T(8,128)} %bitcast_add_fusion.start_ref), custom_call_target="tpu_custom_call" | custom-call | tf_op jit(solution)/shard_map/pallas_call | solution.py:79
  52.3 2.4 %fusion.28 = bf16[1024,256]{1,0:T(8,128)(2,1)S(1)} fusion(bf16[1024,1024]{1,0:T(8,128)(2,1)S(1)} %get-tuple-element.34, bf16[3,1024,1024]{2,1,0:T(8,128)(2,1)} %param.6, bf16[3,2,1024]{2,1,0:T(2,128)(2,1)S(1)} %collective-permute-done, f32[256]{0:T(256)S(1)} %slice-done.2, f32[1024,256]{1,0:T(8,128)} %shard_map.65, f32[256]{0:T(256)S(1)} %bitcast.93, ...), kind=kLoop, calls=%fused_computation.59 | loop fusion | flops 6029312 | bytes 8929280 | tf_op jit(solution)/shard_map/convert_element_type | solution.py:193
  54.7 1.3 %collective-permute-start.8 = (bf16[1024,256]{1,0:T(8,128)(2,1)S(1)}, bf16[1024,256]{1,0:T(8,128)(2,1)S(1)}, u32[]{:S(2)}, u32[]{:S(2)}) collective-permute-start(bf16[1024,256]{1,0:T(8,128)(2,1)S(1)} %fusion.28), channel_id=1, source_target_pairs={{0,2},{1,3},{2,0},{3,1},{4,6},{5,7},{6,4},{7,5},{8,10},{9,11},{10,... | collective-permute-start | bytes 1572872 | tf_op jit(solution)/shard_map/ppermute | solution.py:198
  56.0 6.5 %shard_map.66 = f32[1024,384]{1,0:T(8,128)} custom-call(f32[1024,1024]{1,0:T(8,128)} %get-tuple-element.19.x_ref, f32[16,1024]{1,0:T(8,128)} %get-tuple-element.36.decay_ref, f32[16,1024]{1,0:T(8,128)} %residue_ref.5, f32[16,8,1024]{2,1,0:T(8,128)} %bitcast_add_fusion.start_ref), custom_call_target="tpu_custom_call" | custom-call | tf_op jit(solution)/shard_map/pallas_call | solution.py:79
  62.5 4.0 %fusion.20 = bf16[1024,384]{1,0:T(8,128)(2,1)} fusion(bf16[1024,1024]{1,0:T(8,128)(2,1)S(1)} %get-tuple-element.34, f32[384]{0:T(512)S(1)} %get-tuple-element.46, f32[1024,384]{1,0:T(8,128)} %shard_map.66, f32[384]{0:T(512)S(1)} %get-tuple-element.28, f32[384]{0:T(512)S(1)} %get-tuple-element.29, bf16[3,1024,1024]{2,1,0:T(8,128)(2,1)} %param.6, ...), kind=kLoop, calls=%fused_computation.45 | loop fusion | flops 9043968 | bytes 10242048 | tf_op jit(solution)/shard_map/convert_element_type | solution.py:193
  66.8 6.7 %shard_map.67 = f32[1024,384]{1,0:T(8,128)} custom-call(f32[1024,1024]{1,0:T(8,128)} %get-tuple-element.19.x_ref, f32[16,1024]{1,0:T(8,128)} %get-tuple-element.36.decay_ref, f32[16,1024]{1,0:T(8,128)} %residue_ref.5, f32[16,8,1024]{2,1,0:T(8,128)} %bitcast_add_fusion.start_ref), custom_call_target="tpu_custom_call" | custom-call | tf_op jit(solution)/shard_map/pallas_call | solution.py:79
  73.5 3.1 %fusion.24 = bf16[1024,384]{1,0:T(8,128)(2,1)S(1)} fusion(bf16[1024,1024]{1,0:T(8,128)(2,1)S(1)} %get-tuple-element.34, f32[384]{0:T(512)S(1)} %get-tuple-element.47, f32[1024,384]{1,0:T(8,128)} %shard_map.67, f32[384]{0:T(512)S(1)} %get-tuple-element.31, f32[384]{0:T(512)S(1)} %get-tuple-element.32, bf16[3,1024,1024]{2,1,0:T(8,128)(2,1)} %param.6, ...), kind=kLoop, calls=%fused_computation.52 | loop fusion | flops 9043968 | bytes 10242048 | tf_op jit(solution)/shard_map/convert_element_type | solution.py:193
  76.6 1.4 %pad_maximum_fusion = bf16[1024,1024]{1,0:T(8,128)(2,1)S(1)} fusion(bf16[1024,384]{1,0:T(8,128)(2,1)S(1)} %fusion.24, bf16[1024,384]{1,0:T(8,128)(2,1)} %fusion.20, bf16[1024,256]{1,0:T(8,128)(2,1)S(1)} %fusion.28), kind=kLoop, calls=%fused_computation.37 | loop fusion | flops 6291456 | bytes 4194304 | tf_op jit(solution)/shard_map/concatenate | solution.py:221
  78.1 5.1 %collective-permute-done.10 = bf16[1024,384]{1,0:T(8,128)(2,1)} collective-permute-done((bf16[1024,384]{1,0:T(8,128)(2,1)}, bf16[1024,384]{1,0:T(8,128)(2,1)}, u32[]{:S(2)}, u32[]{:S(2)}) %collective-permute-start.10) | collective-permute-done | bytes 786464 | tf_op jit(solution)/shard_map/ppermute | solution.py:198
  83.2 3.6 %collective-permute-start.11 = (bf16[1024,1024]{1,0:T(8,128)(2,1)S(1)}, bf16[1024,1024]{1,0:T(8,128)(2,1)}, u32[]{:S(2)}, u32[]{:S(2)}) collective-permute-start(bf16[1024,1024]{1,0:T(8,128)(2,1)S(1)} %pad_maximum_fusion), channel_id=1, source_target_pairs={{0,1},{1,0},{2,3},{3,2},{4,5},{5,4},{6,7},{7,6},{8,9},{9,8},{10,11... | collective-permute-start | bytes 6291464 | tf_op jit(solution)/shard_map/ppermute | solution.py:225
  87.8 2.8 %fusion.44 = f32[1024,1024]{1,0:T(8,128)S(1)} fusion(bf16[1024,384]{1,0:T(8,128)(2,1)} %collective-permute-done.10, bf16[4096,1024]{1,0:T(8,128)(2,1)} %param.11, s32[]{:T(128)S(6)} %select_n.31), kind=kOutput, calls=%fused_computation.73 | convolution fusion | flops 805306368 | bytes 5767172 | tf_op jit(solution)/shard_map/dot_general | solution.py:218
  90.6 1.9 %fusion.50 = f32[1024,1024]{1,0:T(8,128)S(1)} fusion(bf16[1024,256]{1,0:T(8,128)(2,1)S(1)} %copy-done.2, bf16[4096,1024]{1,0:T(8,128)(2,1)} %param.11, s32[]{:T(128)S(6)} %select_n.30), kind=kOutput, calls=%fused_computation.81 | convolution fusion | flops 536870912 | bytes 5242884 | tf_op jit(solution)/shard_map/dot_general | solution.py:218
  92.9 2.3 %fusion.16 = f32[1024,1024]{1,0:T(8,128)S(1)} fusion(bf16[1024,1024]{1,0:T(8,128)(2,1)S(1)} %pad_maximum_fusion, bf16[4096,1024]{1,0:T(8,128)(2,1)S(1)} %bitcast.85, s32[]{:T(128)S(6)} %select_n.29), kind=kOutput, calls=%fused_computation.40 | convolution fusion | flops 2147483648 | bytes 8388612 | tf_op jit(solution)/shard_map/dot_general | solution.py:229
  96.0 3.9 %fusion.14 = f32[1024,1024]{1,0:T(8,128)S(1)} fusion(bf16[1024,1024]{1,0:T(8,128)(2,1)} %collective-permute-done.11, bf16[4096,1024]{1,0:T(8,128)(2,1)S(1)} %bitcast.85, s32[]{:T(128)S(6)} %select_n.32), kind=kOutput, calls=%fused_computation.38 | convolution fusion | flops 2147483648 | bytes 8388612 | tf_op jit(solution)/shard_map/dot_general | solution.py:232
  100.0 4.8 %add_add_fusion = f32[1024,1024]{1,0:T(8,128)} fusion(f32[1024,1024]{1,0:T(8,128)S(1)} %fusion.48, f32[1024,1024]{1,0:T(8,128)S(1)} %fusion.14, f32[1024,1024]{1,0:T(8,128)S(1)} %fusion.44, f32[1024,1024]{1,0:T(8,128)S(1)} %fusion.16, f32[1024,1024]{1,0:T(8,128)S(1)} %fusion.50, bf16[1024,384]{1,0:T(8,128)(2,1)S(1)} %collective-permute-done.13, ...), kind=kOutput, calls=%fused_computation.23 | convolution fusion | flops 810549248 | bytes 26738692 | tf_op jit(solution)/shard_map/dot_general | solution.py:218
  104.8 1.3 %collective-permute-done.9 = bf16[1024,384]{1,0:T(8,128)(2,1)} collective-permute-done((bf16[1024,384]{1,0:T(8,128)(2,1)S(1)}, bf16[1024,384]{1,0:T(8,128)(2,1)}, u32[]{:S(2)}, u32[]{:S(2)}) %collective-permute-start.9) | collective-permute-done | bytes 786464 | tf_op jit(solution)/shard_map/ppermute | solution.py:198
  106.8 2.8 %fusion.38 = f32[1024,1024]{1,0:T(8,128)S(1)} fusion(bf16[1024,384]{1,0:T(8,128)(2,1)} %collective-permute-done.9, bf16[4096,1024]{1,0:T(8,128)(2,1)} %param.11, s32[]{:T(128)S(6)} %select_n.35), kind=kOutput, calls=%fused_computation.69 | convolution fusion | flops 805306368 | bytes 5767172 | tf_op jit(solution)/shard_map/dot_general | solution.py:218
  109.6 3.7 %add_convert_fusion = bf16[1024,1024]{1,0:T(8,128)(2,1)} fusion(f32[1024,1024]{1,0:T(8,128)S(1)} %copy-done, f32[1024,1024]{1,0:T(8,128)S(1)} %fusion.38, bf16[1024,384]{1,0:T(8,128)(2,1)S(1)} %collective-permute-done.14, bf16[4096,1024]{1,0:T(8,128)(2,1)} %param.11, s32[]{:T(128)S(6)} %select_n.36), kind=kOutput, calls=%fused_computation.22 | convolution fusion | flops 808452096 | bytes 12058628 | tf_op jit(solution)/shard_map/dot_general | solution.py:218
  (46 shorter events, 8.6 us)
Async XLA Ops:
  0.8 8.7 %collective-permute-start = (bf16[3,2,1024]{2,1,0:T(2,128)(2,1)S(1)}, bf16[3,2,1024]{2,1,0:T(2,128)(2,1)S(1)}, u32[]{:S(2)}, u32[]{:S(2)}) collective-permute-start(bf16[3,2,1024]{2,1,0:T(2,128)(2,1)S(1)} %slice.141), channel_id=1, source_target_pairs={{0,4},{4,8},{8,12},{12,16},{16,20},{20,24},{24,28},{1,5},{5,9},{9,... | collective-permute-start | bytes 36872 | tf_op jit(solution)/shard_map/ppermute | solution.py:15
  18.2 27.8 %copy-start.3 = (f32[16,1024]{1,0:T(8,128)S(1)}, f32[16,1024]{1,0:T(8,128)}, u32[]{:S(2)}) copy-start(f32[16,1024]{1,0:T(8,128)} %param.8) | copy-start | bytes 196612
  28.2 11.8 %collective-permute-start.7 = (f32[16,1024]{1,0:T(8,128)S(1)}, f32[16,1024]{1,0:T(8,128)S(1)}, u32[]{:S(2)}, u32[]{:S(2)}) collective-permute-start(f32[16,1024]{1,0:T(8,128)S(1)} %multiply_reduce_fusion.1), channel_id=1, source_target_pairs={{0,28},{1,29},{2,30},{3,31}} | collective-permute-start | bytes 196616 | tf_op jit(solution)/shard_map/ppermute | solution.py:15
  32.6 9.1 %collective-permute-start.6 = (f32[16,1024]{1,0:T(8,128)S(1)}, f32[16,1024]{1,0:T(8,128)S(1)}, u32[]{:S(2)}, u32[]{:S(2)}) collective-permute-start(f32[16,1024]{1,0:T(8,128)S(1)} %multiply_reduce_fusion.1), channel_id=1, source_target_pairs={{0,24},{4,28},{1,25},{5,29},{2,26},{6,30},{3,27},{7,31}} | collective-permute-start | bytes 196616 | tf_op jit(solution)/shard_map/ppermute | solution.py:15
  34.1 11.8 %collective-permute-start.5 = (f32[16,1024]{1,0:T(8,128)S(1)}, f32[16,1024]{1,0:T(8,128)S(1)}, u32[]{:S(2)}, u32[]{:S(2)}) collective-permute-start(f32[16,1024]{1,0:T(8,128)S(1)} %multiply_reduce_fusion.1), channel_id=1, source_target_pairs={{0,20},{4,24},{8,28},{1,21},{5,25},{9,29},{2,22},{6,26},{10,30},{3... | collective-permute-start | bytes 196616 | tf_op jit(solution)/shard_map/ppermute | solution.py:15
  35.4 10.5 %collective-permute-start.4 = (f32[16,1024]{1,0:T(8,128)S(1)}, f32[16,1024]{1,0:T(8,128)S(1)}, u32[]{:S(2)}, u32[]{:S(2)}) collective-permute-start(f32[16,1024]{1,0:T(8,128)S(1)} %multiply_reduce_fusion.1), channel_id=1, source_target_pairs={{0,16},{4,20},{8,24},{12,28},{1,17},{5,21},{9,25},{13,29},{2,18},{... | collective-permute-start | bytes 196616 | tf_op jit(solution)/shard_map/ppermute | solution.py:15
  36.7 9.2 %collective-permute-start.3 = (f32[16,1024]{1,0:T(8,128)S(1)}, f32[16,1024]{1,0:T(8,128)S(1)}, u32[]{:S(2)}, u32[]{:S(2)}) collective-permute-start(f32[16,1024]{1,0:T(8,128)S(1)} %multiply_reduce_fusion.1), channel_id=1, source_target_pairs={{0,12},{4,16},{8,20},{12,24},{16,28},{1,13},{5,17},{9,21},{13,25},... | collective-permute-start | bytes 196616 | tf_op jit(solution)/shard_map/ppermute | solution.py:15
  40.0 6.0 %collective-permute-start.2 = (f32[16,1024]{1,0:T(8,128)S(1)}, f32[16,1024]{1,0:T(8,128)S(1)}, u32[]{:S(2)}, u32[]{:S(2)}) collective-permute-start(f32[16,1024]{1,0:T(8,128)S(1)} %multiply_reduce_fusion.1), channel_id=1, source_target_pairs={{0,8},{4,12},{8,16},{12,20},{16,24},{20,28},{1,9},{5,13},{9,17},{1... | collective-permute-start | bytes 196616 | tf_op jit(solution)/shard_map/ppermute | solution.py:15
  41.6 4.4 %collective-permute-start.1 = (f32[16,1024]{1,0:T(8,128)S(1)}, f32[16,1024]{1,0:T(8,128)S(1)}, u32[]{:S(2)}, u32[]{:S(2)}) collective-permute-start(f32[16,1024]{1,0:T(8,128)S(1)} %multiply_reduce_fusion.1), channel_id=1, source_target_pairs={{0,4},{4,8},{8,12},{12,16},{16,20},{20,24},{24,28},{1,5},{5,9},{9,... | collective-permute-start | bytes 196616 | tf_op jit(solution)/shard_map/ppermute | solution.py:15
  45.9 6.3 %slice-start.2 = ((f32[1024]{0:T(1024)}), f32[256]{0:T(256)S(1)}, s32[]{:S(2)}) async-start(f32[1024]{0:T(1024)} %param.10), calls=%async_computation.2 | async-start | bytes 2048 | tf_op jit(solution)/shard_map/slice | solution.py:191
  54.7 12.1 %collective-permute-start.8 = (bf16[1024,256]{1,0:T(8,128)(2,1)S(1)}, bf16[1024,256]{1,0:T(8,128)(2,1)S(1)}, u32[]{:S(2)}, u32[]{:S(2)}) collective-permute-start(bf16[1024,256]{1,0:T(8,128)(2,1)S(1)} %fusion.28), channel_id=1, source_target_pairs={{0,2},{1,3},{2,0},{3,1},{4,6},{5,7},{6,4},{7,5},{8,10},{9,11},{10,... | collective-permute-start | bytes 1572872 | tf_op jit(solution)/shard_map/ppermute | solution.py:198
  66.5 16.7 %collective-permute-start.10 = (bf16[1024,384]{1,0:T(8,128)(2,1)}, bf16[1024,384]{1,0:T(8,128)(2,1)}, u32[]{:S(2)}, u32[]{:S(2)}) collective-permute-start(bf16[1024,384]{1,0:T(8,128)(2,1)} %fusion.20), channel_id=1, source_target_pairs={{0,2},{1,3},{2,0},{3,1},{4,6},{5,7},{6,4},{7,5},{8,10},{9,11},{10,... | collective-permute-start | bytes 2359304 | tf_op jit(solution)/shard_map/ppermute | solution.py:198
  66.8 6.8 %copy-start.1 = (bf16[1024,256]{1,0:T(8,128)(2,1)}, bf16[1024,256]{1,0:T(8,128)(2,1)S(1)}, u32[]{:S(2)}) copy-start(bf16[1024,256]{1,0:T(8,128)(2,1)S(1)} %collective-permute-done.8) | copy-start | bytes 1572868
  78.0 12.5 %copy-start.2 = (bf16[1024,256]{1,0:T(8,128)(2,1)S(1)}, bf16[1024,256]{1,0:T(8,128)(2,1)}, u32[]{:S(2)}) copy-start(bf16[1024,256]{1,0:T(8,128)(2,1)} %copy-done.1) | copy-start | bytes 1572868
  83.2 12.8 %collective-permute-start.11 = (bf16[1024,1024]{1,0:T(8,128)(2,1)S(1)}, bf16[1024,1024]{1,0:T(8,128)(2,1)}, u32[]{:S(2)}, u32[]{:S(2)}) collective-permute-start(bf16[1024,1024]{1,0:T(8,128)(2,1)S(1)} %pad_maximum_fusion), channel_id=1, source_target_pairs={{0,1},{1,0},{2,3},{3,2},{4,5},{5,4},{6,7},{7,6},{8,9},{9,8},{10,11... | collective-permute-start | bytes 6291464 | tf_op jit(solution)/shard_map/ppermute | solution.py:225
  86.8 19.3 %collective-permute-start.9 = (bf16[1024,384]{1,0:T(8,128)(2,1)S(1)}, bf16[1024,384]{1,0:T(8,128)(2,1)}, u32[]{:S(2)}, u32[]{:S(2)}) collective-permute-start(bf16[1024,384]{1,0:T(8,128)(2,1)S(1)} %fusion.24), channel_id=1, source_target_pairs={{0,2},{1,3},{2,0},{3,1},{4,6},{5,7},{6,4},{7,5},{8,10},{9,11},{10,... | collective-permute-start | bytes 2359304 | tf_op jit(solution)/shard_map/ppermute | solution.py:198
  87.3 8.0 %collective-permute-start.12 = (bf16[1024,256]{1,0:T(8,128)(2,1)}, bf16[1024,256]{1,0:T(8,128)(2,1)S(1)}, u32[]{:S(2)}, u32[]{:S(2)}) collective-permute-start(bf16[1024,256]{1,0:T(8,128)(2,1)} %copy-done.1), channel_id=1, source_target_pairs={{0,1},{1,0},{2,3},{3,2},{4,5},{5,4},{6,7},{7,6},{8,9},{9,8},{10,11... | collective-permute-start | bytes 1572872 | tf_op jit(solution)/shard_map/ppermute | solution.py:226
  87.6 12.4 %collective-permute-start.13 = (bf16[1024,384]{1,0:T(8,128)(2,1)}, bf16[1024,384]{1,0:T(8,128)(2,1)S(1)}, u32[]{:S(2)}, u32[]{:S(2)}) collective-permute-start(bf16[1024,384]{1,0:T(8,128)(2,1)} %collective-permute-done.10), channel_id=1, source_target_pairs={{0,1},{1,0},{2,3},{3,2},{4,5},{5,4},{6,7},{7,6},{8,9},{9,8},{10,11... | collective-permute-start | bytes 2359304 | tf_op jit(solution)/shard_map/ppermute | solution.py:226
  87.8 4.7 %slice-start = ((s8[8388608]{0:T(1024)(128)(4,1)}), s8[4194304]{0:T(1024)(128)(4,1)S(1)}, s32[]{:S(2)}) async-start(s8[8388608]{0:T(1024)(128)(4,1)} %bitcast.84), calls=%async_computation | async-start | bytes 8388608
  90.6 2.4 %slice-start.1 = ((s8[8388608]{0:T(1024)(128)(4,1)}), s8[4194304]{0:T(1024)(128)(4,1)S(1)}, s32[]{:S(2)}) async-start(s8[8388608]{0:T(1024)(128)(4,1)} %bitcast.84), calls=%async_computation.1 | async-start | bytes 8388608
  106.0 3.6 %collective-permute-start.14 = (bf16[1024,384]{1,0:T(8,128)(2,1)}, bf16[1024,384]{1,0:T(8,128)(2,1)S(1)}, u32[]{:S(2)}, u32[]{:S(2)}) collective-permute-start(bf16[1024,384]{1,0:T(8,128)(2,1)} %collective-permute-done.9), channel_id=1, source_target_pairs={{0,1},{1,0},{2,3},{3,2},{4,5},{5,4},{6,7},{7,6},{8,9},{9,8},{10,11... | collective-permute-start | bytes 2359304 | tf_op jit(solution)/shard_map/ppermute | solution.py:237
  106.8 2.8 %copy-start = (f32[1024,1024]{1,0:T(8,128)S(1)}, f32[1024,1024]{1,0:T(8,128)}, u32[]{:S(2)}) copy-start(f32[1024,1024]{1,0:T(8,128)} %add_add_fusion) | copy-start | bytes 12582916

commit v16 on v14

--- a/solution.py
+++ b/solution.py
@@ -160,8 +160,9 @@
     rim_rows = tap_weights.shape[0] - 1
     prior_rows = shifted(projected[:, row_count - rim_rows :], "ctx", 1)
     extended = jnp.concatenate([prior_rows, projected], 1)
+    widened = lax.optimization_barrier(extended[1:3].astype(jnp.float32))
     mixed_input = (
-        featurize(extended, tap_weights, 1, row_count) * featurize(extended, tap_weights, 2, row_count)
+        featurize(widened, tap_weights[:, 1:3], 0, row_count) * featurize(widened, tap_weights[:, 1:3], 1, row_count)
     ).astype(jnp.bfloat16)
     x = mixed_input.astype(jnp.float32)
     span = row_count // SEGMENTS

time: 114 us -> 112 us (0.982)
  other arithmetic: 27.4 us -> 25.7 us
    convert_element_type x1, other arithmetic: 8.74 us -> 4.2 us  [shards(): x = mixed_input.astype(jnp.float32)]
    convert_element_type x0 -> x1, other arithmetic: none -> 2.86 us  [shards(): widened = lax.optimization_barrier(extended[1:3].astype(jnp.float32))]
where the time goes in v16:
time: 112 us; the launch traced here: 111 us
  starting transfers between devices  26.3 us (23%)
  Pallas kernels  26 us (23%)
  other arithmetic  25.7 us (23%)
  matrix products  22.9 us (20%)
  waiting for transfers between devices  6.5 us (6%)
  local copies, waits for them, and re-layouts  3.38 us (3%)
    ppermute x8, starting transfers between devices, shifted(): lax.ppermute(value, axis, [(source, source + steps) for source in range(i...  19 us
    pallas_call x3, Pallas kernels, run_recurrence(): pl.pallas_call(recurrence_kernel, grid=(group_count,), in_specs=[pl.Block...  17.3 us
    dot_general x6, matrix products, part(): return jnp.dot(value, rows, preferred_element_type=jnp.float32)  16.7 us
    convert_element_type x3, other arithmetic, shards(): gated_mix = gated_mix.astype(jnp.bfloat16)  9.51 us
    pallas_call x1, Pallas kernels, run_end_state(): pl.pallas_call(end_state_kernel, grid=(width // LANES,), in_specs=[pl.Blo...  8.66 us
    ppermute x3, waiting for transfers between devices, shards(): lax.ppermute(gated_mix, 'ch', [(i, i ^ 2) for i in range(ch_count)])  6.43 us
    convert_element_type x1, other arithmetic, shards(): x = mixed_input.astype(jnp.float32)  4.2 us
    dot_general x1, matrix products, project_pieces(): total = total + jnp.dot(near, rows_near, preferred_element_type=jnp.float32)  3.94 us
  transfers between devices with their start and end apart: 15, of which 2 were waited for; matrix products, arithmetic and copies ran while one was open for 31% of the time, Pallas kernels for 11%

profile of v16, /device:TPU:1, one launch (start us, length us, event | category | flops | bytes accessed | tf_op | source)
XLA Modules:
  0.0 111.1 jit_solution(18083259289207549729)
XLA Ops:
  0.8 4.0 %collective-permute-start = (bf16[3,2,1024]{2,1,0:T(2,128)(2,1)S(1)}, bf16[3,2,1024]{2,1,0:T(2,128)(2,1)S(1)}, u32[]{:S(2)}, u32[]{:S(2)}) collective-permute-start(bf16[3,2,1024]{2,1,0:T(2,128)(2,1)S(1)} %slice.152), channel_id=1, source_target_pairs={{0,4},{4,8},{8,12},{12,16},{16,20},{20,24},{24,28},{1,5},{5,9},{9,... | collective-permute-start | bytes 36872 | tf_op jit(solution)/shard_map/ppermute | solution.py:15
  8.0 1.5 %fusion.60 = (f32[16,1024]{1,0:T(8,128)S(1)}, f32[16,1024]{1,0:T(8,128)}) fusion(f32[16,1024]{1,0:T(8,128)} %param.8), kind=kLoop, calls=%fused_computation.108 | loop fusion | flops 16384 | bytes 196608 | tf_op jit(solution)/shard_map/neg | solution.py:170
  9.5 2.9 %fusion.1 = f32[2,1026,1024]{2,1,0:T(8,128)S(1)} fusion(bf16[3,2,1024]{2,1,0:T(2,128)(2,1)S(1)} %collective-permute-done, bf16[3,1024,1024]{2,1,0:T(8,128)(2,1)} %param.6), kind=kLoop, calls=%fused_computation.5 | loop fusion | flops 8404992 | bytes 14708736 | tf_op jit(solution)/shard_map/convert_element_type | solution.py:163
  12.4 4.2 %fusion.58 = (f32[1024,1024]{1,0:T(8,128)}, bf16[1024,1024]{1,0:T(8,128)(2,1)S(1)}) fusion(f32[2,1026,1024]{2,1,0:T(8,128)S(1)} %fusion.1, f32[1024]{0:T(1024)S(1)} %bitcast.115, f32[1024]{0:T(1024)S(1)} %bitcast.111, f32[1024]{0:T(1024)S(1)} %bitcast.112, f32[1024]{0:T(1024)S(1)} %bitcast.113, f32[1024]{0:T(1024)S(1)} %bitcast.114, f32[1024]{0:T(1024)S(1)} %bitcast.110), kind=kLoop, calls=%fused_computation.107 | loop fusion | flops 13631488 | bytes 31481856 | tf_op jit(solution)/shard_map/convert_element_type | solution.py:167
  16.6 8.7 %shard_map.64 = f32[16,8,1024]{2,1,0:T(8,128)} custom-call(f32[1024,1024]{1,0:T(8,128)} %get-tuple-element.19.x_ref, f32[16,1024]{1,0:T(8,128)} %get-tuple-element.36.decay_ref), custom_call_target="tpu_custom_call" | custom-call | tf_op jit(solution)/shard_map/pallas_call | solution.py:62
  25.2 1.3 %multiply_reduce_fusion.1 = f32[16,1024]{1,0:T(8,128)S(1)} fusion(f32[16,8,1024]{2,1,0:T(8,128)} %shard_map.64, f32[8]{0:T(128)S(1)} %subtract_multiply_fusion, f32[16,1024]{1,0:T(8,128)S(1)} %get-tuple-element.35), kind=kLoop, calls=%fused_computation.76 | loop fusion | flops 376832 | bytes 655392 | tf_op jit(solution)/shard_map/reduce_sum | solution.py:110
  26.5 4.3 %collective-permute-start.7 = (f32[16,1024]{1,0:T(8,128)S(1)}, f32[16,1024]{1,0:T(8,128)S(1)}, u32[]{:S(2)}, u32[]{:S(2)}) collective-permute-start(f32[16,1024]{1,0:T(8,128)S(1)} %multiply_reduce_fusion.1), channel_id=1, source_target_pairs={{0,28},{1,29},{2,30},{3,31}} | collective-permute-start | bytes 196616 | tf_op jit(solution)/shard_map/ppermute | solution.py:15
  30.9 1.6 %collective-permute-start.6 = (f32[16,1024]{1,0:T(8,128)S(1)}, f32[16,1024]{1,0:T(8,128)S(1)}, u32[]{:S(2)}, u32[]{:S(2)}) collective-permute-start(f32[16,1024]{1,0:T(8,128)S(1)} %multiply_reduce_fusion.1), channel_id=1, source_target_pairs={{0,24},{4,28},{1,25},{5,29},{2,26},{6,30},{3,27},{7,31}} | collective-permute-start | bytes 196616 | tf_op jit(solution)/shard_map/ppermute | solution.py:15
  32.5 1.3 %collective-permute-start.5 = (f32[16,1024]{1,0:T(8,128)S(1)}, f32[16,1024]{1,0:T(8,128)S(1)}, u32[]{:S(2)}, u32[]{:S(2)}) collective-permute-start(f32[16,1024]{1,0:T(8,128)S(1)} %multiply_reduce_fusion.1), channel_id=1, source_target_pairs={{0,20},{4,24},{8,28},{1,21},{5,25},{9,29},{2,22},{6,26},{10,30},{3... | collective-permute-start | bytes 196616 | tf_op jit(solution)/shard_map/ppermute | solution.py:15
  33.8 1.3 %collective-permute-start.4 = (f32[16,1024]{1,0:T(8,128)S(1)}, f32[16,1024]{1,0:T(8,128)S(1)}, u32[]{:S(2)}, u32[]{:S(2)}) collective-permute-start(f32[16,1024]{1,0:T(8,128)S(1)} %multiply_reduce_fusion.1), channel_id=1, source_target_pairs={{0,16},{4,20},{8,24},{12,28},{1,17},{5,21},{9,25},{13,29},{2,18},{... | collective-permute-start | bytes 196616 | tf_op jit(solution)/shard_map/ppermute | solution.py:15
  35.1 1.9 %collective-permute-start.3 = (f32[16,1024]{1,0:T(8,128)S(1)}, f32[16,1024]{1,0:T(8,128)S(1)}, u32[]{:S(2)}, u32[]{:S(2)}) collective-permute-start(f32[16,1024]{1,0:T(8,128)S(1)} %multiply_reduce_fusion.1), channel_id=1, source_target_pairs={{0,12},{4,16},{8,20},{12,24},{16,28},{1,13},{5,17},{9,21},{13,25},... | collective-permute-start | bytes 196616 | tf_op jit(solution)/shard_map/ppermute | solution.py:15
  37.0 1.4 %copy.15 = f32[16,1024,8]{1,0,2:T(8,128)S(1)} copy(f32[16,1024,8]{1,2,0:T(8,128)} %bitcast.107) | data formatting | bytes 1048576
  38.3 1.6 %collective-permute-start.2 = (f32[16,1024]{1,0:T(8,128)S(1)}, f32[16,1024]{1,0:T(8,128)S(1)}, u32[]{:S(2)}, u32[]{:S(2)}) collective-permute-start(f32[16,1024]{1,0:T(8,128)S(1)} %multiply_reduce_fusion.1), channel_id=1, source_target_pairs={{0,8},{4,12},{8,16},{12,20},{16,24},{20,28},{1,9},{5,13},{9,17},{1... | collective-permute-start | bytes 196616 | tf_op jit(solution)/shard_map/ppermute | solution.py:15
  39.9 3.1 %collective-permute-start.1 = (f32[16,1024]{1,0:T(8,128)S(1)}, f32[16,1024]{1,0:T(8,128)S(1)}, u32[]{:S(2)}, u32[]{:S(2)}) collective-permute-start(f32[16,1024]{1,0:T(8,128)S(1)} %multiply_reduce_fusion.1), channel_id=1, source_target_pairs={{0,4},{4,8},{8,12},{12,16},{16,20},{20,24},{24,28},{1,5},{5,9},{9,... | collective-permute-start | bytes 196616 | tf_op jit(solution)/shard_map/ppermute | solution.py:15
  43.0 1.2 %multiply_reduce_fusion = f32[16,1024,8]{1,0,2:T(8,128)S(1)} fusion(f32[16,1024,8]{1,0,2:T(8,128)S(1)} %copy.15, f32[8,8]{1,0:T(8,128)S(1)} %maximum_multiply_fusion, f32[16,1024]{1,0:T(8,128)S(1)} %get-tuple-element.35, pred[8,8]{1,0:T(8,128)(4,1)S(1)} %iota_compare_fusion), kind=kLoop, calls=%fused_computation.24 | loop fusion | flops 4063232 | bytes 1114432
  45.6 4.7 %shard_map.65 = f32[1024,256]{1,0:T(8,128)} custom-call(f32[1024,1024]{1,0:T(8,128)} %get-tuple-element.19.x_ref, f32[16,1024]{1,0:T(8,128)} %get-tuple-element.36.decay_ref, f32[16,1024]{1,0:T(8,128)} %residue_ref.5, f32[16,8,1024]{2,1,0:T(8,128)} %bitcast_add_fusion.start_ref), custom_call_target="tpu_custom_call" | custom-call | tf_op jit(solution)/shard_map/pallas_call | solution.py:78
  50.4 2.4 %fusion.28 = bf16[1024,256]{1,0:T(8,128)(2,1)S(1)} fusion(bf16[1024,1024]{1,0:T(8,128)(2,1)S(1)} %get-tuple-element.34, bf16[3,1024,1024]{2,1,0:T(8,128)(2,1)} %param.6, bf16[3,2,1024]{2,1,0:T(2,128)(2,1)S(1)} %collective-permute-done, f32[256]{0:T(256)S(1)} %slice-done.2, f32[1024,256]{1,0:T(8,128)} %shard_map.65, f32[256]{0:T(256)S(1)} %bitcast.117, ...), kind=kLoop, calls=%fused_computation.52 | loop fusion | flops 6029312 | bytes 8929280 | tf_op jit(solution)/shard_map/convert_element_type | solution.py:193
  52.8 1.3 %collective-permute-start.8 = (bf16[1024,256]{1,0:T(8,128)(2,1)S(1)}, bf16[1024,256]{1,0:T(8,128)(2,1)S(1)}, u32[]{:S(2)}, u32[]{:S(2)}) collective-permute-start(bf16[1024,256]{1,0:T(8,128)(2,1)S(1)} %fusion.28), channel_id=1, source_target_pairs={{0,2},{1,3},{2,0},{3,1},{4,6},{5,7},{6,4},{7,5},{8,10},{9,11},{10,... | collective-permute-start | bytes 1572872 | tf_op jit(solution)/shard_map/ppermute | solution.py:198
  54.1 6.2 %shard_map.66 = f32[1024,384]{1,0:T(8,128)} custom-call(f32[1024,1024]{1,0:T(8,128)} %get-tuple-element.19.x_ref, f32[16,1024]{1,0:T(8,128)} %get-tuple-element.36.decay_ref, f32[16,1024]{1,0:T(8,128)} %residue_ref.5, f32[16,8,1024]{2,1,0:T(8,128)} %bitcast_add_fusion.start_ref), custom_call_target="tpu_custom_call" | custom-call | tf_op jit(solution)/shard_map/pallas_call | solution.py:78
  60.3 4.0 %fusion.20 = bf16[1024,384]{1,0:T(8,128)(2,1)} fusion(bf16[1024,1024]{1,0:T(8,128)(2,1)S(1)} %get-tuple-element.34, f32[384]{0:T(512)S(1)} %get-tuple-element.46, f32[1024,384]{1,0:T(8,128)} %shard_map.66, f32[384]{0:T(512)S(1)} %get-tuple-element.28, f32[384]{0:T(512)S(1)} %get-tuple-element.29, bf16[3,1024,1024]{2,1,0:T(8,128)(2,1)} %param.6, ...), kind=kLoop, calls=%fused_computation.38 | loop fusion | flops 9043968 | bytes 10242048 | tf_op jit(solution)/shard_map/convert_element_type | solution.py:193
  64.5 6.4 %shard_map.67 = f32[1024,384]{1,0:T(8,128)} custom-call(f32[1024,1024]{1,0:T(8,128)} %get-tuple-element.19.x_ref, f32[16,1024]{1,0:T(8,128)} %get-tuple-element.36.decay_ref, f32[16,1024]{1,0:T(8,128)} %residue_ref.5, f32[16,8,1024]{2,1,0:T(8,128)} %bitcast_add_fusion.start_ref), custom_call_target="tpu_custom_call" | custom-call | tf_op jit(solution)/shard_map/pallas_call | solution.py:78
  70.9 3.1 %fusion.24 = bf16[1024,384]{1,0:T(8,128)(2,1)S(1)} fusion(bf16[1024,1024]{1,0:T(8,128)(2,1)S(1)} %get-tuple-element.34, bf16[3,1024,1024]{2,1,0:T(8,128)(2,1)} %param.6, bf16[3,2,1024]{2,1,0:T(2,128)(2,1)S(1)} %collective-permute-done, f32[384]{0:T(512)S(1)} %get-tuple-element.47, f32[1024,384]{1,0:T(8,128)} %shard_map.67, f32[384]{0:T(512)S(1)} %get-tuple-element.31, ...), kind=kLoop, calls=%fused_computation.45 | loop fusion | flops 9043968 | bytes 10242048 | tf_op jit(solution)/shard_map/convert_element_type | solution.py:193
  74.0 1.4 %pad_maximum_fusion = bf16[1024,1024]{1,0:T(8,128)(2,1)S(1)} fusion(bf16[1024,384]{1,0:T(8,128)(2,1)S(1)} %fusion.24, bf16[1024,384]{1,0:T(8,128)(2,1)} %fusion.20, bf16[1024,256]{1,0:T(8,128)(2,1)S(1)} %fusion.28), kind=kLoop, calls=%fused_computation.30 | loop fusion | flops 6291456 | bytes 4194304 | tf_op jit(solution)/shard_map/concatenate | solution.py:221
  75.5 5.5 %collective-permute-done.10 = bf16[1024,384]{1,0:T(8,128)(2,1)} collective-permute-done((bf16[1024,384]{1,0:T(8,128)(2,1)}, bf16[1024,384]{1,0:T(8,128)(2,1)}, u32[]{:S(2)}, u32[]{:S(2)}) %collective-permute-start.10) | collective-permute-done | bytes 786464 | tf_op jit(solution)/shard_map/ppermute | solution.py:198
  80.9 3.6 %collective-permute-start.11 = (bf16[1024,1024]{1,0:T(8,128)(2,1)S(1)}, bf16[1024,1024]{1,0:T(8,128)(2,1)}, u32[]{:S(2)}, u32[]{:S(2)}) collective-permute-start(bf16[1024,1024]{1,0:T(8,128)(2,1)S(1)} %pad_maximum_fusion), channel_id=1, source_target_pairs={{0,1},{1,0},{2,3},{3,2},{4,5},{5,4},{6,7},{7,6},{8,9},{9,8},{10,11... | collective-permute-start | bytes 6291464 | tf_op jit(solution)/shard_map/ppermute | solution.py:225
  85.9 2.8 %fusion.42 = f32[1024,1024]{1,0:T(8,128)S(1)} fusion(bf16[1024,384]{1,0:T(8,128)(2,1)} %collective-permute-done.10, bf16[4096,1024]{1,0:T(8,128)(2,1)} %param.11, s32[]{:T(128)S(6)} %select_n.31), kind=kOutput, calls=%fused_computation.66 | convolution fusion | flops 805306368 | bytes 5767172 | tf_op jit(solution)/shard_map/dot_general | solution.py:218
  88.7 1.9 %fusion.48 = f32[1024,1024]{1,0:T(8,128)S(1)} fusion(bf16[1024,256]{1,0:T(8,128)(2,1)S(1)} %copy-done.2, bf16[4096,1024]{1,0:T(8,128)(2,1)} %param.11, s32[]{:T(128)S(6)} %select_n.30), kind=kOutput, calls=%fused_computation.74 | convolution fusion | flops 536870912 | bytes 5242884 | tf_op jit(solution)/shard_map/dot_general | solution.py:218
  91.0 2.3 %fusion.16 = f32[1024,1024]{1,0:T(8,128)S(1)} fusion(bf16[1024,1024]{1,0:T(8,128)(2,1)S(1)} %pad_maximum_fusion, bf16[4096,1024]{1,0:T(8,128)(2,1)S(1)} %bitcast.109, s32[]{:T(128)S(6)} %select_n.29), kind=kOutput, calls=%fused_computation.33 | convolution fusion | flops 2147483648 | bytes 8388612 | tf_op jit(solution)/shard_map/dot_general | solution.py:229
  94.1 3.9 %fusion.14 = f32[1024,1024]{1,0:T(8,128)S(1)} fusion(bf16[1024,1024]{1,0:T(8,128)(2,1)} %collective-permute-done.11, bf16[4096,1024]{1,0:T(8,128)(2,1)S(1)} %bitcast.109, s32[]{:T(128)S(6)} %select_n.32), kind=kOutput, calls=%fused_computation.31 | convolution fusion | flops 2147483648 | bytes 8388612 | tf_op jit(solution)/shard_map/dot_general | solution.py:232
  98.1 4.8 %add_add_fusion = f32[1024,1024]{1,0:T(8,128)} fusion(f32[1024,1024]{1,0:T(8,128)S(1)} %fusion.46, f32[1024,1024]{1,0:T(8,128)S(1)} %fusion.14, f32[1024,1024]{1,0:T(8,128)S(1)} %fusion.42, f32[1024,1024]{1,0:T(8,128)S(1)} %fusion.16, f32[1024,1024]{1,0:T(8,128)S(1)} %fusion.48, bf16[1024,384]{1,0:T(8,128)(2,1)S(1)} %collective-permute-done.13, ...), kind=kOutput, calls=%fused_computation.26 | convolution fusion | flops 810549248 | bytes 26738692 | tf_op jit(solution)/shard_map/dot_general | solution.py:218
  104.6 2.8 %fusion.36 = f32[1024,1024]{1,0:T(8,128)S(1)} fusion(bf16[1024,384]{1,0:T(8,128)(2,1)} %collective-permute-done.9, bf16[4096,1024]{1,0:T(8,128)(2,1)} %param.11, s32[]{:T(128)S(6)} %select_n.35), kind=kOutput, calls=%fused_computation.62 | convolution fusion | flops 805306368 | bytes 5767172 | tf_op jit(solution)/shard_map/dot_general | solution.py:218
  107.4 3.7 %add_convert_fusion = bf16[1024,1024]{1,0:T(8,128)(2,1)} fusion(f32[1024,1024]{1,0:T(8,128)S(1)} %copy-done, f32[1024,1024]{1,0:T(8,128)S(1)} %fusion.36, bf16[1024,384]{1,0:T(8,128)(2,1)S(1)} %collective-permute-done.14, bf16[4096,1024]{1,0:T(8,128)(2,1)} %param.11, s32[]{:T(128)S(6)} %select_n.36), kind=kOutput, calls=%fused_computation.25 | convolution fusion | flops 808452096 | bytes 12058628 | tf_op jit(solution)/shard_map/dot_general | solution.py:218
  (47 shorter events, 9.9 us)
Async XLA Ops:
  0.8 8.7 %collective-permute-start = (bf16[3,2,1024]{2,1,0:T(2,128)(2,1)S(1)}, bf16[3,2,1024]{2,1,0:T(2,128)(2,1)S(1)}, u32[]{:S(2)}, u32[]{:S(2)}) collective-permute-start(bf16[3,2,1024]{2,1,0:T(2,128)(2,1)S(1)} %slice.152), channel_id=1, source_target_pairs={{0,4},{4,8},{8,12},{12,16},{16,20},{20,24},{24,28},{1,5},{5,9},{9,... | collective-permute-start | bytes 36872 | tf_op jit(solution)/shard_map/ppermute | solution.py:15
  16.6 27.8 %copy-start.3 = (f32[16,1024]{1,0:T(8,128)S(1)}, f32[16,1024]{1,0:T(8,128)}, u32[]{:S(2)}) copy-start(f32[16,1024]{1,0:T(8,128)} %param.8) | copy-start | bytes 196612
  26.5 11.8 %collective-permute-start.7 = (f32[16,1024]{1,0:T(8,128)S(1)}, f32[16,1024]{1,0:T(8,128)S(1)}, u32[]{:S(2)}, u32[]{:S(2)}) collective-permute-start(f32[16,1024]{1,0:T(8,128)S(1)} %multiply_reduce_fusion.1), channel_id=1, source_target_pairs={{0,28},{1,29},{2,30},{3,31}} | collective-permute-start | bytes 196616 | tf_op jit(solution)/shard_map/ppermute | solution.py:15
  30.9 9.1 %collective-permute-start.6 = (f32[16,1024]{1,0:T(8,128)S(1)}, f32[16,1024]{1,0:T(8,128)S(1)}, u32[]{:S(2)}, u32[]{:S(2)}) collective-permute-start(f32[16,1024]{1,0:T(8,128)S(1)} %multiply_reduce_fusion.1), channel_id=1, source_target_pairs={{0,24},{4,28},{1,25},{5,29},{2,26},{6,30},{3,27},{7,31}} | collective-permute-start | bytes 196616 | tf_op jit(solution)/shard_map/ppermute | solution.py:15
  32.5 11.8 %collective-permute-start.5 = (f32[16,1024]{1,0:T(8,128)S(1)}, f32[16,1024]{1,0:T(8,128)S(1)}, u32[]{:S(2)}, u32[]{:S(2)}) collective-permute-start(f32[16,1024]{1,0:T(8,128)S(1)} %multiply_reduce_fusion.1), channel_id=1, source_target_pairs={{0,20},{4,24},{8,28},{1,21},{5,25},{9,29},{2,22},{6,26},{10,30},{3... | collective-permute-start | bytes 196616 | tf_op jit(solution)/shard_map/ppermute | solution.py:15
  33.8 10.5 %collective-permute-start.4 = (f32[16,1024]{1,0:T(8,128)S(1)}, f32[16,1024]{1,0:T(8,128)S(1)}, u32[]{:S(2)}, u32[]{:S(2)}) collective-permute-start(f32[16,1024]{1,0:T(8,128)S(1)} %multiply_reduce_fusion.1), channel_id=1, source_target_pairs={{0,16},{4,20},{8,24},{12,28},{1,17},{5,21},{9,25},{13,29},{2,18},{... | collective-permute-start | bytes 196616 | tf_op jit(solution)/shard_map/ppermute | solution.py:15
  35.1 9.2 %collective-permute-start.3 = (f32[16,1024]{1,0:T(8,128)S(1)}, f32[16,1024]{1,0:T(8,128)S(1)}, u32[]{:S(2)}, u32[]{:S(2)}) collective-permute-start(f32[16,1024]{1,0:T(8,128)S(1)} %multiply_reduce_fusion.1), channel_id=1, source_target_pairs={{0,12},{4,16},{8,20},{12,24},{16,28},{1,13},{5,17},{9,21},{13,25},... | collective-permute-start | bytes 196616 | tf_op jit(solution)/shard_map/ppermute | solution.py:15
  38.3 6.0 %collective-permute-start.2 = (f32[16,1024]{1,0:T(8,128)S(1)}, f32[16,1024]{1,0:T(8,128)S(1)}, u32[]{:S(2)}, u32[]{:S(2)}) collective-permute-start(f32[16,1024]{1,0:T(8,128)S(1)} %multiply_reduce_fusion.1), channel_id=1, source_target_pairs={{0,8},{4,12},{8,16},{12,20},{16,24},{20,28},{1,9},{5,13},{9,17},{1... | collective-permute-start | bytes 196616 | tf_op jit(solution)/shard_map/ppermute | solution.py:15
  39.9 4.4 %collective-permute-start.1 = (f32[16,1024]{1,0:T(8,128)S(1)}, f32[16,1024]{1,0:T(8,128)S(1)}, u32[]{:S(2)}, u32[]{:S(2)}) collective-permute-start(f32[16,1024]{1,0:T(8,128)S(1)} %multiply_reduce_fusion.1), channel_id=1, source_target_pairs={{0,4},{4,8},{8,12},{12,16},{16,20},{20,24},{24,28},{1,5},{5,9},{9,... | collective-permute-start | bytes 196616 | tf_op jit(solution)/shard_map/ppermute | solution.py:15
  44.3 6.1 %slice-start.2 = ((f32[1024]{0:T(1024)}), f32[256]{0:T(256)S(1)}, s32[]{:S(2)}) async-start(f32[1024]{0:T(1024)} %param.10), calls=%async_computation.2 | async-start | bytes 2048 | tf_op jit(solution)/shard_map/slice | solution.py:191
  52.8 11.7 %collective-permute-start.8 = (bf16[1024,256]{1,0:T(8,128)(2,1)S(1)}, bf16[1024,256]{1,0:T(8,128)(2,1)S(1)}, u32[]{:S(2)}, u32[]{:S(2)}) collective-permute-start(bf16[1024,256]{1,0:T(8,128)(2,1)S(1)} %fusion.28), channel_id=1, source_target_pairs={{0,2},{1,3},{2,0},{3,1},{4,6},{5,7},{6,4},{7,5},{8,10},{9,11},{10,... | collective-permute-start | bytes 1572872 | tf_op jit(solution)/shard_map/ppermute | solution.py:198
  64.2 16.7 %collective-permute-start.10 = (bf16[1024,384]{1,0:T(8,128)(2,1)}, bf16[1024,384]{1,0:T(8,128)(2,1)}, u32[]{:S(2)}, u32[]{:S(2)}) collective-permute-start(bf16[1024,384]{1,0:T(8,128)(2,1)} %fusion.20), channel_id=1, source_target_pairs={{0,2},{1,3},{2,0},{3,1},{4,6},{5,7},{6,4},{7,5},{8,10},{9,11},{10,... | collective-permute-start | bytes 2359304 | tf_op jit(solution)/shard_map/ppermute | solution.py:198
  64.5 6.4 %copy-start.1 = (bf16[1024,256]{1,0:T(8,128)(2,1)}, bf16[1024,256]{1,0:T(8,128)(2,1)S(1)}, u32[]{:S(2)}) copy-start(bf16[1024,256]{1,0:T(8,128)(2,1)S(1)} %collective-permute-done.8) | copy-start | bytes 1572868
  75.4 13.2 %copy-start.2 = (bf16[1024,256]{1,0:T(8,128)(2,1)S(1)}, bf16[1024,256]{1,0:T(8,128)(2,1)}, u32[]{:S(2)}) copy-start(bf16[1024,256]{1,0:T(8,128)(2,1)} %copy-done.1) | copy-start | bytes 1572868
  80.9 13.2 %collective-permute-start.11 = (bf16[1024,1024]{1,0:T(8,128)(2,1)S(1)}, bf16[1024,1024]{1,0:T(8,128)(2,1)}, u32[]{:S(2)}, u32[]{:S(2)}) collective-permute-start(bf16[1024,1024]{1,0:T(8,128)(2,1)S(1)} %pad_maximum_fusion), channel_id=1, source_target_pairs={{0,1},{1,0},{2,3},{3,2},{4,5},{5,4},{6,7},{7,6},{8,9},{9,8},{10,11... | collective-permute-start | bytes 6291464 | tf_op jit(solution)/shard_map/ppermute | solution.py:225
  84.5 19.3 %collective-permute-start.9 = (bf16[1024,384]{1,0:T(8,128)(2,1)S(1)}, bf16[1024,384]{1,0:T(8,128)(2,1)}, u32[]{:S(2)}, u32[]{:S(2)}) collective-permute-start(bf16[1024,384]{1,0:T(8,128)(2,1)S(1)} %fusion.24), channel_id=1, source_target_pairs={{0,2},{1,3},{2,0},{3,1},{4,6},{5,7},{6,4},{7,5},{8,10},{9,11},{10,... | collective-permute-start | bytes 2359304 | tf_op jit(solution)/shard_map/ppermute | solution.py:198
  85.4 8.0 %collective-permute-start.12 = (bf16[1024,256]{1,0:T(8,128)(2,1)}, bf16[1024,256]{1,0:T(8,128)(2,1)S(1)}, u32[]{:S(2)}, u32[]{:S(2)}) collective-permute-start(bf16[1024,256]{1,0:T(8,128)(2,1)} %copy-done.1), channel_id=1, source_target_pairs={{0,1},{1,0},{2,3},{3,2},{4,5},{5,4},{6,7},{7,6},{8,9},{9,8},{10,11... | collective-permute-start | bytes 1572872 | tf_op jit(solution)/shard_map/ppermute | solution.py:226
  85.6 12.4 %collective-permute-start.13 = (bf16[1024,384]{1,0:T(8,128)(2,1)}, bf16[1024,384]{1,0:T(8,128)(2,1)S(1)}, u32[]{:S(2)}, u32[]{:S(2)}) collective-permute-start(bf16[1024,384]{1,0:T(8,128)(2,1)} %collective-permute-done.10), channel_id=1, source_target_pairs={{0,1},{1,0},{2,3},{3,2},{4,5},{5,4},{6,7},{7,6},{8,9},{9,8},{10,11... | collective-permute-start | bytes 2359304 | tf_op jit(solution)/shard_map/ppermute | solution.py:226
  85.9 4.7 %slice-start = ((s8[8388608]{0:T(1024)(128)(4,1)}), s8[4194304]{0:T(1024)(128)(4,1)S(1)}, s32[]{:S(2)}) async-start(s8[8388608]{0:T(1024)(128)(4,1)} %bitcast.108), calls=%async_computation | async-start | bytes 8388608
  88.7 2.4 %slice-start.1 = ((s8[8388608]{0:T(1024)(128)(4,1)}), s8[4194304]{0:T(1024)(128)(4,1)S(1)}, s32[]{:S(2)}) async-start(s8[8388608]{0:T(1024)(128)(4,1)} %bitcast.108), calls=%async_computation.1 | async-start | bytes 8388608
  103.8 3.6 %collective-permute-start.14 = (bf16[1024,384]{1,0:T(8,128)(2,1)}, bf16[1024,384]{1,0:T(8,128)(2,1)S(1)}, u32[]{:S(2)}, u32[]{:S(2)}) collective-permute-start(bf16[1024,384]{1,0:T(8,128)(2,1)} %collective-permute-done.9), channel_id=1, source_target_pairs={{0,1},{1,0},{2,3},{3,2},{4,5},{5,4},{6,7},{7,6},{8,9},{9,8},{10,11... | collective-permute-start | bytes 2359304 | tf_op jit(solution)/shard_map/ppermute | solution.py:237
  104.6 2.8 %copy-start = (f32[1024,1024]{1,0:T(8,128)S(1)}, f32[1024,1024]{1,0:T(8,128)}, u32[]{:S(2)}) copy-start(f32[1024,1024]{1,0:T(8,128)} %add_add_fusion) | copy-start | bytes 12582916

commit v17 on v16

--- a/solution.py
+++ b/solution.py
@@ -178,6 +178,7 @@
     else:
         bounds = [0, width]
     pieces = len(bounds) - 1
+    widened0 = lax.optimization_barrier(extended[0:1].astype(jnp.float32))
     gated = []
     far = []
     x_next = x
@@ -186,7 +187,7 @@
         group_count = (cols.stop - cols.start) // LANES
         long_part = run_recurrence(x_next, decay, residues, starts, cols.start // LANES, group_count)
         long_mix = long_part.astype(jnp.bfloat16)
-        stream0 = featurize(extended[:, :, cols], tap_weights[:, :, cols], 0, row_count)
+        stream0 = featurize(widened0[:, :, cols], tap_weights[:, 0:1, cols], 0, row_count)
         gated_mix = stream0 * (
             long_mix.astype(jnp.float32) + long_bias[None, cols] * mixed_input[:, cols].astype(jnp.float32)
         )

time: 112 us -> 117 us (1.045)
  other arithmetic: 25.7 us -> 32.3 us
    convert_element_type x0 -> x1, other arithmetic: none -> 4.17 us  [shards(): widened0 = lax.optimization_barrier(extended[0:1].astype(jnp.float32))]
    convert_element_type x3, other arithmetic: 9.51 us -> 11.4 us  [shards(): gated_mix = gated_mix.astype(jnp.bfloat16)]
  transfers between devices with their start and end apart: 15 -> 15, of which waited for: 2 -> 2; matrix products, arithmetic and copies ran while one was open for 31% -> 34% of each run, Pallas kernels for 11% -> 11%
where the time goes in v17:
time: 117 us; the launch traced here: 116 us
  other arithmetic  32.3 us (28%)
  Pallas kernels  26 us (22%)
  starting transfers between devices  25.8 us (22%)
  matrix products  22.9 us (20%)
  waiting for transfers between devices  6.35 us (5%)
  local copies, waits for them, and re-layouts  2.34 us (2%)
    ppermute x8, starting transfers between devices, shifted(): lax.ppermute(value, axis, [(source, source + steps) for source in range(i...  19.2 us
    pallas_call x3, Pallas kernels, run_recurrence(): pl.pallas_call(recurrence_kernel, grid=(group_count,), in_specs=[pl.Block...  17.3 us
    dot_general x6, matrix products, part(): return jnp.dot(value, rows, preferred_element_type=jnp.float32)  16.6 us
    convert_element_type x3, other arithmetic, shards(): gated_mix = gated_mix.astype(jnp.bfloat16)  11.4 us
    pallas_call x1, Pallas kernels, run_end_state(): pl.pallas_call(end_state_kernel, grid=(width // LANES,), in_specs=[pl.Blo...  8.63 us
    ppermute x3, waiting for transfers between devices, shards(): lax.ppermute(gated_mix, 'ch', [(i, i ^ 2) for i in range(ch_count)])  6.29 us
    convert_element_type x1, other arithmetic, shards(): x = mixed_input.astype(jnp.float32)  4.21 us
    convert_element_type x1, other arithmetic, shards(): widened0 = lax.optimization_barrier(extended[0:1].astype(jnp.float32))  4.17 us
  transfers between devices with their start and end apart: 15, of which 2 were waited for; matrix products, arithmetic and copies ran while one was open for 34% of the time, Pallas kernels for 11%

profile of v17, /device:TPU:1, one launch (start us, length us, event | category | flops | bytes accessed | tf_op | source)
XLA Modules:
  0.0 116.0 jit_solution(10627067782271785714)
XLA Ops:
  0.8 4.0 %collective-permute-start = (bf16[3,2,1024]{2,1,0:T(2,128)(2,1)S(1)}, bf16[3,2,1024]{2,1,0:T(2,128)(2,1)S(1)}, u32[]{:S(2)}, u32[]{:S(2)}) collective-permute-start(bf16[3,2,1024]{2,1,0:T(2,128)(2,1)S(1)} %slice.150), channel_id=1, source_target_pairs={{0,4},{4,8},{8,12},{12,16},{16,20},{20,24},{24,28},{1,5},{5,9},{9,... | collective-permute-start | bytes 36872 | tf_op jit(solution)/shard_map/ppermute | solution.py:15
  8.0 1.5 %fusion.64 = (f32[16,1024]{1,0:T(8,128)S(1)}, f32[16,1024]{1,0:T(8,128)}) fusion(f32[16,1024]{1,0:T(8,128)} %param.8), kind=kLoop, calls=%fused_computation.104 | loop fusion | flops 16384 | bytes 196608 | tf_op jit(solution)/shard_map/neg | solution.py:170
  9.5 3.4 %fusion = f32[2,1026,1024]{2,1,0:T(8,128)S(1)} fusion(bf16[3,1024,1024]{2,1,0:T(8,128)(2,1)} %param.6, bf16[3,2,1024]{2,1,0:T(2,128)(2,1)S(1)} %collective-permute-done), kind=kLoop, calls=%fused_computation.1 | loop fusion | flops 8404992 | bytes 14708736 | tf_op jit(solution)/shard_map/convert_element_type | solution.py:163
  12.9 4.2 %fusion.62 = (f32[1024,1024]{1,0:T(8,128)}, bf16[1024,1024]{1,0:T(8,128)(2,1)S(1)}) fusion(f32[2,1026,1024]{2,1,0:T(8,128)S(1)} %fusion, f32[1024]{0:T(1024)S(1)} %bitcast.154, f32[1024]{0:T(1024)S(1)} %bitcast.150, f32[1024]{0:T(1024)S(1)} %bitcast.151, f32[1024]{0:T(1024)S(1)} %bitcast.152, f32[1024]{0:T(1024)S(1)} %bitcast.153, f32[1024]{0:T(1024)S(1)} %bitcast.149), kind=kLoop, calls=%fused_computation.103 | loop fusion | flops 13631488 | bytes 31481856 | tf_op jit(solution)/shard_map/convert_element_type | solution.py:167
  17.1 8.6 %shard_map.64 = f32[16,8,1024]{2,1,0:T(8,128)} custom-call(f32[1024,1024]{1,0:T(8,128)} %get-tuple-element.19.x_ref, f32[16,1024]{1,0:T(8,128)} %get-tuple-element.36.decay_ref), custom_call_target="tpu_custom_call" | custom-call | tf_op jit(solution)/shard_map/pallas_call | solution.py:62
  25.8 1.3 %multiply_reduce_fusion.1 = f32[16,1024]{1,0:T(8,128)S(1)} fusion(f32[16,8,1024]{2,1,0:T(8,128)} %shard_map.64, f32[8]{0:T(128)S(1)} %subtract_multiply_fusion, f32[16,1024]{1,0:T(8,128)S(1)} %get-tuple-element.35), kind=kLoop, calls=%fused_computation.72 | loop fusion | flops 376832 | bytes 655392 | tf_op jit(solution)/shard_map/reduce_sum | solution.py:110
  27.1 4.5 %collective-permute-start.7 = (f32[16,1024]{1,0:T(8,128)S(1)}, f32[16,1024]{1,0:T(8,128)S(1)}, u32[]{:S(2)}, u32[]{:S(2)}) collective-permute-start(f32[16,1024]{1,0:T(8,128)S(1)} %multiply_reduce_fusion.1), channel_id=1, source_target_pairs={{0,28},{1,29},{2,30},{3,31}} | collective-permute-start | bytes 196616 | tf_op jit(solution)/shard_map/ppermute | solution.py:15
  31.6 1.6 %collective-permute-start.6 = (f32[16,1024]{1,0:T(8,128)S(1)}, f32[16,1024]{1,0:T(8,128)S(1)}, u32[]{:S(2)}, u32[]{:S(2)}) collective-permute-start(f32[16,1024]{1,0:T(8,128)S(1)} %multiply_reduce_fusion.1), channel_id=1, source_target_pairs={{0,24},{4,28},{1,25},{5,29},{2,26},{6,30},{3,27},{7,31}} | collective-permute-start | bytes 196616 | tf_op jit(solution)/shard_map/ppermute | solution.py:15
  33.1 1.3 %collective-permute-start.5 = (f32[16,1024]{1,0:T(8,128)S(1)}, f32[16,1024]{1,0:T(8,128)S(1)}, u32[]{:S(2)}, u32[]{:S(2)}) collective-permute-start(f32[16,1024]{1,0:T(8,128)S(1)} %multiply_reduce_fusion.1), channel_id=1, source_target_pairs={{0,20},{4,24},{8,28},{1,21},{5,25},{9,29},{2,22},{6,26},{10,30},{3... | collective-permute-start | bytes 196616 | tf_op jit(solution)/shard_map/ppermute | solution.py:15
  34.4 1.3 %collective-permute-start.4 = (f32[16,1024]{1,0:T(8,128)S(1)}, f32[16,1024]{1,0:T(8,128)S(1)}, u32[]{:S(2)}, u32[]{:S(2)}) collective-permute-start(f32[16,1024]{1,0:T(8,128)S(1)} %multiply_reduce_fusion.1), channel_id=1, source_target_pairs={{0,16},{4,20},{8,24},{12,28},{1,17},{5,21},{9,25},{13,29},{2,18},{... | collective-permute-start | bytes 196616 | tf_op jit(solution)/shard_map/ppermute | solution.py:15
  35.7 1.9 %collective-permute-start.3 = (f32[16,1024]{1,0:T(8,128)S(1)}, f32[16,1024]{1,0:T(8,128)S(1)}, u32[]{:S(2)}, u32[]{:S(2)}) collective-permute-start(f32[16,1024]{1,0:T(8,128)S(1)} %multiply_reduce_fusion.1), channel_id=1, source_target_pairs={{0,12},{4,16},{8,20},{12,24},{16,28},{1,13},{5,17},{9,21},{13,25},... | collective-permute-start | bytes 196616 | tf_op jit(solution)/shard_map/ppermute | solution.py:15
  37.7 4.2 %maximum_convert_fusion = f32[1,1026,1024]{2,1,0:T(8,128)} fusion(bf16[3,1024,1024]{2,1,0:T(8,128)(2,1)} %param.6, bf16[3,2,1024]{2,1,0:T(2,128)(2,1)S(1)} %collective-permute-done), kind=kLoop, calls=%fused_computation.23 | loop fusion | flops 4202496 | bytes 10506240 | tf_op jit(solution)/shard_map/convert_element_type | solution.py:181
  42.2 1.6 %collective-permute-start.2 = (f32[16,1024]{1,0:T(8,128)S(1)}, f32[16,1024]{1,0:T(8,128)S(1)}, u32[]{:S(2)}, u32[]{:S(2)}) collective-permute-start(f32[16,1024]{1,0:T(8,128)S(1)} %multiply_reduce_fusion.1), channel_id=1, source_target_pairs={{0,8},{4,12},{8,16},{12,20},{16,24},{20,28},{1,9},{5,13},{9,17},{1... | collective-permute-start | bytes 196616 | tf_op jit(solution)/shard_map/ppermute | solution.py:15
  43.7 3.1 %collective-permute-start.1 = (f32[16,1024]{1,0:T(8,128)S(1)}, f32[16,1024]{1,0:T(8,128)S(1)}, u32[]{:S(2)}, u32[]{:S(2)}) collective-permute-start(f32[16,1024]{1,0:T(8,128)S(1)} %multiply_reduce_fusion.1), channel_id=1, source_target_pairs={{0,4},{4,8},{8,12},{12,16},{16,20},{20,24},{24,28},{1,5},{5,9},{9,... | collective-permute-start | bytes 196616 | tf_op jit(solution)/shard_map/ppermute | solution.py:15
  49.4 4.7 %shard_map.65 = f32[1024,256]{1,0:T(8,128)} custom-call(f32[1024,1024]{1,0:T(8,128)} %get-tuple-element.19.x_ref, f32[16,1024]{1,0:T(8,128)} %get-tuple-element.36.decay_ref, f32[16,1024]{1,0:T(8,128)} %residue_ref.5, f32[16,8,1024]{2,1,0:T(8,128)} %bitcast_add_fusion.start_ref), custom_call_target="tpu_custom_call" | custom-call | tf_op jit(solution)/shard_map/pallas_call | solution.py:78
  54.2 2.8 %fusion.34 = bf16[1024,256]{1,0:T(8,128)(2,1)S(1)} fusion(f32[1,1026,1024]{2,1,0:T(8,128)} %maximum_convert_fusion, bf16[1024,1024]{1,0:T(8,128)(2,1)S(1)} %get-tuple-element.34, f32[256]{0:T(256)S(1)} %slice-done.2, f32[1024,256]{1,0:T(8,128)} %shard_map.65, f32[256]{0:T(256)S(1)} %bitcast.156, f32[256]{0:T(256)S(1)} %bitcast.157, f32[256]{0:T(256)S(1)} %bitcast.155), kind=kLoop, calls=%fused_computation.53 | loop fusion | flops 3145728 | bytes 5246976 | tf_op jit(solution)/shard_map/convert_element_type | solution.py:194
  57.0 1.3 %collective-permute-start.8 = (bf16[1024,256]{1,0:T(8,128)(2,1)S(1)}, bf16[1024,256]{1,0:T(8,128)(2,1)S(1)}, u32[]{:S(2)}, u32[]{:S(2)}) collective-permute-start(bf16[1024,256]{1,0:T(8,128)(2,1)S(1)} %fusion.34), channel_id=1, source_target_pairs={{0,2},{1,3},{2,0},{3,1},{4,6},{5,7},{6,4},{7,5},{8,10},{9,11},{10,... | collective-permute-start | bytes 1572872 | tf_op jit(solution)/shard_map/ppermute | solution.py:199
  58.3 6.2 %shard_map.66 = f32[1024,384]{1,0:T(8,128)} custom-call(f32[1024,1024]{1,0:T(8,128)} %get-tuple-element.19.x_ref, f32[16,1024]{1,0:T(8,128)} %get-tuple-element.36.decay_ref, f32[16,1024]{1,0:T(8,128)} %residue_ref.5, f32[16,8,1024]{2,1,0:T(8,128)} %bitcast_add_fusion.start_ref), custom_call_target="tpu_custom_call" | custom-call | tf_op jit(solution)/shard_map/pallas_call | solution.py:78
  64.5 4.7 %fusion.20 = bf16[1024,384]{1,0:T(8,128)(2,1)} fusion(f32[1,1026,1024]{2,1,0:T(8,128)} %maximum_convert_fusion, bf16[1024,1024]{1,0:T(8,128)(2,1)S(1)} %get-tuple-element.34, f32[384]{0:T(512)S(1)} %get-tuple-element.46, f32[1024,384]{1,0:T(8,128)} %shard_map.66, f32[384]{0:T(512)S(1)} %get-tuple-element.28, f32[384]{0:T(512)S(1)} %get-tuple-element.29, ...), kind=kLoop, calls=%fused_computation.33 | loop fusion | flops 4718592 | bytes 7870464 | tf_op jit(solution)/shard_map/convert_element_type | solution.py:194
  69.5 6.4 %shard_map.67 = f32[1024,384]{1,0:T(8,128)} custom-call(f32[1024,1024]{1,0:T(8,128)} %get-tuple-element.19.x_ref, f32[16,1024]{1,0:T(8,128)} %get-tuple-element.36.decay_ref, f32[16,1024]{1,0:T(8,128)} %residue_ref.5, f32[16,8,1024]{2,1,0:T(8,128)} %bitcast_add_fusion.start_ref), custom_call_target="tpu_custom_call" | custom-call | tf_op jit(solution)/shard_map/pallas_call | solution.py:78
  75.9 3.9 %fusion.27 = bf16[1024,384]{1,0:T(8,128)(2,1)S(1)} fusion(f32[1,1026,1024]{2,1,0:T(8,128)} %maximum_convert_fusion, bf16[1024,1024]{1,0:T(8,128)(2,1)S(1)} %get-tuple-element.34, f32[384]{0:T(512)S(1)} %get-tuple-element.47, f32[1024,384]{1,0:T(8,128)} %shard_map.67, f32[384]{0:T(512)S(1)} %get-tuple-element.31, f32[384]{0:T(512)S(1)} %get-tuple-element.32, ...), kind=kLoop, calls=%fused_computation.43 | loop fusion | flops 4718592 | bytes 7870464 | tf_op jit(solution)/shard_map/convert_element_type | solution.py:194
  79.7 1.4 %pad_maximum_fusion.1 = bf16[1024,1024]{1,0:T(8,128)(2,1)S(1)} fusion(bf16[1024,384]{1,0:T(8,128)(2,1)S(1)} %fusion.27, bf16[1024,384]{1,0:T(8,128)(2,1)} %fusion.20, bf16[1024,256]{1,0:T(8,128)(2,1)S(1)} %fusion.34), kind=kLoop, calls=%fused_computation.24 | loop fusion | flops 6291456 | bytes 4194304 | tf_op jit(solution)/shard_map/concatenate | solution.py:222
  81.2 4.7 %collective-permute-done.10 = bf16[1024,384]{1,0:T(8,128)(2,1)} collective-permute-done((bf16[1024,384]{1,0:T(8,128)(2,1)}, bf16[1024,384]{1,0:T(8,128)(2,1)}, u32[]{:S(2)}, u32[]{:S(2)}) %collective-permute-start.10) | collective-permute-done | bytes 786464 | tf_op jit(solution)/shard_map/ppermute | solution.py:199
  85.9 3.6 %collective-permute-start.11 = (bf16[1024,1024]{1,0:T(8,128)(2,1)S(1)}, bf16[1024,1024]{1,0:T(8,128)(2,1)}, u32[]{:S(2)}, u32[]{:S(2)}) collective-permute-start(bf16[1024,1024]{1,0:T(8,128)(2,1)S(1)} %pad_maximum_fusion.1), channel_id=1, source_target_pairs={{0,1},{1,0},{2,3},{3,2},{4,5},{5,4},{6,7},{7,6},{8,9},{9,8},{10,11... | collective-permute-start | bytes 6291464 | tf_op jit(solution)/shard_map/ppermute | solution.py:226
  90.2 2.8 %fusion.48 = f32[1024,1024]{1,0:T(8,128)S(1)} fusion(bf16[1024,384]{1,0:T(8,128)(2,1)} %collective-permute-done.10, bf16[4096,1024]{1,0:T(8,128)(2,1)} %param.11, s32[]{:T(128)S(6)} %select_n.31), kind=kOutput, calls=%fused_computation.65 | convolution fusion | flops 805306368 | bytes 5767172 | tf_op jit(solution)/shard_map/dot_general | solution.py:219
  93.0 1.9 %fusion.52 = f32[1024,1024]{1,0:T(8,128)S(1)} fusion(bf16[1024,256]{1,0:T(8,128)(2,1)S(1)} %copy-done.3, bf16[4096,1024]{1,0:T(8,128)(2,1)} %param.11, s32[]{:T(128)S(6)} %select_n.30), kind=kOutput, calls=%fused_computation.70 | convolution fusion | flops 536870912 | bytes 5242884 | tf_op jit(solution)/shard_map/dot_general | solution.py:219
  95.4 2.3 %fusion.15 = f32[1024,1024]{1,0:T(8,128)S(1)} fusion(bf16[1024,1024]{1,0:T(8,128)(2,1)S(1)} %pad_maximum_fusion.1, bf16[4096,1024]{1,0:T(8,128)(2,1)S(1)} %bitcast.148, s32[]{:T(128)S(6)} %select_n.29), kind=kOutput, calls=%fused_computation.27 | convolution fusion | flops 2147483648 | bytes 8388612 | tf_op jit(solution)/shard_map/dot_general | solution.py:230
  98.5 3.9 %fusion.13 = f32[1024,1024]{1,0:T(8,128)S(1)} fusion(bf16[1024,1024]{1,0:T(8,128)(2,1)} %collective-permute-done.11, bf16[4096,1024]{1,0:T(8,128)(2,1)S(1)} %bitcast.148, s32[]{:T(128)S(6)} %select_n.32), kind=kOutput, calls=%fused_computation.25 | convolution fusion | flops 2147483648 | bytes 8388612 | tf_op jit(solution)/shard_map/dot_general | solution.py:233
  102.4 4.8 %add_add_fusion = f32[1024,1024]{1,0:T(8,128)} fusion(f32[1024,1024]{1,0:T(8,128)S(1)} %fusion.50, f32[1024,1024]{1,0:T(8,128)S(1)} %fusion.13, f32[1024,1024]{1,0:T(8,128)S(1)} %fusion.48, f32[1024,1024]{1,0:T(8,128)S(1)} %fusion.15, f32[1024,1024]{1,0:T(8,128)S(1)} %fusion.52, bf16[1024,384]{1,0:T(8,128)(2,1)S(1)} %collective-permute-done.13, ...), kind=kOutput, calls=%fused_computation.22 | convolution fusion | flops 810549248 | bytes 26738692 | tf_op jit(solution)/shard_map/dot_general | solution.py:219
  107.2 1.5 %collective-permute-done.9 = bf16[1024,384]{1,0:T(8,128)(2,1)} collective-permute-done((bf16[1024,384]{1,0:T(8,128)(2,1)S(1)}, bf16[1024,384]{1,0:T(8,128)(2,1)}, u32[]{:S(2)}, u32[]{:S(2)}) %collective-permute-start.9) | collective-permute-done | bytes 786464 | tf_op jit(solution)/shard_map/ppermute | solution.py:199
  109.5 2.8 %fusion.42 = f32[1024,1024]{1,0:T(8,128)S(1)} fusion(bf16[1024,384]{1,0:T(8,128)(2,1)} %collective-permute-done.9, bf16[4096,1024]{1,0:T(8,128)(2,1)} %param.11, s32[]{:T(128)S(6)} %select_n.35), kind=kOutput, calls=%fused_computation.61 | convolution fusion | flops 805306368 | bytes 5767172 | tf_op jit(solution)/shard_map/dot_general | solution.py:219
  112.3 3.7 %add_convert_fusion = bf16[1024,1024]{1,0:T(8,128)(2,1)} fusion(f32[1024,1024]{1,0:T(8,128)S(1)} %copy-done, f32[1024,1024]{1,0:T(8,128)S(1)} %fusion.42, bf16[1024,384]{1,0:T(8,128)(2,1)S(1)} %collective-permute-done.14, bf16[4096,1024]{1,0:T(8,128)(2,1)} %param.11, s32[]{:T(128)S(6)} %select_n.36), kind=kOutput, calls=%fused_computation.21 | convolution fusion | flops 808452096 | bytes 12058628 | tf_op jit(solution)/shard_map/dot_general | solution.py:219
  (50 shorter events, 9.9 us)
Async XLA Ops:
  0.8 8.7 %collective-permute-start = (bf16[3,2,1024]{2,1,0:T(2,128)(2,1)S(1)}, bf16[3,2,1024]{2,1,0:T(2,128)(2,1)S(1)}, u32[]{:S(2)}, u32[]{:S(2)}) collective-permute-start(bf16[3,2,1024]{2,1,0:T(2,128)(2,1)S(1)} %slice.150), channel_id=1, source_target_pairs={{0,4},{4,8},{8,12},{12,16},{16,20},{20,24},{24,28},{1,5},{5,9},{9,... | collective-permute-start | bytes 36872 | tf_op jit(solution)/shard_map/ppermute | solution.py:15
  27.1 14.8 %copy-start.1 = (f32[16,8,1024]{2,1,0:T(8,128)S(1)}, f32[16,8,1024]{2,1,0:T(8,128)}, u32[]{:S(2)}) copy-start(f32[16,8,1024]{2,1,0:T(8,128)} %shard_map.64) | copy-start | bytes 1572868
  27.1 21.1 %copy-start.4 = (f32[16,1024]{1,0:T(8,128)S(1)}, f32[16,1024]{1,0:T(8,128)}, u32[]{:S(2)}) copy-start(f32[16,1024]{1,0:T(8,128)} %param.8) | copy-start | bytes 196612
  27.1 15.1 %collective-permute-start.7 = (f32[16,1024]{1,0:T(8,128)S(1)}, f32[16,1024]{1,0:T(8,128)S(1)}, u32[]{:S(2)}, u32[]{:S(2)}) collective-permute-start(f32[16,1024]{1,0:T(8,128)S(1)} %multiply_reduce_fusion.1), channel_id=1, source_target_pairs={{0,28},{1,29},{2,30},{3,31}} | collective-permute-start | bytes 196616 | tf_op jit(solution)/shard_map/ppermute | solution.py:15
  31.6 12.2 %collective-permute-start.6 = (f32[16,1024]{1,0:T(8,128)S(1)}, f32[16,1024]{1,0:T(8,128)S(1)}, u32[]{:S(2)}, u32[]{:S(2)}) collective-permute-start(f32[16,1024]{1,0:T(8,128)S(1)} %multiply_reduce_fusion.1), channel_id=1, source_target_pairs={{0,24},{4,28},{1,25},{5,29},{2,26},{6,30},{3,27},{7,31}} | collective-permute-start | bytes 196616 | tf_op jit(solution)/shard_map/ppermute | solution.py:15
  33.1 14.9 %collective-permute-start.5 = (f32[16,1024]{1,0:T(8,128)S(1)}, f32[16,1024]{1,0:T(8,128)S(1)}, u32[]{:S(2)}, u32[]{:S(2)}) collective-permute-start(f32[16,1024]{1,0:T(8,128)S(1)} %multiply_reduce_fusion.1), channel_id=1, source_target_pairs={{0,20},{4,24},{8,28},{1,21},{5,25},{9,29},{2,22},{6,26},{10,30},{3... | collective-permute-start | bytes 196616 | tf_op jit(solution)/shard_map/ppermute | solution.py:15
  34.4 13.7 %collective-permute-start.4 = (f32[16,1024]{1,0:T(8,128)S(1)}, f32[16,1024]{1,0:T(8,128)S(1)}, u32[]{:S(2)}, u32[]{:S(2)}) collective-permute-start(f32[16,1024]{1,0:T(8,128)S(1)} %multiply_reduce_fusion.1), channel_id=1, source_target_pairs={{0,16},{4,20},{8,24},{12,28},{1,17},{5,21},{9,25},{13,29},{2,18},{... | collective-permute-start | bytes 196616 | tf_op jit(solution)/shard_map/ppermute | solution.py:15
  35.7 12.4 %collective-permute-start.3 = (f32[16,1024]{1,0:T(8,128)S(1)}, f32[16,1024]{1,0:T(8,128)S(1)}, u32[]{:S(2)}, u32[]{:S(2)}) collective-permute-start(f32[16,1024]{1,0:T(8,128)S(1)} %multiply_reduce_fusion.1), channel_id=1, source_target_pairs={{0,12},{4,16},{8,20},{12,24},{16,28},{1,13},{5,17},{9,21},{13,25},... | collective-permute-start | bytes 196616 | tf_op jit(solution)/shard_map/ppermute | solution.py:15
  42.2 6.0 %collective-permute-start.2 = (f32[16,1024]{1,0:T(8,128)S(1)}, f32[16,1024]{1,0:T(8,128)S(1)}, u32[]{:S(2)}, u32[]{:S(2)}) collective-permute-start(f32[16,1024]{1,0:T(8,128)S(1)} %multiply_reduce_fusion.1), channel_id=1, source_target_pairs={{0,8},{4,12},{8,16},{12,20},{16,24},{20,28},{1,9},{5,13},{9,17},{1... | collective-permute-start | bytes 196616 | tf_op jit(solution)/shard_map/ppermute | solution.py:15
  43.7 4.4 %collective-permute-start.1 = (f32[16,1024]{1,0:T(8,128)S(1)}, f32[16,1024]{1,0:T(8,128)S(1)}, u32[]{:S(2)}, u32[]{:S(2)}) collective-permute-start(f32[16,1024]{1,0:T(8,128)S(1)} %multiply_reduce_fusion.1), channel_id=1, source_target_pairs={{0,4},{4,8},{8,12},{12,16},{16,20},{20,24},{24,28},{1,5},{5,9},{9,... | collective-permute-start | bytes 196616 | tf_op jit(solution)/shard_map/ppermute | solution.py:15
  48.1 6.1 %slice-start.2 = ((f32[1024]{0:T(1024)}), f32[256]{0:T(256)S(1)}, s32[]{:S(2)}) async-start(f32[1024]{0:T(1024)} %param.10), calls=%async_computation.2 | async-start | bytes 2048 | tf_op jit(solution)/shard_map/slice | solution.py:192
  57.0 12.5 %collective-permute-start.8 = (bf16[1024,256]{1,0:T(8,128)(2,1)S(1)}, bf16[1024,256]{1,0:T(8,128)(2,1)S(1)}, u32[]{:S(2)}, u32[]{:S(2)}) collective-permute-start(bf16[1024,256]{1,0:T(8,128)(2,1)S(1)} %fusion.34), channel_id=1, source_target_pairs={{0,2},{1,3},{2,0},{3,1},{4,6},{5,7},{6,4},{7,5},{8,10},{9,11},{10,... | collective-permute-start | bytes 1572872 | tf_op jit(solution)/shard_map/ppermute | solution.py:199
  69.2 16.7 %collective-permute-start.10 = (bf16[1024,384]{1,0:T(8,128)(2,1)}, bf16[1024,384]{1,0:T(8,128)(2,1)}, u32[]{:S(2)}, u32[]{:S(2)}) collective-permute-start(bf16[1024,384]{1,0:T(8,128)(2,1)} %fusion.20), channel_id=1, source_target_pairs={{0,2},{1,3},{2,0},{3,1},{4,6},{5,7},{6,4},{7,5},{8,10},{9,11},{10,... | collective-permute-start | bytes 2359304 | tf_op jit(solution)/shard_map/ppermute | solution.py:199
  69.5 6.4 %copy-start.2 = (bf16[1024,256]{1,0:T(8,128)(2,1)}, bf16[1024,256]{1,0:T(8,128)(2,1)S(1)}, u32[]{:S(2)}) copy-start(bf16[1024,256]{1,0:T(8,128)(2,1)S(1)} %collective-permute-done.8) | copy-start | bytes 1572868
  81.1 11.9 %copy-start.3 = (bf16[1024,256]{1,0:T(8,128)(2,1)S(1)}, bf16[1024,256]{1,0:T(8,128)(2,1)}, u32[]{:S(2)}) copy-start(bf16[1024,256]{1,0:T(8,128)(2,1)} %copy-done.2) | copy-start | bytes 1572868
  85.9 12.6 %collective-permute-start.11 = (bf16[1024,1024]{1,0:T(8,128)(2,1)S(1)}, bf16[1024,1024]{1,0:T(8,128)(2,1)}, u32[]{:S(2)}, u32[]{:S(2)}) collective-permute-start(bf16[1024,1024]{1,0:T(8,128)(2,1)S(1)} %pad_maximum_fusion.1), channel_id=1, source_target_pairs={{0,1},{1,0},{2,3},{3,2},{4,5},{5,4},{6,7},{7,6},{8,9},{9,8},{10,11... | collective-permute-start | bytes 6291464 | tf_op jit(solution)/shard_map/ppermute | solution.py:226
  89.5 19.3 %collective-permute-start.9 = (bf16[1024,384]{1,0:T(8,128)(2,1)S(1)}, bf16[1024,384]{1,0:T(8,128)(2,1)}, u32[]{:S(2)}, u32[]{:S(2)}) collective-permute-start(bf16[1024,384]{1,0:T(8,128)(2,1)S(1)} %fusion.27), channel_id=1, source_target_pairs={{0,2},{1,3},{2,0},{3,1},{4,6},{5,7},{6,4},{7,5},{8,10},{9,11},{10,... | collective-permute-start | bytes 2359304 | tf_op jit(solution)/shard_map/ppermute | solution.py:199
  89.7 8.0 %collective-permute-start.12 = (bf16[1024,256]{1,0:T(8,128)(2,1)}, bf16[1024,256]{1,0:T(8,128)(2,1)S(1)}, u32[]{:S(2)}, u32[]{:S(2)}) collective-permute-start(bf16[1024,256]{1,0:T(8,128)(2,1)} %copy-done.2), channel_id=1, source_target_pairs={{0,1},{1,0},{2,3},{3,2},{4,5},{5,4},{6,7},{7,6},{8,9},{9,8},{10,11... | collective-permute-start | bytes 1572872 | tf_op jit(solution)/shard_map/ppermute | solution.py:227
  90.0 12.4 %collective-permute-start.13 = (bf16[1024,384]{1,0:T(8,128)(2,1)}, bf16[1024,384]{1,0:T(8,128)(2,1)S(1)}, u32[]{:S(2)}, u32[]{:S(2)}) collective-permute-start(bf16[1024,384]{1,0:T(8,128)(2,1)} %collective-permute-done.10), channel_id=1, source_target_pairs={{0,1},{1,0},{2,3},{3,2},{4,5},{5,4},{6,7},{7,6},{8,9},{9,8},{10,11... | collective-permute-start | bytes 2359304 | tf_op jit(solution)/shard_map/ppermute | solution.py:227
  90.2 4.7 %slice-start = ((s8[8388608]{0:T(1024)(128)(4,1)}), s8[4194304]{0:T(1024)(128)(4,1)S(1)}, s32[]{:S(2)}) async-start(s8[8388608]{0:T(1024)(128)(4,1)} %bitcast.147), calls=%async_computation | async-start | bytes 8388608
  93.0 2.4 %slice-start.1 = ((s8[8388608]{0:T(1024)(128)(4,1)}), s8[4194304]{0:T(1024)(128)(4,1)S(1)}, s32[]{:S(2)}) async-start(s8[8388608]{0:T(1024)(128)(4,1)} %bitcast.147), calls=%async_computation.1 | async-start | bytes 8388608
  108.8 3.6 %collective-permute-start.14 = (bf16[1024,384]{1,0:T(8,128)(2,1)}, bf16[1024,384]{1,0:T(8,128)(2,1)S(1)}, u32[]{:S(2)}, u32[]{:S(2)}) collective-permute-start(bf16[1024,384]{1,0:T(8,128)(2,1)} %collective-permute-done.9), channel_id=1, source_target_pairs={{0,1},{1,0},{2,3},{3,2},{4,5},{5,4},{6,7},{7,6},{8,9},{9,8},{10,11... | collective-permute-start | bytes 2359304 | tf_op jit(solution)/shard_map/ppermute | solution.py:238
  109.5 2.8 %copy-start = (f32[1024,1024]{1,0:T(8,128)S(1)}, f32[1024,1024]{1,0:T(8,128)}, u32[]{:S(2)}) copy-start(f32[1024,1024]{1,0:T(8,128)} %add_add_fusion) | copy-start | bytes 12582916

commit v18 on v16

--- a/solution.py
+++ b/solution.py
@@ -42,7 +42,7 @@
             y_ref[pl.ds(t, segments, stride=span), :] = total
         return tuple(updated)
 
-    states = lax.fori_loop(0, span, body, states, unroll=16)
+    states = lax.fori_loop(0, span, body, states, unroll=32)
     if end_ref is not None:
         for p in range(pole_count):
             end_ref[p] = states[p]

time: 112 us -> 112 us (level)
  transfers between devices with their start and end apart: 15 -> 15, of which waited for: 2 -> 2; matrix products, arithmetic and copies ran while one was open for 31% -> 32% of each run, Pallas kernels for 11% -> 11%
where the time goes in v18:
time: 112 us; the launch traced here: 111 us
  starting transfers between devices  26.5 us (24%)
  other arithmetic  25.7 us (23%)
  Pallas kernels  25.2 us (22%)
  matrix products  22.9 us (20%)
  waiting for transfers between devices  6.5 us (6%)
  local copies, waits for them, and re-layouts  3.38 us (3%)
    ppermute x8, starting transfers between devices, shifted(): lax.ppermute(value, axis, [(source, source + steps) for source in range(i...  19 us
    dot_general x6, matrix products, part(): return jnp.dot(value, rows, preferred_element_type=jnp.float32)  16.7 us
    pallas_call x3, Pallas kernels, run_recurrence(): pl.pallas_call(recurrence_kernel, grid=(group_count,), in_specs=[pl.Block...  16.6 us
    convert_element_type x3, other arithmetic, shards(): gated_mix = gated_mix.astype(jnp.bfloat16)  9.51 us
    pallas_call x1, Pallas kernels, run_end_state(): pl.pallas_call(end_state_kernel, grid=(width // LANES,), in_specs=[pl.Blo...  8.52 us
    ppermute x3, waiting for transfers between devices, shards(): lax.ppermute(gated_mix, 'ch', [(i, i ^ 2) for i in range(ch_count)])  6.43 us
    convert_element_type x1, other arithmetic, shards(): x = mixed_input.astype(jnp.float32)  4.2 us
    dot_general x1, matrix products, project_pieces(): total = total + jnp.dot(near, rows_near, preferred_element_type=jnp.float32)  3.94 us
  transfers between devices with their start and end apart: 15, of which 2 were waited for; matrix products, arithmetic and copies ran while one was open for 32% of the time, Pallas kernels for 11%

profile of v18, /device:TPU:1, one launch (start us, length us, event | category | flops | bytes accessed | tf_op | source)
XLA Modules:
  0.0 110.5 jit_solution(15812404169164636443)
XLA Ops:
  0.8 4.0 %collective-permute-start = (bf16[3,2,1024]{2,1,0:T(2,128)(2,1)S(1)}, bf16[3,2,1024]{2,1,0:T(2,128)(2,1)S(1)}, u32[]{:S(2)}, u32[]{:S(2)}) collective-permute-start(bf16[3,2,1024]{2,1,0:T(2,128)(2,1)S(1)} %slice.152), channel_id=1, source_target_pairs={{0,4},{4,8},{8,12},{12,16},{16,20},{20,24},{24,28},{1,5},{5,9},{9,... | collective-permute-start | bytes 36872 | tf_op jit(solution)/shard_map/ppermute | solution.py:15
  8.0 1.5 %fusion.60 = (f32[16,1024]{1,0:T(8,128)S(1)}, f32[16,1024]{1,0:T(8,128)}) fusion(f32[16,1024]{1,0:T(8,128)} %param.8), kind=kLoop, calls=%fused_computation.108 | loop fusion | flops 16384 | bytes 196608 | tf_op jit(solution)/shard_map/neg | solution.py:170
  9.5 2.9 %fusion.1 = f32[2,1026,1024]{2,1,0:T(8,128)S(1)} fusion(bf16[3,2,1024]{2,1,0:T(2,128)(2,1)S(1)} %collective-permute-done, bf16[3,1024,1024]{2,1,0:T(8,128)(2,1)} %param.6), kind=kLoop, calls=%fused_computation.5 | loop fusion | flops 8404992 | bytes 14708736 | tf_op jit(solution)/shard_map/convert_element_type | solution.py:163
  12.4 4.2 %fusion.58 = (f32[1024,1024]{1,0:T(8,128)}, bf16[1024,1024]{1,0:T(8,128)(2,1)S(1)}) fusion(f32[2,1026,1024]{2,1,0:T(8,128)S(1)} %fusion.1, f32[1024]{0:T(1024)S(1)} %bitcast.115, f32[1024]{0:T(1024)S(1)} %bitcast.111, f32[1024]{0:T(1024)S(1)} %bitcast.112, f32[1024]{0:T(1024)S(1)} %bitcast.113, f32[1024]{0:T(1024)S(1)} %bitcast.114, f32[1024]{0:T(1024)S(1)} %bitcast.110), kind=kLoop, calls=%fused_computation.107 | loop fusion | flops 13631488 | bytes 31481856 | tf_op jit(solution)/shard_map/convert_element_type | solution.py:167
  16.6 8.5 %shard_map.64 = f32[16,8,1024]{2,1,0:T(8,128)} custom-call(f32[1024,1024]{1,0:T(8,128)} %get-tuple-element.19.x_ref, f32[16,1024]{1,0:T(8,128)} %get-tuple-element.36.decay_ref), custom_call_target="tpu_custom_call" | custom-call | tf_op jit(solution)/shard_map/pallas_call | solution.py:62
  25.1 1.3 %multiply_reduce_fusion.1 = f32[16,1024]{1,0:T(8,128)S(1)} fusion(f32[16,8,1024]{2,1,0:T(8,128)} %shard_map.64, f32[8]{0:T(128)S(1)} %subtract_multiply_fusion, f32[16,1024]{1,0:T(8,128)S(1)} %get-tuple-element.35), kind=kLoop, calls=%fused_computation.76 | loop fusion | flops 376832 | bytes 655392 | tf_op jit(solution)/shard_map/reduce_sum | solution.py:110
  26.4 4.3 %collective-permute-start.7 = (f32[16,1024]{1,0:T(8,128)S(1)}, f32[16,1024]{1,0:T(8,128)S(1)}, u32[]{:S(2)}, u32[]{:S(2)}) collective-permute-start(f32[16,1024]{1,0:T(8,128)S(1)} %multiply_reduce_fusion.1), channel_id=1, source_target_pairs={{0,28},{1,29},{2,30},{3,31}} | collective-permute-start | bytes 196616 | tf_op jit(solution)/shard_map/ppermute | solution.py:15
  30.7 1.6 %collective-permute-start.6 = (f32[16,1024]{1,0:T(8,128)S(1)}, f32[16,1024]{1,0:T(8,128)S(1)}, u32[]{:S(2)}, u32[]{:S(2)}) collective-permute-start(f32[16,1024]{1,0:T(8,128)S(1)} %multiply_reduce_fusion.1), channel_id=1, source_target_pairs={{0,24},{4,28},{1,25},{5,29},{2,26},{6,30},{3,27},{7,31}} | collective-permute-start | bytes 196616 | tf_op jit(solution)/shard_map/ppermute | solution.py:15
  32.3 1.3 %collective-permute-start.5 = (f32[16,1024]{1,0:T(8,128)S(1)}, f32[16,1024]{1,0:T(8,128)S(1)}, u32[]{:S(2)}, u32[]{:S(2)}) collective-permute-start(f32[16,1024]{1,0:T(8,128)S(1)} %multiply_reduce_fusion.1), channel_id=1, source_target_pairs={{0,20},{4,24},{8,28},{1,21},{5,25},{9,29},{2,22},{6,26},{10,30},{3... | collective-permute-start | bytes 196616 | tf_op jit(solution)/shard_map/ppermute | solution.py:15
  33.6 1.3 %collective-permute-start.4 = (f32[16,1024]{1,0:T(8,128)S(1)}, f32[16,1024]{1,0:T(8,128)S(1)}, u32[]{:S(2)}, u32[]{:S(2)}) collective-permute-start(f32[16,1024]{1,0:T(8,128)S(1)} %multiply_reduce_fusion.1), channel_id=1, source_target_pairs={{0,16},{4,20},{8,24},{12,28},{1,17},{5,21},{9,25},{13,29},{2,18},{... | collective-permute-start | bytes 196616 | tf_op jit(solution)/shard_map/ppermute | solution.py:15
  34.9 1.9 %collective-permute-start.3 = (f32[16,1024]{1,0:T(8,128)S(1)}, f32[16,1024]{1,0:T(8,128)S(1)}, u32[]{:S(2)}, u32[]{:S(2)}) collective-permute-start(f32[16,1024]{1,0:T(8,128)S(1)} %multiply_reduce_fusion.1), channel_id=1, source_target_pairs={{0,12},{4,16},{8,20},{12,24},{16,28},{1,13},{5,17},{9,21},{13,25},... | collective-permute-start | bytes 196616 | tf_op jit(solution)/shard_map/ppermute | solution.py:15
  36.8 1.4 %copy.15 = f32[16,1024,8]{1,0,2:T(8,128)S(1)} copy(f32[16,1024,8]{1,2,0:T(8,128)} %bitcast.107) | data formatting | bytes 1048576
  38.2 1.6 %collective-permute-start.2 = (f32[16,1024]{1,0:T(8,128)S(1)}, f32[16,1024]{1,0:T(8,128)S(1)}, u32[]{:S(2)}, u32[]{:S(2)}) collective-permute-start(f32[16,1024]{1,0:T(8,128)S(1)} %multiply_reduce_fusion.1), channel_id=1, source_target_pairs={{0,8},{4,12},{8,16},{12,20},{16,24},{20,28},{1,9},{5,13},{9,17},{1... | collective-permute-start | bytes 196616 | tf_op jit(solution)/shard_map/ppermute | solution.py:15
  39.8 3.1 %collective-permute-start.1 = (f32[16,1024]{1,0:T(8,128)S(1)}, f32[16,1024]{1,0:T(8,128)S(1)}, u32[]{:S(2)}, u32[]{:S(2)}) collective-permute-start(f32[16,1024]{1,0:T(8,128)S(1)} %multiply_reduce_fusion.1), channel_id=1, source_target_pairs={{0,4},{4,8},{8,12},{12,16},{16,20},{20,24},{24,28},{1,5},{5,9},{9,... | collective-permute-start | bytes 196616 | tf_op jit(solution)/shard_map/ppermute | solution.py:15
  42.9 1.2 %multiply_reduce_fusion = f32[16,1024,8]{1,0,2:T(8,128)S(1)} fusion(f32[16,1024,8]{1,0,2:T(8,128)S(1)} %copy.15, f32[8,8]{1,0:T(8,128)S(1)} %maximum_multiply_fusion, f32[16,1024]{1,0:T(8,128)S(1)} %get-tuple-element.35, pred[8,8]{1,0:T(8,128)(4,1)S(1)} %iota_compare_fusion), kind=kLoop, calls=%fused_computation.24 | loop fusion | flops 4063232 | bytes 1114432
  45.5 4.6 %shard_map.65 = f32[1024,256]{1,0:T(8,128)} custom-call(f32[1024,1024]{1,0:T(8,128)} %get-tuple-element.19.x_ref, f32[16,1024]{1,0:T(8,128)} %get-tuple-element.36.decay_ref, f32[16,1024]{1,0:T(8,128)} %residue_ref.5, f32[16,8,1024]{2,1,0:T(8,128)} %bitcast_add_fusion.start_ref), custom_call_target="tpu_custom_call" | custom-call | tf_op jit(solution)/shard_map/pallas_call | solution.py:78
  50.0 2.4 %fusion.28 = bf16[1024,256]{1,0:T(8,128)(2,1)S(1)} fusion(bf16[1024,1024]{1,0:T(8,128)(2,1)S(1)} %get-tuple-element.34, bf16[3,1024,1024]{2,1,0:T(8,128)(2,1)} %param.6, bf16[3,2,1024]{2,1,0:T(2,128)(2,1)S(1)} %collective-permute-done, f32[256]{0:T(256)S(1)} %slice-done.2, f32[1024,256]{1,0:T(8,128)} %shard_map.65, f32[256]{0:T(256)S(1)} %bitcast.117, ...), kind=kLoop, calls=%fused_computation.52 | loop fusion | flops 6029312 | bytes 8929280 | tf_op jit(solution)/shard_map/convert_element_type | solution.py:193
  52.5 1.3 %collective-permute-start.8 = (bf16[1024,256]{1,0:T(8,128)(2,1)S(1)}, bf16[1024,256]{1,0:T(8,128)(2,1)S(1)}, u32[]{:S(2)}, u32[]{:S(2)}) collective-permute-start(bf16[1024,256]{1,0:T(8,128)(2,1)S(1)} %fusion.28), channel_id=1, source_target_pairs={{0,2},{1,3},{2,0},{3,1},{4,6},{5,7},{6,4},{7,5},{8,10},{9,11},{10,... | collective-permute-start | bytes 1572872 | tf_op jit(solution)/shard_map/ppermute | solution.py:198
  53.8 5.9 %shard_map.66 = f32[1024,384]{1,0:T(8,128)} custom-call(f32[1024,1024]{1,0:T(8,128)} %get-tuple-element.19.x_ref, f32[16,1024]{1,0:T(8,128)} %get-tuple-element.36.decay_ref, f32[16,1024]{1,0:T(8,128)} %residue_ref.5, f32[16,8,1024]{2,1,0:T(8,128)} %bitcast_add_fusion.start_ref), custom_call_target="tpu_custom_call" | custom-call | tf_op jit(solution)/shard_map/pallas_call | solution.py:78
  59.7 4.0 %fusion.20 = bf16[1024,384]{1,0:T(8,128)(2,1)} fusion(bf16[1024,1024]{1,0:T(8,128)(2,1)S(1)} %get-tuple-element.34, f32[384]{0:T(512)S(1)} %get-tuple-element.46, f32[1024,384]{1,0:T(8,128)} %shard_map.66, f32[384]{0:T(512)S(1)} %get-tuple-element.28, f32[384]{0:T(512)S(1)} %get-tuple-element.29, bf16[3,1024,1024]{2,1,0:T(8,128)(2,1)} %param.6, ...), kind=kLoop, calls=%fused_computation.38 | loop fusion | flops 9043968 | bytes 10242048 | tf_op jit(solution)/shard_map/convert_element_type | solution.py:193
  63.9 6.1 %shard_map.67 = f32[1024,384]{1,0:T(8,128)} custom-call(f32[1024,1024]{1,0:T(8,128)} %get-tuple-element.19.x_ref, f32[16,1024]{1,0:T(8,128)} %get-tuple-element.36.decay_ref, f32[16,1024]{1,0:T(8,128)} %residue_ref.5, f32[16,8,1024]{2,1,0:T(8,128)} %bitcast_add_fusion.start_ref), custom_call_target="tpu_custom_call" | custom-call | tf_op jit(solution)/shard_map/pallas_call | solution.py:78
  70.1 3.1 %fusion.24 = bf16[1024,384]{1,0:T(8,128)(2,1)S(1)} fusion(bf16[1024,1024]{1,0:T(8,128)(2,1)S(1)} %get-tuple-element.34, bf16[3,1024,1024]{2,1,0:T(8,128)(2,1)} %param.6, bf16[3,2,1024]{2,1,0:T(2,128)(2,1)S(1)} %collective-permute-done, f32[384]{0:T(512)S(1)} %get-tuple-element.47, f32[1024,384]{1,0:T(8,128)} %shard_map.67, f32[384]{0:T(512)S(1)} %get-tuple-element.31, ...), kind=kLoop, calls=%fused_computation.45 | loop fusion | flops 9043968 | bytes 10242048 | tf_op jit(solution)/shard_map/convert_element_type | solution.py:193
  73.2 1.4 %pad_maximum_fusion = bf16[1024,1024]{1,0:T(8,128)(2,1)S(1)} fusion(bf16[1024,384]{1,0:T(8,128)(2,1)S(1)} %fusion.24, bf16[1024,384]{1,0:T(8,128)(2,1)} %fusion.20, bf16[1024,256]{1,0:T(8,128)(2,1)S(1)} %fusion.28), kind=kLoop, calls=%fused_computation.30 | loop fusion | flops 6291456 | bytes 4194304 | tf_op jit(solution)/shard_map/concatenate | solution.py:221
  74.6 5.7 %collective-permute-done.10 = bf16[1024,384]{1,0:T(8,128)(2,1)} collective-permute-done((bf16[1024,384]{1,0:T(8,128)(2,1)}, bf16[1024,384]{1,0:T(8,128)(2,1)}, u32[]{:S(2)}, u32[]{:S(2)}) %collective-permute-start.10) | collective-permute-done | bytes 786464 | tf_op jit(solution)/shard_map/ppermute | solution.py:198
  80.4 3.6 %collective-permute-start.11 = (bf16[1024,1024]{1,0:T(8,128)(2,1)S(1)}, bf16[1024,1024]{1,0:T(8,128)(2,1)}, u32[]{:S(2)}, u32[]{:S(2)}) collective-permute-start(bf16[1024,1024]{1,0:T(8,128)(2,1)S(1)} %pad_maximum_fusion), channel_id=1, source_target_pairs={{0,1},{1,0},{2,3},{3,2},{4,5},{5,4},{6,7},{7,6},{8,9},{9,8},{10,11... | collective-permute-start | bytes 6291464 | tf_op jit(solution)/shard_map/ppermute | solution.py:225
  85.6 2.8 %fusion.42 = f32[1024,1024]{1,0:T(8,128)S(1)} fusion(bf16[1024,384]{1,0:T(8,128)(2,1)} %collective-permute-done.10, bf16[4096,1024]{1,0:T(8,128)(2,1)} %param.11, s32[]{:T(128)S(6)} %select_n.31), kind=kOutput, calls=%fused_computation.66 | convolution fusion | flops 805306368 | bytes 5767172 | tf_op jit(solution)/shard_map/dot_general | solution.py:218
  88.4 1.9 %fusion.48 = f32[1024,1024]{1,0:T(8,128)S(1)} fusion(bf16[1024,256]{1,0:T(8,128)(2,1)S(1)} %copy-done.2, bf16[4096,1024]{1,0:T(8,128)(2,1)} %param.11, s32[]{:T(128)S(6)} %select_n.30), kind=kOutput, calls=%fused_computation.74 | convolution fusion | flops 536870912 | bytes 5242884 | tf_op jit(solution)/shard_map/dot_general | solution.py:218
  90.7 2.3 %fusion.16 = f32[1024,1024]{1,0:T(8,128)S(1)} fusion(bf16[1024,1024]{1,0:T(8,128)(2,1)S(1)} %pad_maximum_fusion, bf16[4096,1024]{1,0:T(8,128)(2,1)S(1)} %bitcast.109, s32[]{:T(128)S(6)} %select_n.29), kind=kOutput, calls=%fused_computation.33 | convolution fusion | flops 2147483648 | bytes 8388612 | tf_op jit(solution)/shard_map/dot_general | solution.py:229
  93.8 3.9 %fusion.14 = f32[1024,1024]{1,0:T(8,128)S(1)} fusion(bf16[1024,1024]{1,0:T(8,128)(2,1)} %collective-permute-done.11, bf16[4096,1024]{1,0:T(8,128)(2,1)S(1)} %bitcast.109, s32[]{:T(128)S(6)} %select_n.32), kind=kOutput, calls=%fused_computation.31 | convolution fusion | flops 2147483648 | bytes 8388612 | tf_op jit(solution)/shard_map/dot_general | solution.py:232
  97.7 4.8 %add_add_fusion = f32[1024,1024]{1,0:T(8,128)} fusion(f32[1024,1024]{1,0:T(8,128)S(1)} %fusion.46, f32[1024,1024]{1,0:T(8,128)S(1)} %fusion.14, f32[1024,1024]{1,0:T(8,128)S(1)} %fusion.42, f32[1024,1024]{1,0:T(8,128)S(1)} %fusion.16, f32[1024,1024]{1,0:T(8,128)S(1)} %fusion.48, bf16[1024,384]{1,0:T(8,128)(2,1)S(1)} %collective-permute-done.13, ...), kind=kOutput, calls=%fused_computation.26 | convolution fusion | flops 810549248 | bytes 26738692 | tf_op jit(solution)/shard_map/dot_general | solution.py:218
  104.0 2.8 %fusion.36 = f32[1024,1024]{1,0:T(8,128)S(1)} fusion(bf16[1024,384]{1,0:T(8,128)(2,1)} %collective-permute-done.9, bf16[4096,1024]{1,0:T(8,128)(2,1)} %param.11, s32[]{:T(128)S(6)} %select_n.35), kind=kOutput, calls=%fused_computation.62 | convolution fusion | flops 805306368 | bytes 5767172 | tf_op jit(solution)/shard_map/dot_general | solution.py:218
  106.8 3.7 %add_convert_fusion = bf16[1024,1024]{1,0:T(8,128)(2,1)} fusion(f32[1024,1024]{1,0:T(8,128)S(1)} %copy-done, f32[1024,1024]{1,0:T(8,128)S(1)} %fusion.36, bf16[1024,384]{1,0:T(8,128)(2,1)S(1)} %collective-permute-done.14, bf16[4096,1024]{1,0:T(8,128)(2,1)} %param.11, s32[]{:T(128)S(6)} %select_n.36), kind=kOutput, calls=%fused_computation.25 | convolution fusion | flops 808452096 | bytes 12058628 | tf_op jit(solution)/shard_map/dot_general | solution.py:218
  (47 shorter events, 9.9 us)
Async XLA Ops:
  0.8 8.7 %collective-permute-start = (bf16[3,2,1024]{2,1,0:T(2,128)(2,1)S(1)}, bf16[3,2,1024]{2,1,0:T(2,128)(2,1)S(1)}, u32[]{:S(2)}, u32[]{:S(2)}) collective-permute-start(bf16[3,2,1024]{2,1,0:T(2,128)(2,1)S(1)} %slice.152), channel_id=1, source_target_pairs={{0,4},{4,8},{8,12},{12,16},{16,20},{20,24},{24,28},{1,5},{5,9},{9,... | collective-permute-start | bytes 36872 | tf_op jit(solution)/shard_map/ppermute | solution.py:15
  16.6 27.6 %copy-start.3 = (f32[16,1024]{1,0:T(8,128)S(1)}, f32[16,1024]{1,0:T(8,128)}, u32[]{:S(2)}) copy-start(f32[16,1024]{1,0:T(8,128)} %param.8) | copy-start | bytes 196612
  26.4 11.8 %collective-permute-start.7 = (f32[16,1024]{1,0:T(8,128)S(1)}, f32[16,1024]{1,0:T(8,128)S(1)}, u32[]{:S(2)}, u32[]{:S(2)}) collective-permute-start(f32[16,1024]{1,0:T(8,128)S(1)} %multiply_reduce_fusion.1), channel_id=1, source_target_pairs={{0,28},{1,29},{2,30},{3,31}} | collective-permute-start | bytes 196616 | tf_op jit(solution)/shard_map/ppermute | solution.py:15
  30.7 9.1 %collective-permute-start.6 = (f32[16,1024]{1,0:T(8,128)S(1)}, f32[16,1024]{1,0:T(8,128)S(1)}, u32[]{:S(2)}, u32[]{:S(2)}) collective-permute-start(f32[16,1024]{1,0:T(8,128)S(1)} %multiply_reduce_fusion.1), channel_id=1, source_target_pairs={{0,24},{4,28},{1,25},{5,29},{2,26},{6,30},{3,27},{7,31}} | collective-permute-start | bytes 196616 | tf_op jit(solution)/shard_map/ppermute | solution.py:15
  32.3 11.8 %collective-permute-start.5 = (f32[16,1024]{1,0:T(8,128)S(1)}, f32[16,1024]{1,0:T(8,128)S(1)}, u32[]{:S(2)}, u32[]{:S(2)}) collective-permute-start(f32[16,1024]{1,0:T(8,128)S(1)} %multiply_reduce_fusion.1), channel_id=1, source_target_pairs={{0,20},{4,24},{8,28},{1,21},{5,25},{9,29},{2,22},{6,26},{10,30},{3... | collective-permute-start | bytes 196616 | tf_op jit(solution)/shard_map/ppermute | solution.py:15
  33.6 10.5 %collective-permute-start.4 = (f32[16,1024]{1,0:T(8,128)S(1)}, f32[16,1024]{1,0:T(8,128)S(1)}, u32[]{:S(2)}, u32[]{:S(2)}) collective-permute-start(f32[16,1024]{1,0:T(8,128)S(1)} %multiply_reduce_fusion.1), channel_id=1, source_target_pairs={{0,16},{4,20},{8,24},{12,28},{1,17},{5,21},{9,25},{13,29},{2,18},{... | collective-permute-start | bytes 196616 | tf_op jit(solution)/shard_map/ppermute | solution.py:15
  34.9 9.2 %collective-permute-start.3 = (f32[16,1024]{1,0:T(8,128)S(1)}, f32[16,1024]{1,0:T(8,128)S(1)}, u32[]{:S(2)}, u32[]{:S(2)}) collective-permute-start(f32[16,1024]{1,0:T(8,128)S(1)} %multiply_reduce_fusion.1), channel_id=1, source_target_pairs={{0,12},{4,16},{8,20},{12,24},{16,28},{1,13},{5,17},{9,21},{13,25},... | collective-permute-start | bytes 196616 | tf_op jit(solution)/shard_map/ppermute | solution.py:15
  38.2 6.0 %collective-permute-start.2 = (f32[16,1024]{1,0:T(8,128)S(1)}, f32[16,1024]{1,0:T(8,128)S(1)}, u32[]{:S(2)}, u32[]{:S(2)}) collective-permute-start(f32[16,1024]{1,0:T(8,128)S(1)} %multiply_reduce_fusion.1), channel_id=1, source_target_pairs={{0,8},{4,12},{8,16},{12,20},{16,24},{20,28},{1,9},{5,13},{9,17},{1... | collective-permute-start | bytes 196616 | tf_op jit(solution)/shard_map/ppermute | solution.py:15
  39.8 4.4 %collective-permute-start.1 = (f32[16,1024]{1,0:T(8,128)S(1)}, f32[16,1024]{1,0:T(8,128)S(1)}, u32[]{:S(2)}, u32[]{:S(2)}) collective-permute-start(f32[16,1024]{1,0:T(8,128)S(1)} %multiply_reduce_fusion.1), channel_id=1, source_target_pairs={{0,4},{4,8},{8,12},{12,16},{16,20},{20,24},{24,28},{1,5},{5,9},{9,... | collective-permute-start | bytes 196616 | tf_op jit(solution)/shard_map/ppermute | solution.py:15
  44.1 5.9 %slice-start.2 = ((f32[1024]{0:T(1024)}), f32[256]{0:T(256)S(1)}, s32[]{:S(2)}) async-start(f32[1024]{0:T(1024)} %param.10), calls=%async_computation.2 | async-start | bytes 2048 | tf_op jit(solution)/shard_map/slice | solution.py:191
  52.5 11.4 %collective-permute-start.8 = (bf16[1024,256]{1,0:T(8,128)(2,1)S(1)}, bf16[1024,256]{1,0:T(8,128)(2,1)S(1)}, u32[]{:S(2)}, u32[]{:S(2)}) collective-permute-start(bf16[1024,256]{1,0:T(8,128)(2,1)S(1)} %fusion.28), channel_id=1, source_target_pairs={{0,2},{1,3},{2,0},{3,1},{4,6},{5,7},{6,4},{7,5},{8,10},{9,11},{10,... | collective-permute-start | bytes 1572872 | tf_op jit(solution)/shard_map/ppermute | solution.py:198
  63.7 16.7 %collective-permute-start.10 = (bf16[1024,384]{1,0:T(8,128)(2,1)}, bf16[1024,384]{1,0:T(8,128)(2,1)}, u32[]{:S(2)}, u32[]{:S(2)}) collective-permute-start(bf16[1024,384]{1,0:T(8,128)(2,1)} %fusion.20), channel_id=1, source_target_pairs={{0,2},{1,3},{2,0},{3,1},{4,6},{5,7},{6,4},{7,5},{8,10},{9,11},{10,... | collective-permute-start | bytes 2359304 | tf_op jit(solution)/shard_map/ppermute | solution.py:198
  63.9 6.1 %copy-start.1 = (bf16[1024,256]{1,0:T(8,128)(2,1)}, bf16[1024,256]{1,0:T(8,128)(2,1)S(1)}, u32[]{:S(2)}) copy-start(bf16[1024,256]{1,0:T(8,128)(2,1)S(1)} %collective-permute-done.8) | copy-start | bytes 1572868
  74.6 13.7 %copy-start.2 = (bf16[1024,256]{1,0:T(8,128)(2,1)S(1)}, bf16[1024,256]{1,0:T(8,128)(2,1)}, u32[]{:S(2)}) copy-start(bf16[1024,256]{1,0:T(8,128)(2,1)} %copy-done.1) | copy-start | bytes 1572868
  80.4 13.4 %collective-permute-start.11 = (bf16[1024,1024]{1,0:T(8,128)(2,1)S(1)}, bf16[1024,1024]{1,0:T(8,128)(2,1)}, u32[]{:S(2)}, u32[]{:S(2)}) collective-permute-start(bf16[1024,1024]{1,0:T(8,128)(2,1)S(1)} %pad_maximum_fusion), channel_id=1, source_target_pairs={{0,1},{1,0},{2,3},{3,2},{4,5},{5,4},{6,7},{7,6},{8,9},{9,8},{10,11... | collective-permute-start | bytes 6291464 | tf_op jit(solution)/shard_map/ppermute | solution.py:225
  83.9 19.3 %collective-permute-start.9 = (bf16[1024,384]{1,0:T(8,128)(2,1)S(1)}, bf16[1024,384]{1,0:T(8,128)(2,1)}, u32[]{:S(2)}, u32[]{:S(2)}) collective-permute-start(bf16[1024,384]{1,0:T(8,128)(2,1)S(1)} %fusion.24), channel_id=1, source_target_pairs={{0,2},{1,3},{2,0},{3,1},{4,6},{5,7},{6,4},{7,5},{8,10},{9,11},{10,... | collective-permute-start | bytes 2359304 | tf_op jit(solution)/shard_map/ppermute | solution.py:198
  85.1 8.0 %collective-permute-start.12 = (bf16[1024,256]{1,0:T(8,128)(2,1)}, bf16[1024,256]{1,0:T(8,128)(2,1)S(1)}, u32[]{:S(2)}, u32[]{:S(2)}) collective-permute-start(bf16[1024,256]{1,0:T(8,128)(2,1)} %copy-done.1), channel_id=1, source_target_pairs={{0,1},{1,0},{2,3},{3,2},{4,5},{5,4},{6,7},{7,6},{8,9},{9,8},{10,11... | collective-permute-start | bytes 1572872 | tf_op jit(solution)/shard_map/ppermute | solution.py:226
  85.3 12.4 %collective-permute-start.13 = (bf16[1024,384]{1,0:T(8,128)(2,1)}, bf16[1024,384]{1,0:T(8,128)(2,1)S(1)}, u32[]{:S(2)}, u32[]{:S(2)}) collective-permute-start(bf16[1024,384]{1,0:T(8,128)(2,1)} %collective-permute-done.10), channel_id=1, source_target_pairs={{0,1},{1,0},{2,3},{3,2},{4,5},{5,4},{6,7},{7,6},{8,9},{9,8},{10,11... | collective-permute-start | bytes 2359304 | tf_op jit(solution)/shard_map/ppermute | solution.py:226
  85.6 4.7 %slice-start = ((s8[8388608]{0:T(1024)(128)(4,1)}), s8[4194304]{0:T(1024)(128)(4,1)S(1)}, s32[]{:S(2)}) async-start(s8[8388608]{0:T(1024)(128)(4,1)} %bitcast.108), calls=%async_computation | async-start | bytes 8388608
  88.3 2.4 %slice-start.1 = ((s8[8388608]{0:T(1024)(128)(4,1)}), s8[4194304]{0:T(1024)(128)(4,1)S(1)}, s32[]{:S(2)}) async-start(s8[8388608]{0:T(1024)(128)(4,1)} %bitcast.108), calls=%async_computation.1 | async-start | bytes 8388608
  103.2 3.6 %collective-permute-start.14 = (bf16[1024,384]{1,0:T(8,128)(2,1)}, bf16[1024,384]{1,0:T(8,128)(2,1)S(1)}, u32[]{:S(2)}, u32[]{:S(2)}) collective-permute-start(bf16[1024,384]{1,0:T(8,128)(2,1)} %collective-permute-done.9), channel_id=1, source_target_pairs={{0,1},{1,0},{2,3},{3,2},{4,5},{5,4},{6,7},{7,6},{8,9},{9,8},{10,11... | collective-permute-start | bytes 2359304 | tf_op jit(solution)/shard_map/ppermute | solution.py:237
  104.0 2.8 %copy-start = (f32[1024,1024]{1,0:T(8,128)S(1)}, f32[1024,1024]{1,0:T(8,128)}, u32[]{:S(2)}) copy-start(f32[1024,1024]{1,0:T(8,128)} %add_add_fusion) | copy-start | bytes 12582916

commit v19 on v18

--- a/solution.py
+++ b/solution.py
@@ -42,7 +42,7 @@
             y_ref[pl.ds(t, segments, stride=span), :] = total
         return tuple(updated)
 
-    states = lax.fori_loop(0, span, body, states, unroll=32)
+    states = lax.fori_loop(0, span, body, states, unroll=128)
     if end_ref is not None:
         for p in range(pole_count):
             end_ref[p] = states[p]

time: 112 us -> 112 us (level)
  no operation moved by 1% of the time
where the time goes in v19:
time: 112 us; the launch traced here: 111 us
  starting transfers between devices  26.6 us (24%)
  other arithmetic  25.7 us (23%)
  Pallas kernels  25.4 us (23%)
  matrix products  22.9 us (20%)
  waiting for transfers between devices  6.73 us (6%)
  local copies, waits for them, and re-layouts  3.37 us (3%)
    ppermute x8, starting transfers between devices, shifted(): lax.ppermute(value, axis, [(source, source + steps) for source in range(i...  19 us
    dot_general x6, matrix products, part(): return jnp.dot(value, rows, preferred_element_type=jnp.float32)  16.7 us
    pallas_call x3, Pallas kernels, run_recurrence(): pl.pallas_call(recurrence_kernel, grid=(group_count,), in_specs=[pl.Block...  16.2 us
    convert_element_type x3, other arithmetic, shards(): gated_mix = gated_mix.astype(jnp.bfloat16)  9.51 us
    pallas_call x1, Pallas kernels, run_end_state(): pl.pallas_call(end_state_kernel, grid=(width // LANES,), in_specs=[pl.Blo...  9.27 us
    ppermute x3, waiting for transfers between devices, shards(): lax.ppermute(gated_mix, 'ch', [(i, i ^ 2) for i in range(ch_count)])  6.67 us
    convert_element_type x1, other arithmetic, shards(): x = mixed_input.astype(jnp.float32)  4.2 us
    dot_general x1, matrix products, project_pieces(): total = total + jnp.dot(near, rows_near, preferred_element_type=jnp.float32)  3.94 us
  transfers between devices with their start and end apart: 15, of which 2 were waited for; matrix products, arithmetic and copies ran while one was open for 32% of the time, Pallas kernels for 11%

profile of v19, /device:TPU:1, one launch (start us, length us, event | category | flops | bytes accessed | tf_op | source)
XLA Modules:
  0.0 111.0 jit_solution(10727138405011846587)
XLA Ops:
  0.8 4.0 %collective-permute-start = (bf16[3,2,1024]{2,1,0:T(2,128)(2,1)S(1)}, bf16[3,2,1024]{2,1,0:T(2,128)(2,1)S(1)}, u32[]{:S(2)}, u32[]{:S(2)}) collective-permute-start(bf16[3,2,1024]{2,1,0:T(2,128)(2,1)S(1)} %slice.152), channel_id=1, source_target_pairs={{0,4},{4,8},{8,12},{12,16},{16,20},{20,24},{24,28},{1,5},{5,9},{9,... | collective-permute-start | bytes 36872 | tf_op jit(solution)/shard_map/ppermute | solution.py:15
  8.0 1.5 %fusion.60 = (f32[16,1024]{1,0:T(8,128)S(1)}, f32[16,1024]{1,0:T(8,128)}) fusion(f32[16,1024]{1,0:T(8,128)} %param.8), kind=kLoop, calls=%fused_computation.108 | loop fusion | flops 16384 | bytes 196608 | tf_op jit(solution)/shard_map/neg | solution.py:170
  9.5 2.9 %fusion.1 = f32[2,1026,1024]{2,1,0:T(8,128)S(1)} fusion(bf16[3,2,1024]{2,1,0:T(2,128)(2,1)S(1)} %collective-permute-done, bf16[3,1024,1024]{2,1,0:T(8,128)(2,1)} %param.6), kind=kLoop, calls=%fused_computation.5 | loop fusion | flops 8404992 | bytes 14708736 | tf_op jit(solution)/shard_map/convert_element_type | solution.py:163
  12.4 4.2 %fusion.58 = (f32[1024,1024]{1,0:T(8,128)}, bf16[1024,1024]{1,0:T(8,128)(2,1)S(1)}) fusion(f32[2,1026,1024]{2,1,0:T(8,128)S(1)} %fusion.1, f32[1024]{0:T(1024)S(1)} %bitcast.115, f32[1024]{0:T(1024)S(1)} %bitcast.111, f32[1024]{0:T(1024)S(1)} %bitcast.112, f32[1024]{0:T(1024)S(1)} %bitcast.113, f32[1024]{0:T(1024)S(1)} %bitcast.114, f32[1024]{0:T(1024)S(1)} %bitcast.110), kind=kLoop, calls=%fused_computation.107 | loop fusion | flops 13631488 | bytes 31481856 | tf_op jit(solution)/shard_map/convert_element_type | solution.py:167
  16.6 9.3 %shard_map.64 = f32[16,8,1024]{2,1,0:T(8,128)} custom-call(f32[1024,1024]{1,0:T(8,128)} %get-tuple-element.19.x_ref, f32[16,1024]{1,0:T(8,128)} %get-tuple-element.36.decay_ref), custom_call_target="tpu_custom_call" | custom-call | tf_op jit(solution)/shard_map/pallas_call | solution.py:62
  25.8 1.3 %multiply_reduce_fusion.1 = f32[16,1024]{1,0:T(8,128)S(1)} fusion(f32[16,8,1024]{2,1,0:T(8,128)} %shard_map.64, f32[8]{0:T(128)S(1)} %subtract_multiply_fusion, f32[16,1024]{1,0:T(8,128)S(1)} %get-tuple-element.35), kind=kLoop, calls=%fused_computation.76 | loop fusion | flops 376832 | bytes 655392 | tf_op jit(solution)/shard_map/reduce_sum | solution.py:110
  27.1 4.3 %collective-permute-start.7 = (f32[16,1024]{1,0:T(8,128)S(1)}, f32[16,1024]{1,0:T(8,128)S(1)}, u32[]{:S(2)}, u32[]{:S(2)}) collective-permute-start(f32[16,1024]{1,0:T(8,128)S(1)} %multiply_reduce_fusion.1), channel_id=1, source_target_pairs={{0,28},{1,29},{2,30},{3,31}} | collective-permute-start | bytes 196616 | tf_op jit(solution)/shard_map/ppermute | solution.py:15
  31.5 1.6 %collective-permute-start.6 = (f32[16,1024]{1,0:T(8,128)S(1)}, f32[16,1024]{1,0:T(8,128)S(1)}, u32[]{:S(2)}, u32[]{:S(2)}) collective-permute-start(f32[16,1024]{1,0:T(8,128)S(1)} %multiply_reduce_fusion.1), channel_id=1, source_target_pairs={{0,24},{4,28},{1,25},{5,29},{2,26},{6,30},{3,27},{7,31}} | collective-permute-start | bytes 196616 | tf_op jit(solution)/shard_map/ppermute | solution.py:15
  33.1 1.3 %collective-permute-start.5 = (f32[16,1024]{1,0:T(8,128)S(1)}, f32[16,1024]{1,0:T(8,128)S(1)}, u32[]{:S(2)}, u32[]{:S(2)}) collective-permute-start(f32[16,1024]{1,0:T(8,128)S(1)} %multiply_reduce_fusion.1), channel_id=1, source_target_pairs={{0,20},{4,24},{8,28},{1,21},{5,25},{9,29},{2,22},{6,26},{10,30},{3... | collective-permute-start | bytes 196616 | tf_op jit(solution)/shard_map/ppermute | solution.py:15
  34.4 1.3 %collective-permute-start.4 = (f32[16,1024]{1,0:T(8,128)S(1)}, f32[16,1024]{1,0:T(8,128)S(1)}, u32[]{:S(2)}, u32[]{:S(2)}) collective-permute-start(f32[16,1024]{1,0:T(8,128)S(1)} %multiply_reduce_fusion.1), channel_id=1, source_target_pairs={{0,16},{4,20},{8,24},{12,28},{1,17},{5,21},{9,25},{13,29},{2,18},{... | collective-permute-start | bytes 196616 | tf_op jit(solution)/shard_map/ppermute | solution.py:15
  35.7 1.9 %collective-permute-start.3 = (f32[16,1024]{1,0:T(8,128)S(1)}, f32[16,1024]{1,0:T(8,128)S(1)}, u32[]{:S(2)}, u32[]{:S(2)}) collective-permute-start(f32[16,1024]{1,0:T(8,128)S(1)} %multiply_reduce_fusion.1), channel_id=1, source_target_pairs={{0,12},{4,16},{8,20},{12,24},{16,28},{1,13},{5,17},{9,21},{13,25},... | collective-permute-start | bytes 196616 | tf_op jit(solution)/shard_map/ppermute | solution.py:15
  37.6 1.4 %copy.15 = f32[16,1024,8]{1,0,2:T(8,128)S(1)} copy(f32[16,1024,8]{1,2,0:T(8,128)} %bitcast.107) | data formatting | bytes 1048576
  39.0 1.6 %collective-permute-start.2 = (f32[16,1024]{1,0:T(8,128)S(1)}, f32[16,1024]{1,0:T(8,128)S(1)}, u32[]{:S(2)}, u32[]{:S(2)}) collective-permute-start(f32[16,1024]{1,0:T(8,128)S(1)} %multiply_reduce_fusion.1), channel_id=1, source_target_pairs={{0,8},{4,12},{8,16},{12,20},{16,24},{20,28},{1,9},{5,13},{9,17},{1... | collective-permute-start | bytes 196616 | tf_op jit(solution)/shard_map/ppermute | solution.py:15
  40.5 3.1 %collective-permute-start.1 = (f32[16,1024]{1,0:T(8,128)S(1)}, f32[16,1024]{1,0:T(8,128)S(1)}, u32[]{:S(2)}, u32[]{:S(2)}) collective-permute-start(f32[16,1024]{1,0:T(8,128)S(1)} %multiply_reduce_fusion.1), channel_id=1, source_target_pairs={{0,4},{4,8},{8,12},{12,16},{16,20},{20,24},{24,28},{1,5},{5,9},{9,... | collective-permute-start | bytes 196616 | tf_op jit(solution)/shard_map/ppermute | solution.py:15
  43.6 1.2 %multiply_reduce_fusion = f32[16,1024,8]{1,0,2:T(8,128)S(1)} fusion(f32[16,1024,8]{1,0,2:T(8,128)S(1)} %copy.15, f32[8,8]{1,0:T(8,128)S(1)} %maximum_multiply_fusion, f32[16,1024]{1,0:T(8,128)S(1)} %get-tuple-element.35, pred[8,8]{1,0:T(8,128)(4,1)S(1)} %iota_compare_fusion), kind=kLoop, calls=%fused_computation.24 | loop fusion | flops 4063232 | bytes 1114432
  46.2 4.4 %shard_map.65 = f32[1024,256]{1,0:T(8,128)} custom-call(f32[1024,1024]{1,0:T(8,128)} %get-tuple-element.19.x_ref, f32[16,1024]{1,0:T(8,128)} %get-tuple-element.36.decay_ref, f32[16,1024]{1,0:T(8,128)} %residue_ref.5, f32[16,8,1024]{2,1,0:T(8,128)} %bitcast_add_fusion.start_ref), custom_call_target="tpu_custom_call" | custom-call | tf_op jit(solution)/shard_map/pallas_call | solution.py:78
  50.7 2.4 %fusion.28 = bf16[1024,256]{1,0:T(8,128)(2,1)S(1)} fusion(bf16[1024,1024]{1,0:T(8,128)(2,1)S(1)} %get-tuple-element.34, bf16[3,1024,1024]{2,1,0:T(8,128)(2,1)} %param.6, bf16[3,2,1024]{2,1,0:T(2,128)(2,1)S(1)} %collective-permute-done, f32[256]{0:T(256)S(1)} %slice-done.2, f32[1024,256]{1,0:T(8,128)} %shard_map.65, f32[256]{0:T(256)S(1)} %bitcast.117, ...), kind=kLoop, calls=%fused_computation.52 | loop fusion | flops 6029312 | bytes 8929280 | tf_op jit(solution)/shard_map/convert_element_type | solution.py:193
  53.1 1.3 %collective-permute-start.8 = (bf16[1024,256]{1,0:T(8,128)(2,1)S(1)}, bf16[1024,256]{1,0:T(8,128)(2,1)S(1)}, u32[]{:S(2)}, u32[]{:S(2)}) collective-permute-start(bf16[1024,256]{1,0:T(8,128)(2,1)S(1)} %fusion.28), channel_id=1, source_target_pairs={{0,2},{1,3},{2,0},{3,1},{4,6},{5,7},{6,4},{7,5},{8,10},{9,11},{10,... | collective-permute-start | bytes 1572872 | tf_op jit(solution)/shard_map/ppermute | solution.py:198
  54.4 5.8 %shard_map.66 = f32[1024,384]{1,0:T(8,128)} custom-call(f32[1024,1024]{1,0:T(8,128)} %get-tuple-element.19.x_ref, f32[16,1024]{1,0:T(8,128)} %get-tuple-element.36.decay_ref, f32[16,1024]{1,0:T(8,128)} %residue_ref.5, f32[16,8,1024]{2,1,0:T(8,128)} %bitcast_add_fusion.start_ref), custom_call_target="tpu_custom_call" | custom-call | tf_op jit(solution)/shard_map/pallas_call | solution.py:78
  60.1 4.0 %fusion.20 = bf16[1024,384]{1,0:T(8,128)(2,1)} fusion(bf16[1024,1024]{1,0:T(8,128)(2,1)S(1)} %get-tuple-element.34, f32[384]{0:T(512)S(1)} %get-tuple-element.46, f32[1024,384]{1,0:T(8,128)} %shard_map.66, f32[384]{0:T(512)S(1)} %get-tuple-element.28, f32[384]{0:T(512)S(1)} %get-tuple-element.29, bf16[3,1024,1024]{2,1,0:T(8,128)(2,1)} %param.6, ...), kind=kLoop, calls=%fused_computation.38 | loop fusion | flops 9043968 | bytes 10242048 | tf_op jit(solution)/shard_map/convert_element_type | solution.py:193
  64.4 6.0 %shard_map.67 = f32[1024,384]{1,0:T(8,128)} custom-call(f32[1024,1024]{1,0:T(8,128)} %get-tuple-element.19.x_ref, f32[16,1024]{1,0:T(8,128)} %get-tuple-element.36.decay_ref, f32[16,1024]{1,0:T(8,128)} %residue_ref.5, f32[16,8,1024]{2,1,0:T(8,128)} %bitcast_add_fusion.start_ref), custom_call_target="tpu_custom_call" | custom-call | tf_op jit(solution)/shard_map/pallas_call | solution.py:78
  70.3 3.1 %fusion.24 = bf16[1024,384]{1,0:T(8,128)(2,1)S(1)} fusion(bf16[1024,1024]{1,0:T(8,128)(2,1)S(1)} %get-tuple-element.34, bf16[3,1024,1024]{2,1,0:T(8,128)(2,1)} %param.6, bf16[3,2,1024]{2,1,0:T(2,128)(2,1)S(1)} %collective-permute-done, f32[384]{0:T(512)S(1)} %get-tuple-element.47, f32[1024,384]{1,0:T(8,128)} %shard_map.67, f32[384]{0:T(512)S(1)} %get-tuple-element.31, ...), kind=kLoop, calls=%fused_computation.45 | loop fusion | flops 9043968 | bytes 10242048 | tf_op jit(solution)/shard_map/convert_element_type | solution.py:193
  73.5 1.4 %pad_maximum_fusion = bf16[1024,1024]{1,0:T(8,128)(2,1)S(1)} fusion(bf16[1024,384]{1,0:T(8,128)(2,1)S(1)} %fusion.24, bf16[1024,384]{1,0:T(8,128)(2,1)} %fusion.20, bf16[1024,256]{1,0:T(8,128)(2,1)S(1)} %fusion.28), kind=kLoop, calls=%fused_computation.30 | loop fusion | flops 6291456 | bytes 4194304 | tf_op jit(solution)/shard_map/concatenate | solution.py:221
  74.9 6.1 %collective-permute-done.10 = bf16[1024,384]{1,0:T(8,128)(2,1)} collective-permute-done((bf16[1024,384]{1,0:T(8,128)(2,1)}, bf16[1024,384]{1,0:T(8,128)(2,1)}, u32[]{:S(2)}, u32[]{:S(2)}) %collective-permute-start.10) | collective-permute-done | bytes 786464 | tf_op jit(solution)/shard_map/ppermute | solution.py:198
  81.0 3.5 %collective-permute-start.11 = (bf16[1024,1024]{1,0:T(8,128)(2,1)S(1)}, bf16[1024,1024]{1,0:T(8,128)(2,1)}, u32[]{:S(2)}, u32[]{:S(2)}) collective-permute-start(bf16[1024,1024]{1,0:T(8,128)(2,1)S(1)} %pad_maximum_fusion), channel_id=1, source_target_pairs={{0,1},{1,0},{2,3},{3,2},{4,5},{5,4},{6,7},{7,6},{8,9},{9,8},{10,11... | collective-permute-start | bytes 6291464 | tf_op jit(solution)/shard_map/ppermute | solution.py:225
  86.2 2.8 %fusion.42 = f32[1024,1024]{1,0:T(8,128)S(1)} fusion(bf16[1024,384]{1,0:T(8,128)(2,1)} %collective-permute-done.10, bf16[4096,1024]{1,0:T(8,128)(2,1)} %param.11, s32[]{:T(128)S(6)} %select_n.31), kind=kOutput, calls=%fused_computation.66 | convolution fusion | flops 805306368 | bytes 5767172 | tf_op jit(solution)/shard_map/dot_general | solution.py:218
  89.0 1.9 %fusion.48 = f32[1024,1024]{1,0:T(8,128)S(1)} fusion(bf16[1024,256]{1,0:T(8,128)(2,1)S(1)} %copy-done.2, bf16[4096,1024]{1,0:T(8,128)(2,1)} %param.11, s32[]{:T(128)S(6)} %select_n.30), kind=kOutput, calls=%fused_computation.74 | convolution fusion | flops 536870912 | bytes 5242884 | tf_op jit(solution)/shard_map/dot_general | solution.py:218
  91.3 2.3 %fusion.16 = f32[1024,1024]{1,0:T(8,128)S(1)} fusion(bf16[1024,1024]{1,0:T(8,128)(2,1)S(1)} %pad_maximum_fusion, bf16[4096,1024]{1,0:T(8,128)(2,1)S(1)} %bitcast.109, s32[]{:T(128)S(6)} %select_n.29), kind=kOutput, calls=%fused_computation.33 | convolution fusion | flops 2147483648 | bytes 8388612 | tf_op jit(solution)/shard_map/dot_general | solution.py:229
  94.4 3.9 %fusion.14 = f32[1024,1024]{1,0:T(8,128)S(1)} fusion(bf16[1024,1024]{1,0:T(8,128)(2,1)} %collective-permute-done.11, bf16[4096,1024]{1,0:T(8,128)(2,1)S(1)} %bitcast.109, s32[]{:T(128)S(6)} %select_n.32), kind=kOutput, calls=%fused_computation.31 | convolution fusion | flops 2147483648 | bytes 8388612 | tf_op jit(solution)/shard_map/dot_general | solution.py:232
  98.4 4.8 %add_add_fusion = f32[1024,1024]{1,0:T(8,128)} fusion(f32[1024,1024]{1,0:T(8,128)S(1)} %fusion.46, f32[1024,1024]{1,0:T(8,128)S(1)} %fusion.14, f32[1024,1024]{1,0:T(8,128)S(1)} %fusion.42, f32[1024,1024]{1,0:T(8,128)S(1)} %fusion.16, f32[1024,1024]{1,0:T(8,128)S(1)} %fusion.48, bf16[1024,384]{1,0:T(8,128)(2,1)S(1)} %collective-permute-done.13, ...), kind=kOutput, calls=%fused_computation.26 | convolution fusion | flops 810549248 | bytes 26738692 | tf_op jit(solution)/shard_map/dot_general | solution.py:218
  104.5 2.8 %fusion.36 = f32[1024,1024]{1,0:T(8,128)S(1)} fusion(bf16[1024,384]{1,0:T(8,128)(2,1)} %collective-permute-done.9, bf16[4096,1024]{1,0:T(8,128)(2,1)} %param.11, s32[]{:T(128)S(6)} %select_n.35), kind=kOutput, calls=%fused_computation.62 | convolution fusion | flops 805306368 | bytes 5767172 | tf_op jit(solution)/shard_map/dot_general | solution.py:218
  107.3 3.7 %add_convert_fusion = bf16[1024,1024]{1,0:T(8,128)(2,1)} fusion(f32[1024,1024]{1,0:T(8,128)S(1)} %copy-done, f32[1024,1024]{1,0:T(8,128)S(1)} %fusion.36, bf16[1024,384]{1,0:T(8,128)(2,1)S(1)} %collective-permute-done.14, bf16[4096,1024]{1,0:T(8,128)(2,1)} %param.11, s32[]{:T(128)S(6)} %select_n.36), kind=kOutput, calls=%fused_computation.25 | convolution fusion | flops 808452096 | bytes 12058628 | tf_op jit(solution)/shard_map/dot_general | solution.py:218
  (47 shorter events, 9.9 us)
Async XLA Ops:
  0.8 8.7 %collective-permute-start = (bf16[3,2,1024]{2,1,0:T(2,128)(2,1)S(1)}, bf16[3,2,1024]{2,1,0:T(2,128)(2,1)S(1)}, u32[]{:S(2)}, u32[]{:S(2)}) collective-permute-start(bf16[3,2,1024]{2,1,0:T(2,128)(2,1)S(1)} %slice.152), channel_id=1, source_target_pairs={{0,4},{4,8},{8,12},{12,16},{16,20},{20,24},{24,28},{1,5},{5,9},{9,... | collective-permute-start | bytes 36872 | tf_op jit(solution)/shard_map/ppermute | solution.py:15
  16.6 28.4 %copy-start.3 = (f32[16,1024]{1,0:T(8,128)S(1)}, f32[16,1024]{1,0:T(8,128)}, u32[]{:S(2)}) copy-start(f32[16,1024]{1,0:T(8,128)} %param.8) | copy-start | bytes 196612
  27.1 11.8 %collective-permute-start.7 = (f32[16,1024]{1,0:T(8,128)S(1)}, f32[16,1024]{1,0:T(8,128)S(1)}, u32[]{:S(2)}, u32[]{:S(2)}) collective-permute-start(f32[16,1024]{1,0:T(8,128)S(1)} %multiply_reduce_fusion.1), channel_id=1, source_target_pairs={{0,28},{1,29},{2,30},{3,31}} | collective-permute-start | bytes 196616 | tf_op jit(solution)/shard_map/ppermute | solution.py:15
  31.5 9.1 %collective-permute-start.6 = (f32[16,1024]{1,0:T(8,128)S(1)}, f32[16,1024]{1,0:T(8,128)S(1)}, u32[]{:S(2)}, u32[]{:S(2)}) collective-permute-start(f32[16,1024]{1,0:T(8,128)S(1)} %multiply_reduce_fusion.1), channel_id=1, source_target_pairs={{0,24},{4,28},{1,25},{5,29},{2,26},{6,30},{3,27},{7,31}} | collective-permute-start | bytes 196616 | tf_op jit(solution)/shard_map/ppermute | solution.py:15
  33.1 11.8 %collective-permute-start.5 = (f32[16,1024]{1,0:T(8,128)S(1)}, f32[16,1024]{1,0:T(8,128)S(1)}, u32[]{:S(2)}, u32[]{:S(2)}) collective-permute-start(f32[16,1024]{1,0:T(8,128)S(1)} %multiply_reduce_fusion.1), channel_id=1, source_target_pairs={{0,20},{4,24},{8,28},{1,21},{5,25},{9,29},{2,22},{6,26},{10,30},{3... | collective-permute-start | bytes 196616 | tf_op jit(solution)/shard_map/ppermute | solution.py:15
  34.4 10.5 %collective-permute-start.4 = (f32[16,1024]{1,0:T(8,128)S(1)}, f32[16,1024]{1,0:T(8,128)S(1)}, u32[]{:S(2)}, u32[]{:S(2)}) collective-permute-start(f32[16,1024]{1,0:T(8,128)S(1)} %multiply_reduce_fusion.1), channel_id=1, source_target_pairs={{0,16},{4,20},{8,24},{12,28},{1,17},{5,21},{9,25},{13,29},{2,18},{... | collective-permute-start | bytes 196616 | tf_op jit(solution)/shard_map/ppermute | solution.py:15
  35.7 9.2 %collective-permute-start.3 = (f32[16,1024]{1,0:T(8,128)S(1)}, f32[16,1024]{1,0:T(8,128)S(1)}, u32[]{:S(2)}, u32[]{:S(2)}) collective-permute-start(f32[16,1024]{1,0:T(8,128)S(1)} %multiply_reduce_fusion.1), channel_id=1, source_target_pairs={{0,12},{4,16},{8,20},{12,24},{16,28},{1,13},{5,17},{9,21},{13,25},... | collective-permute-start | bytes 196616 | tf_op jit(solution)/shard_map/ppermute | solution.py:15
  39.0 6.0 %collective-permute-start.2 = (f32[16,1024]{1,0:T(8,128)S(1)}, f32[16,1024]{1,0:T(8,128)S(1)}, u32[]{:S(2)}, u32[]{:S(2)}) collective-permute-start(f32[16,1024]{1,0:T(8,128)S(1)} %multiply_reduce_fusion.1), channel_id=1, source_target_pairs={{0,8},{4,12},{8,16},{12,20},{16,24},{20,28},{1,9},{5,13},{9,17},{1... | collective-permute-start | bytes 196616 | tf_op jit(solution)/shard_map/ppermute | solution.py:15
  40.5 4.4 %collective-permute-start.1 = (f32[16,1024]{1,0:T(8,128)S(1)}, f32[16,1024]{1,0:T(8,128)S(1)}, u32[]{:S(2)}, u32[]{:S(2)}) collective-permute-start(f32[16,1024]{1,0:T(8,128)S(1)} %multiply_reduce_fusion.1), channel_id=1, source_target_pairs={{0,4},{4,8},{8,12},{12,16},{16,20},{20,24},{24,28},{1,5},{5,9},{9,... | collective-permute-start | bytes 196616 | tf_op jit(solution)/shard_map/ppermute | solution.py:15
  44.9 5.8 %slice-start.2 = ((f32[1024]{0:T(1024)}), f32[256]{0:T(256)S(1)}, s32[]{:S(2)}) async-start(f32[1024]{0:T(1024)} %param.10), calls=%async_computation.2 | async-start | bytes 2048 | tf_op jit(solution)/shard_map/slice | solution.py:191
  53.1 11.3 %collective-permute-start.8 = (bf16[1024,256]{1,0:T(8,128)(2,1)S(1)}, bf16[1024,256]{1,0:T(8,128)(2,1)S(1)}, u32[]{:S(2)}, u32[]{:S(2)}) collective-permute-start(bf16[1024,256]{1,0:T(8,128)(2,1)S(1)} %fusion.28), channel_id=1, source_target_pairs={{0,2},{1,3},{2,0},{3,1},{4,6},{5,7},{6,4},{7,5},{8,10},{9,11},{10,... | collective-permute-start | bytes 1572872 | tf_op jit(solution)/shard_map/ppermute | solution.py:198
  64.1 16.9 %collective-permute-start.10 = (bf16[1024,384]{1,0:T(8,128)(2,1)}, bf16[1024,384]{1,0:T(8,128)(2,1)}, u32[]{:S(2)}, u32[]{:S(2)}) collective-permute-start(bf16[1024,384]{1,0:T(8,128)(2,1)} %fusion.20), channel_id=1, source_target_pairs={{0,2},{1,3},{2,0},{3,1},{4,6},{5,7},{6,4},{7,5},{8,10},{9,11},{10,... | collective-permute-start | bytes 2359304 | tf_op jit(solution)/shard_map/ppermute | solution.py:198
  64.4 6.0 %copy-start.1 = (bf16[1024,256]{1,0:T(8,128)(2,1)}, bf16[1024,256]{1,0:T(8,128)(2,1)S(1)}, u32[]{:S(2)}) copy-start(bf16[1024,256]{1,0:T(8,128)(2,1)S(1)} %collective-permute-done.8) | copy-start | bytes 1572868
  74.9 14.1 %copy-start.2 = (bf16[1024,256]{1,0:T(8,128)(2,1)S(1)}, bf16[1024,256]{1,0:T(8,128)(2,1)}, u32[]{:S(2)}) copy-start(bf16[1024,256]{1,0:T(8,128)(2,1)} %copy-done.1) | copy-start | bytes 1572868
  81.0 13.4 %collective-permute-start.11 = (bf16[1024,1024]{1,0:T(8,128)(2,1)S(1)}, bf16[1024,1024]{1,0:T(8,128)(2,1)}, u32[]{:S(2)}, u32[]{:S(2)}) collective-permute-start(bf16[1024,1024]{1,0:T(8,128)(2,1)S(1)} %pad_maximum_fusion), channel_id=1, source_target_pairs={{0,1},{1,0},{2,3},{3,2},{4,5},{5,4},{6,7},{7,6},{8,9},{9,8},{10,11... | collective-permute-start | bytes 6291464 | tf_op jit(solution)/shard_map/ppermute | solution.py:225
  84.5 19.3 %collective-permute-start.9 = (bf16[1024,384]{1,0:T(8,128)(2,1)S(1)}, bf16[1024,384]{1,0:T(8,128)(2,1)}, u32[]{:S(2)}, u32[]{:S(2)}) collective-permute-start(bf16[1024,384]{1,0:T(8,128)(2,1)S(1)} %fusion.24), channel_id=1, source_target_pairs={{0,2},{1,3},{2,0},{3,1},{4,6},{5,7},{6,4},{7,5},{8,10},{9,11},{10,... | collective-permute-start | bytes 2359304 | tf_op jit(solution)/shard_map/ppermute | solution.py:198
  85.7 8.0 %collective-permute-start.12 = (bf16[1024,256]{1,0:T(8,128)(2,1)}, bf16[1024,256]{1,0:T(8,128)(2,1)S(1)}, u32[]{:S(2)}, u32[]{:S(2)}) collective-permute-start(bf16[1024,256]{1,0:T(8,128)(2,1)} %copy-done.1), channel_id=1, source_target_pairs={{0,1},{1,0},{2,3},{3,2},{4,5},{5,4},{6,7},{7,6},{8,9},{9,8},{10,11... | collective-permute-start | bytes 1572872 | tf_op jit(solution)/shard_map/ppermute | solution.py:226
  86.0 12.4 %collective-permute-start.13 = (bf16[1024,384]{1,0:T(8,128)(2,1)}, bf16[1024,384]{1,0:T(8,128)(2,1)S(1)}, u32[]{:S(2)}, u32[]{:S(2)}) collective-permute-start(bf16[1024,384]{1,0:T(8,128)(2,1)} %collective-permute-done.10), channel_id=1, source_target_pairs={{0,1},{1,0},{2,3},{3,2},{4,5},{5,4},{6,7},{7,6},{8,9},{9,8},{10,11... | collective-permute-start | bytes 2359304 | tf_op jit(solution)/shard_map/ppermute | solution.py:226
  86.2 4.7 %slice-start = ((s8[8388608]{0:T(1024)(128)(4,1)}), s8[4194304]{0:T(1024)(128)(4,1)S(1)}, s32[]{:S(2)}) async-start(s8[8388608]{0:T(1024)(128)(4,1)} %bitcast.108), calls=%async_computation | async-start | bytes 8388608
  89.0 2.4 %slice-start.1 = ((s8[8388608]{0:T(1024)(128)(4,1)}), s8[4194304]{0:T(1024)(128)(4,1)S(1)}, s32[]{:S(2)}) async-start(s8[8388608]{0:T(1024)(128)(4,1)} %bitcast.108), calls=%async_computation.1 | async-start | bytes 8388608
  103.7 3.6 %collective-permute-start.14 = (bf16[1024,384]{1,0:T(8,128)(2,1)}, bf16[1024,384]{1,0:T(8,128)(2,1)S(1)}, u32[]{:S(2)}, u32[]{:S(2)}) collective-permute-start(bf16[1024,384]{1,0:T(8,128)(2,1)} %collective-permute-done.9), channel_id=1, source_target_pairs={{0,1},{1,0},{2,3},{3,2},{4,5},{5,4},{6,7},{7,6},{8,9},{9,8},{10,11... | collective-permute-start | bytes 2359304 | tf_op jit(solution)/shard_map/ppermute | solution.py:237
  104.5 2.8 %copy-start = (f32[1024,1024]{1,0:T(8,128)S(1)}, f32[1024,1024]{1,0:T(8,128)}, u32[]{:S(2)}) copy-start(f32[1024,1024]{1,0:T(8,128)} %add_add_fusion) | copy-start | bytes 12582916

commit v20 on v19

--- a/solution.py
+++ b/solution.py
@@ -15,7 +15,7 @@
     return lax.ppermute(value, axis, [(source, source + steps) for source in range(initial, last)])
 
 
-def segment_pass(x_ref, decay_ref, residue_ref, start_ref, y_ref, end_ref):
+def segment_pass(x_ref, decay_ref, residue_ref, start_ref, y_ref, end_ref, unroll):
     pole_count = decay_ref.shape[0]
     segments = SEGMENTS
     span = x_ref.shape[0] // segments
@@ -42,18 +42,18 @@
             y_ref[pl.ds(t, segments, stride=span), :] = total
         return tuple(updated)
 
-    states = lax.fori_loop(0, span, body, states, unroll=128)
+    states = lax.fori_loop(0, span, body, states, unroll=min(unroll, span))
     if end_ref is not None:
         for p in range(pole_count):
             end_ref[p] = states[p]
 
 
 def end_state_kernel(x_ref, decay_ref, end_ref):
-    segment_pass(x_ref, decay_ref, None, None, None, end_ref)
+    segment_pass(x_ref, decay_ref, None, None, None, end_ref, 32)
 
 
 def recurrence_kernel(x_ref, decay_ref, residue_ref, start_ref, y_ref):
-    segment_pass(x_ref, decay_ref, residue_ref, start_ref, y_ref, None)
+    segment_pass(x_ref, decay_ref, residue_ref, start_ref, y_ref, None, 128)
 
 
 def run_end_state(x, decay):

time: 112 us -> 111 us (level)
  no operation moved by 1% of the time
where the time goes in v20:
time: 111 us; the launch traced here: 110 us
  starting transfers between devices  26.6 us (24%)
  other arithmetic  25.7 us (23%)
  Pallas kernels  24.7 us (22%)
  matrix products  22.9 us (21%)
  waiting for transfers between devices  6.73 us (6%)
  local copies, waits for them, and re-layouts  3.38 us (3%)
    ppermute x8, starting transfers between devices, shifted(): lax.ppermute(value, axis, [(source, source + steps) for source in range(i...  19 us
    dot_general x6, matrix products, part(): return jnp.dot(value, rows, preferred_element_type=jnp.float32)  16.6 us
    pallas_call x3, Pallas kernels, run_recurrence(): pl.pallas_call(recurrence_kernel, grid=(group_count,), in_specs=[pl.Block...  16.2 us
    convert_element_type x3, other arithmetic, shards(): gated_mix = gated_mix.astype(jnp.bfloat16)  9.51 us
    pallas_call x1, Pallas kernels, run_end_state(): pl.pallas_call(end_state_kernel, grid=(width // LANES,), in_specs=[pl.Blo...  8.52 us
    ppermute x3, waiting for transfers between devices, shards(): lax.ppermute(gated_mix, 'ch', [(i, i ^ 2) for i in range(ch_count)])  6.67 us
    convert_element_type x1, other arithmetic, shards(): x = mixed_input.astype(jnp.float32)  4.2 us
    dot_general x1, matrix products, project_pieces(): total = total + jnp.dot(near, rows_near, preferred_element_type=jnp.float32)  3.94 us
  transfers between devices with their start and end apart: 15, of which 2 were waited for; matrix products, arithmetic and copies ran while one was open for 32% of the time, Pallas kernels for 11%

profile of v20, /device:TPU:1, one launch (start us, length us, event | category | flops | bytes accessed | tf_op | source)
XLA Modules:
  0.0 110.3 jit_solution(9416374882308192192)
XLA Ops:
  0.8 4.0 %collective-permute-start = (bf16[3,2,1024]{2,1,0:T(2,128)(2,1)S(1)}, bf16[3,2,1024]{2,1,0:T(2,128)(2,1)S(1)}, u32[]{:S(2)}, u32[]{:S(2)}) collective-permute-start(bf16[3,2,1024]{2,1,0:T(2,128)(2,1)S(1)} %slice.152), channel_id=1, source_target_pairs={{0,4},{4,8},{8,12},{12,16},{16,20},{20,24},{24,28},{1,5},{5,9},{9,... | collective-permute-start | bytes 36872 | tf_op jit(solution)/shard_map/ppermute | solution.py:15
  8.0 1.5 %fusion.60 = (f32[16,1024]{1,0:T(8,128)S(1)}, f32[16,1024]{1,0:T(8,128)}) fusion(f32[16,1024]{1,0:T(8,128)} %param.8), kind=kLoop, calls=%fused_computation.108 | loop fusion | flops 16384 | bytes 196608 | tf_op jit(solution)/shard_map/neg | solution.py:170
  9.5 2.9 %fusion.1 = f32[2,1026,1024]{2,1,0:T(8,128)S(1)} fusion(bf16[3,2,1024]{2,1,0:T(2,128)(2,1)S(1)} %collective-permute-done, bf16[3,1024,1024]{2,1,0:T(8,128)(2,1)} %param.6), kind=kLoop, calls=%fused_computation.5 | loop fusion | flops 8404992 | bytes 14708736 | tf_op jit(solution)/shard_map/convert_element_type | solution.py:163
  12.4 4.2 %fusion.58 = (f32[1024,1024]{1,0:T(8,128)}, bf16[1024,1024]{1,0:T(8,128)(2,1)S(1)}) fusion(f32[2,1026,1024]{2,1,0:T(8,128)S(1)} %fusion.1, f32[1024]{0:T(1024)S(1)} %bitcast.115, f32[1024]{0:T(1024)S(1)} %bitcast.111, f32[1024]{0:T(1024)S(1)} %bitcast.112, f32[1024]{0:T(1024)S(1)} %bitcast.113, f32[1024]{0:T(1024)S(1)} %bitcast.114, f32[1024]{0:T(1024)S(1)} %bitcast.110), kind=kLoop, calls=%fused_computation.107 | loop fusion | flops 13631488 | bytes 31481856 | tf_op jit(solution)/shard_map/convert_element_type | solution.py:167
  16.6 8.5 %shard_map.64 = f32[16,8,1024]{2,1,0:T(8,128)} custom-call(f32[1024,1024]{1,0:T(8,128)} %get-tuple-element.19.x_ref, f32[16,1024]{1,0:T(8,128)} %get-tuple-element.36.decay_ref), custom_call_target="tpu_custom_call" | custom-call | tf_op jit(solution)/shard_map/pallas_call | solution.py:62
  25.1 1.3 %multiply_reduce_fusion.1 = f32[16,1024]{1,0:T(8,128)S(1)} fusion(f32[16,8,1024]{2,1,0:T(8,128)} %shard_map.64, f32[8]{0:T(128)S(1)} %subtract_multiply_fusion, f32[16,1024]{1,0:T(8,128)S(1)} %get-tuple-element.35), kind=kLoop, calls=%fused_computation.76 | loop fusion | flops 376832 | bytes 655392 | tf_op jit(solution)/shard_map/reduce_sum | solution.py:110
  26.4 4.3 %collective-permute-start.7 = (f32[16,1024]{1,0:T(8,128)S(1)}, f32[16,1024]{1,0:T(8,128)S(1)}, u32[]{:S(2)}, u32[]{:S(2)}) collective-permute-start(f32[16,1024]{1,0:T(8,128)S(1)} %multiply_reduce_fusion.1), channel_id=1, source_target_pairs={{0,28},{1,29},{2,30},{3,31}} | collective-permute-start | bytes 196616 | tf_op jit(solution)/shard_map/ppermute | solution.py:15
  30.7 1.6 %collective-permute-start.6 = (f32[16,1024]{1,0:T(8,128)S(1)}, f32[16,1024]{1,0:T(8,128)S(1)}, u32[]{:S(2)}, u32[]{:S(2)}) collective-permute-start(f32[16,1024]{1,0:T(8,128)S(1)} %multiply_reduce_fusion.1), channel_id=1, source_target_pairs={{0,24},{4,28},{1,25},{5,29},{2,26},{6,30},{3,27},{7,31}} | collective-permute-start | bytes 196616 | tf_op jit(solution)/shard_map/ppermute | solution.py:15
  32.3 1.3 %collective-permute-start.5 = (f32[16,1024]{1,0:T(8,128)S(1)}, f32[16,1024]{1,0:T(8,128)S(1)}, u32[]{:S(2)}, u32[]{:S(2)}) collective-permute-start(f32[16,1024]{1,0:T(8,128)S(1)} %multiply_reduce_fusion.1), channel_id=1, source_target_pairs={{0,20},{4,24},{8,28},{1,21},{5,25},{9,29},{2,22},{6,26},{10,30},{3... | collective-permute-start | bytes 196616 | tf_op jit(solution)/shard_map/ppermute | solution.py:15
  33.6 1.3 %collective-permute-start.4 = (f32[16,1024]{1,0:T(8,128)S(1)}, f32[16,1024]{1,0:T(8,128)S(1)}, u32[]{:S(2)}, u32[]{:S(2)}) collective-permute-start(f32[16,1024]{1,0:T(8,128)S(1)} %multiply_reduce_fusion.1), channel_id=1, source_target_pairs={{0,16},{4,20},{8,24},{12,28},{1,17},{5,21},{9,25},{13,29},{2,18},{... | collective-permute-start | bytes 196616 | tf_op jit(solution)/shard_map/ppermute | solution.py:15
  34.9 1.9 %collective-permute-start.3 = (f32[16,1024]{1,0:T(8,128)S(1)}, f32[16,1024]{1,0:T(8,128)S(1)}, u32[]{:S(2)}, u32[]{:S(2)}) collective-permute-start(f32[16,1024]{1,0:T(8,128)S(1)} %multiply_reduce_fusion.1), channel_id=1, source_target_pairs={{0,12},{4,16},{8,20},{12,24},{16,28},{1,13},{5,17},{9,21},{13,25},... | collective-permute-start | bytes 196616 | tf_op jit(solution)/shard_map/ppermute | solution.py:15
  36.8 1.4 %copy.15 = f32[16,1024,8]{1,0,2:T(8,128)S(1)} copy(f32[16,1024,8]{1,2,0:T(8,128)} %bitcast.107) | data formatting | bytes 1048576
  38.2 1.6 %collective-permute-start.2 = (f32[16,1024]{1,0:T(8,128)S(1)}, f32[16,1024]{1,0:T(8,128)S(1)}, u32[]{:S(2)}, u32[]{:S(2)}) collective-permute-start(f32[16,1024]{1,0:T(8,128)S(1)} %multiply_reduce_fusion.1), channel_id=1, source_target_pairs={{0,8},{4,12},{8,16},{12,20},{16,24},{20,28},{1,9},{5,13},{9,17},{1... | collective-permute-start | bytes 196616 | tf_op jit(solution)/shard_map/ppermute | solution.py:15
  39.8 3.1 %collective-permute-start.1 = (f32[16,1024]{1,0:T(8,128)S(1)}, f32[16,1024]{1,0:T(8,128)S(1)}, u32[]{:S(2)}, u32[]{:S(2)}) collective-permute-start(f32[16,1024]{1,0:T(8,128)S(1)} %multiply_reduce_fusion.1), channel_id=1, source_target_pairs={{0,4},{4,8},{8,12},{12,16},{16,20},{20,24},{24,28},{1,5},{5,9},{9,... | collective-permute-start | bytes 196616 | tf_op jit(solution)/shard_map/ppermute | solution.py:15
  42.9 1.2 %multiply_reduce_fusion = f32[16,1024,8]{1,0,2:T(8,128)S(1)} fusion(f32[16,1024,8]{1,0,2:T(8,128)S(1)} %copy.15, f32[8,8]{1,0:T(8,128)S(1)} %maximum_multiply_fusion, f32[16,1024]{1,0:T(8,128)S(1)} %get-tuple-element.35, pred[8,8]{1,0:T(8,128)(4,1)S(1)} %iota_compare_fusion), kind=kLoop, calls=%fused_computation.24 | loop fusion | flops 4063232 | bytes 1114432
  45.5 4.4 %shard_map.65 = f32[1024,256]{1,0:T(8,128)} custom-call(f32[1024,1024]{1,0:T(8,128)} %get-tuple-element.19.x_ref, f32[16,1024]{1,0:T(8,128)} %get-tuple-element.36.decay_ref, f32[16,1024]{1,0:T(8,128)} %residue_ref.5, f32[16,8,1024]{2,1,0:T(8,128)} %bitcast_add_fusion.start_ref), custom_call_target="tpu_custom_call" | custom-call | tf_op jit(solution)/shard_map/pallas_call | solution.py:78
  49.9 2.4 %fusion.28 = bf16[1024,256]{1,0:T(8,128)(2,1)S(1)} fusion(bf16[1024,1024]{1,0:T(8,128)(2,1)S(1)} %get-tuple-element.34, bf16[3,1024,1024]{2,1,0:T(8,128)(2,1)} %param.6, bf16[3,2,1024]{2,1,0:T(2,128)(2,1)S(1)} %collective-permute-done, f32[256]{0:T(256)S(1)} %slice-done.2, f32[1024,256]{1,0:T(8,128)} %shard_map.65, f32[256]{0:T(256)S(1)} %bitcast.117, ...), kind=kLoop, calls=%fused_computation.52 | loop fusion | flops 6029312 | bytes 8929280 | tf_op jit(solution)/shard_map/convert_element_type | solution.py:193
  52.4 1.3 %collective-permute-start.8 = (bf16[1024,256]{1,0:T(8,128)(2,1)S(1)}, bf16[1024,256]{1,0:T(8,128)(2,1)S(1)}, u32[]{:S(2)}, u32[]{:S(2)}) collective-permute-start(bf16[1024,256]{1,0:T(8,128)(2,1)S(1)} %fusion.28), channel_id=1, source_target_pairs={{0,2},{1,3},{2,0},{3,1},{4,6},{5,7},{6,4},{7,5},{8,10},{9,11},{10,... | collective-permute-start | bytes 1572872 | tf_op jit(solution)/shard_map/ppermute | solution.py:198
  53.6 5.8 %shard_map.66 = f32[1024,384]{1,0:T(8,128)} custom-call(f32[1024,1024]{1,0:T(8,128)} %get-tuple-element.19.x_ref, f32[16,1024]{1,0:T(8,128)} %get-tuple-element.36.decay_ref, f32[16,1024]{1,0:T(8,128)} %residue_ref.5, f32[16,8,1024]{2,1,0:T(8,128)} %bitcast_add_fusion.start_ref), custom_call_target="tpu_custom_call" | custom-call | tf_op jit(solution)/shard_map/pallas_call | solution.py:78
  59.4 4.0 %fusion.20 = bf16[1024,384]{1,0:T(8,128)(2,1)} fusion(bf16[1024,1024]{1,0:T(8,128)(2,1)S(1)} %get-tuple-element.34, f32[384]{0:T(512)S(1)} %get-tuple-element.46, f32[1024,384]{1,0:T(8,128)} %shard_map.66, f32[384]{0:T(512)S(1)} %get-tuple-element.28, f32[384]{0:T(512)S(1)} %get-tuple-element.29, bf16[3,1024,1024]{2,1,0:T(8,128)(2,1)} %param.6, ...), kind=kLoop, calls=%fused_computation.38 | loop fusion | flops 9043968 | bytes 10242048 | tf_op jit(solution)/shard_map/convert_element_type | solution.py:193
  63.6 6.0 %shard_map.67 = f32[1024,384]{1,0:T(8,128)} custom-call(f32[1024,1024]{1,0:T(8,128)} %get-tuple-element.19.x_ref, f32[16,1024]{1,0:T(8,128)} %get-tuple-element.36.decay_ref, f32[16,1024]{1,0:T(8,128)} %residue_ref.5, f32[16,8,1024]{2,1,0:T(8,128)} %bitcast_add_fusion.start_ref), custom_call_target="tpu_custom_call" | custom-call | tf_op jit(solution)/shard_map/pallas_call | solution.py:78
  69.6 3.1 %fusion.24 = bf16[1024,384]{1,0:T(8,128)(2,1)S(1)} fusion(bf16[1024,1024]{1,0:T(8,128)(2,1)S(1)} %get-tuple-element.34, bf16[3,1024,1024]{2,1,0:T(8,128)(2,1)} %param.6, bf16[3,2,1024]{2,1,0:T(2,128)(2,1)S(1)} %collective-permute-done, f32[384]{0:T(512)S(1)} %get-tuple-element.47, f32[1024,384]{1,0:T(8,128)} %shard_map.67, f32[384]{0:T(512)S(1)} %get-tuple-element.31, ...), kind=kLoop, calls=%fused_computation.45 | loop fusion | flops 9043968 | bytes 10242048 | tf_op jit(solution)/shard_map/convert_element_type | solution.py:193
  72.7 1.4 %pad_maximum_fusion = bf16[1024,1024]{1,0:T(8,128)(2,1)S(1)} fusion(bf16[1024,384]{1,0:T(8,128)(2,1)S(1)} %fusion.24, bf16[1024,384]{1,0:T(8,128)(2,1)} %fusion.20, bf16[1024,256]{1,0:T(8,128)(2,1)S(1)} %fusion.28), kind=kLoop, calls=%fused_computation.30 | loop fusion | flops 6291456 | bytes 4194304 | tf_op jit(solution)/shard_map/concatenate | solution.py:221
  74.1 6.1 %collective-permute-done.10 = bf16[1024,384]{1,0:T(8,128)(2,1)} collective-permute-done((bf16[1024,384]{1,0:T(8,128)(2,1)}, bf16[1024,384]{1,0:T(8,128)(2,1)}, u32[]{:S(2)}, u32[]{:S(2)}) %collective-permute-start.10) | collective-permute-done | bytes 786464 | tf_op jit(solution)/shard_map/ppermute | solution.py:198
  80.2 3.5 %collective-permute-start.11 = (bf16[1024,1024]{1,0:T(8,128)(2,1)S(1)}, bf16[1024,1024]{1,0:T(8,128)(2,1)}, u32[]{:S(2)}, u32[]{:S(2)}) collective-permute-start(bf16[1024,1024]{1,0:T(8,128)(2,1)S(1)} %pad_maximum_fusion), channel_id=1, source_target_pairs={{0,1},{1,0},{2,3},{3,2},{4,5},{5,4},{6,7},{7,6},{8,9},{9,8},{10,11... | collective-permute-start | bytes 6291464 | tf_op jit(solution)/shard_map/ppermute | solution.py:225
  85.4 2.8 %fusion.42 = f32[1024,1024]{1,0:T(8,128)S(1)} fusion(bf16[1024,384]{1,0:T(8,128)(2,1)} %collective-permute-done.10, bf16[4096,1024]{1,0:T(8,128)(2,1)} %param.11, s32[]{:T(128)S(6)} %select_n.31), kind=kOutput, calls=%fused_computation.66 | convolution fusion | flops 805306368 | bytes 5767172 | tf_op jit(solution)/shard_map/dot_general | solution.py:218
  88.2 1.9 %fusion.48 = f32[1024,1024]{1,0:T(8,128)S(1)} fusion(bf16[1024,256]{1,0:T(8,128)(2,1)S(1)} %copy-done.2, bf16[4096,1024]{1,0:T(8,128)(2,1)} %param.11, s32[]{:T(128)S(6)} %select_n.30), kind=kOutput, calls=%fused_computation.74 | convolution fusion | flops 536870912 | bytes 5242884 | tf_op jit(solution)/shard_map/dot_general | solution.py:218
  90.6 2.3 %fusion.16 = f32[1024,1024]{1,0:T(8,128)S(1)} fusion(bf16[1024,1024]{1,0:T(8,128)(2,1)S(1)} %pad_maximum_fusion, bf16[4096,1024]{1,0:T(8,128)(2,1)S(1)} %bitcast.109, s32[]{:T(128)S(6)} %select_n.29), kind=kOutput, calls=%fused_computation.33 | convolution fusion | flops 2147483648 | bytes 8388612 | tf_op jit(solution)/shard_map/dot_general | solution.py:229
  93.7 3.9 %fusion.14 = f32[1024,1024]{1,0:T(8,128)S(1)} fusion(bf16[1024,1024]{1,0:T(8,128)(2,1)} %collective-permute-done.11, bf16[4096,1024]{1,0:T(8,128)(2,1)S(1)} %bitcast.109, s32[]{:T(128)S(6)} %select_n.32), kind=kOutput, calls=%fused_computation.31 | convolution fusion | flops 2147483648 | bytes 8388612 | tf_op jit(solution)/shard_map/dot_general | solution.py:232
  97.6 4.8 %add_add_fusion = f32[1024,1024]{1,0:T(8,128)} fusion(f32[1024,1024]{1,0:T(8,128)S(1)} %fusion.46, f32[1024,1024]{1,0:T(8,128)S(1)} %fusion.14, f32[1024,1024]{1,0:T(8,128)S(1)} %fusion.42, f32[1024,1024]{1,0:T(8,128)S(1)} %fusion.16, f32[1024,1024]{1,0:T(8,128)S(1)} %fusion.48, bf16[1024,384]{1,0:T(8,128)(2,1)S(1)} %collective-permute-done.13, ...), kind=kOutput, calls=%fused_computation.26 | convolution fusion | flops 810549248 | bytes 26738692 | tf_op jit(solution)/shard_map/dot_general | solution.py:218
  103.8 2.8 %fusion.36 = f32[1024,1024]{1,0:T(8,128)S(1)} fusion(bf16[1024,384]{1,0:T(8,128)(2,1)} %collective-permute-done.9, bf16[4096,1024]{1,0:T(8,128)(2,1)} %param.11, s32[]{:T(128)S(6)} %select_n.35), kind=kOutput, calls=%fused_computation.62 | convolution fusion | flops 805306368 | bytes 5767172 | tf_op jit(solution)/shard_map/dot_general | solution.py:218
  106.6 3.7 %add_convert_fusion = bf16[1024,1024]{1,0:T(8,128)(2,1)} fusion(f32[1024,1024]{1,0:T(8,128)S(1)} %copy-done, f32[1024,1024]{1,0:T(8,128)S(1)} %fusion.36, bf16[1024,384]{1,0:T(8,128)(2,1)S(1)} %collective-permute-done.14, bf16[4096,1024]{1,0:T(8,128)(2,1)} %param.11, s32[]{:T(128)S(6)} %select_n.36), kind=kOutput, calls=%fused_computation.25 | convolution fusion | flops 808452096 | bytes 12058628 | tf_op jit(solution)/shard_map/dot_general | solution.py:218
  (47 shorter events, 9.9 us)
Async XLA Ops:
  0.8 8.7 %collective-permute-start = (bf16[3,2,1024]{2,1,0:T(2,128)(2,1)S(1)}, bf16[3,2,1024]{2,1,0:T(2,128)(2,1)S(1)}, u32[]{:S(2)}, u32[]{:S(2)}) collective-permute-start(bf16[3,2,1024]{2,1,0:T(2,128)(2,1)S(1)} %slice.152), channel_id=1, source_target_pairs={{0,4},{4,8},{8,12},{12,16},{16,20},{20,24},{24,28},{1,5},{5,9},{9,... | collective-permute-start | bytes 36872 | tf_op jit(solution)/shard_map/ppermute | solution.py:15
  16.6 27.6 %copy-start.3 = (f32[16,1024]{1,0:T(8,128)S(1)}, f32[16,1024]{1,0:T(8,128)}, u32[]{:S(2)}) copy-start(f32[16,1024]{1,0:T(8,128)} %param.8) | copy-start | bytes 196612
  26.4 11.8 %collective-permute-start.7 = (f32[16,1024]{1,0:T(8,128)S(1)}, f32[16,1024]{1,0:T(8,128)S(1)}, u32[]{:S(2)}, u32[]{:S(2)}) collective-permute-start(f32[16,1024]{1,0:T(8,128)S(1)} %multiply_reduce_fusion.1), channel_id=1, source_target_pairs={{0,28},{1,29},{2,30},{3,31}} | collective-permute-start | bytes 196616 | tf_op jit(solution)/shard_map/ppermute | solution.py:15
  30.7 9.1 %collective-permute-start.6 = (f32[16,1024]{1,0:T(8,128)S(1)}, f32[16,1024]{1,0:T(8,128)S(1)}, u32[]{:S(2)}, u32[]{:S(2)}) collective-permute-start(f32[16,1024]{1,0:T(8,128)S(1)} %multiply_reduce_fusion.1), channel_id=1, source_target_pairs={{0,24},{4,28},{1,25},{5,29},{2,26},{6,30},{3,27},{7,31}} | collective-permute-start | bytes 196616 | tf_op jit(solution)/shard_map/ppermute | solution.py:15
  32.3 11.8 %collective-permute-start.5 = (f32[16,1024]{1,0:T(8,128)S(1)}, f32[16,1024]{1,0:T(8,128)S(1)}, u32[]{:S(2)}, u32[]{:S(2)}) collective-permute-start(f32[16,1024]{1,0:T(8,128)S(1)} %multiply_reduce_fusion.1), channel_id=1, source_target_pairs={{0,20},{4,24},{8,28},{1,21},{5,25},{9,29},{2,22},{6,26},{10,30},{3... | collective-permute-start | bytes 196616 | tf_op jit(solution)/shard_map/ppermute | solution.py:15
  33.6 10.5 %collective-permute-start.4 = (f32[16,1024]{1,0:T(8,128)S(1)}, f32[16,1024]{1,0:T(8,128)S(1)}, u32[]{:S(2)}, u32[]{:S(2)}) collective-permute-start(f32[16,1024]{1,0:T(8,128)S(1)} %multiply_reduce_fusion.1), channel_id=1, source_target_pairs={{0,16},{4,20},{8,24},{12,28},{1,17},{5,21},{9,25},{13,29},{2,18},{... | collective-permute-start | bytes 196616 | tf_op jit(solution)/shard_map/ppermute | solution.py:15
  34.9 9.2 %collective-permute-start.3 = (f32[16,1024]{1,0:T(8,128)S(1)}, f32[16,1024]{1,0:T(8,128)S(1)}, u32[]{:S(2)}, u32[]{:S(2)}) collective-permute-start(f32[16,1024]{1,0:T(8,128)S(1)} %multiply_reduce_fusion.1), channel_id=1, source_target_pairs={{0,12},{4,16},{8,20},{12,24},{16,28},{1,13},{5,17},{9,21},{13,25},... | collective-permute-start | bytes 196616 | tf_op jit(solution)/shard_map/ppermute | solution.py:15
  38.2 6.0 %collective-permute-start.2 = (f32[16,1024]{1,0:T(8,128)S(1)}, f32[16,1024]{1,0:T(8,128)S(1)}, u32[]{:S(2)}, u32[]{:S(2)}) collective-permute-start(f32[16,1024]{1,0:T(8,128)S(1)} %multiply_reduce_fusion.1), channel_id=1, source_target_pairs={{0,8},{4,12},{8,16},{12,20},{16,24},{20,28},{1,9},{5,13},{9,17},{1... | collective-permute-start | bytes 196616 | tf_op jit(solution)/shard_map/ppermute | solution.py:15
  39.8 4.4 %collective-permute-start.1 = (f32[16,1024]{1,0:T(8,128)S(1)}, f32[16,1024]{1,0:T(8,128)S(1)}, u32[]{:S(2)}, u32[]{:S(2)}) collective-permute-start(f32[16,1024]{1,0:T(8,128)S(1)} %multiply_reduce_fusion.1), channel_id=1, source_target_pairs={{0,4},{4,8},{8,12},{12,16},{16,20},{20,24},{24,28},{1,5},{5,9},{9,... | collective-permute-start | bytes 196616 | tf_op jit(solution)/shard_map/ppermute | solution.py:15
  44.1 5.8 %slice-start.2 = ((f32[1024]{0:T(1024)}), f32[256]{0:T(256)S(1)}, s32[]{:S(2)}) async-start(f32[1024]{0:T(1024)} %param.10), calls=%async_computation.2 | async-start | bytes 2048 | tf_op jit(solution)/shard_map/slice | solution.py:191
  52.4 11.3 %collective-permute-start.8 = (bf16[1024,256]{1,0:T(8,128)(2,1)S(1)}, bf16[1024,256]{1,0:T(8,128)(2,1)S(1)}, u32[]{:S(2)}, u32[]{:S(2)}) collective-permute-start(bf16[1024,256]{1,0:T(8,128)(2,1)S(1)} %fusion.28), channel_id=1, source_target_pairs={{0,2},{1,3},{2,0},{3,1},{4,6},{5,7},{6,4},{7,5},{8,10},{9,11},{10,... | collective-permute-start | bytes 1572872 | tf_op jit(solution)/shard_map/ppermute | solution.py:198
  63.4 16.9 %collective-permute-start.10 = (bf16[1024,384]{1,0:T(8,128)(2,1)}, bf16[1024,384]{1,0:T(8,128)(2,1)}, u32[]{:S(2)}, u32[]{:S(2)}) collective-permute-start(bf16[1024,384]{1,0:T(8,128)(2,1)} %fusion.20), channel_id=1, source_target_pairs={{0,2},{1,3},{2,0},{3,1},{4,6},{5,7},{6,4},{7,5},{8,10},{9,11},{10,... | collective-permute-start | bytes 2359304 | tf_op jit(solution)/shard_map/ppermute | solution.py:198
  63.6 6.0 %copy-start.1 = (bf16[1024,256]{1,0:T(8,128)(2,1)}, bf16[1024,256]{1,0:T(8,128)(2,1)S(1)}, u32[]{:S(2)}) copy-start(bf16[1024,256]{1,0:T(8,128)(2,1)S(1)} %collective-permute-done.8) | copy-start | bytes 1572868
  74.1 14.1 %copy-start.2 = (bf16[1024,256]{1,0:T(8,128)(2,1)S(1)}, bf16[1024,256]{1,0:T(8,128)(2,1)}, u32[]{:S(2)}) copy-start(bf16[1024,256]{1,0:T(8,128)(2,1)} %copy-done.1) | copy-start | bytes 1572868
  80.2 13.4 %collective-permute-start.11 = (bf16[1024,1024]{1,0:T(8,128)(2,1)S(1)}, bf16[1024,1024]{1,0:T(8,128)(2,1)}, u32[]{:S(2)}, u32[]{:S(2)}) collective-permute-start(bf16[1024,1024]{1,0:T(8,128)(2,1)S(1)} %pad_maximum_fusion), channel_id=1, source_target_pairs={{0,1},{1,0},{2,3},{3,2},{4,5},{5,4},{6,7},{7,6},{8,9},{9,8},{10,11... | collective-permute-start | bytes 6291464 | tf_op jit(solution)/shard_map/ppermute | solution.py:225
  83.7 19.3 %collective-permute-start.9 = (bf16[1024,384]{1,0:T(8,128)(2,1)S(1)}, bf16[1024,384]{1,0:T(8,128)(2,1)}, u32[]{:S(2)}, u32[]{:S(2)}) collective-permute-start(bf16[1024,384]{1,0:T(8,128)(2,1)S(1)} %fusion.24), channel_id=1, source_target_pairs={{0,2},{1,3},{2,0},{3,1},{4,6},{5,7},{6,4},{7,5},{8,10},{9,11},{10,... | collective-permute-start | bytes 2359304 | tf_op jit(solution)/shard_map/ppermute | solution.py:198
  84.9 8.0 %collective-permute-start.12 = (bf16[1024,256]{1,0:T(8,128)(2,1)}, bf16[1024,256]{1,0:T(8,128)(2,1)S(1)}, u32[]{:S(2)}, u32[]{:S(2)}) collective-permute-start(bf16[1024,256]{1,0:T(8,128)(2,1)} %copy-done.1), channel_id=1, source_target_pairs={{0,1},{1,0},{2,3},{3,2},{4,5},{5,4},{6,7},{7,6},{8,9},{9,8},{10,11... | collective-permute-start | bytes 1572872 | tf_op jit(solution)/shard_map/ppermute | solution.py:226
  85.2 12.4 %collective-permute-start.13 = (bf16[1024,384]{1,0:T(8,128)(2,1)}, bf16[1024,384]{1,0:T(8,128)(2,1)S(1)}, u32[]{:S(2)}, u32[]{:S(2)}) collective-permute-start(bf16[1024,384]{1,0:T(8,128)(2,1)} %collective-permute-done.10), channel_id=1, source_target_pairs={{0,1},{1,0},{2,3},{3,2},{4,5},{5,4},{6,7},{7,6},{8,9},{9,8},{10,11... | collective-permute-start | bytes 2359304 | tf_op jit(solution)/shard_map/ppermute | solution.py:226
  85.4 4.7 %slice-start = ((s8[8388608]{0:T(1024)(128)(4,1)}), s8[4194304]{0:T(1024)(128)(4,1)S(1)}, s32[]{:S(2)}) async-start(s8[8388608]{0:T(1024)(128)(4,1)} %bitcast.108), calls=%async_computation | async-start | bytes 8388608
  88.2 2.4 %slice-start.1 = ((s8[8388608]{0:T(1024)(128)(4,1)}), s8[4194304]{0:T(1024)(128)(4,1)S(1)}, s32[]{:S(2)}) async-start(s8[8388608]{0:T(1024)(128)(4,1)} %bitcast.108), calls=%async_computation.1 | async-start | bytes 8388608
  103.0 3.6 %collective-permute-start.14 = (bf16[1024,384]{1,0:T(8,128)(2,1)}, bf16[1024,384]{1,0:T(8,128)(2,1)S(1)}, u32[]{:S(2)}, u32[]{:S(2)}) collective-permute-start(bf16[1024,384]{1,0:T(8,128)(2,1)} %collective-permute-done.9), channel_id=1, source_target_pairs={{0,1},{1,0},{2,3},{3,2},{4,5},{5,4},{6,7},{7,6},{8,9},{9,8},{10,11... | collective-permute-start | bytes 2359304 | tf_op jit(solution)/shard_map/ppermute | solution.py:237
  103.8 2.8 %copy-start = (f32[1024,1024]{1,0:T(8,128)S(1)}, f32[1024,1024]{1,0:T(8,128)}, u32[]{:S(2)}) copy-start(f32[1024,1024]{1,0:T(8,128)} %add_add_fusion) | copy-start | bytes 12582916

commit v21 on v20

--- a/solution.py
+++ b/solution.py
@@ -49,7 +49,7 @@
 
 
 def end_state_kernel(x_ref, decay_ref, end_ref):
-    segment_pass(x_ref, decay_ref, None, None, None, end_ref, 32)
+    segment_pass(x_ref, decay_ref, None, None, None, end_ref, 64)
 
 
 def recurrence_kernel(x_ref, decay_ref, residue_ref, start_ref, y_ref):

time: 111 us -> 111 us (level)
  no operation moved by 1% of the time
where the time goes in v21:
time: 111 us; the launch traced here: 110 us
  starting transfers between devices  26.6 us (24%)
  other arithmetic  25.7 us (23%)
  Pallas kernels  24.6 us (22%)
  matrix products  22.9 us (21%)
  waiting for transfers between devices  6.73 us (6%)
  local copies, waits for them, and re-layouts  3.38 us (3%)
    ppermute x8, starting transfers between devices, shifted(): lax.ppermute(value, axis, [(source, source + steps) for source in range(i...  19 us
    dot_general x6, matrix products, part(): return jnp.dot(value, rows, preferred_element_type=jnp.float32)  16.7 us
    pallas_call x3, Pallas kernels, run_recurrence(): pl.pallas_call(recurrence_kernel, grid=(group_count,), in_specs=[pl.Block...  16.2 us
    convert_element_type x3, other arithmetic, shards(): gated_mix = gated_mix.astype(jnp.bfloat16)  9.51 us
    pallas_call x1, Pallas kernels, run_end_state(): pl.pallas_call(end_state_kernel, grid=(width // LANES,), in_specs=[pl.Blo...  8.46 us
    ppermute x3, waiting for transfers between devices, shards(): lax.ppermute(gated_mix, 'ch', [(i, i ^ 2) for i in range(ch_count)])  6.66 us
    convert_element_type x1, other arithmetic, shards(): x = mixed_input.astype(jnp.float32)  4.2 us
    dot_general x1, matrix products, project_pieces(): total = total + jnp.dot(near, rows_near, preferred_element_type=jnp.float32)  3.94 us
  transfers between devices with their start and end apart: 15, of which 2 were waited for; matrix products, arithmetic and copies ran while one was open for 32% of the time, Pallas kernels for 11%

profile of v21, /device:TPU:1, one launch (start us, length us, event | category | flops | bytes accessed | tf_op | source)
XLA Modules:
  0.0 110.2 jit_solution(592009812628955997)
XLA Ops:
  0.8 4.0 %collective-permute-start = (bf16[3,2,1024]{2,1,0:T(2,128)(2,1)S(1)}, bf16[3,2,1024]{2,1,0:T(2,128)(2,1)S(1)}, u32[]{:S(2)}, u32[]{:S(2)}) collective-permute-start(bf16[3,2,1024]{2,1,0:T(2,128)(2,1)S(1)} %slice.152), channel_id=1, source_target_pairs={{0,4},{4,8},{8,12},{12,16},{16,20},{20,24},{24,28},{1,5},{5,9},{9,... | collective-permute-start | bytes 36872 | tf_op jit(solution)/shard_map/ppermute | solution.py:15
  8.0 1.5 %fusion.60 = (f32[16,1024]{1,0:T(8,128)S(1)}, f32[16,1024]{1,0:T(8,128)}) fusion(f32[16,1024]{1,0:T(8,128)} %param.8), kind=kLoop, calls=%fused_computation.108 | loop fusion | flops 16384 | bytes 196608 | tf_op jit(solution)/shard_map/neg | solution.py:170
  9.5 2.9 %fusion.1 = f32[2,1026,1024]{2,1,0:T(8,128)S(1)} fusion(bf16[3,2,1024]{2,1,0:T(2,128)(2,1)S(1)} %collective-permute-done, bf16[3,1024,1024]{2,1,0:T(8,128)(2,1)} %param.6), kind=kLoop, calls=%fused_computation.5 | loop fusion | flops 8404992 | bytes 14708736 | tf_op jit(solution)/shard_map/convert_element_type | solution.py:163
  12.4 4.2 %fusion.58 = (f32[1024,1024]{1,0:T(8,128)}, bf16[1024,1024]{1,0:T(8,128)(2,1)S(1)}) fusion(f32[2,1026,1024]{2,1,0:T(8,128)S(1)} %fusion.1, f32[1024]{0:T(1024)S(1)} %bitcast.115, f32[1024]{0:T(1024)S(1)} %bitcast.111, f32[1024]{0:T(1024)S(1)} %bitcast.112, f32[1024]{0:T(1024)S(1)} %bitcast.113, f32[1024]{0:T(1024)S(1)} %bitcast.114, f32[1024]{0:T(1024)S(1)} %bitcast.110), kind=kLoop, calls=%fused_computation.107 | loop fusion | flops 13631488 | bytes 31481856 | tf_op jit(solution)/shard_map/convert_element_type | solution.py:167
  16.6 8.5 %shard_map.64 = f32[16,8,1024]{2,1,0:T(8,128)} custom-call(f32[1024,1024]{1,0:T(8,128)} %get-tuple-element.19.x_ref, f32[16,1024]{1,0:T(8,128)} %get-tuple-element.36.decay_ref), custom_call_target="tpu_custom_call" | custom-call | tf_op jit(solution)/shard_map/pallas_call | solution.py:62
  25.0 1.3 %multiply_reduce_fusion.1 = f32[16,1024]{1,0:T(8,128)S(1)} fusion(f32[16,8,1024]{2,1,0:T(8,128)} %shard_map.64, f32[8]{0:T(128)S(1)} %subtract_multiply_fusion, f32[16,1024]{1,0:T(8,128)S(1)} %get-tuple-element.35), kind=kLoop, calls=%fused_computation.76 | loop fusion | flops 376832 | bytes 655392 | tf_op jit(solution)/shard_map/reduce_sum | solution.py:110
  26.3 4.3 %collective-permute-start.7 = (f32[16,1024]{1,0:T(8,128)S(1)}, f32[16,1024]{1,0:T(8,128)S(1)}, u32[]{:S(2)}, u32[]{:S(2)}) collective-permute-start(f32[16,1024]{1,0:T(8,128)S(1)} %multiply_reduce_fusion.1), channel_id=1, source_target_pairs={{0,28},{1,29},{2,30},{3,31}} | collective-permute-start | bytes 196616 | tf_op jit(solution)/shard_map/ppermute | solution.py:15
  30.7 1.6 %collective-permute-start.6 = (f32[16,1024]{1,0:T(8,128)S(1)}, f32[16,1024]{1,0:T(8,128)S(1)}, u32[]{:S(2)}, u32[]{:S(2)}) collective-permute-start(f32[16,1024]{1,0:T(8,128)S(1)} %multiply_reduce_fusion.1), channel_id=1, source_target_pairs={{0,24},{4,28},{1,25},{5,29},{2,26},{6,30},{3,27},{7,31}} | collective-permute-start | bytes 196616 | tf_op jit(solution)/shard_map/ppermute | solution.py:15
  32.3 1.3 %collective-permute-start.5 = (f32[16,1024]{1,0:T(8,128)S(1)}, f32[16,1024]{1,0:T(8,128)S(1)}, u32[]{:S(2)}, u32[]{:S(2)}) collective-permute-start(f32[16,1024]{1,0:T(8,128)S(1)} %multiply_reduce_fusion.1), channel_id=1, source_target_pairs={{0,20},{4,24},{8,28},{1,21},{5,25},{9,29},{2,22},{6,26},{10,30},{3... | collective-permute-start | bytes 196616 | tf_op jit(solution)/shard_map/ppermute | solution.py:15
  33.6 1.3 %collective-permute-start.4 = (f32[16,1024]{1,0:T(8,128)S(1)}, f32[16,1024]{1,0:T(8,128)S(1)}, u32[]{:S(2)}, u32[]{:S(2)}) collective-permute-start(f32[16,1024]{1,0:T(8,128)S(1)} %multiply_reduce_fusion.1), channel_id=1, source_target_pairs={{0,16},{4,20},{8,24},{12,28},{1,17},{5,21},{9,25},{13,29},{2,18},{... | collective-permute-start | bytes 196616 | tf_op jit(solution)/shard_map/ppermute | solution.py:15
  34.9 1.9 %collective-permute-start.3 = (f32[16,1024]{1,0:T(8,128)S(1)}, f32[16,1024]{1,0:T(8,128)S(1)}, u32[]{:S(2)}, u32[]{:S(2)}) collective-permute-start(f32[16,1024]{1,0:T(8,128)S(1)} %multiply_reduce_fusion.1), channel_id=1, source_target_pairs={{0,12},{4,16},{8,20},{12,24},{16,28},{1,13},{5,17},{9,21},{13,25},... | collective-permute-start | bytes 196616 | tf_op jit(solution)/shard_map/ppermute | solution.py:15
  36.8 1.4 %copy.15 = f32[16,1024,8]{1,0,2:T(8,128)S(1)} copy(f32[16,1024,8]{1,2,0:T(8,128)} %bitcast.107) | data formatting | bytes 1048576
  38.1 1.6 %collective-permute-start.2 = (f32[16,1024]{1,0:T(8,128)S(1)}, f32[16,1024]{1,0:T(8,128)S(1)}, u32[]{:S(2)}, u32[]{:S(2)}) collective-permute-start(f32[16,1024]{1,0:T(8,128)S(1)} %multiply_reduce_fusion.1), channel_id=1, source_target_pairs={{0,8},{4,12},{8,16},{12,20},{16,24},{20,28},{1,9},{5,13},{9,17},{1... | collective-permute-start | bytes 196616 | tf_op jit(solution)/shard_map/ppermute | solution.py:15
  39.7 3.1 %collective-permute-start.1 = (f32[16,1024]{1,0:T(8,128)S(1)}, f32[16,1024]{1,0:T(8,128)S(1)}, u32[]{:S(2)}, u32[]{:S(2)}) collective-permute-start(f32[16,1024]{1,0:T(8,128)S(1)} %multiply_reduce_fusion.1), channel_id=1, source_target_pairs={{0,4},{4,8},{8,12},{12,16},{16,20},{20,24},{24,28},{1,5},{5,9},{9,... | collective-permute-start | bytes 196616 | tf_op jit(solution)/shard_map/ppermute | solution.py:15
  42.8 1.2 %multiply_reduce_fusion = f32[16,1024,8]{1,0,2:T(8,128)S(1)} fusion(f32[16,1024,8]{1,0,2:T(8,128)S(1)} %copy.15, f32[8,8]{1,0:T(8,128)S(1)} %maximum_multiply_fusion, f32[16,1024]{1,0:T(8,128)S(1)} %get-tuple-element.35, pred[8,8]{1,0:T(8,128)(4,1)S(1)} %iota_compare_fusion), kind=kLoop, calls=%fused_computation.24 | loop fusion | flops 4063232 | bytes 1114432
  45.4 4.4 %shard_map.65 = f32[1024,256]{1,0:T(8,128)} custom-call(f32[1024,1024]{1,0:T(8,128)} %get-tuple-element.19.x_ref, f32[16,1024]{1,0:T(8,128)} %get-tuple-element.36.decay_ref, f32[16,1024]{1,0:T(8,128)} %residue_ref.5, f32[16,8,1024]{2,1,0:T(8,128)} %bitcast_add_fusion.start_ref), custom_call_target="tpu_custom_call" | custom-call | tf_op jit(solution)/shard_map/pallas_call | solution.py:78
  49.9 2.4 %fusion.28 = bf16[1024,256]{1,0:T(8,128)(2,1)S(1)} fusion(bf16[1024,1024]{1,0:T(8,128)(2,1)S(1)} %get-tuple-element.34, bf16[3,1024,1024]{2,1,0:T(8,128)(2,1)} %param.6, bf16[3,2,1024]{2,1,0:T(2,128)(2,1)S(1)} %collective-permute-done, f32[256]{0:T(256)S(1)} %slice-done.2, f32[1024,256]{1,0:T(8,128)} %shard_map.65, f32[256]{0:T(256)S(1)} %bitcast.117, ...), kind=kLoop, calls=%fused_computation.52 | loop fusion | flops 6029312 | bytes 8929280 | tf_op jit(solution)/shard_map/convert_element_type | solution.py:193
  52.3 1.3 %collective-permute-start.8 = (bf16[1024,256]{1,0:T(8,128)(2,1)S(1)}, bf16[1024,256]{1,0:T(8,128)(2,1)S(1)}, u32[]{:S(2)}, u32[]{:S(2)}) collective-permute-start(bf16[1024,256]{1,0:T(8,128)(2,1)S(1)} %fusion.28), channel_id=1, source_target_pairs={{0,2},{1,3},{2,0},{3,1},{4,6},{5,7},{6,4},{7,5},{8,10},{9,11},{10,... | collective-permute-start | bytes 1572872 | tf_op jit(solution)/shard_map/ppermute | solution.py:198
  53.6 5.8 %shard_map.66 = f32[1024,384]{1,0:T(8,128)} custom-call(f32[1024,1024]{1,0:T(8,128)} %get-tuple-element.19.x_ref, f32[16,1024]{1,0:T(8,128)} %get-tuple-element.36.decay_ref, f32[16,1024]{1,0:T(8,128)} %residue_ref.5, f32[16,8,1024]{2,1,0:T(8,128)} %bitcast_add_fusion.start_ref), custom_call_target="tpu_custom_call" | custom-call | tf_op jit(solution)/shard_map/pallas_call | solution.py:78
  59.3 4.0 %fusion.20 = bf16[1024,384]{1,0:T(8,128)(2,1)} fusion(bf16[1024,1024]{1,0:T(8,128)(2,1)S(1)} %get-tuple-element.34, f32[384]{0:T(512)S(1)} %get-tuple-element.46, f32[1024,384]{1,0:T(8,128)} %shard_map.66, f32[384]{0:T(512)S(1)} %get-tuple-element.28, f32[384]{0:T(512)S(1)} %get-tuple-element.29, bf16[3,1024,1024]{2,1,0:T(8,128)(2,1)} %param.6, ...), kind=kLoop, calls=%fused_computation.38 | loop fusion | flops 9043968 | bytes 10242048 | tf_op jit(solution)/shard_map/convert_element_type | solution.py:193
  63.6 6.0 %shard_map.67 = f32[1024,384]{1,0:T(8,128)} custom-call(f32[1024,1024]{1,0:T(8,128)} %get-tuple-element.19.x_ref, f32[16,1024]{1,0:T(8,128)} %get-tuple-element.36.decay_ref, f32[16,1024]{1,0:T(8,128)} %residue_ref.5, f32[16,8,1024]{2,1,0:T(8,128)} %bitcast_add_fusion.start_ref), custom_call_target="tpu_custom_call" | custom-call | tf_op jit(solution)/shard_map/pallas_call | solution.py:78
  69.5 3.1 %fusion.24 = bf16[1024,384]{1,0:T(8,128)(2,1)S(1)} fusion(bf16[1024,1024]{1,0:T(8,128)(2,1)S(1)} %get-tuple-element.34, bf16[3,1024,1024]{2,1,0:T(8,128)(2,1)} %param.6, bf16[3,2,1024]{2,1,0:T(2,128)(2,1)S(1)} %collective-permute-done, f32[384]{0:T(512)S(1)} %get-tuple-element.47, f32[1024,384]{1,0:T(8,128)} %shard_map.67, f32[384]{0:T(512)S(1)} %get-tuple-element.31, ...), kind=kLoop, calls=%fused_computation.45 | loop fusion | flops 9043968 | bytes 10242048 | tf_op jit(solution)/shard_map/convert_element_type | solution.py:193
  72.6 1.4 %pad_maximum_fusion = bf16[1024,1024]{1,0:T(8,128)(2,1)S(1)} fusion(bf16[1024,384]{1,0:T(8,128)(2,1)S(1)} %fusion.24, bf16[1024,384]{1,0:T(8,128)(2,1)} %fusion.20, bf16[1024,256]{1,0:T(8,128)(2,1)S(1)} %fusion.28), kind=kLoop, calls=%fused_computation.30 | loop fusion | flops 6291456 | bytes 4194304 | tf_op jit(solution)/shard_map/concatenate | solution.py:221
  74.1 6.1 %collective-permute-done.10 = bf16[1024,384]{1,0:T(8,128)(2,1)} collective-permute-done((bf16[1024,384]{1,0:T(8,128)(2,1)}, bf16[1024,384]{1,0:T(8,128)(2,1)}, u32[]{:S(2)}, u32[]{:S(2)}) %collective-permute-start.10) | collective-permute-done | bytes 786464 | tf_op jit(solution)/shard_map/ppermute | solution.py:198
  80.2 3.5 %collective-permute-start.11 = (bf16[1024,1024]{1,0:T(8,128)(2,1)S(1)}, bf16[1024,1024]{1,0:T(8,128)(2,1)}, u32[]{:S(2)}, u32[]{:S(2)}) collective-permute-start(bf16[1024,1024]{1,0:T(8,128)(2,1)S(1)} %pad_maximum_fusion), channel_id=1, source_target_pairs={{0,1},{1,0},{2,3},{3,2},{4,5},{5,4},{6,7},{7,6},{8,9},{9,8},{10,11... | collective-permute-start | bytes 6291464 | tf_op jit(solution)/shard_map/ppermute | solution.py:225
  85.4 2.8 %fusion.42 = f32[1024,1024]{1,0:T(8,128)S(1)} fusion(bf16[1024,384]{1,0:T(8,128)(2,1)} %collective-permute-done.10, bf16[4096,1024]{1,0:T(8,128)(2,1)} %param.11, s32[]{:T(128)S(6)} %select_n.31), kind=kOutput, calls=%fused_computation.66 | convolution fusion | flops 805306368 | bytes 5767172 | tf_op jit(solution)/shard_map/dot_general | solution.py:218
  88.2 1.9 %fusion.48 = f32[1024,1024]{1,0:T(8,128)S(1)} fusion(bf16[1024,256]{1,0:T(8,128)(2,1)S(1)} %copy-done.2, bf16[4096,1024]{1,0:T(8,128)(2,1)} %param.11, s32[]{:T(128)S(6)} %select_n.30), kind=kOutput, calls=%fused_computation.74 | convolution fusion | flops 536870912 | bytes 5242884 | tf_op jit(solution)/shard_map/dot_general | solution.py:218
  90.5 2.3 %fusion.16 = f32[1024,1024]{1,0:T(8,128)S(1)} fusion(bf16[1024,1024]{1,0:T(8,128)(2,1)S(1)} %pad_maximum_fusion, bf16[4096,1024]{1,0:T(8,128)(2,1)S(1)} %bitcast.109, s32[]{:T(128)S(6)} %select_n.29), kind=kOutput, calls=%fused_computation.33 | convolution fusion | flops 2147483648 | bytes 8388612 | tf_op jit(solution)/shard_map/dot_general | solution.py:229
  93.6 3.9 %fusion.14 = f32[1024,1024]{1,0:T(8,128)S(1)} fusion(bf16[1024,1024]{1,0:T(8,128)(2,1)} %collective-permute-done.11, bf16[4096,1024]{1,0:T(8,128)(2,1)S(1)} %bitcast.109, s32[]{:T(128)S(6)} %select_n.32), kind=kOutput, calls=%fused_computation.31 | convolution fusion | flops 2147483648 | bytes 8388612 | tf_op jit(solution)/shard_map/dot_general | solution.py:232
  97.6 4.8 %add_add_fusion = f32[1024,1024]{1,0:T(8,128)} fusion(f32[1024,1024]{1,0:T(8,128)S(1)} %fusion.46, f32[1024,1024]{1,0:T(8,128)S(1)} %fusion.14, f32[1024,1024]{1,0:T(8,128)S(1)} %fusion.42, f32[1024,1024]{1,0:T(8,128)S(1)} %fusion.16, f32[1024,1024]{1,0:T(8,128)S(1)} %fusion.48, bf16[1024,384]{1,0:T(8,128)(2,1)S(1)} %collective-permute-done.13, ...), kind=kOutput, calls=%fused_computation.26 | convolution fusion | flops 810549248 | bytes 26738692 | tf_op jit(solution)/shard_map/dot_general | solution.py:218
  103.7 2.8 %fusion.36 = f32[1024,1024]{1,0:T(8,128)S(1)} fusion(bf16[1024,384]{1,0:T(8,128)(2,1)} %collective-permute-done.9, bf16[4096,1024]{1,0:T(8,128)(2,1)} %param.11, s32[]{:T(128)S(6)} %select_n.35), kind=kOutput, calls=%fused_computation.62 | convolution fusion | flops 805306368 | bytes 5767172 | tf_op jit(solution)/shard_map/dot_general | solution.py:218
  106.5 3.7 %add_convert_fusion = bf16[1024,1024]{1,0:T(8,128)(2,1)} fusion(f32[1024,1024]{1,0:T(8,128)S(1)} %copy-done, f32[1024,1024]{1,0:T(8,128)S(1)} %fusion.36, bf16[1024,384]{1,0:T(8,128)(2,1)S(1)} %collective-permute-done.14, bf16[4096,1024]{1,0:T(8,128)(2,1)} %param.11, s32[]{:T(128)S(6)} %select_n.36), kind=kOutput, calls=%fused_computation.25 | convolution fusion | flops 808452096 | bytes 12058628 | tf_op jit(solution)/shard_map/dot_general | solution.py:218
  (47 shorter events, 9.9 us)
Async XLA Ops:
  0.8 8.7 %collective-permute-start = (bf16[3,2,1024]{2,1,0:T(2,128)(2,1)S(1)}, bf16[3,2,1024]{2,1,0:T(2,128)(2,1)S(1)}, u32[]{:S(2)}, u32[]{:S(2)}) collective-permute-start(bf16[3,2,1024]{2,1,0:T(2,128)(2,1)S(1)} %slice.152), channel_id=1, source_target_pairs={{0,4},{4,8},{8,12},{12,16},{16,20},{20,24},{24,28},{1,5},{5,9},{9,... | collective-permute-start | bytes 36872 | tf_op jit(solution)/shard_map/ppermute | solution.py:15
  16.6 27.6 %copy-start.3 = (f32[16,1024]{1,0:T(8,128)S(1)}, f32[16,1024]{1,0:T(8,128)}, u32[]{:S(2)}) copy-start(f32[16,1024]{1,0:T(8,128)} %param.8) | copy-start | bytes 196612
  26.3 11.8 %collective-permute-start.7 = (f32[16,1024]{1,0:T(8,128)S(1)}, f32[16,1024]{1,0:T(8,128)S(1)}, u32[]{:S(2)}, u32[]{:S(2)}) collective-permute-start(f32[16,1024]{1,0:T(8,128)S(1)} %multiply_reduce_fusion.1), channel_id=1, source_target_pairs={{0,28},{1,29},{2,30},{3,31}} | collective-permute-start | bytes 196616 | tf_op jit(solution)/shard_map/ppermute | solution.py:15
  30.7 9.1 %collective-permute-start.6 = (f32[16,1024]{1,0:T(8,128)S(1)}, f32[16,1024]{1,0:T(8,128)S(1)}, u32[]{:S(2)}, u32[]{:S(2)}) collective-permute-start(f32[16,1024]{1,0:T(8,128)S(1)} %multiply_reduce_fusion.1), channel_id=1, source_target_pairs={{0,24},{4,28},{1,25},{5,29},{2,26},{6,30},{3,27},{7,31}} | collective-permute-start | bytes 196616 | tf_op jit(solution)/shard_map/ppermute | solution.py:15
  32.3 11.8 %collective-permute-start.5 = (f32[16,1024]{1,0:T(8,128)S(1)}, f32[16,1024]{1,0:T(8,128)S(1)}, u32[]{:S(2)}, u32[]{:S(2)}) collective-permute-start(f32[16,1024]{1,0:T(8,128)S(1)} %multiply_reduce_fusion.1), channel_id=1, source_target_pairs={{0,20},{4,24},{8,28},{1,21},{5,25},{9,29},{2,22},{6,26},{10,30},{3... | collective-permute-start | bytes 196616 | tf_op jit(solution)/shard_map/ppermute | solution.py:15
  33.6 10.5 %collective-permute-start.4 = (f32[16,1024]{1,0:T(8,128)S(1)}, f32[16,1024]{1,0:T(8,128)S(1)}, u32[]{:S(2)}, u32[]{:S(2)}) collective-permute-start(f32[16,1024]{1,0:T(8,128)S(1)} %multiply_reduce_fusion.1), channel_id=1, source_target_pairs={{0,16},{4,20},{8,24},{12,28},{1,17},{5,21},{9,25},{13,29},{2,18},{... | collective-permute-start | bytes 196616 | tf_op jit(solution)/shard_map/ppermute | solution.py:15
  34.9 9.2 %collective-permute-start.3 = (f32[16,1024]{1,0:T(8,128)S(1)}, f32[16,1024]{1,0:T(8,128)S(1)}, u32[]{:S(2)}, u32[]{:S(2)}) collective-permute-start(f32[16,1024]{1,0:T(8,128)S(1)} %multiply_reduce_fusion.1), channel_id=1, source_target_pairs={{0,12},{4,16},{8,20},{12,24},{16,28},{1,13},{5,17},{9,21},{13,25},... | collective-permute-start | bytes 196616 | tf_op jit(solution)/shard_map/ppermute | solution.py:15
  38.1 6.0 %collective-permute-start.2 = (f32[16,1024]{1,0:T(8,128)S(1)}, f32[16,1024]{1,0:T(8,128)S(1)}, u32[]{:S(2)}, u32[]{:S(2)}) collective-permute-start(f32[16,1024]{1,0:T(8,128)S(1)} %multiply_reduce_fusion.1), channel_id=1, source_target_pairs={{0,8},{4,12},{8,16},{12,20},{16,24},{20,28},{1,9},{5,13},{9,17},{1... | collective-permute-start | bytes 196616 | tf_op jit(solution)/shard_map/ppermute | solution.py:15
  39.7 4.4 %collective-permute-start.1 = (f32[16,1024]{1,0:T(8,128)S(1)}, f32[16,1024]{1,0:T(8,128)S(1)}, u32[]{:S(2)}, u32[]{:S(2)}) collective-permute-start(f32[16,1024]{1,0:T(8,128)S(1)} %multiply_reduce_fusion.1), channel_id=1, source_target_pairs={{0,4},{4,8},{8,12},{12,16},{16,20},{20,24},{24,28},{1,5},{5,9},{9,... | collective-permute-start | bytes 196616 | tf_op jit(solution)/shard_map/ppermute | solution.py:15
  44.0 5.8 %slice-start.2 = ((f32[1024]{0:T(1024)}), f32[256]{0:T(256)S(1)}, s32[]{:S(2)}) async-start(f32[1024]{0:T(1024)} %param.10), calls=%async_computation.2 | async-start | bytes 2048 | tf_op jit(solution)/shard_map/slice | solution.py:191
  52.3 11.3 %collective-permute-start.8 = (bf16[1024,256]{1,0:T(8,128)(2,1)S(1)}, bf16[1024,256]{1,0:T(8,128)(2,1)S(1)}, u32[]{:S(2)}, u32[]{:S(2)}) collective-permute-start(bf16[1024,256]{1,0:T(8,128)(2,1)S(1)} %fusion.28), channel_id=1, source_target_pairs={{0,2},{1,3},{2,0},{3,1},{4,6},{5,7},{6,4},{7,5},{8,10},{9,11},{10,... | collective-permute-start | bytes 1572872 | tf_op jit(solution)/shard_map/ppermute | solution.py:198
  63.3 16.9 %collective-permute-start.10 = (bf16[1024,384]{1,0:T(8,128)(2,1)}, bf16[1024,384]{1,0:T(8,128)(2,1)}, u32[]{:S(2)}, u32[]{:S(2)}) collective-permute-start(bf16[1024,384]{1,0:T(8,128)(2,1)} %fusion.20), channel_id=1, source_target_pairs={{0,2},{1,3},{2,0},{3,1},{4,6},{5,7},{6,4},{7,5},{8,10},{9,11},{10,... | collective-permute-start | bytes 2359304 | tf_op jit(solution)/shard_map/ppermute | solution.py:198
  63.6 6.0 %copy-start.1 = (bf16[1024,256]{1,0:T(8,128)(2,1)}, bf16[1024,256]{1,0:T(8,128)(2,1)S(1)}, u32[]{:S(2)}) copy-start(bf16[1024,256]{1,0:T(8,128)(2,1)S(1)} %collective-permute-done.8) | copy-start | bytes 1572868
  74.1 14.1 %copy-start.2 = (bf16[1024,256]{1,0:T(8,128)(2,1)S(1)}, bf16[1024,256]{1,0:T(8,128)(2,1)}, u32[]{:S(2)}) copy-start(bf16[1024,256]{1,0:T(8,128)(2,1)} %copy-done.1) | copy-start | bytes 1572868
  80.2 13.4 %collective-permute-start.11 = (bf16[1024,1024]{1,0:T(8,128)(2,1)S(1)}, bf16[1024,1024]{1,0:T(8,128)(2,1)}, u32[]{:S(2)}, u32[]{:S(2)}) collective-permute-start(bf16[1024,1024]{1,0:T(8,128)(2,1)S(1)} %pad_maximum_fusion), channel_id=1, source_target_pairs={{0,1},{1,0},{2,3},{3,2},{4,5},{5,4},{6,7},{7,6},{8,9},{9,8},{10,11... | collective-permute-start | bytes 6291464 | tf_op jit(solution)/shard_map/ppermute | solution.py:225
  83.7 19.3 %collective-permute-start.9 = (bf16[1024,384]{1,0:T(8,128)(2,1)S(1)}, bf16[1024,384]{1,0:T(8,128)(2,1)}, u32[]{:S(2)}, u32[]{:S(2)}) collective-permute-start(bf16[1024,384]{1,0:T(8,128)(2,1)S(1)} %fusion.24), channel_id=1, source_target_pairs={{0,2},{1,3},{2,0},{3,1},{4,6},{5,7},{6,4},{7,5},{8,10},{9,11},{10,... | collective-permute-start | bytes 2359304 | tf_op jit(solution)/shard_map/ppermute | solution.py:198
  84.9 8.0 %collective-permute-start.12 = (bf16[1024,256]{1,0:T(8,128)(2,1)}, bf16[1024,256]{1,0:T(8,128)(2,1)S(1)}, u32[]{:S(2)}, u32[]{:S(2)}) collective-permute-start(bf16[1024,256]{1,0:T(8,128)(2,1)} %copy-done.1), channel_id=1, source_target_pairs={{0,1},{1,0},{2,3},{3,2},{4,5},{5,4},{6,7},{7,6},{8,9},{9,8},{10,11... | collective-permute-start | bytes 1572872 | tf_op jit(solution)/shard_map/ppermute | solution.py:226
  85.2 12.4 %collective-permute-start.13 = (bf16[1024,384]{1,0:T(8,128)(2,1)}, bf16[1024,384]{1,0:T(8,128)(2,1)S(1)}, u32[]{:S(2)}, u32[]{:S(2)}) collective-permute-start(bf16[1024,384]{1,0:T(8,128)(2,1)} %collective-permute-done.10), channel_id=1, source_target_pairs={{0,1},{1,0},{2,3},{3,2},{4,5},{5,4},{6,7},{7,6},{8,9},{9,8},{10,11... | collective-permute-start | bytes 2359304 | tf_op jit(solution)/shard_map/ppermute | solution.py:226
  85.4 4.7 %slice-start = ((s8[8388608]{0:T(1024)(128)(4,1)}), s8[4194304]{0:T(1024)(128)(4,1)S(1)}, s32[]{:S(2)}) async-start(s8[8388608]{0:T(1024)(128)(4,1)} %bitcast.108), calls=%async_computation | async-start | bytes 8388608
  88.2 2.4 %slice-start.1 = ((s8[8388608]{0:T(1024)(128)(4,1)}), s8[4194304]{0:T(1024)(128)(4,1)S(1)}, s32[]{:S(2)}) async-start(s8[8388608]{0:T(1024)(128)(4,1)} %bitcast.108), calls=%async_computation.1 | async-start | bytes 8388608
  102.9 3.6 %collective-permute-start.14 = (bf16[1024,384]{1,0:T(8,128)(2,1)}, bf16[1024,384]{1,0:T(8,128)(2,1)S(1)}, u32[]{:S(2)}, u32[]{:S(2)}) collective-permute-start(bf16[1024,384]{1,0:T(8,128)(2,1)} %collective-permute-done.9), channel_id=1, source_target_pairs={{0,1},{1,0},{2,3},{3,2},{4,5},{5,4},{6,7},{7,6},{8,9},{9,8},{10,11... | collective-permute-start | bytes 2359304 | tf_op jit(solution)/shard_map/ppermute | solution.py:237
  103.7 2.8 %copy-start = (f32[1024,1024]{1,0:T(8,128)S(1)}, f32[1024,1024]{1,0:T(8,128)}, u32[]{:S(2)}) copy-start(f32[1024,1024]{1,0:T(8,128)} %add_add_fusion) | copy-start | bytes 12582916

commit v22 on v20

--- a/solution.py
+++ b/solution.py
@@ -53,7 +53,7 @@
 
 
 def recurrence_kernel(x_ref, decay_ref, residue_ref, start_ref, y_ref):
-    segment_pass(x_ref, decay_ref, residue_ref, start_ref, y_ref, None, 128)
+    segment_pass(x_ref, decay_ref, residue_ref, start_ref, y_ref, None, 64)
 
 
 def run_end_state(x, decay):

time: 111 us -> 111 us (level)
  no operation moved by 1% of the time
where the time goes in v22:
time: 111 us; the launch traced here: 110 us
  starting transfers between devices  26.6 us (24%)
  other arithmetic  25.7 us (23%)
  Pallas kernels  24.9 us (22%)
  matrix products  22.9 us (21%)
  waiting for transfers between devices  6.51 us (6%)
  local copies, waits for them, and re-layouts  3.38 us (3%)
    ppermute x8, starting transfers between devices, shifted(): lax.ppermute(value, axis, [(source, source + steps) for source in range(i...  19 us
    dot_general x6, matrix products, part(): return jnp.dot(value, rows, preferred_element_type=jnp.float32)  16.6 us
    pallas_call x3, Pallas kernels, run_recurrence(): pl.pallas_call(recurrence_kernel, grid=(group_count,), in_specs=[pl.Block...  16.4 us
    convert_element_type x3, other arithmetic, shards(): gated_mix = gated_mix.astype(jnp.bfloat16)  9.51 us
    pallas_call x1, Pallas kernels, run_end_state(): pl.pallas_call(end_state_kernel, grid=(width // LANES,), in_specs=[pl.Blo...  8.52 us
    ppermute x3, waiting for transfers between devices, shards(): lax.ppermute(gated_mix, 'ch', [(i, i ^ 2) for i in range(ch_count)])  6.44 us
    convert_element_type x1, other arithmetic, shards(): x = mixed_input.astype(jnp.float32)  4.2 us
    dot_general x1, matrix products, project_pieces(): total = total + jnp.dot(near, rows_near, preferred_element_type=jnp.float32)  3.94 us
  transfers between devices with their start and end apart: 15, of which 2 were waited for; matrix products, arithmetic and copies ran while one was open for 32% of the time, Pallas kernels for 11%

profile of v22, /device:TPU:1, one launch (start us, length us, event | category | flops | bytes accessed | tf_op | source)
XLA Modules:
  0.0 110.3 jit_solution(6275821898312334942)
XLA Ops:
  0.8 4.0 %collective-permute-start = (bf16[3,2,1024]{2,1,0:T(2,128)(2,1)S(1)}, bf16[3,2,1024]{2,1,0:T(2,128)(2,1)S(1)}, u32[]{:S(2)}, u32[]{:S(2)}) collective-permute-start(bf16[3,2,1024]{2,1,0:T(2,128)(2,1)S(1)} %slice.152), channel_id=1, source_target_pairs={{0,4},{4,8},{8,12},{12,16},{16,20},{20,24},{24,28},{1,5},{5,9},{9,... | collective-permute-start | bytes 36872 | tf_op jit(solution)/shard_map/ppermute | solution.py:15
  8.0 1.5 %fusion.60 = (f32[16,1024]{1,0:T(8,128)S(1)}, f32[16,1024]{1,0:T(8,128)}) fusion(f32[16,1024]{1,0:T(8,128)} %param.8), kind=kLoop, calls=%fused_computation.108 | loop fusion | flops 16384 | bytes 196608 | tf_op jit(solution)/shard_map/neg | solution.py:170
  9.5 2.9 %fusion.1 = f32[2,1026,1024]{2,1,0:T(8,128)S(1)} fusion(bf16[3,2,1024]{2,1,0:T(2,128)(2,1)S(1)} %collective-permute-done, bf16[3,1024,1024]{2,1,0:T(8,128)(2,1)} %param.6), kind=kLoop, calls=%fused_computation.5 | loop fusion | flops 8404992 | bytes 14708736 | tf_op jit(solution)/shard_map/convert_element_type | solution.py:163
  12.4 4.2 %fusion.58 = (f32[1024,1024]{1,0:T(8,128)}, bf16[1024,1024]{1,0:T(8,128)(2,1)S(1)}) fusion(f32[2,1026,1024]{2,1,0:T(8,128)S(1)} %fusion.1, f32[1024]{0:T(1024)S(1)} %bitcast.115, f32[1024]{0:T(1024)S(1)} %bitcast.111, f32[1024]{0:T(1024)S(1)} %bitcast.112, f32[1024]{0:T(1024)S(1)} %bitcast.113, f32[1024]{0:T(1024)S(1)} %bitcast.114, f32[1024]{0:T(1024)S(1)} %bitcast.110), kind=kLoop, calls=%fused_computation.107 | loop fusion | flops 13631488 | bytes 31481856 | tf_op jit(solution)/shard_map/convert_element_type | solution.py:167
  16.6 8.5 %shard_map.64 = f32[16,8,1024]{2,1,0:T(8,128)} custom-call(f32[1024,1024]{1,0:T(8,128)} %get-tuple-element.19.x_ref, f32[16,1024]{1,0:T(8,128)} %get-tuple-element.36.decay_ref), custom_call_target="tpu_custom_call" | custom-call | tf_op jit(solution)/shard_map/pallas_call | solution.py:62
  25.1 1.3 %multiply_reduce_fusion.1 = f32[16,1024]{1,0:T(8,128)S(1)} fusion(f32[16,8,1024]{2,1,0:T(8,128)} %shard_map.64, f32[8]{0:T(128)S(1)} %subtract_multiply_fusion, f32[16,1024]{1,0:T(8,128)S(1)} %get-tuple-element.35), kind=kLoop, calls=%fused_computation.76 | loop fusion | flops 376832 | bytes 655392 | tf_op jit(solution)/shard_map/reduce_sum | solution.py:110
  26.4 4.3 %collective-permute-start.7 = (f32[16,1024]{1,0:T(8,128)S(1)}, f32[16,1024]{1,0:T(8,128)S(1)}, u32[]{:S(2)}, u32[]{:S(2)}) collective-permute-start(f32[16,1024]{1,0:T(8,128)S(1)} %multiply_reduce_fusion.1), channel_id=1, source_target_pairs={{0,28},{1,29},{2,30},{3,31}} | collective-permute-start | bytes 196616 | tf_op jit(solution)/shard_map/ppermute | solution.py:15
  30.7 1.6 %collective-permute-start.6 = (f32[16,1024]{1,0:T(8,128)S(1)}, f32[16,1024]{1,0:T(8,128)S(1)}, u32[]{:S(2)}, u32[]{:S(2)}) collective-permute-start(f32[16,1024]{1,0:T(8,128)S(1)} %multiply_reduce_fusion.1), channel_id=1, source_target_pairs={{0,24},{4,28},{1,25},{5,29},{2,26},{6,30},{3,27},{7,31}} | collective-permute-start | bytes 196616 | tf_op jit(solution)/shard_map/ppermute | solution.py:15
  32.3 1.3 %collective-permute-start.5 = (f32[16,1024]{1,0:T(8,128)S(1)}, f32[16,1024]{1,0:T(8,128)S(1)}, u32[]{:S(2)}, u32[]{:S(2)}) collective-permute-start(f32[16,1024]{1,0:T(8,128)S(1)} %multiply_reduce_fusion.1), channel_id=1, source_target_pairs={{0,20},{4,24},{8,28},{1,21},{5,25},{9,29},{2,22},{6,26},{10,30},{3... | collective-permute-start | bytes 196616 | tf_op jit(solution)/shard_map/ppermute | solution.py:15
  33.6 1.3 %collective-permute-start.4 = (f32[16,1024]{1,0:T(8,128)S(1)}, f32[16,1024]{1,0:T(8,128)S(1)}, u32[]{:S(2)}, u32[]{:S(2)}) collective-permute-start(f32[16,1024]{1,0:T(8,128)S(1)} %multiply_reduce_fusion.1), channel_id=1, source_target_pairs={{0,16},{4,20},{8,24},{12,28},{1,17},{5,21},{9,25},{13,29},{2,18},{... | collective-permute-start | bytes 196616 | tf_op jit(solution)/shard_map/ppermute | solution.py:15
  34.9 1.9 %collective-permute-start.3 = (f32[16,1024]{1,0:T(8,128)S(1)}, f32[16,1024]{1,0:T(8,128)S(1)}, u32[]{:S(2)}, u32[]{:S(2)}) collective-permute-start(f32[16,1024]{1,0:T(8,128)S(1)} %multiply_reduce_fusion.1), channel_id=1, source_target_pairs={{0,12},{4,16},{8,20},{12,24},{16,28},{1,13},{5,17},{9,21},{13,25},... | collective-permute-start | bytes 196616 | tf_op jit(solution)/shard_map/ppermute | solution.py:15
  36.8 1.4 %copy.15 = f32[16,1024,8]{1,0,2:T(8,128)S(1)} copy(f32[16,1024,8]{1,2,0:T(8,128)} %bitcast.107) | data formatting | bytes 1048576
  38.2 1.6 %collective-permute-start.2 = (f32[16,1024]{1,0:T(8,128)S(1)}, f32[16,1024]{1,0:T(8,128)S(1)}, u32[]{:S(2)}, u32[]{:S(2)}) collective-permute-start(f32[16,1024]{1,0:T(8,128)S(1)} %multiply_reduce_fusion.1), channel_id=1, source_target_pairs={{0,8},{4,12},{8,16},{12,20},{16,24},{20,28},{1,9},{5,13},{9,17},{1... | collective-permute-start | bytes 196616 | tf_op jit(solution)/shard_map/ppermute | solution.py:15
  39.8 3.1 %collective-permute-start.1 = (f32[16,1024]{1,0:T(8,128)S(1)}, f32[16,1024]{1,0:T(8,128)S(1)}, u32[]{:S(2)}, u32[]{:S(2)}) collective-permute-start(f32[16,1024]{1,0:T(8,128)S(1)} %multiply_reduce_fusion.1), channel_id=1, source_target_pairs={{0,4},{4,8},{8,12},{12,16},{16,20},{20,24},{24,28},{1,5},{5,9},{9,... | collective-permute-start | bytes 196616 | tf_op jit(solution)/shard_map/ppermute | solution.py:15
  42.9 1.2 %multiply_reduce_fusion = f32[16,1024,8]{1,0,2:T(8,128)S(1)} fusion(f32[16,1024,8]{1,0,2:T(8,128)S(1)} %copy.15, f32[8,8]{1,0:T(8,128)S(1)} %maximum_multiply_fusion, f32[16,1024]{1,0:T(8,128)S(1)} %get-tuple-element.35, pred[8,8]{1,0:T(8,128)(4,1)S(1)} %iota_compare_fusion), kind=kLoop, calls=%fused_computation.24 | loop fusion | flops 4063232 | bytes 1114432
  45.5 4.5 %shard_map.65 = f32[1024,256]{1,0:T(8,128)} custom-call(f32[1024,1024]{1,0:T(8,128)} %get-tuple-element.19.x_ref, f32[16,1024]{1,0:T(8,128)} %get-tuple-element.36.decay_ref, f32[16,1024]{1,0:T(8,128)} %residue_ref.5, f32[16,8,1024]{2,1,0:T(8,128)} %bitcast_add_fusion.start_ref), custom_call_target="tpu_custom_call" | custom-call | tf_op jit(solution)/shard_map/pallas_call | solution.py:78
  50.0 2.4 %fusion.28 = bf16[1024,256]{1,0:T(8,128)(2,1)S(1)} fusion(bf16[1024,1024]{1,0:T(8,128)(2,1)S(1)} %get-tuple-element.34, bf16[3,1024,1024]{2,1,0:T(8,128)(2,1)} %param.6, bf16[3,2,1024]{2,1,0:T(2,128)(2,1)S(1)} %collective-permute-done, f32[256]{0:T(256)S(1)} %slice-done.2, f32[1024,256]{1,0:T(8,128)} %shard_map.65, f32[256]{0:T(256)S(1)} %bitcast.117, ...), kind=kLoop, calls=%fused_computation.52 | loop fusion | flops 6029312 | bytes 8929280 | tf_op jit(solution)/shard_map/convert_element_type | solution.py:193
  52.4 1.3 %collective-permute-start.8 = (bf16[1024,256]{1,0:T(8,128)(2,1)S(1)}, bf16[1024,256]{1,0:T(8,128)(2,1)S(1)}, u32[]{:S(2)}, u32[]{:S(2)}) collective-permute-start(bf16[1024,256]{1,0:T(8,128)(2,1)S(1)} %fusion.28), channel_id=1, source_target_pairs={{0,2},{1,3},{2,0},{3,1},{4,6},{5,7},{6,4},{7,5},{8,10},{9,11},{10,... | collective-permute-start | bytes 1572872 | tf_op jit(solution)/shard_map/ppermute | solution.py:198
  53.7 5.8 %shard_map.66 = f32[1024,384]{1,0:T(8,128)} custom-call(f32[1024,1024]{1,0:T(8,128)} %get-tuple-element.19.x_ref, f32[16,1024]{1,0:T(8,128)} %get-tuple-element.36.decay_ref, f32[16,1024]{1,0:T(8,128)} %residue_ref.5, f32[16,8,1024]{2,1,0:T(8,128)} %bitcast_add_fusion.start_ref), custom_call_target="tpu_custom_call" | custom-call | tf_op jit(solution)/shard_map/pallas_call | solution.py:78
  59.5 4.0 %fusion.20 = bf16[1024,384]{1,0:T(8,128)(2,1)} fusion(bf16[1024,1024]{1,0:T(8,128)(2,1)S(1)} %get-tuple-element.34, f32[384]{0:T(512)S(1)} %get-tuple-element.46, f32[1024,384]{1,0:T(8,128)} %shard_map.66, f32[384]{0:T(512)S(1)} %get-tuple-element.28, f32[384]{0:T(512)S(1)} %get-tuple-element.29, bf16[3,1024,1024]{2,1,0:T(8,128)(2,1)} %param.6, ...), kind=kLoop, calls=%fused_computation.38 | loop fusion | flops 9043968 | bytes 10242048 | tf_op jit(solution)/shard_map/convert_element_type | solution.py:193
  63.8 6.0 %shard_map.67 = f32[1024,384]{1,0:T(8,128)} custom-call(f32[1024,1024]{1,0:T(8,128)} %get-tuple-element.19.x_ref, f32[16,1024]{1,0:T(8,128)} %get-tuple-element.36.decay_ref, f32[16,1024]{1,0:T(8,128)} %residue_ref.5, f32[16,8,1024]{2,1,0:T(8,128)} %bitcast_add_fusion.start_ref), custom_call_target="tpu_custom_call" | custom-call | tf_op jit(solution)/shard_map/pallas_call | solution.py:78
  69.8 3.1 %fusion.24 = bf16[1024,384]{1,0:T(8,128)(2,1)S(1)} fusion(bf16[1024,1024]{1,0:T(8,128)(2,1)S(1)} %get-tuple-element.34, bf16[3,1024,1024]{2,1,0:T(8,128)(2,1)} %param.6, bf16[3,2,1024]{2,1,0:T(2,128)(2,1)S(1)} %collective-permute-done, f32[384]{0:T(512)S(1)} %get-tuple-element.47, f32[1024,384]{1,0:T(8,128)} %shard_map.67, f32[384]{0:T(512)S(1)} %get-tuple-element.31, ...), kind=kLoop, calls=%fused_computation.45 | loop fusion | flops 9043968 | bytes 10242048 | tf_op jit(solution)/shard_map/convert_element_type | solution.py:193
  72.9 1.4 %pad_maximum_fusion = bf16[1024,1024]{1,0:T(8,128)(2,1)S(1)} fusion(bf16[1024,384]{1,0:T(8,128)(2,1)S(1)} %fusion.24, bf16[1024,384]{1,0:T(8,128)(2,1)} %fusion.20, bf16[1024,256]{1,0:T(8,128)(2,1)S(1)} %fusion.28), kind=kLoop, calls=%fused_computation.30 | loop fusion | flops 6291456 | bytes 4194304 | tf_op jit(solution)/shard_map/concatenate | solution.py:221
  74.3 5.9 %collective-permute-done.10 = bf16[1024,384]{1,0:T(8,128)(2,1)} collective-permute-done((bf16[1024,384]{1,0:T(8,128)(2,1)}, bf16[1024,384]{1,0:T(8,128)(2,1)}, u32[]{:S(2)}, u32[]{:S(2)}) %collective-permute-start.10) | collective-permute-done | bytes 786464 | tf_op jit(solution)/shard_map/ppermute | solution.py:198
  80.2 3.6 %collective-permute-start.11 = (bf16[1024,1024]{1,0:T(8,128)(2,1)S(1)}, bf16[1024,1024]{1,0:T(8,128)(2,1)}, u32[]{:S(2)}, u32[]{:S(2)}) collective-permute-start(bf16[1024,1024]{1,0:T(8,128)(2,1)S(1)} %pad_maximum_fusion), channel_id=1, source_target_pairs={{0,1},{1,0},{2,3},{3,2},{4,5},{5,4},{6,7},{7,6},{8,9},{9,8},{10,11... | collective-permute-start | bytes 6291464 | tf_op jit(solution)/shard_map/ppermute | solution.py:225
  85.5 2.8 %fusion.42 = f32[1024,1024]{1,0:T(8,128)S(1)} fusion(bf16[1024,384]{1,0:T(8,128)(2,1)} %collective-permute-done.10, bf16[4096,1024]{1,0:T(8,128)(2,1)} %param.11, s32[]{:T(128)S(6)} %select_n.31), kind=kOutput, calls=%fused_computation.66 | convolution fusion | flops 805306368 | bytes 5767172 | tf_op jit(solution)/shard_map/dot_general | solution.py:218
  88.3 1.9 %fusion.48 = f32[1024,1024]{1,0:T(8,128)S(1)} fusion(bf16[1024,256]{1,0:T(8,128)(2,1)S(1)} %copy-done.2, bf16[4096,1024]{1,0:T(8,128)(2,1)} %param.11, s32[]{:T(128)S(6)} %select_n.30), kind=kOutput, calls=%fused_computation.74 | convolution fusion | flops 536870912 | bytes 5242884 | tf_op jit(solution)/shard_map/dot_general | solution.py:218
  90.6 2.3 %fusion.16 = f32[1024,1024]{1,0:T(8,128)S(1)} fusion(bf16[1024,1024]{1,0:T(8,128)(2,1)S(1)} %pad_maximum_fusion, bf16[4096,1024]{1,0:T(8,128)(2,1)S(1)} %bitcast.109, s32[]{:T(128)S(6)} %select_n.29), kind=kOutput, calls=%fused_computation.33 | convolution fusion | flops 2147483648 | bytes 8388612 | tf_op jit(solution)/shard_map/dot_general | solution.py:229
  93.7 3.9 %fusion.14 = f32[1024,1024]{1,0:T(8,128)S(1)} fusion(bf16[1024,1024]{1,0:T(8,128)(2,1)} %collective-permute-done.11, bf16[4096,1024]{1,0:T(8,128)(2,1)S(1)} %bitcast.109, s32[]{:T(128)S(6)} %select_n.32), kind=kOutput, calls=%fused_computation.31 | convolution fusion | flops 2147483648 | bytes 8388612 | tf_op jit(solution)/shard_map/dot_general | solution.py:232
  97.7 4.8 %add_add_fusion = f32[1024,1024]{1,0:T(8,128)} fusion(f32[1024,1024]{1,0:T(8,128)S(1)} %fusion.46, f32[1024,1024]{1,0:T(8,128)S(1)} %fusion.14, f32[1024,1024]{1,0:T(8,128)S(1)} %fusion.42, f32[1024,1024]{1,0:T(8,128)S(1)} %fusion.16, f32[1024,1024]{1,0:T(8,128)S(1)} %fusion.48, bf16[1024,384]{1,0:T(8,128)(2,1)S(1)} %collective-permute-done.13, ...), kind=kOutput, calls=%fused_computation.26 | convolution fusion | flops 810549248 | bytes 26738692 | tf_op jit(solution)/shard_map/dot_general | solution.py:218
  103.8 2.8 %fusion.36 = f32[1024,1024]{1,0:T(8,128)S(1)} fusion(bf16[1024,384]{1,0:T(8,128)(2,1)} %collective-permute-done.9, bf16[4096,1024]{1,0:T(8,128)(2,1)} %param.11, s32[]{:T(128)S(6)} %select_n.35), kind=kOutput, calls=%fused_computation.62 | convolution fusion | flops 805306368 | bytes 5767172 | tf_op jit(solution)/shard_map/dot_general | solution.py:218
  106.6 3.7 %add_convert_fusion = bf16[1024,1024]{1,0:T(8,128)(2,1)} fusion(f32[1024,1024]{1,0:T(8,128)S(1)} %copy-done, f32[1024,1024]{1,0:T(8,128)S(1)} %fusion.36, bf16[1024,384]{1,0:T(8,128)(2,1)S(1)} %collective-permute-done.14, bf16[4096,1024]{1,0:T(8,128)(2,1)} %param.11, s32[]{:T(128)S(6)} %select_n.36), kind=kOutput, calls=%fused_computation.25 | convolution fusion | flops 808452096 | bytes 12058628 | tf_op jit(solution)/shard_map/dot_general | solution.py:218
  (47 shorter events, 9.9 us)
Async XLA Ops:
  0.8 8.7 %collective-permute-start = (bf16[3,2,1024]{2,1,0:T(2,128)(2,1)S(1)}, bf16[3,2,1024]{2,1,0:T(2,128)(2,1)S(1)}, u32[]{:S(2)}, u32[]{:S(2)}) collective-permute-start(bf16[3,2,1024]{2,1,0:T(2,128)(2,1)S(1)} %slice.152), channel_id=1, source_target_pairs={{0,4},{4,8},{8,12},{12,16},{16,20},{20,24},{24,28},{1,5},{5,9},{9,... | collective-permute-start | bytes 36872 | tf_op jit(solution)/shard_map/ppermute | solution.py:15
  16.6 27.6 %copy-start.3 = (f32[16,1024]{1,0:T(8,128)S(1)}, f32[16,1024]{1,0:T(8,128)}, u32[]{:S(2)}) copy-start(f32[16,1024]{1,0:T(8,128)} %param.8) | copy-start | bytes 196612
  26.4 11.8 %collective-permute-start.7 = (f32[16,1024]{1,0:T(8,128)S(1)}, f32[16,1024]{1,0:T(8,128)S(1)}, u32[]{:S(2)}, u32[]{:S(2)}) collective-permute-start(f32[16,1024]{1,0:T(8,128)S(1)} %multiply_reduce_fusion.1), channel_id=1, source_target_pairs={{0,28},{1,29},{2,30},{3,31}} | collective-permute-start | bytes 196616 | tf_op jit(solution)/shard_map/ppermute | solution.py:15
  30.7 9.1 %collective-permute-start.6 = (f32[16,1024]{1,0:T(8,128)S(1)}, f32[16,1024]{1,0:T(8,128)S(1)}, u32[]{:S(2)}, u32[]{:S(2)}) collective-permute-start(f32[16,1024]{1,0:T(8,128)S(1)} %multiply_reduce_fusion.1), channel_id=1, source_target_pairs={{0,24},{4,28},{1,25},{5,29},{2,26},{6,30},{3,27},{7,31}} | collective-permute-start | bytes 196616 | tf_op jit(solution)/shard_map/ppermute | solution.py:15
  32.3 11.8 %collective-permute-start.5 = (f32[16,1024]{1,0:T(8,128)S(1)}, f32[16,1024]{1,0:T(8,128)S(1)}, u32[]{:S(2)}, u32[]{:S(2)}) collective-permute-start(f32[16,1024]{1,0:T(8,128)S(1)} %multiply_reduce_fusion.1), channel_id=1, source_target_pairs={{0,20},{4,24},{8,28},{1,21},{5,25},{9,29},{2,22},{6,26},{10,30},{3... | collective-permute-start | bytes 196616 | tf_op jit(solution)/shard_map/ppermute | solution.py:15
  33.6 10.5 %collective-permute-start.4 = (f32[16,1024]{1,0:T(8,128)S(1)}, f32[16,1024]{1,0:T(8,128)S(1)}, u32[]{:S(2)}, u32[]{:S(2)}) collective-permute-start(f32[16,1024]{1,0:T(8,128)S(1)} %multiply_reduce_fusion.1), channel_id=1, source_target_pairs={{0,16},{4,20},{8,24},{12,28},{1,17},{5,21},{9,25},{13,29},{2,18},{... | collective-permute-start | bytes 196616 | tf_op jit(solution)/shard_map/ppermute | solution.py:15
  34.9 9.2 %collective-permute-start.3 = (f32[16,1024]{1,0:T(8,128)S(1)}, f32[16,1024]{1,0:T(8,128)S(1)}, u32[]{:S(2)}, u32[]{:S(2)}) collective-permute-start(f32[16,1024]{1,0:T(8,128)S(1)} %multiply_reduce_fusion.1), channel_id=1, source_target_pairs={{0,12},{4,16},{8,20},{12,24},{16,28},{1,13},{5,17},{9,21},{13,25},... | collective-permute-start | bytes 196616 | tf_op jit(solution)/shard_map/ppermute | solution.py:15
  38.2 6.0 %collective-permute-start.2 = (f32[16,1024]{1,0:T(8,128)S(1)}, f32[16,1024]{1,0:T(8,128)S(1)}, u32[]{:S(2)}, u32[]{:S(2)}) collective-permute-start(f32[16,1024]{1,0:T(8,128)S(1)} %multiply_reduce_fusion.1), channel_id=1, source_target_pairs={{0,8},{4,12},{8,16},{12,20},{16,24},{20,28},{1,9},{5,13},{9,17},{1... | collective-permute-start | bytes 196616 | tf_op jit(solution)/shard_map/ppermute | solution.py:15
  39.8 4.4 %collective-permute-start.1 = (f32[16,1024]{1,0:T(8,128)S(1)}, f32[16,1024]{1,0:T(8,128)S(1)}, u32[]{:S(2)}, u32[]{:S(2)}) collective-permute-start(f32[16,1024]{1,0:T(8,128)S(1)} %multiply_reduce_fusion.1), channel_id=1, source_target_pairs={{0,4},{4,8},{8,12},{12,16},{16,20},{20,24},{24,28},{1,5},{5,9},{9,... | collective-permute-start | bytes 196616 | tf_op jit(solution)/shard_map/ppermute | solution.py:15
  44.1 5.9 %slice-start.2 = ((f32[1024]{0:T(1024)}), f32[256]{0:T(256)S(1)}, s32[]{:S(2)}) async-start(f32[1024]{0:T(1024)} %param.10), calls=%async_computation.2 | async-start | bytes 2048 | tf_op jit(solution)/shard_map/slice | solution.py:191
  52.4 11.3 %collective-permute-start.8 = (bf16[1024,256]{1,0:T(8,128)(2,1)S(1)}, bf16[1024,256]{1,0:T(8,128)(2,1)S(1)}, u32[]{:S(2)}, u32[]{:S(2)}) collective-permute-start(bf16[1024,256]{1,0:T(8,128)(2,1)S(1)} %fusion.28), channel_id=1, source_target_pairs={{0,2},{1,3},{2,0},{3,1},{4,6},{5,7},{6,4},{7,5},{8,10},{9,11},{10,... | collective-permute-start | bytes 1572872 | tf_op jit(solution)/shard_map/ppermute | solution.py:198
  63.5 16.7 %collective-permute-start.10 = (bf16[1024,384]{1,0:T(8,128)(2,1)}, bf16[1024,384]{1,0:T(8,128)(2,1)}, u32[]{:S(2)}, u32[]{:S(2)}) collective-permute-start(bf16[1024,384]{1,0:T(8,128)(2,1)} %fusion.20), channel_id=1, source_target_pairs={{0,2},{1,3},{2,0},{3,1},{4,6},{5,7},{6,4},{7,5},{8,10},{9,11},{10,... | collective-permute-start | bytes 2359304 | tf_op jit(solution)/shard_map/ppermute | solution.py:198
  63.8 6.0 %copy-start.1 = (bf16[1024,256]{1,0:T(8,128)(2,1)}, bf16[1024,256]{1,0:T(8,128)(2,1)S(1)}, u32[]{:S(2)}) copy-start(bf16[1024,256]{1,0:T(8,128)(2,1)S(1)} %collective-permute-done.8) | copy-start | bytes 1572868
  74.3 13.9 %copy-start.2 = (bf16[1024,256]{1,0:T(8,128)(2,1)S(1)}, bf16[1024,256]{1,0:T(8,128)(2,1)}, u32[]{:S(2)}) copy-start(bf16[1024,256]{1,0:T(8,128)(2,1)} %copy-done.1) | copy-start | bytes 1572868
  80.2 13.5 %collective-permute-start.11 = (bf16[1024,1024]{1,0:T(8,128)(2,1)S(1)}, bf16[1024,1024]{1,0:T(8,128)(2,1)}, u32[]{:S(2)}, u32[]{:S(2)}) collective-permute-start(bf16[1024,1024]{1,0:T(8,128)(2,1)S(1)} %pad_maximum_fusion), channel_id=1, source_target_pairs={{0,1},{1,0},{2,3},{3,2},{4,5},{5,4},{6,7},{7,6},{8,9},{9,8},{10,11... | collective-permute-start | bytes 6291464 | tf_op jit(solution)/shard_map/ppermute | solution.py:225
  83.8 19.3 %collective-permute-start.9 = (bf16[1024,384]{1,0:T(8,128)(2,1)S(1)}, bf16[1024,384]{1,0:T(8,128)(2,1)}, u32[]{:S(2)}, u32[]{:S(2)}) collective-permute-start(bf16[1024,384]{1,0:T(8,128)(2,1)S(1)} %fusion.24), channel_id=1, source_target_pairs={{0,2},{1,3},{2,0},{3,1},{4,6},{5,7},{6,4},{7,5},{8,10},{9,11},{10,... | collective-permute-start | bytes 2359304 | tf_op jit(solution)/shard_map/ppermute | solution.py:198
  85.0 8.0 %collective-permute-start.12 = (bf16[1024,256]{1,0:T(8,128)(2,1)}, bf16[1024,256]{1,0:T(8,128)(2,1)S(1)}, u32[]{:S(2)}, u32[]{:S(2)}) collective-permute-start(bf16[1024,256]{1,0:T(8,128)(2,1)} %copy-done.1), channel_id=1, source_target_pairs={{0,1},{1,0},{2,3},{3,2},{4,5},{5,4},{6,7},{7,6},{8,9},{9,8},{10,11... | collective-permute-start | bytes 1572872 | tf_op jit(solution)/shard_map/ppermute | solution.py:226
  85.3 12.4 %collective-permute-start.13 = (bf16[1024,384]{1,0:T(8,128)(2,1)}, bf16[1024,384]{1,0:T(8,128)(2,1)S(1)}, u32[]{:S(2)}, u32[]{:S(2)}) collective-permute-start(bf16[1024,384]{1,0:T(8,128)(2,1)} %collective-permute-done.10), channel_id=1, source_target_pairs={{0,1},{1,0},{2,3},{3,2},{4,5},{5,4},{6,7},{7,6},{8,9},{9,8},{10,11... | collective-permute-start | bytes 2359304 | tf_op jit(solution)/shard_map/ppermute | solution.py:226
  85.5 4.7 %slice-start = ((s8[8388608]{0:T(1024)(128)(4,1)}), s8[4194304]{0:T(1024)(128)(4,1)S(1)}, s32[]{:S(2)}) async-start(s8[8388608]{0:T(1024)(128)(4,1)} %bitcast.108), calls=%async_computation | async-start | bytes 8388608
  88.3 2.4 %slice-start.1 = ((s8[8388608]{0:T(1024)(128)(4,1)}), s8[4194304]{0:T(1024)(128)(4,1)S(1)}, s32[]{:S(2)}) async-start(s8[8388608]{0:T(1024)(128)(4,1)} %bitcast.108), calls=%async_computation.1 | async-start | bytes 8388608
  103.0 3.6 %collective-permute-start.14 = (bf16[1024,384]{1,0:T(8,128)(2,1)}, bf16[1024,384]{1,0:T(8,128)(2,1)S(1)}, u32[]{:S(2)}, u32[]{:S(2)}) collective-permute-start(bf16[1024,384]{1,0:T(8,128)(2,1)} %collective-permute-done.9), channel_id=1, source_target_pairs={{0,1},{1,0},{2,3},{3,2},{4,5},{5,4},{6,7},{7,6},{8,9},{9,8},{10,11... | collective-permute-start | bytes 2359304 | tf_op jit(solution)/shard_map/ppermute | solution.py:237
  103.8 2.8 %copy-start = (f32[1024,1024]{1,0:T(8,128)S(1)}, f32[1024,1024]{1,0:T(8,128)}, u32[]{:S(2)}) copy-start(f32[1024,1024]{1,0:T(8,128)} %add_add_fusion) | copy-start | bytes 12582916
